TPU v7x, 256 devices: a whole 4x4x8 slice. The times are simulated.
256 devices in a mesh: sens: 64 (over x, z_hi, y), grp: 4 (over z_lo, core).
Axes of the slice: x: 4, y: 4, z: 8 (z_hi: 4, z_lo: 2; z = z_hi * 2 + z_lo), core: 2. Of those that a mesh axis runs over, the one named last changes fastest.
Arguments:
- histories: bfloat16 [2048, 4096], P('sens', 'grp'), may hold values from -6 to 6
- bin_index: int32 [16], replicated, may hold values from 1 to 2047
- delays: int32 [2048, 4096], P('sens'), may hold values from 0 to 4095
- map_adjoint: float32 [4096], replicated, may hold values from -48 to 48
Outputs:
- history_adjoint: bfloat16 [2048, 4096], P('sens', 'grp')
Inputs may be any that keep to these rules, and one draw needn't show every extreme that they name: `delays`: each delay is already reduced modulo 4096.
All inputs are finite; a program needn't handle non-finite values.
Results may differ from a plain program's by a relative error of at most 0.0059.
Values may be sent and summed in bfloat16 or wider, within the bound.
No kernel may reach another device: no remote copies, remote signals or barrier semaphores. Data moves between devices by JAX's collectives and lax.ppermute only.
A program may use at most 64 MiB of HBM per device.

v0:
```python
import math

import jax
import jax.numpy as jnp
from jax import lax
from jax.sharding import PartitionSpec as P

NT = 4096


two_pi = 2.0 * math.pi


def grouped_transform(sample_count, bin_index, length, groups):
    sample_times = lax.iota(jnp.int32, sample_count)
    phase_index = sample_times[:, None] * bin_index[None, :] % length
    phase_angle = phase_index.astype(jnp.float32) * (two_pi / length)
    factor = 1.0 / math.sqrt(length)
    bin_width = bin_index.shape[0] // groups
    cosine = (jnp.cos(phase_angle) * factor).reshape(sample_count, groups, 1, bin_width)
    sine_part = (-jnp.sin(phase_angle) * factor).reshape(sample_count, groups, 1, bin_width)
    joined_parts = jnp.concatenate([cosine, sine_part], 2)
    return joined_parts.reshape(sample_count, 2 * bin_index.shape[0]).astype(jnp.bfloat16)


def split_halves(spectra, groups):
    row_count = spectra.shape[0]
    bin_width = spectra.shape[1] // (2 * groups)
    shaped = spectra.reshape(row_count, groups, 2, bin_width)
    return (
        shaped[:, :, 0, :].reshape(row_count, groups * bin_width),
        shaped[:, :, 1, :].reshape(row_count, groups * bin_width),
    )


def join_halves(real_part, imag_part, groups):
    row_count = real_part.shape[0]
    bin_width = real_part.shape[1] // groups
    shaped = jnp.stack(
        [
            real_part.reshape(row_count, groups, bin_width),
            imag_part.reshape(row_count, groups, bin_width),
        ],
        2,
    )
    return shaped.reshape(row_count, 2 * groups * bin_width)


def angles(bin_index, delay_block, length):
    phase_index = bin_index[:, None, None] * delay_block[None, :, :] % length
    return phase_index.astype(jnp.float32) * (two_pi / length)


def steer_forward(real_part, imag_part, delays, bin_index, length, steer_scale):
    scan_count = delays.shape[1]
    block_size = math.gcd(scan_count, 512)
    real_trans = real_part.T
    imag_trans = imag_part.T
    highest = lax.Precision.HIGHEST

    def one_block(block_index):
        delay_block = lax.dynamic_slice_in_dim(delays, block_index * block_size, block_size, 1)
        phase_angle = angles(bin_index, delay_block, length)
        cosine = jnp.cos(phase_angle)
        sine_part = jnp.sin(phase_angle)
        steer_real = jnp.einsum("fs,fsg->fg", real_trans, cosine, precision=highest) - jnp.einsum(
            "fs,fsg->fg", imag_trans, sine_part, precision=highest
        )
        steer_imag = jnp.einsum(
            "fs,fsg->fg", real_trans, sine_part, precision=highest
        ) + jnp.einsum("fs,fsg->fg", imag_trans, cosine, precision=highest)
        return (steer_real * steer_scale, steer_imag * steer_scale)

    blocks_real, blocks_imag = lax.map(
        one_block, jnp.arange(scan_count // block_size, dtype=jnp.int32)
    )
    bin_count = bin_index.shape[0]
    return (
        blocks_real.transpose(1, 0, 2).reshape(bin_count, scan_count),
        blocks_imag.transpose(1, 0, 2).reshape(bin_count, scan_count),
    )


def steer_back(bar_real, bar_imag, delays, bin_index, length, steer_scale):
    scan_count = delays.shape[1]
    block_size = math.gcd(scan_count, 512)
    highest = lax.Precision.HIGHEST

    def add_block(block_index, totals):
        delay_block = lax.dynamic_slice_in_dim(delays, block_index * block_size, block_size, 1)
        block_real = lax.dynamic_slice_in_dim(bar_real, block_index * block_size, block_size, 1)
        block_imag = lax.dynamic_slice_in_dim(bar_imag, block_index * block_size, block_size, 1)
        phase_angle = angles(bin_index, delay_block, length)
        cosine = jnp.cos(phase_angle)
        sine_part = jnp.sin(phase_angle)
        back_real = jnp.einsum("fg,fsg->fs", block_real, cosine, precision=highest) + jnp.einsum(
            "fg,fsg->fs", block_imag, sine_part, precision=highest
        )
        back_imag = jnp.einsum("fg,fsg->fs", block_imag, cosine, precision=highest) - jnp.einsum(
            "fg,fsg->fs", block_real, sine_part, precision=highest
        )
        return (totals[0] + back_real, totals[1] + back_imag)

    zeros_start = jnp.zeros((bin_index.shape[0], delays.shape[0]), jnp.float32)
    total_real, total_imag = lax.fori_loop(
        0, scan_count // block_size, add_block, (zeros_start, zeros_start)
    )
    return (total_real.T * steer_scale, total_imag.T * steer_scale)


def on_device(histories, bin_index, delays, map_adjoint):
    groups = lax.axis_size("grp")
    sensors = delays.shape[0] * lax.axis_size("sens")
    steer_scale = 1.0 / math.sqrt(sensors)
    position = lax.axis_index("grp")
    weight = 2.0 * map_adjoint[None, :]
    regrouped = lax.all_to_all(histories, "grp", split_axis=0, concat_axis=1, tiled=True)
    transform = grouped_transform(regrouped.shape[1], bin_index, NT, groups)
    spectra = jnp.dot(regrouped, transform, preferred_element_type=jnp.float32)
    real_part, imag_part = split_halves(spectra, groups)
    row_count = regrouped.shape[0]
    own_delays = lax.dynamic_slice_in_dim(delays, position * row_count, row_count, 0)
    steer_real, steer_imag = steer_forward(
        real_part, imag_part, own_delays, bin_index, NT, steer_scale
    )
    steer_real, steer_imag = lax.psum((steer_real, steer_imag), ("sens", "grp"))
    back_real, back_imag = steer_back(
        weight * steer_real, weight * steer_imag, own_delays, bin_index, NT, steer_scale
    )
    adjoint = join_halves(back_real, back_imag, groups).astype(jnp.bfloat16)
    local_part = lax.dot_general(
        adjoint, transform, (((1,), (1,)), ((), ())), preferred_element_type=jnp.float32
    ).astype(jnp.bfloat16)
    return lax.all_to_all(local_part, "grp", split_axis=1, concat_axis=0, tiled=True)


def solution(mesh):
    placed = (P("sens", "grp"), P(), P("sens", None), P())
    return jax.shard_map(
        on_device, mesh=mesh, in_specs=placed, out_specs=P("sens", "grp"), check_vma=False
    )
```

profile of v0, /device:TPU:1, one launch (start us, length us, event | category | flops | bytes accessed | tf_op | source)
XLA Modules:
  0.0 400.9 jit_solution(6123489965022852944)
XLA Ops:
  6.5 6.6 %all-to-all-start = ((bf16[4,8,1024]{2,1,0:T(8,128)(2,1)}), bf16[4,8,1024]{2,1,0:T(8,128)(2,1)S(1)}, u32[]{:S(2)}, u32[]{:S(2)}) async-start(bf16[4,8,1024]{2,1,0:T(8,128)(2,1)} %bitcast.126), calls=%async_computation | async-start | bytes 131072 | tf_op jit(solution)/shard_map/all_to_all | solution.py:117
  13.9 2.5 multiply_convert_fusion.1
  17.1 56.5 %while.32 = (s32[]{:T(128)}, f32[8,16,512]{2,1,0:T(8,128)S(1)}, f32[8,16,512]{2,1,0:T(8,128)S(1)}, s32[16]{0:T(128)S(1)}, s32[8]{0:T(128)S(1)}, /*index=5*/s32[8...) while((s32[]{:T(128)}, f32[8,16,512]{2,1,0:T(8,128)S(1)}, ...), condition=%wide.region_1.2_spmd, body=%wide.region_0.1_spmd.sunk | while | flops 6848518 | bytes 430519 | solution.py:74
  75.7 255.0 %all-reduce.3.cloned.1.call-done = (f32[16,4096]{1,0:T(8,128)}, f32[16,4096]{1,0:T(8,128)}) async-done(((f32[16,4096]{1,0:T(8,128)}, f32[16,4096]{1,0:T(8,128)}), (f32[16,4096]{1,0:T(8,128)}, f32[16,4096]{1,0:T(8,128)})) %all-reduce.3.cloned.1.call-update) | async-done | bytes 524304 | tf_op jit(solution)/shard_map/psum | solution.py:126
  331.8 53.4 %while.33 = (s32[]{:T(128)}, f32[16,8]{0,1:T(8,128)S(1)}, f32[16,8]{0,1:T(8,128)S(1)}, f32[16,4096]{1,0:T(8,128)S(1)}, s32[16]{0:T(128)S(1)}, /*index=5*/s32[8,4...) while((s32[]{:T(128)}, f32[16,8]{0,1:T(8,128)S(1)}, ...), condition=%wide.region_5.6_spmd.clone, body=%wide.region_4.5_spmd.clone.sunk | while | flops 6816519 | bytes 371118 | solution.py:105
  333.7 1.6 fusion.134
  335.4 1.6 fusion.131
  337.0 1.6 fusion.130
  340.3 1.6 fusion.134
  342.0 1.6 fusion.131
  343.7 1.6 fusion.130
  347.0 1.6 fusion.134
  348.7 1.6 fusion.131
  353.6 1.6 fusion.134
  355.3 1.6 fusion.131
  360.3 1.6 fusion.134
  362.0 1.6 fusion.131
  366.9 1.6 fusion.134
  368.6 1.6 fusion.131
  373.6 1.6 fusion.134
  375.3 1.6 fusion.131
  380.3 1.6 fusion.134
  381.9 1.6 fusion.131
  385.7 7.8 %all_to_all.38 = bf16[8,4,1024]{2,0,1:T(8,128)(2,1)S(1)} all-to-all(bf16[8,4,1024]{2,0,1:T(8,128)(2,1)S(1)} %bitcast.127), channel_id=1, replica_groups=mesh['sens'=64,'grp'=4] {'grp'}, dimensions={1} | all-to-all | bytes 131072 | tf_op jit(solution)/shard_map/all_to_all | solution.py:134
  (182 shorter events, 81.1 us)
Async XLA Ops:
  6.5 10.0 %copy-start = (s32[32,4096]{1,0:T(8,128)S(1)}, s32[32,4096]{1,0:T(8,128)}, u32[]{:S(2)}) copy-start(s32[32,4096]{1,0:T(8,128)} %param.10) | copy-start | bytes 1572868
  6.5 10.1 %all-to-all-start = ((bf16[4,8,1024]{2,1,0:T(8,128)(2,1)}), bf16[4,8,1024]{2,1,0:T(8,128)(2,1)S(1)}, u32[]{:S(2)}, u32[]{:S(2)}) async-start(bf16[4,8,1024]{2,1,0:T(8,128)(2,1)} %bitcast.126), calls=%async_computation | async-start | bytes 131072 | tf_op jit(solution)/shard_map/all_to_all | solution.py:117
  13.1 317.6 %all-reduce.3.cloned.1.call-start = ((), (), s32[]{:S(2)}) async-start(), calls=%async_computation.2 | async-start | bytes 1048576 | tf_op jit(solution)/shard_map/psum | solution.py:126
  13.1 0.7 copy-start.2
  75.0 0.7 copy-start.1
Sparse Core Ops, SparseCore 0:
  75.2 255.5 all-reduce.2
where the time goes:
time: 401 us
  waiting for transfers between devices  255 us (64%)
  matrix products  95.4 us (24%)
  between operations  13.5 us (3%)
  local copies, waits for them, and re-layouts  12.8 us (3%)
  blocking collectives  7.76 us (2%)
  starting transfers between devices  6.58 us (2%)
  loops' own time  5.9 us (1%)
  other arithmetic  4.02 us (1%)
    psum x1, waiting for transfers between devices, on_device(): steer_real, steer_imag = lax.psum((steer_real, steer_imag), ('sens', 'grp'))  255 us
    dot_general x8, matrix products, add_block(): jnp.einsum('fg,fsg->fs', block_real, cosine, precision=highest)  12.7 us
    dot_general x8, matrix products, add_block(): jnp.einsum('fg,fsg->fs', block_imag, cosine, precision=highest)  12.7 us
    dot_general x8, matrix products, add_block(): jnp.einsum('fg,fsg->fs', block_imag, sine_part, precision=highest)  12.6 us
    dot_general x8, matrix products, add_block(): jnp.einsum('fg,fsg->fs', block_real, sine_part, precision=highest)  12.5 us
    dot_general x8, matrix products, one_block(): jnp.einsum('fs,fsg->fg', real_trans, sine_part, precision=highest)  11.1 us
    dot_general x8, matrix products, one_block(): jnp.einsum('fs,fsg->fg', imag_trans, sine_part, precision=highest)  11.1 us
    dot_general x8, matrix products, one_block(): jnp.einsum('fs,fsg->fg', imag_trans, cosine, precision=highest)  11.1 us
  transfers between devices with their start and end apart: 2, of which 1 were waited for; matrix products, arithmetic and copies ran while one was open for 1% of the time, Pallas kernels for 0%

commit v1 on v0

v1 whole, which is shorter than its diff:
```python
import math

import jax
import jax.numpy as jnp
from jax import lax
from jax.sharding import PartitionSpec as P

NT = 4096

two_pi = 2.0 * math.pi


def transform_rows(first, count, bin_index, length):
    sample_times = first + lax.iota(jnp.int32, count)
    phase_index = sample_times[:, None] * bin_index[None, :] % length
    phase_angle = phase_index.astype(jnp.float32) * (two_pi / length)
    factor = 1.0 / math.sqrt(length)
    cosine = jnp.cos(phase_angle) * factor
    sine_part = -jnp.sin(phase_angle) * factor
    return jnp.concatenate([cosine, sine_part], 1).astype(jnp.bfloat16)


def on_device(histories, bin_index, delays, map_adjoint):
    groups = lax.axis_size("grp")
    position = lax.axis_index("grp")
    bins = bin_index.shape[0]
    sensors = delays.shape[0] * lax.axis_size(SENS_AXES)
    steer_scale = 1.0 / math.sqrt(sensors)
    samples = histories.shape[1]
    scan_share = delays.shape[1] // groups

    transform = transform_rows(position * samples, samples, bin_index, NT)
    spectra = jnp.dot(histories, transform, preferred_element_type=jnp.float32)
    spectra = lax.psum(spectra, "grp")
    real_t = spectra[:, :bins].T
    imag_t = spectra[:, bins:].T

    own_delays = lax.dynamic_slice_in_dim(delays, position * scan_share, scan_share, 1)
    own_weight = 2.0 * lax.dynamic_slice_in_dim(map_adjoint, position * scan_share, scan_share, 0)
    phase_index = (bin_index[:, None, None] * own_delays[None, :, :]) % NT
    phase_angle = phase_index.astype(jnp.float32) * (two_pi / NT)
    cosine = jnp.cos(phase_angle)
    sine_part = jnp.sin(phase_angle)

    steer_real = jnp.sum(real_t[:, :, None] * cosine - imag_t[:, :, None] * sine_part, axis=1)
    steer_imag = jnp.sum(real_t[:, :, None] * sine_part + imag_t[:, :, None] * cosine, axis=1)
    steered = jnp.stack([steer_real, steer_imag]) * steer_scale
    for axis in SENS_AXES[::-1]:
        steered = lax.psum(steered, axis)
    bar_real = own_weight[None, :] * steered[0]
    bar_imag = own_weight[None, :] * steered[1]

    back_real = jnp.sum(bar_real[:, None, :] * cosine + bar_imag[:, None, :] * sine_part, axis=2)
    back_imag = jnp.sum(bar_imag[:, None, :] * cosine - bar_real[:, None, :] * sine_part, axis=2)
    back = jnp.concatenate([back_real.T, back_imag.T], 1) * steer_scale
    back = jnp.sum(lax.all_gather(back, "grp"), axis=0)
    adjoint = back.astype(jnp.bfloat16)
    local_part = lax.dot_general(
        adjoint, transform, (((1,), (1,)), ((), ())), preferred_element_type=jnp.float32
    )
    return local_part.astype(jnp.bfloat16)


SENS_AXES = ("sx", "sz", "sy")


def solution(mesh):
    sens_size = mesh.shape["sens"]
    side = round(sens_size ** (1.0 / 3.0))
    assert side ** 3 == sens_size
    fine = jax.sharding.Mesh(
        mesh.devices.reshape(side, side, side, mesh.shape["grp"]), SENS_AXES + ("grp",)
    )
    placed = (P(SENS_AXES, "grp"), P(), P(SENS_AXES, None), P())
    return jax.shard_map(
        on_device, mesh=fine, in_specs=placed, out_specs=P(SENS_AXES, "grp"), check_vma=False
    )
```

time: 401 us -> 204 us (0.51)
  waiting for transfers between devices: 255 us -> 148 us
  matrix products: 95.4 us -> 1.75 us
  other arithmetic: 4.02 us -> 21.9 us
  local copies, waits for them, and re-layouts: 12.8 us -> 0.11 us
  blocking collectives: 7.76 us -> 18.8 us
  starting transfers between devices: 6.58 us -> 0.08 us
  loops' own time: 5.9 us -> 0 us
    psum x1 -> x3, waiting for transfers between devices: 255 us -> 148 us  [on_device(): steered = lax.psum(steered, axis)]
    dot_general x65 -> x1, matrix products: 95.1 us -> 0.97 us  [on_device(): spectra = jnp.dot(histories, transform, preferred_element_type=jnp.float32)]
    reduce_sum x0 -> x3, other arithmetic: none -> 18.6 us  [the longest x1 9.33 us: on_device(): jnp.sum(bar_real[:, None, :] * cosine + bar_imag[:, None, :] * sine_part,...]
    psum x0 -> x1, blocking collectives: none -> 11 us  [on_device(): spectra = lax.psum(spectra, 'grp')]
    all_gather x0 -> x1, blocking collectives: none -> 7.8 us  [on_device(): back = jnp.sum(lax.all_gather(back, 'grp'), axis=0)]
    all_to_all x1 -> x0, blocking collectives: 7.76 us -> none  [on_device(): lax.all_to_all(local_part, 'grp', split_axis=1, concat_axis=0, tiled=True)]
    all_to_all x1 -> x0, starting transfers between devices: 6.58 us -> none  [on_device(): lax.all_to_all(histories, 'grp', split_axis=0, concat_axis=1, tiled=True)]
    another operation x2 -> x0, loops' own time: 5.9 us -> none  [the longest x1 5.54 us: steer_forward(): lax.map(one_block, jnp.arange(scan_count // block_size, dtype=jnp.int32))]
  transfers between devices with their start and end apart: 2 -> 3, of which waited for: 1 -> 3; matrix products, arithmetic and copies ran while one was open for 1% -> 0% of each run, Pallas kernels for 0% -> 0%
where the time goes in v1:
time: 204 us
  waiting for transfers between devices  148 us (73%)
  other arithmetic  21.9 us (11%)
  blocking collectives  18.8 us (9%)
  between operations  13.1 us (6%)
    psum x3, waiting for transfers between devices, on_device(): steered = lax.psum(steered, axis)  148 us
    psum x1, blocking collectives, on_device(): spectra = lax.psum(spectra, 'grp')  11 us
    reduce_sum x1, other arithmetic, on_device(): jnp.sum(bar_real[:, None, :] * cosine + bar_imag[:, None, :] * sine_part,...  9.33 us
    reduce_sum x1, other arithmetic, on_device(): jnp.sum(real_t[:, :, None] * cosine - imag_t[:, :, None] * sine_part, axi...  9.27 us
    all_gather x1, blocking collectives, on_device(): back = jnp.sum(lax.all_gather(back, 'grp'), axis=0)  7.8 us
  transfers between devices with their start and end apart: 3, of which 3 were waited for; matrix products, arithmetic and copies ran while one was open for 0% of the time, Pallas kernels for 0%

profile of v1, /device:TPU:1, one launch (start us, length us, event | category | flops | bytes accessed | tf_op | source)
XLA Modules:
  0.0 203.7 jit_solution(2474051978357454061)
XLA Ops:
  6.5 0.0 copy-start
  6.5 0.0 copy-start.1
  6.5 0.0 all-reduce.4.cloned.1.call-start
  6.5 1.1 multiply_convert_fusion.1
  7.6 1.0 convolution_bitcast_fusion
  8.6 11.0 %psum.28 = f32[32,32]{0,1:T(8,128)S(1)} all-reduce(f32[32,32]{0,1:T(8,128)S(1)} %convolution_bitcast_fusion), channel_id=1, replica_groups=mesh['sx'=4,'sz'=4,'sy'=4,'grp'=4] {'grp'}, use_global_device_ids=true, to_apply=%region_0.1 | all-reduce | flops 1024 | bytes 8192 | tf_op jit(solution)/shard_map/psum | solution.py:34
  19.6 0.0 copy-done
  19.6 0.0 copy-done.1
  19.6 9.3 %subtract_reduce_fusion.1 = (f32[16,1024]{1,0:T(8,128)S(1)}, f32[16,1024]{1,0:T(8,128)S(1)}) fusion(f32[16,32]{1,0:T(8,128)S(1)} %get-tuple-element.12, s32[32,1024]{1,0:T(8,128)S(1)} %constant_dynamic-slice_fusion, s32[16]{0:T(128)S(1)} %copy-done.1, f32[16,32]{1,0:T(8,128)S(1)} %get-tuple-element.11), kind=kLoop, calls=%fused_computation.11 | loop fusion | flops 11501568 | bytes 266304 | tf_op jit(solution)/shard_map/reduce_sum | solution.py:45
  28.9 0.7 maximum_multiply_fusion
  29.6 0.0 all-reduce.4.cloned.1.call-update
  29.6 0.0 all-reduce.6.cloned.1.call-start
  29.6 48.2 %all-reduce.4.cloned.1.call-done = f32[2,16,1024]{2,1,0:T(8,128)} async-done(((f32[2,16,1024]{2,1,0:T(8,128)}), f32[2,16,1024]{2,1,0:T(8,128)}) %all-reduce.4.cloned.1.call-update) | async-done | bytes 131088 | tf_op jit(solution)/shard_map/psum | solution.py:49
  77.8 0.0 all-reduce.6.cloned.1.call-update
  77.8 0.0 all-reduce.8.cloned.1.call-start
  77.9 53.0 %all-reduce.6.cloned.1.call-done = f32[2,16,1024]{2,1,0:T(8,128)} async-done(((f32[2,16,1024]{2,1,0:T(8,128)}), f32[2,16,1024]{2,1,0:T(8,128)}) %all-reduce.6.cloned.1.call-update) | async-done | bytes 131088 | tf_op jit(solution)/shard_map/psum | solution.py:49
  130.8 0.0 all-reduce.8.cloned.1.call-update
  130.8 0.7 dynamic-slice_multiply_fusion
  131.5 46.7 %all-reduce.8.cloned.1.call-done = f32[2,16,1024]{2,1,0:T(8,128)} async-done(((f32[2,16,1024]{2,1,0:T(8,128)}), f32[2,16,1024]{2,1,0:T(8,128)}) %all-reduce.8.cloned.1.call-update) | async-done | bytes 131088 | tf_op jit(solution)/shard_map/psum | solution.py:49
  178.3 0.9 fusion.9
  179.2 9.3 %add_reduce_fusion = (f32[16,32]{1,0:T(8,128)S(1)}, f32[16,32]{1,0:T(8,128)S(1)}) fusion(f32[16,1024]{1,0:T(8,128)S(1)} %get-tuple-element.10, f32[16,1024]{1,0:T(8,128)S(1)} %get-tuple-element.9, s32[32,1024]{1,0:T(8,128)S(1)} %constant_dynamic-slice_fusion, s32[16]{0:T(128)S(1)} %copy-done.1), kind=kLoop, calls=%fused_computation.9 | loop fusion | flops 11533312 | bytes 266304 | tf_op jit(solution)/shard_map/reduce_sum | solution.py:53
  188.5 0.1 copy.5
  188.6 7.8 %all_gather.4 = f32[4,32,32]{2,1,0:T(8,128)S(1)} all-gather(f32[1,32,32]{2,1,0:T(8,128)S(1)} %copy.5), channel_id=1, replica_groups=mesh['sx'=4,'sz'=4,'sy'=4,'grp'=4] {'grp'}, dimensions={0}, use_global_device_ids=true | all-gather | bytes 20480 | tf_op jit(solution)/shard_map/all_gather | solution.py:56
  196.4 0.8 convolution_convert_fusion
  (5 shorter events, 0.0 us)
Async XLA Ops:
  6.5 13.0 %copy-start = (s32[32,4096]{1,0:T(8,128)S(1)}, s32[32,4096]{1,0:T(8,128)}, u32[]{:S(2)}) copy-start(s32[32,4096]{1,0:T(8,128)} %param.6) | copy-start | bytes 1572868
  6.5 13.1 %copy-start.1 = (s32[16]{0:T(128)S(1)}, s32[16]{0:T(128)}, u32[]{:S(2)}) copy-start(s32[16]{0:T(128)} %param.5) | copy-start | bytes 196
  6.5 71.3 %all-reduce.4.cloned.1.call-start = ((), (), s32[]{:S(2)}) async-start(), calls=%async_computation | async-start | bytes 262144 | tf_op jit(solution)/shard_map/psum | solution.py:49
  29.6 101.2 %all-reduce.6.cloned.1.call-start = ((), (), s32[]{:S(2)}) async-start(), calls=%async_computation.1 | async-start | bytes 262144 | tf_op jit(solution)/shard_map/psum | solution.py:49
  77.8 100.5 %all-reduce.8.cloned.1.call-start = ((), (), s32[]{:S(2)}) async-start(), calls=%async_computation.2 | async-start | bytes 262144 | tf_op jit(solution)/shard_map/psum | solution.py:49
Sparse Core Ops, SparseCore 0:
  29.7 48.0 all-reduce.3
  80.4 50.3 all-reduce.5
  133.1 45.1 all-reduce.7

commit v2 on v1

--- a/solution.py
+++ b/solution.py
@@ -20,6 +20,20 @@
     return jnp.concatenate([cosine, sine_part], 1).astype(jnp.bfloat16)
 
 
+def scatter_sum(x, axis):
+    count = lax.axis_size(axis)
+    parts = x.reshape(x.shape[:-1] + (count, x.shape[-1] // count))
+    parts = jnp.moveaxis(parts, -2, 0)
+    return jnp.sum(lax.all_to_all(parts, axis, 0, 0, tiled=True), axis=0)
+
+
+def gather_last(x, axis):
+    count = lax.axis_size(axis)
+    copies = jnp.broadcast_to(x[None], (count,) + x.shape)
+    joined = jnp.moveaxis(lax.all_to_all(copies, axis, 0, 0, tiled=True), 0, -2)
+    return joined.reshape(x.shape[:-1] + (count * x.shape[-1],))
+
+
 def on_device(histories, bin_index, delays, map_adjoint):
     groups = lax.axis_size("grp")
     position = lax.axis_index("grp")
@@ -31,7 +45,7 @@
 
     transform = transform_rows(position * samples, samples, bin_index, NT)
     spectra = jnp.dot(histories, transform, preferred_element_type=jnp.float32)
-    spectra = lax.psum(spectra, "grp")
+    spectra = jnp.sum(lax.all_gather(spectra, "grp"), axis=0)
     real_t = spectra[:, :bins].T
     imag_t = spectra[:, bins:].T
 
@@ -45,10 +59,16 @@
     steer_real = jnp.sum(real_t[:, :, None] * cosine - imag_t[:, :, None] * sine_part, axis=1)
     steer_imag = jnp.sum(real_t[:, :, None] * sine_part + imag_t[:, :, None] * cosine, axis=1)
     steered = jnp.stack([steer_real, steer_imag]) * steer_scale
+    offset = 0
     for axis in SENS_AXES[::-1]:
-        steered = lax.psum(steered, axis)
-    bar_real = own_weight[None, :] * steered[0]
-    bar_imag = own_weight[None, :] * steered[1]
+        steered = scatter_sum(steered, axis)
+        offset = offset * lax.axis_size(axis) + lax.axis_index(axis)
+    width = steered.shape[-1]
+    bar = lax.dynamic_slice_in_dim(own_weight, offset * width, width, 0) * steered
+    for axis in SENS_AXES:
+        bar = gather_last(bar, axis)
+    bar_real = bar[0]
+    bar_imag = bar[1]
 
     back_real = jnp.sum(bar_real[:, None, :] * cosine + bar_imag[:, None, :] * sine_part, axis=2)
     back_imag = jnp.sum(bar_imag[:, None, :] * cosine - bar_real[:, None, :] * sine_part, axis=2)

time: 204 us -> 102 us (0.50)
  waiting for transfers between devices: 148 us -> 3.4 us
  blocking collectives: 18.8 us -> 65.8 us
  between operations: 13.1 us -> 0.23 us
  starting transfers between devices: 0.08 us -> 4.01 us
  local copies, waits for them, and re-layouts: 0.11 us -> 3.13 us
    psum x3 -> x0, waiting for transfers between devices: 148 us -> none  [on_device(): steered = lax.psum(steered, axis)]
    all_to_all x0 -> x5, blocking collectives: none -> 44.7 us  [the longest x3 22.8 us: gather_last(): joined = jnp.moveaxis(lax.all_to_all(copies, axis, 0, 0, tiled=True), 0, -2)]
    psum x1 -> x0, blocking collectives: 11 us -> none  [on_device(): spectra = lax.psum(spectra, 'grp')]
    all_gather x0 -> x1, blocking collectives: none -> 8.28 us  [on_device(): spectra = jnp.sum(lax.all_gather(spectra, 'grp'), axis=0)]
    all_gather x1, blocking collectives: 7.8 us -> 12.9 us  [on_device(): back = jnp.sum(lax.all_gather(back, 'grp'), axis=0)]
    all_to_all x0 -> x1, starting transfers between devices: none -> 4.01 us  [scatter_sum(): return jnp.sum(lax.all_to_all(parts, axis, 0, 0, tiled=True), axis=0)]
    all_to_all x0 -> x1, waiting for transfers between devices: none -> 3.4 us  [scatter_sum(): return jnp.sum(lax.all_to_all(parts, axis, 0, 0, tiled=True), axis=0)]
    all_to_all x0 -> x4, other arithmetic: none -> 2.98 us  [the longest x2 1.49 us: gather_last(): joined = jnp.moveaxis(lax.all_to_all(copies, axis, 0, 0, tiled=True), 0, -2)]
  transfers between devices with their start and end apart: 3 -> 1, of which waited for: 3 -> 1; matrix products, arithmetic and copies ran while one was open for 0% -> 1% of each run, Pallas kernels for 0% -> 0%
where the time goes in v2:
time: 102 us
  blocking collectives  65.8 us (65%)
  other arithmetic  23.4 us (23%)
  starting transfers between devices  4.01 us (4%)
  waiting for transfers between devices  3.4 us (3%)
  local copies, waits for them, and re-layouts  3.13 us (3%)
  matrix products  1.75 us (2%)
    all_to_all x3, blocking collectives, gather_last(): joined = jnp.moveaxis(lax.all_to_all(copies, axis, 0, 0, tiled=True), 0, -2)  22.8 us
    all_to_all x2, blocking collectives, scatter_sum(): return jnp.sum(lax.all_to_all(parts, axis, 0, 0, tiled=True), axis=0)  21.9 us
    all_gather x1, blocking collectives, on_device(): back = jnp.sum(lax.all_gather(back, 'grp'), axis=0)  12.9 us
    reduce_sum x1, other arithmetic, on_device(): jnp.sum(bar_real[:, None, :] * cosine + bar_imag[:, None, :] * sine_part,...  9.3 us
    reduce_sum x1, other arithmetic, on_device(): jnp.sum(real_t[:, :, None] * cosine - imag_t[:, :, None] * sine_part, axi...  9.25 us
    all_gather x1, blocking collectives, on_device(): spectra = jnp.sum(lax.all_gather(spectra, 'grp'), axis=0)  8.28 us
    all_to_all x1, starting transfers between devices, scatter_sum(): return jnp.sum(lax.all_to_all(parts, axis, 0, 0, tiled=True), axis=0)  4.01 us
    all_to_all x1, waiting for transfers between devices, scatter_sum(): return jnp.sum(lax.all_to_all(parts, axis, 0, 0, tiled=True), axis=0)  3.4 us
  transfers between devices with their start and end apart: 1, of which 1 were waited for; matrix products, arithmetic and copies ran while one was open for 1% of the time, Pallas kernels for 0%

profile of v2, /device:TPU:1, one launch (start us, length us, event | category | flops | bytes accessed | tf_op | source)
XLA Modules:
  0.0 101.7 jit_solution(2493853716217837092)
XLA Ops:
  0.0 1.1 %multiply_convert_fusion.1 = (bf16[1024,16]{0,1:T(8,128)(2,1)S(1)}, bf16[1024,16]{0,1:T(8,128)(2,1)S(1)}) fusion(s32[16]{0:T(128)} %param.5, s32[1024]{0:T(1024)S(1)} %iota_add_fusion), kind=kLoop, calls=%fused_computation.28 | loop fusion | flops 311296 | bytes 69696 | tf_op jit(solution)/shard_map/convert
  1.1 1.0 convolution_bitcast_fusion
  2.1 8.3 %all-gather = f32[128,32]{1,0:T(8,128)S(1)} all-gather(f32[32,32]{1,0:T(8,128)S(1)} %copy.18), channel_id=2, replica_groups=mesh['sx'=4,'sz'=4,'sy'=4,'grp'=4] {'grp'}, dimensions={0}, use_global_device_ids=true | all-gather | bytes 20480 | tf_op jit(solution)/shard_map/all_gather | solution.py:48
  10.7 9.2 %subtract_reduce_fusion.1 = (f32[16,1024]{1,0:T(8,128)S(1)}, f32[16,1024]{1,0:T(8,128)S(1)}) fusion(f32[16,32]{1,0:T(8,128)S(1)} %bitcast.37, s32[32,1024]{1,0:T(8,128)S(1)} %constant_dynamic-slice_fusion, s32[16]{0:T(128)S(1)} %copy-done.1, f32[16,32]{1,0:T(8,128)S(1)} %bitcast.36), kind=kLoop, calls=%fused_computation.11 | loop fusion | flops 11501568 | bytes 266304 | tf_op jit(solution)/shard_map/reduce_sum | solution.py:59
  20.1 7.2 %all_to_all.30 = f32[4,2,16,256]{3,2,1,0:T(8,128)S(1)} all-to-all(f32[4,2,16,256]{3,2,1,0:T(8,128)S(1)} %copy.20), channel_id=1, replica_groups=mesh['sx'=4,'sz'=4,'sy'=4,'grp'=4] {'sy'}, dimensions={0} | all-to-all | bytes 262144 | tf_op jit(solution)/shard_map/all_to_all | solution.py:27
  27.5 14.7 %all_to_all.31 = f32[4,1,2048]{2,1,0:T(1,128)S(1)} all-to-all(f32[4,1,2048]{2,1,0:T(1,128)S(1)} %reshape.65), channel_id=1, replica_groups=mesh['sx'=4,'sz'=4,'sy'=4,'grp'=4] {'sz'}, dimensions={0} | all-to-all | bytes 65536 | tf_op jit(solution)/shard_map/all_to_all | solution.py:27
  42.2 0.6 broadcast.68
  42.8 0.8 reduce
  43.6 0.1 reshape.66
  43.8 0.7 reshape.67
  44.5 4.0 %all-to-all-start.2 = ((f32[4,1,512]{2,1,0:T(1,128)}), f32[4,1,512]{2,1,0:T(1,128)S(1)}, u32[]{:S(2)}, u32[]{:S(2)}) async-start(f32[4,1,512]{2,1,0:T(1,128)} %reshape.67), calls=%async_computation.2 | async-start | bytes 16384 | tf_op jit(solution)/shard_map/all_to_all | solution.py:27
  48.5 0.7 dynamic-slice_multiply_fusion
  49.3 3.4 %all-to-all-done.2 = f32[4,1,512]{2,1,0:T(1,128)S(1)} async-done(((f32[4,1,512]{2,1,0:T(1,128)}), f32[4,1,512]{2,1,0:T(1,128)S(1)}, u32[]{:S(2)}, u32[]{:S(2)}) %all-to-all-start.2) | async-done | bytes 8224 | tf_op jit(solution)/shard_map/all_to_all | solution.py:27
  52.7 0.7 reduce.1
  53.6 6.5 %all_to_all.32 = f32[4,1,512]{2,1,0:T(1,128)S(1)} all-to-all(f32[4,1,512]{2,1,0:T(1,128)S(1)} %reshape.69), channel_id=1, replica_groups=mesh['sx'=4,'sz'=4,'sy'=4,'grp'=4] {'sx'}, dimensions={0} | all-to-all | bytes 16384 | tf_op jit(solution)/shard_map/all_to_all | solution.py:33
  60.1 0.7 reduce.2
  61.2 9.1 %all_to_all.33 = f32[4,1,2048]{2,1,0:T(1,128)S(1)} all-to-all(f32[4,1,2048]{2,1,0:T(1,128)S(1)} %reshape.71), channel_id=1, replica_groups=mesh['sx'=4,'sz'=4,'sy'=4,'grp'=4] {'sz'}, dimensions={0} | all-to-all | bytes 65536 | tf_op jit(solution)/shard_map/all_to_all | solution.py:33
  70.3 0.8 reduce.3
  71.0 0.1 reshape.72
  71.2 0.1 broadcast_in_dim.13
  71.3 7.2 %all_to_all.34 = f32[4,2,16,256]{3,2,1,0:T(8,128)S(1)} all-to-all(f32[4,2,16,256]{3,2,1,0:T(8,128)S(1)} %broadcast_in_dim.14), channel_id=1, replica_groups=mesh['sx'=4,'sz'=4,'sy'=4,'grp'=4] {'sy'}, dimensions={0} | all-to-all | bytes 262144 | tf_op jit(solution)/shard_map/all_to_all | solution.py:33
  78.7 9.3 %add_reduce_fusion = (f32[16,32]{1,0:T(8,128)S(1)}, f32[16,32]{1,0:T(8,128)S(1)}) fusion(f32[16,1024]{1,0:T(8,128)S(1)} %bitcast.35, f32[16,1024]{1,0:T(8,128)S(1)} %bitcast.34, s32[32,1024]{1,0:T(8,128)S(1)} %constant_dynamic-slice_fusion, s32[16]{0:T(128)S(1)} %copy-done.1), kind=kLoop, calls=%fused_computation.9 | loop fusion | flops 11533312 | bytes 266304 | tf_op jit(solution)/shard_map/reduce_sum | solution.py:73
  88.1 12.9 %all_gather.12 = f32[4,32,32]{2,1,0:T(8,128)S(1)} all-gather(f32[1,32,32]{2,1,0:T(8,128)S(1)} %copy.27), channel_id=1, replica_groups=mesh['sx'=4,'sz'=4,'sy'=4,'grp'=4] {'grp'}, dimensions={0}, use_global_device_ids=true | all-gather | bytes 20480 | tf_op jit(solution)/shard_map/all_gather | solution.py:76
  101.0 0.8 convolution_convert_fusion
  (43 shorter events, 1.7 us)
Async XLA Ops:
  0.0 10.6 %copy-start = (s32[32,4096]{1,0:T(8,128)S(1)}, s32[32,4096]{1,0:T(8,128)}, u32[]{:S(2)}) copy-start(s32[32,4096]{1,0:T(8,128)} %param.6) | copy-start | bytes 1572868
  0.0 10.6 %copy-start.1 = (s32[16]{0:T(128)S(1)}, s32[16]{0:T(128)}, u32[]{:S(2)}) copy-start(s32[16]{0:T(128)} %param.5) | copy-start | bytes 196
  44.5 8.2 %all-to-all-start.2 = ((f32[4,1,512]{2,1,0:T(1,128)}), f32[4,1,512]{2,1,0:T(1,128)S(1)}, u32[]{:S(2)}, u32[]{:S(2)}) async-start(f32[4,1,512]{2,1,0:T(1,128)} %reshape.67), calls=%async_computation.2 | async-start | bytes 16384 | tf_op jit(solution)/shard_map/all_to_all | solution.py:27

commit v3 on v2

--- a/solution.py
+++ b/solution.py
@@ -22,15 +22,18 @@
 
 def scatter_sum(x, axis):
     count = lax.axis_size(axis)
-    parts = x.reshape(x.shape[:-1] + (count, x.shape[-1] // count))
-    parts = jnp.moveaxis(parts, -2, 0)
-    return jnp.sum(lax.all_to_all(parts, axis, 0, 0, tiled=True), axis=0)
+    lead = x.shape[:-1]
+    parts = x.reshape(lead + (count, x.shape[-1] // count))
+    parts = jnp.moveaxis(parts, -2, 0).reshape(count, -1)
+    total = jnp.sum(lax.all_to_all(parts, axis, 0, 0, tiled=True), axis=0)
+    return total.reshape(lead + (x.shape[-1] // count,))
 
 
 def gather_last(x, axis):
     count = lax.axis_size(axis)
-    copies = jnp.broadcast_to(x[None], (count,) + x.shape)
-    joined = jnp.moveaxis(lax.all_to_all(copies, axis, 0, 0, tiled=True), 0, -2)
+    copies = jnp.broadcast_to(x.reshape(1, -1), (count, x.size))
+    joined = lax.all_to_all(copies, axis, 0, 0, tiled=True).reshape((count,) + x.shape)
+    joined = jnp.moveaxis(joined, 0, -2)
     return joined.reshape(x.shape[:-1] + (count * x.shape[-1],))
 
 
@@ -60,13 +63,12 @@
     steer_imag = jnp.sum(real_t[:, :, None] * sine_part + imag_t[:, :, None] * cosine, axis=1)
     steered = jnp.stack([steer_real, steer_imag]) * steer_scale
     offset = 0
-    for axis in SENS_AXES[::-1]:
-        steered = scatter_sum(steered, axis)
+    for axis in SENS_AXES:
         offset = offset * lax.axis_size(axis) + lax.axis_index(axis)
+    steered = scatter_sum(steered, SENS_AXES)
     width = steered.shape[-1]
     bar = lax.dynamic_slice_in_dim(own_weight, offset * width, width, 0) * steered
-    for axis in SENS_AXES:
-        bar = gather_last(bar, axis)
+    bar = gather_last(bar, SENS_AXES)
     bar_real = bar[0]
     bar_imag = bar[1]
 

time: 102 us -> 81.2 us (0.80)
  blocking collectives: 65.8 us -> 31.6 us
  starting transfers between devices: 4.01 us -> 12.6 us
  waiting for transfers between devices: 3.4 us -> 11.2 us
  other arithmetic: 23.4 us -> 20.5 us
    all_to_all x5 -> x1, blocking collectives: 44.7 us -> 15.9 us  [gather_last(): lax.all_to_all(copies, axis, 0, 0, tiled=True).reshape((count,) + x.shape)]
    all_to_all x1, starting transfers between devices: 4.01 us -> 12.6 us  [scatter_sum(): total = jnp.sum(lax.all_to_all(parts, axis, 0, 0, tiled=True), axis=0)]
    all_to_all x1, waiting for transfers between devices: 3.4 us -> 11.2 us  [scatter_sum(): total = jnp.sum(lax.all_to_all(parts, axis, 0, 0, tiled=True), axis=0)]
    all_gather x1, blocking collectives: 12.9 us -> 7.43 us  [on_device(): back = jnp.sum(lax.all_gather(back, 'grp'), axis=0)]
    all_to_all x4 -> x0, other arithmetic: 2.98 us -> none  [the longest x2 1.49 us: gather_last(): joined = jnp.moveaxis(lax.all_to_all(copies, axis, 0, 0, tiled=True), 0, -2)]
    unnamed x16 -> x6, local copies, waits for them, and re-layouts: 1.52 us -> 0.14 us
where the time goes in v3:
time: 81.2 us; the launch traced here: 81 us
  blocking collectives  31.6 us (39%)
  other arithmetic  20.5 us (25%)
  starting transfers between devices  12.6 us (16%)
  waiting for transfers between devices  11.2 us (14%)
  local copies, waits for them, and re-layouts  3.24 us (4%)
  matrix products  1.75 us (2%)
    all_to_all x1, blocking collectives, gather_last(): lax.all_to_all(copies, axis, 0, 0, tiled=True).reshape((count,) + x.shape)  15.9 us
    all_to_all x1, starting transfers between devices, scatter_sum(): total = jnp.sum(lax.all_to_all(parts, axis, 0, 0, tiled=True), axis=0)  12.6 us
    all_to_all x1, waiting for transfers between devices, scatter_sum(): total = jnp.sum(lax.all_to_all(parts, axis, 0, 0, tiled=True), axis=0)  11.2 us
    reduce_sum x1, other arithmetic, on_device(): jnp.sum(bar_real[:, None, :] * cosine + bar_imag[:, None, :] * sine_part,...  9.3 us
    reduce_sum x1, other arithmetic, on_device(): jnp.sum(real_t[:, :, None] * cosine - imag_t[:, :, None] * sine_part, axi...  9.25 us
    all_gather x1, blocking collectives, on_device(): spectra = jnp.sum(lax.all_gather(spectra, 'grp'), axis=0)  8.28 us
    all_gather x1, blocking collectives, on_device(): back = jnp.sum(lax.all_gather(back, 'grp'), axis=0)  7.43 us
  transfers between devices with their start and end apart: 1, of which 1 were waited for; matrix products, arithmetic and copies ran while one was open for 1% of the time, Pallas kernels for 0%

profile of v3, /device:TPU:1, one launch (start us, length us, event | category | flops | bytes accessed | tf_op | source)
XLA Modules:
  0.0 81.0 jit_solution(583988358752162989)
XLA Ops:
  0.0 1.1 %multiply_convert_fusion.1 = (bf16[1024,16]{0,1:T(8,128)(2,1)S(1)}, bf16[1024,16]{0,1:T(8,128)(2,1)S(1)}) fusion(s32[16]{0:T(128)} %param.5, s32[1024]{0:T(1024)S(1)} %iota_add_fusion), kind=kLoop, calls=%fused_computation.27 | loop fusion | flops 311296 | bytes 69696 | tf_op jit(solution)/shard_map/convert
  1.1 1.0 %convolution_bitcast_fusion = f32[32,32]{0,1:T(8,128)S(1)} fusion(bf16[32,1024]{1,0:T(8,128)(2,1)} %param.4, bf16[1024,16]{0,1:T(8,128)(2,1)S(1)} %get-tuple-element.14, bf16[1024,16]{0,1:T(8,128)(2,1)S(1)} %get-tuple-element.13), kind=kOutput, calls=%fused_computation.13 | convolution fusion | flops 2228224 | bytes 135168 | tf_op jit(solution)/shard_map/dot_general | solution.py:50
  2.1 8.3 %all-gather = f32[128,32]{1,0:T(8,128)S(1)} all-gather(f32[32,32]{1,0:T(8,128)S(1)} %copy.20), channel_id=2, replica_groups=mesh['sx'=4,'sz'=4,'sy'=4,'grp'=4] {'grp'}, dimensions={0}, use_global_device_ids=true | all-gather | bytes 20480 | tf_op jit(solution)/shard_map/all_gather | solution.py:51
  10.7 9.2 %subtract_reduce_fusion.1 = (f32[16,1024]{1,0:T(8,128)S(1)}, f32[16,1024]{1,0:T(8,128)S(1)}) fusion(f32[16,32]{1,0:T(8,128)S(1)} %bitcast.27, s32[32,1024]{1,0:T(8,128)S(1)} %constant_dynamic-slice_fusion, s32[16]{0:T(128)S(1)} %copy-done.1, f32[16,32]{1,0:T(8,128)S(1)} %bitcast.26), kind=kLoop, calls=%fused_computation.11 | loop fusion | flops 11501568 | bytes 266304 | tf_op jit(solution)/shard_map/reduce_sum | solution.py:62
  19.9 0.2 stack.9
  20.1 0.2 copy.22
  20.3 0.2 stack.10
  20.5 0.2 copy.23
  20.8 0.8 copy.24
  21.5 12.6 %all-to-all-start = ((f32[64,1,512]{2,1,0:T(1,128)}), f32[64,1,512]{2,1,0:T(1,128)S(1)}, u32[]{:S(2)}, u32[]{:S(2)}) async-start(f32[64,1,512]{2,1,0:T(1,128)} %copy.24), calls=%async_computation | async-start | bytes 262144 | tf_op jit(solution)/shard_map/all_to_all | solution.py:28
  34.1 0.7 dynamic-slice_multiply_fusion
  34.8 0.1 dynamic_slice.10
  34.9 0.1 mul.165
  35.0 11.2 %all-to-all-done = f32[64,1,512]{2,1,0:T(1,128)S(1)} async-done(((f32[64,1,512]{2,1,0:T(1,128)}), f32[64,1,512]{2,1,0:T(1,128)S(1)}, u32[]{:S(2)}, u32[]{:S(2)}) %all-to-all-start) | async-done | bytes 131104 | tf_op jit(solution)/shard_map/all_to_all | solution.py:28
  46.1 0.1 reduce_sum.66
  46.3 15.9 %all_to_all.15 = f32[64,1,512]{2,1,0:T(1,128)S(1)} all-to-all(f32[64,1,512]{2,1,0:T(1,128)S(1)} %broadcast_in_dim.2), channel_id=1, replica_groups=mesh['sx'=4,'sz'=4,'sy'=4,'grp'=4] {'sx','sz','sy'}, dimensions={0} | all-to-all | bytes 262144 | tf_op jit(solution)/shard_map/all_to_all | solution.py:35
  62.2 0.1 copy.25
  62.4 0.2 copy.26
  62.6 0.3 mul.187
  62.9 0.2 copy.27
  63.1 0.3 mul.190
  63.4 9.3 %add_reduce_fusion = (f32[16,32]{1,0:T(8,128)S(1)}, f32[16,32]{1,0:T(8,128)S(1)}) fusion(f32[16,1024]{1,0:T(8,128)S(1)} %mul.190, f32[16,1024]{1,0:T(8,128)S(1)} %mul.187, s32[32,1024]{1,0:T(8,128)S(1)} %constant_dynamic-slice_fusion, s32[16]{0:T(128)S(1)} %copy-done.1), kind=kLoop, calls=%fused_computation.9 | loop fusion | flops 11533312 | bytes 266304 | tf_op jit(solution)/shard_map/reduce_sum | solution.py:75
  72.7 7.4 %all_gather.12 = f32[4,32,32]{2,1,0:T(8,128)S(1)} all-gather(f32[1,32,32]{2,1,0:T(8,128)S(1)} %copy.28), channel_id=1, replica_groups=mesh['sx'=4,'sz'=4,'sy'=4,'grp'=4] {'grp'}, dimensions={0}, use_global_device_ids=true | all-gather | bytes 20480 | tf_op jit(solution)/shard_map/all_gather | solution.py:78
  80.2 0.8 convolution_convert_fusion
  (19 shorter events, 0.6 us)
Async XLA Ops:
  0.0 10.6 %copy-start = (s32[32,4096]{1,0:T(8,128)S(1)}, s32[32,4096]{1,0:T(8,128)}, u32[]{:S(2)}) copy-start(s32[32,4096]{1,0:T(8,128)} %param.6) | copy-start | bytes 1572868
  0.0 10.6 %copy-start.1 = (s32[16]{0:T(128)S(1)}, s32[16]{0:T(128)}, u32[]{:S(2)}) copy-start(s32[16]{0:T(128)} %param.5) | copy-start | bytes 196
  21.5 24.6 %all-to-all-start = ((f32[64,1,512]{2,1,0:T(1,128)}), f32[64,1,512]{2,1,0:T(1,128)S(1)}, u32[]{:S(2)}, u32[]{:S(2)}) async-start(f32[64,1,512]{2,1,0:T(1,128)} %copy.24), calls=%async_computation | async-start | bytes 262144 | tf_op jit(solution)/shard_map/all_to_all | solution.py:28

commit v4 on v2

--- a/solution.py
+++ b/solution.py
@@ -20,18 +20,33 @@
     return jnp.concatenate([cosine, sine_part], 1).astype(jnp.bfloat16)
 
 
+def shifted(x, axis, shift):
+    count = lax.axis_size(axis)
+    return lax.ppermute(x, axis, [(j, (j + shift) % count) for j in range(count)])
+
+
 def scatter_sum(x, axis):
     count = lax.axis_size(axis)
-    parts = x.reshape(x.shape[:-1] + (count, x.shape[-1] // count))
-    parts = jnp.moveaxis(parts, -2, 0)
-    return jnp.sum(lax.all_to_all(parts, axis, 0, 0, tiled=True), axis=0)
+    me = lax.axis_index(axis)
+    lead = x.shape[:-1]
+    width = x.shape[-1] // count
+    parts = jnp.moveaxis(x.reshape(lead + (count, width)), -2, 0)
+    total = parts[me]
+    for shift in range(1, count):
+        total = total + shifted(parts[(me + shift) % count], axis, shift)
+    return total
+
+
+def gather_stack(x, axis):
+    count = lax.axis_size(axis)
+    me = lax.axis_index(axis)
+    stack = jnp.stack([x] + [shifted(x, axis, shift) for shift in range(1, count)])
+    return stack[(me - jnp.arange(count)) % count]
 
 
 def gather_last(x, axis):
-    count = lax.axis_size(axis)
-    copies = jnp.broadcast_to(x[None], (count,) + x.shape)
-    joined = jnp.moveaxis(lax.all_to_all(copies, axis, 0, 0, tiled=True), 0, -2)
-    return joined.reshape(x.shape[:-1] + (count * x.shape[-1],))
+    joined = jnp.moveaxis(gather_stack(x, axis), 0, -2)
+    return joined.reshape(x.shape[:-1] + (joined.shape[-2] * x.shape[-1],))
 
 
 def on_device(histories, bin_index, delays, map_adjoint):
@@ -45,7 +60,7 @@
 
     transform = transform_rows(position * samples, samples, bin_index, NT)
     spectra = jnp.dot(histories, transform, preferred_element_type=jnp.float32)
-    spectra = jnp.sum(lax.all_gather(spectra, "grp"), axis=0)
+    spectra = jnp.sum(gather_stack(spectra, "grp"), axis=0)
     real_t = spectra[:, :bins].T
     imag_t = spectra[:, bins:].T
 
@@ -60,12 +75,12 @@
     steer_imag = jnp.sum(real_t[:, :, None] * sine_part + imag_t[:, :, None] * cosine, axis=1)
     steered = jnp.stack([steer_real, steer_imag]) * steer_scale
     offset = 0
-    for axis in SENS_AXES[::-1]:
+    for axis in REDUCE_ORDER:
         steered = scatter_sum(steered, axis)
         offset = offset * lax.axis_size(axis) + lax.axis_index(axis)
     width = steered.shape[-1]
     bar = lax.dynamic_slice_in_dim(own_weight, offset * width, width, 0) * steered
-    for axis in SENS_AXES:
+    for axis in REDUCE_ORDER[::-1]:
         bar = gather_last(bar, axis)
     bar_real = bar[0]
     bar_imag = bar[1]
@@ -73,7 +88,7 @@
     back_real = jnp.sum(bar_real[:, None, :] * cosine + bar_imag[:, None, :] * sine_part, axis=2)
     back_imag = jnp.sum(bar_imag[:, None, :] * cosine - bar_real[:, None, :] * sine_part, axis=2)
     back = jnp.concatenate([back_real.T, back_imag.T], 1) * steer_scale
-    back = jnp.sum(lax.all_gather(back, "grp"), axis=0)
+    back = jnp.sum(gather_stack(back, "grp"), axis=0)
     adjoint = back.astype(jnp.bfloat16)
     local_part = lax.dot_general(
         adjoint, transform, (((1,), (1,)), ((), ())), preferred_element_type=jnp.float32
@@ -82,6 +97,7 @@
 
 
 SENS_AXES = ("sx", "sz", "sy")
+REDUCE_ORDER = ("sy", "sx", "sz")
 
 
 def solution(mesh):

time: 102 us -> 92.1 us (0.903)
  blocking collectives: 65.8 us -> 0 us
  starting transfers between devices: 4.01 us -> 48.2 us
  waiting for transfers between devices: 3.4 us -> 17 us
  other arithmetic: 23.4 us -> 20.5 us
    ppermute x0 -> x24, starting transfers between devices: none -> 48.2 us  [shifted(): lax.ppermute(x, axis, [(j, (j + shift) % count) for j in range(count)])]
    all_to_all x5 -> x0, blocking collectives: 44.7 us -> none  [the longest x3 22.8 us: gather_last(): joined = jnp.moveaxis(lax.all_to_all(copies, axis, 0, 0, tiled=True), 0, -2)]
    all_gather x2 -> x0, blocking collectives: 21.2 us -> none  [the longest x1 12.9 us: on_device(): back = jnp.sum(lax.all_gather(back, 'grp'), axis=0)]
    ppermute x0 -> x24, waiting for transfers between devices: none -> 17 us  [shifted(): lax.ppermute(x, axis, [(j, (j + shift) % count) for j in range(count)])]
    all_to_all x1 -> x0, starting transfers between devices: 4.01 us -> none  [scatter_sum(): return jnp.sum(lax.all_to_all(parts, axis, 0, 0, tiled=True), axis=0)]
    all_to_all x1 -> x0, waiting for transfers between devices: 3.4 us -> none  [scatter_sum(): return jnp.sum(lax.all_to_all(parts, axis, 0, 0, tiled=True), axis=0)]
    all_to_all x4 -> x0, other arithmetic: 2.98 us -> none  [the longest x2 1.49 us: gather_last(): joined = jnp.moveaxis(lax.all_to_all(copies, axis, 0, 0, tiled=True), 0, -2)]
    gather x0 -> x5, local copies, waits for them, and re-layouts: none -> 2.77 us  [gather_stack(): return stack[(me - jnp.arange(count)) % count]]
  transfers between devices with their start and end apart: 1 -> 24, of which waited for: 1 -> 19; matrix products, arithmetic and copies ran while one was open for 1% -> 1% of each run, Pallas kernels for 0% -> 0%
where the time goes in v4:
time: 92.1 us; the launch traced here: 91.9 us
  starting transfers between devices  48.2 us (52%)
  other arithmetic  20.5 us (22%)
  waiting for transfers between devices  17 us (18%)
  local copies, waits for them, and re-layouts  4 us (4%)
  matrix products  1.79 us (2%)
    ppermute x24, starting transfers between devices, shifted(): lax.ppermute(x, axis, [(j, (j + shift) % count) for j in range(count)])  48.2 us
    ppermute x24, waiting for transfers between devices, shifted(): lax.ppermute(x, axis, [(j, (j + shift) % count) for j in range(count)])  17 us
    reduce_sum x1, other arithmetic, on_device(): jnp.sum(bar_real[:, None, :] * cosine + bar_imag[:, None, :] * sine_part,...  9.3 us
    reduce_sum x1, other arithmetic, on_device(): jnp.sum(real_t[:, :, None] * cosine - imag_t[:, :, None] * sine_part, axi...  9.25 us
    gather x5, local copies, waits for them, and re-layouts, gather_stack(): return stack[(me - jnp.arange(count)) % count]  2.77 us
  transfers between devices with their start and end apart: 24, of which 19 were waited for; matrix products, arithmetic and copies ran while one was open for 1% of the time, Pallas kernels for 0%

profile of v4, /device:TPU:1, one launch (start us, length us, event | category | flops | bytes accessed | tf_op | source)
XLA Modules:
  0.0 91.9 jit_solution(12609678367873148540)
XLA Ops:
  0.0 1.1 %multiply_convert_fusion.1 = (bf16[1024,16]{0,1:T(8,128)(2,1)S(1)}, bf16[1024,16]{0,1:T(8,128)(2,1)S(1)}) fusion(s32[16]{0:T(128)} %param.5, s32[1024]{0:T(1024)S(1)} %iota_add_fusion), kind=kLoop, calls=%fused_computation.36 | loop fusion | flops 311296 | bytes 69696 | tf_op jit(solution)/shard_map/convert
  2.0 3.0 %collective-permute-start = (f32[32,32]{0,1:T(8,128)S(1)}, f32[32,32]{0,1:T(8,128)S(1)}, u32[]{:S(2)}, u32[]{:S(2)}) collective-permute-start(f32[32,32]{0,1:T(8,128)S(1)} %bitcast.91), channel_id=1, source_target_pairs={{0,1},{1,2},{2,3},{3,0},{4,5},{5,6},{6,7},{7,4},{8,9},{9,10},{10,1... | collective-permute-start | bytes 12296 | tf_op jit(solution)/shard_map/ppermute | solution.py:25
  5.1 1.5 %collective-permute-start.1 = (f32[32,32]{0,1:T(8,128)S(1)}, f32[32,32]{0,1:T(8,128)S(1)}, u32[]{:S(2)}, u32[]{:S(2)}) collective-permute-start(f32[32,32]{0,1:T(8,128)S(1)} %bitcast.92), channel_id=1, source_target_pairs={{0,2},{1,3},{2,0},{3,1},{4,6},{5,7},{6,4},{7,5},{8,10},{9,11},{10,... | collective-permute-start | bytes 12296 | tf_op jit(solution)/shard_map/ppermute | solution.py:25
  8.0 1.7 %collective-permute-done.2 = f32[32,32]{0,1:T(8,128)S(1)} collective-permute-done((f32[32,32]{0,1:T(8,128)S(1)}, f32[32,32]{0,1:T(8,128)S(1)}, u32[]{:S(2)}, u32[]{:S(2)}) %collective-permute-start.2) | collective-permute-done | bytes 4128 | tf_op jit(solution)/shard_map/ppermute | solution.py:25
  10.4 9.2 %subtract_reduce_fusion.1 = (f32[16,1024]{1,0:T(8,128)S(1)}, f32[16,1024]{1,0:T(8,128)S(1)}) fusion(f32[16,32]{1,0:T(8,128)S(1)} %get-tuple-element.24, s32[32,1024]{1,0:T(8,128)S(1)} %constant_dynamic-slice_fusion.12, s32[16]{0:T(128)S(1)} %copy-done.1, f32[16,32]{1,0:T(8,128)S(1)} %get-tuple-element.23), kind=kLoop, calls=%fused_computation.16 | loop fusion | flops 11501568 | bytes 266304 | tf_op jit(solution)/shard_map/reduce_sum | solution.py:74
  20.0 2.4 %collective-permute-start.4 = (f32[2,16,256]{2,1,0:T(8,128)S(1)}, f32[2,16,256]{2,1,0:T(8,128)S(1)}, u32[]{:S(2)}, u32[]{:S(2)}) collective-permute-start(f32[2,16,256]{2,1,0:T(8,128)S(1)} %bitcast.82), channel_id=1, source_target_pairs={{0,8},{4,12},{8,0},{12,4},{1,9},{5,13},{9,1},{13,5},{2,10},{6,14},... | collective-permute-start | bytes 98312 | tf_op jit(solution)/shard_map/ppermute | solution.py:25
  22.4 1.1 %collective-permute-start.5 = (f32[2,16,256]{2,1,0:T(8,128)S(1)}, f32[2,16,256]{2,1,0:T(8,128)S(1)}, u32[]{:S(2)}, u32[]{:S(2)}) collective-permute-start(f32[2,16,256]{2,1,0:T(8,128)S(1)} %bitcast.83), channel_id=1, source_target_pairs={{0,12},{4,0},{8,4},{12,8},{1,13},{5,1},{9,5},{13,9},{2,14},{6,2},{... | collective-permute-start | bytes 98312 | tf_op jit(solution)/shard_map/ppermute | solution.py:25
  25.5 1.2 %collective-permute-start.6 = (f32[2,16,64]{2,1,0:T(8,128)S(1)}, f32[2,16,64]{2,1,0:T(8,128)S(1)}, u32[]{:S(2)}, u32[]{:S(2)}) collective-permute-start(f32[2,16,64]{2,1,0:T(8,128)S(1)} %bitcast.100), channel_id=1, source_target_pairs={{0,64},{64,128},{128,192},{192,0},{1,65},{65,129},{129,193},{193,1... | collective-permute-start | bytes 24584 | tf_op jit(solution)/shard_map/ppermute | solution.py:25
  26.7 2.5 %collective-permute-start.7 = (f32[2,16,64]{2,1,0:T(8,128)S(1)}, f32[2,16,64]{2,1,0:T(8,128)S(1)}, u32[]{:S(2)}, u32[]{:S(2)}) collective-permute-start(f32[2,16,64]{2,1,0:T(8,128)S(1)} %bitcast.99), channel_id=1, source_target_pairs={{0,128},{64,192},{128,0},{192,64},{1,129},{65,193},{129,1},{193,65... | collective-permute-start | bytes 24584 | tf_op jit(solution)/shard_map/ppermute | solution.py:25
  29.1 1.2 %collective-permute-start.8 = (f32[2,16,64]{2,1,0:T(8,128)S(1)}, f32[2,16,64]{2,1,0:T(8,128)S(1)}, u32[]{:S(2)}, u32[]{:S(2)}) collective-permute-start(f32[2,16,64]{2,1,0:T(8,128)S(1)} %bitcast.98), channel_id=1, source_target_pairs={{0,192},{64,0},{128,64},{192,128},{1,193},{65,1},{129,65},{193,129... | collective-permute-start | bytes 24584 | tf_op jit(solution)/shard_map/ppermute | solution.py:25
  32.0 7.1 %collective-permute-start.10 = (f32[2,16,16]{2,1,0:T(8,128)S(1)}, f32[2,16,16]{2,1,0:T(8,128)S(1)}, u32[]{:S(2)}, u32[]{:S(2)}) collective-permute-start(f32[2,16,16]{2,1,0:T(8,128)S(1)} %bitcast.103), channel_id=1, source_target_pairs={{0,32},{16,48},{32,0},{48,16},{1,33},{17,49},{33,1},{49,17},{2,34}... | collective-permute-start | bytes 6152 | tf_op jit(solution)/shard_map/ppermute | solution.py:25
  39.1 2.4 %collective-permute-start.9 = (f32[2,16,16]{2,1,0:T(8,128)S(1)}, f32[2,16,16]{2,1,0:T(8,128)S(1)}, u32[]{:S(2)}, u32[]{:S(2)}) collective-permute-start(f32[2,16,16]{2,1,0:T(8,128)S(1)} %bitcast.101), channel_id=1, source_target_pairs={{0,16},{16,32},{32,48},{48,0},{1,17},{17,33},{33,49},{49,1},{2,18}... | collective-permute-start | bytes 6152 | tf_op jit(solution)/shard_map/ppermute | solution.py:25
  41.6 1.3 %collective-permute-done.11 = f32[2,16,16]{2,1,0:T(8,128)S(1)} collective-permute-done((f32[2,16,16]{2,1,0:T(8,128)S(1)}, f32[2,16,16]{2,1,0:T(8,128)S(1)}, u32[]{:S(2)}, u32[]{:S(2)}) %collective-permute-start.11) | collective-permute-done | bytes 2080 | tf_op jit(solution)/shard_map/ppermute | solution.py:25
  44.0 1.6 %collective-permute-start.12 = (f32[2,16,16]{2,1,0:T(8,128)S(1)}, f32[2,16,16]{2,1,0:T(8,128)S(1)}, u32[]{:S(2)}, u32[]{:S(2)}) collective-permute-start(f32[2,16,16]{2,1,0:T(8,128)S(1)} %add_multiply_fusion), channel_id=1, source_target_pairs={{0,16},{16,32},{32,48},{48,0},{1,17},{17,33},{33,49},{49,1},{2,18}... | collective-permute-start | bytes 6152 | tf_op jit(solution)/shard_map/ppermute | solution.py:25
  45.6 3.4 %collective-permute-start.13 = (f32[2,16,16]{2,1,0:T(8,128)S(1)}, f32[2,16,16]{2,1,0:T(8,128)S(1)}, u32[]{:S(2)}, u32[]{:S(2)}) collective-permute-start(f32[2,16,16]{2,1,0:T(8,128)S(1)} %add_multiply_fusion), channel_id=1, source_target_pairs={{0,32},{16,48},{32,0},{48,16},{1,33},{17,49},{33,1},{49,17},{2,34}... | collective-permute-start | bytes 6152 | tf_op jit(solution)/shard_map/ppermute | solution.py:25
  49.0 3.5 %collective-permute-start.14 = (f32[2,16,16]{2,1,0:T(8,128)S(1)}, f32[2,16,16]{2,1,0:T(8,128)S(1)}, u32[]{:S(2)}, u32[]{:S(2)}) collective-permute-start(f32[2,16,16]{2,1,0:T(8,128)S(1)} %add_multiply_fusion), channel_id=1, source_target_pairs={{0,48},{16,0},{32,16},{48,32},{1,49},{17,1},{33,17},{49,33},{2,50}... | collective-permute-start | bytes 6152 | tf_op jit(solution)/shard_map/ppermute | solution.py:25
  54.1 3.5 %collective-permute-start.16 = (f32[2,16,64]{2,1,0:T(8,128)S(1)}, f32[2,16,64]{2,1,0:T(8,128)S(1)}, u32[]{:S(2)}, u32[]{:S(2)}) collective-permute-start(f32[2,16,64]{2,1,0:T(8,128)S(1)} %reshape.285), channel_id=1, source_target_pairs={{0,128},{64,192},{128,0},{192,64},{1,129},{65,193},{129,1},{193,65... | collective-permute-start | bytes 24584 | tf_op jit(solution)/shard_map/ppermute | solution.py:25
  59.0 1.3 %collective-permute-done.17 = f32[2,16,64]{2,1,0:T(8,128)S(1)} collective-permute-done((f32[2,16,64]{2,1,0:T(8,128)S(1)}, f32[2,16,64]{2,1,0:T(8,128)S(1)}, u32[]{:S(2)}, u32[]{:S(2)}) %collective-permute-start.17) | collective-permute-done | bytes 8224 | tf_op jit(solution)/shard_map/ppermute | solution.py:25
  61.2 3.3 %collective-permute-start.19 = (f32[2,16,256]{2,1,0:T(8,128)S(1)}, f32[2,16,256]{2,1,0:T(8,128)S(1)}, u32[]{:S(2)}, u32[]{:S(2)}) collective-permute-start(f32[2,16,256]{2,1,0:T(8,128)S(1)} %reshape.286), channel_id=1, source_target_pairs={{0,8},{4,12},{8,0},{12,4},{1,9},{5,13},{9,1},{13,5},{2,10},{6,14},... | collective-permute-start | bytes 98312 | tf_op jit(solution)/shard_map/ppermute | solution.py:25
  65.0 1.1 %collective-permute-done.19 = f32[2,16,256]{2,1,0:T(8,128)S(1)} collective-permute-done((f32[2,16,256]{2,1,0:T(8,128)S(1)}, f32[2,16,256]{2,1,0:T(8,128)S(1)}, u32[]{:S(2)}, u32[]{:S(2)}) %collective-permute-start.19) | collective-permute-done | bytes 32800 | tf_op jit(solution)/shard_map/ppermute | solution.py:25
  66.1 1.1 %collective-permute-done.20 = f32[2,16,256]{2,1,0:T(8,128)S(1)} collective-permute-done((f32[2,16,256]{2,1,0:T(8,128)S(1)}, f32[2,16,256]{2,1,0:T(8,128)S(1)}, u32[]{:S(2)}, u32[]{:S(2)}) %collective-permute-start.20) | collective-permute-done | bytes 32800 | tf_op jit(solution)/shard_map/ppermute | solution.py:25
  68.0 9.3 %add_reduce_fusion = (f32[16,32]{1,0:T(8,128)S(1)}, f32[16,32]{1,0:T(8,128)S(1)}) fusion(f32[16,1024]{1,0:T(8,128)S(1)} %bitcast.77, f32[16,1024]{1,0:T(8,128)S(1)} %bitcast.76, s32[32,1024]{1,0:T(8,128)S(1)} %constant_dynamic-slice_fusion.12, s32[16]{0:T(128)S(1)} %copy-done.1), kind=kLoop, calls=%fused_computation.14 | loop fusion | flops 11533312 | bytes 266304 | tf_op jit(solution)/shard_map/reduce_sum | solution.py:88
  77.3 9.3 %collective-permute-start.21 = (f32[32,32]{0,1:T(8,128)S(1)}, f32[32,32]{0,1:T(8,128)S(1)}, u32[]{:S(2)}, u32[]{:S(2)}) collective-permute-start(f32[32,32]{0,1:T(8,128)S(1)} %maximum_multiply_fusion.2), channel_id=1, source_target_pairs={{0,1},{1,2},{2,3},{3,0},{4,5},{5,6},{6,7},{7,4},{8,9},{9,10},{10,1... | collective-permute-start | bytes 12296 | tf_op jit(solution)/shard_map/ppermute | solution.py:25
  87.5 2.1 %collective-permute-done.22 = f32[32,32]{0,1:T(8,128)S(1)} collective-permute-done((f32[32,32]{0,1:T(8,128)S(1)}, f32[32,32]{0,1:T(8,128)S(1)}, u32[]{:S(2)}, u32[]{:S(2)}) %collective-permute-start.22) | collective-permute-done | bytes 4128 | tf_op jit(solution)/shard_map/ppermute | solution.py:25
  (85 shorter events, 16.3 us)
Async XLA Ops:
  2.0 5.3 %collective-permute-start = (f32[32,32]{0,1:T(8,128)S(1)}, f32[32,32]{0,1:T(8,128)S(1)}, u32[]{:S(2)}, u32[]{:S(2)}) collective-permute-start(f32[32,32]{0,1:T(8,128)S(1)} %bitcast.91), channel_id=1, source_target_pairs={{0,1},{1,2},{2,3},{3,0},{4,5},{5,6},{6,7},{7,4},{8,9},{9,10},{10,1... | collective-permute-start | bytes 12296 | tf_op jit(solution)/shard_map/ppermute | solution.py:25
  5.1 3.0 %collective-permute-start.1 = (f32[32,32]{0,1:T(8,128)S(1)}, f32[32,32]{0,1:T(8,128)S(1)}, u32[]{:S(2)}, u32[]{:S(2)}) collective-permute-start(f32[32,32]{0,1:T(8,128)S(1)} %bitcast.92), channel_id=1, source_target_pairs={{0,2},{1,3},{2,0},{3,1},{4,6},{5,7},{6,4},{7,5},{8,10},{9,11},{10,... | collective-permute-start | bytes 12296 | tf_op jit(solution)/shard_map/ppermute | solution.py:25
  6.6 3.2 %collective-permute-start.2 = (f32[32,32]{0,1:T(8,128)S(1)}, f32[32,32]{0,1:T(8,128)S(1)}, u32[]{:S(2)}, u32[]{:S(2)}) collective-permute-start(f32[32,32]{0,1:T(8,128)S(1)} %bitcast.93), channel_id=1, source_target_pairs={{0,3},{1,0},{2,1},{3,2},{4,7},{5,4},{6,5},{7,6},{8,11},{9,8},{10,9... | collective-permute-start | bytes 12296 | tf_op jit(solution)/shard_map/ppermute | solution.py:25
  19.9 4.2 %collective-permute-start.3 = (f32[2,16,256]{2,1,0:T(8,128)S(1)}, f32[2,16,256]{2,1,0:T(8,128)S(1)}, u32[]{:S(2)}, u32[]{:S(2)}) collective-permute-start(f32[2,16,256]{2,1,0:T(8,128)S(1)} %bitcast.81), channel_id=1, source_target_pairs={{0,4},{4,8},{8,12},{12,0},{1,5},{5,9},{9,13},{13,1},{2,6},{6,10},{... | collective-permute-start | bytes 98312 | tf_op jit(solution)/shard_map/ppermute | solution.py:25
  20.0 5.0 %collective-permute-start.4 = (f32[2,16,256]{2,1,0:T(8,128)S(1)}, f32[2,16,256]{2,1,0:T(8,128)S(1)}, u32[]{:S(2)}, u32[]{:S(2)}) collective-permute-start(f32[2,16,256]{2,1,0:T(8,128)S(1)} %bitcast.82), channel_id=1, source_target_pairs={{0,8},{4,12},{8,0},{12,4},{1,9},{5,13},{9,1},{13,5},{2,10},{6,14},... | collective-permute-start | bytes 98312 | tf_op jit(solution)/shard_map/ppermute | solution.py:25
  22.4 2.9 %collective-permute-start.5 = (f32[2,16,256]{2,1,0:T(8,128)S(1)}, f32[2,16,256]{2,1,0:T(8,128)S(1)}, u32[]{:S(2)}, u32[]{:S(2)}) collective-permute-start(f32[2,16,256]{2,1,0:T(8,128)S(1)} %bitcast.83), channel_id=1, source_target_pairs={{0,12},{4,0},{8,4},{12,8},{1,13},{5,1},{9,5},{13,9},{2,14},{6,2},{... | collective-permute-start | bytes 98312 | tf_op jit(solution)/shard_map/ppermute | solution.py:25
  25.5 4.8 %collective-permute-start.6 = (f32[2,16,64]{2,1,0:T(8,128)S(1)}, f32[2,16,64]{2,1,0:T(8,128)S(1)}, u32[]{:S(2)}, u32[]{:S(2)}) collective-permute-start(f32[2,16,64]{2,1,0:T(8,128)S(1)} %bitcast.100), channel_id=1, source_target_pairs={{0,64},{64,128},{128,192},{192,0},{1,65},{65,129},{129,193},{193,1... | collective-permute-start | bytes 24584 | tf_op jit(solution)/shard_map/ppermute | solution.py:25
  26.7 4.1 %collective-permute-start.7 = (f32[2,16,64]{2,1,0:T(8,128)S(1)}, f32[2,16,64]{2,1,0:T(8,128)S(1)}, u32[]{:S(2)}, u32[]{:S(2)}) collective-permute-start(f32[2,16,64]{2,1,0:T(8,128)S(1)} %bitcast.99), channel_id=1, source_target_pairs={{0,128},{64,192},{128,0},{192,64},{1,129},{65,193},{129,1},{193,65... | collective-permute-start | bytes 24584 | tf_op jit(solution)/shard_map/ppermute | solution.py:25
  29.1 2.7 %collective-permute-start.8 = (f32[2,16,64]{2,1,0:T(8,128)S(1)}, f32[2,16,64]{2,1,0:T(8,128)S(1)}, u32[]{:S(2)}, u32[]{:S(2)}) collective-permute-start(f32[2,16,64]{2,1,0:T(8,128)S(1)} %bitcast.98), channel_id=1, source_target_pairs={{0,192},{64,0},{128,64},{192,128},{1,193},{65,1},{129,65},{193,129... | collective-permute-start | bytes 24584 | tf_op jit(solution)/shard_map/ppermute | solution.py:25
  32.0 9.6 %collective-permute-start.10 = (f32[2,16,16]{2,1,0:T(8,128)S(1)}, f32[2,16,16]{2,1,0:T(8,128)S(1)}, u32[]{:S(2)}, u32[]{:S(2)}) collective-permute-start(f32[2,16,16]{2,1,0:T(8,128)S(1)} %bitcast.103), channel_id=1, source_target_pairs={{0,32},{16,48},{32,0},{48,16},{1,33},{17,49},{33,1},{49,17},{2,34}... | collective-permute-start | bytes 6152 | tf_op jit(solution)/shard_map/ppermute | solution.py:25
  39.1 3.8 %collective-permute-start.11 = (f32[2,16,16]{2,1,0:T(8,128)S(1)}, f32[2,16,16]{2,1,0:T(8,128)S(1)}, u32[]{:S(2)}, u32[]{:S(2)}) collective-permute-start(f32[2,16,16]{2,1,0:T(8,128)S(1)} %bitcast.102), channel_id=1, source_target_pairs={{0,48},{16,0},{32,16},{48,32},{1,49},{17,1},{33,17},{49,33},{2,50}... | collective-permute-start | bytes 6152 | tf_op jit(solution)/shard_map/ppermute | solution.py:25
  39.1 4.8 %collective-permute-start.9 = (f32[2,16,16]{2,1,0:T(8,128)S(1)}, f32[2,16,16]{2,1,0:T(8,128)S(1)}, u32[]{:S(2)}, u32[]{:S(2)}) collective-permute-start(f32[2,16,16]{2,1,0:T(8,128)S(1)} %bitcast.101), channel_id=1, source_target_pairs={{0,16},{16,32},{32,48},{48,0},{1,17},{17,33},{33,49},{49,1},{2,18}... | collective-permute-start | bytes 6152 | tf_op jit(solution)/shard_map/ppermute | solution.py:25
  44.0 8.5 %collective-permute-start.12 = (f32[2,16,16]{2,1,0:T(8,128)S(1)}, f32[2,16,16]{2,1,0:T(8,128)S(1)}, u32[]{:S(2)}, u32[]{:S(2)}) collective-permute-start(f32[2,16,16]{2,1,0:T(8,128)S(1)} %add_multiply_fusion), channel_id=1, source_target_pairs={{0,16},{16,32},{32,48},{48,0},{1,17},{17,33},{33,49},{49,1},{2,18}... | collective-permute-start | bytes 6152 | tf_op jit(solution)/shard_map/ppermute | solution.py:25
  45.6 6.9 %collective-permute-start.13 = (f32[2,16,16]{2,1,0:T(8,128)S(1)}, f32[2,16,16]{2,1,0:T(8,128)S(1)}, u32[]{:S(2)}, u32[]{:S(2)}) collective-permute-start(f32[2,16,16]{2,1,0:T(8,128)S(1)} %add_multiply_fusion), channel_id=1, source_target_pairs={{0,32},{16,48},{32,0},{48,16},{1,33},{17,49},{33,1},{49,17},{2,34}... | collective-permute-start | bytes 6152 | tf_op jit(solution)/shard_map/ppermute | solution.py:25
  49.0 4.3 %collective-permute-start.14 = (f32[2,16,16]{2,1,0:T(8,128)S(1)}, f32[2,16,16]{2,1,0:T(8,128)S(1)}, u32[]{:S(2)}, u32[]{:S(2)}) collective-permute-start(f32[2,16,16]{2,1,0:T(8,128)S(1)} %add_multiply_fusion), channel_id=1, source_target_pairs={{0,48},{16,0},{32,16},{48,32},{1,49},{17,1},{33,17},{49,33},{2,50}... | collective-permute-start | bytes 6152 | tf_op jit(solution)/shard_map/ppermute | solution.py:25
  54.0 3.9 %collective-permute-start.15 = (f32[2,16,64]{2,1,0:T(8,128)S(1)}, f32[2,16,64]{2,1,0:T(8,128)S(1)}, u32[]{:S(2)}, u32[]{:S(2)}) collective-permute-start(f32[2,16,64]{2,1,0:T(8,128)S(1)} %reshape.285), channel_id=1, source_target_pairs={{0,64},{64,128},{128,192},{192,0},{1,65},{65,129},{129,193},{193,1... | collective-permute-start | bytes 24584 | tf_op jit(solution)/shard_map/ppermute | solution.py:25
  54.1 4.8 %collective-permute-start.16 = (f32[2,16,64]{2,1,0:T(8,128)S(1)}, f32[2,16,64]{2,1,0:T(8,128)S(1)}, u32[]{:S(2)}, u32[]{:S(2)}) collective-permute-start(f32[2,16,64]{2,1,0:T(8,128)S(1)} %reshape.285), channel_id=1, source_target_pairs={{0,128},{64,192},{128,0},{192,64},{1,129},{65,193},{129,1},{193,65... | collective-permute-start | bytes 24584 | tf_op jit(solution)/shard_map/ppermute | solution.py:25
  57.7 2.6 %collective-permute-start.17 = (f32[2,16,64]{2,1,0:T(8,128)S(1)}, f32[2,16,64]{2,1,0:T(8,128)S(1)}, u32[]{:S(2)}, u32[]{:S(2)}) collective-permute-start(f32[2,16,64]{2,1,0:T(8,128)S(1)} %reshape.285), channel_id=1, source_target_pairs={{0,192},{64,0},{128,64},{192,128},{1,193},{65,1},{129,65},{193,129... | collective-permute-start | bytes 24584 | tf_op jit(solution)/shard_map/ppermute | solution.py:25
  61.0 4.0 %collective-permute-start.18 = (f32[2,16,256]{2,1,0:T(8,128)S(1)}, f32[2,16,256]{2,1,0:T(8,128)S(1)}, u32[]{:S(2)}, u32[]{:S(2)}) collective-permute-start(f32[2,16,256]{2,1,0:T(8,128)S(1)} %reshape.286), channel_id=1, source_target_pairs={{0,4},{4,8},{8,12},{12,0},{1,5},{5,9},{9,13},{13,1},{2,6},{6,10},{... | collective-permute-start | bytes 98312 | tf_op jit(solution)/shard_map/ppermute | solution.py:25
  61.2 4.9 %collective-permute-start.19 = (f32[2,16,256]{2,1,0:T(8,128)S(1)}, f32[2,16,256]{2,1,0:T(8,128)S(1)}, u32[]{:S(2)}, u32[]{:S(2)}) collective-permute-start(f32[2,16,256]{2,1,0:T(8,128)S(1)} %reshape.286), channel_id=1, source_target_pairs={{0,8},{4,12},{8,0},{12,4},{1,9},{5,13},{9,1},{13,5},{2,10},{6,14},... | collective-permute-start | bytes 98312 | tf_op jit(solution)/shard_map/ppermute | solution.py:25
  64.5 2.8 %collective-permute-start.20 = (f32[2,16,256]{2,1,0:T(8,128)S(1)}, f32[2,16,256]{2,1,0:T(8,128)S(1)}, u32[]{:S(2)}, u32[]{:S(2)}) collective-permute-start(f32[2,16,256]{2,1,0:T(8,128)S(1)} %reshape.286), channel_id=1, source_target_pairs={{0,12},{4,0},{8,4},{12,8},{1,13},{5,1},{9,5},{13,9},{2,14},{6,2},{... | collective-permute-start | bytes 98312 | tf_op jit(solution)/shard_map/ppermute | solution.py:25
  77.3 10.2 %collective-permute-start.21 = (f32[32,32]{0,1:T(8,128)S(1)}, f32[32,32]{0,1:T(8,128)S(1)}, u32[]{:S(2)}, u32[]{:S(2)}) collective-permute-start(f32[32,32]{0,1:T(8,128)S(1)} %maximum_multiply_fusion.2), channel_id=1, source_target_pairs={{0,1},{1,2},{2,3},{3,0},{4,5},{5,6},{6,7},{7,4},{8,9},{9,10},{10,1... | collective-permute-start | bytes 12296 | tf_op jit(solution)/shard_map/ppermute | solution.py:25
  86.6 3.0 %collective-permute-start.22 = (f32[32,32]{0,1:T(8,128)S(1)}, f32[32,32]{0,1:T(8,128)S(1)}, u32[]{:S(2)}, u32[]{:S(2)}) collective-permute-start(f32[32,32]{0,1:T(8,128)S(1)} %maximum_multiply_fusion.2), channel_id=1, source_target_pairs={{0,2},{1,3},{2,0},{3,1},{4,6},{5,7},{6,4},{7,5},{8,10},{9,11},{10,... | collective-permute-start | bytes 12296 | tf_op jit(solution)/shard_map/ppermute | solution.py:25
  87.4 3.2 %collective-permute-start.23 = (f32[32,32]{0,1:T(8,128)S(1)}, f32[32,32]{0,1:T(8,128)S(1)}, u32[]{:S(2)}, u32[]{:S(2)}) collective-permute-start(f32[32,32]{0,1:T(8,128)S(1)} %maximum_multiply_fusion.2), channel_id=1, source_target_pairs={{0,3},{1,0},{2,1},{3,2},{4,7},{5,4},{6,5},{7,6},{8,11},{9,8},{10,9... | collective-permute-start | bytes 12296 | tf_op jit(solution)/shard_map/ppermute | solution.py:25
  (2 other events, 17.0 us)

commit v5 on v3

--- a/solution.py
+++ b/solution.py
@@ -18,6 +18,36 @@
     cosine = jnp.cos(phase_angle) * factor
     sine_part = -jnp.sin(phase_angle) * factor
     return jnp.concatenate([cosine, sine_part], 1).astype(jnp.bfloat16)
+
+
+def circle_point(phase_index, length):
+    quarter = length // 4
+    eighth = length // 8
+    quadrant = phase_index // quarter
+    rest = phase_index - quadrant * quarter
+    flip = rest > eighth
+    folded = jnp.where(flip, quarter - rest, rest)
+    x = folded.astype(jnp.float32) * (two_pi / length)
+    x2 = x * x
+    sin_x = x * (1.0 + x2 * (-1.0 / 6.0 + x2 * (1.0 / 120.0 + x2 * (-1.0 / 5040.0))))
+    cos_x = 1.0 + x2 * (-0.5 + x2 * (1.0 / 24.0 + x2 * (-1.0 / 720.0 + x2 * (1.0 / 40320.0))))
+    sin_r = jnp.where(flip, cos_x, sin_x)
+    cos_r = jnp.where(flip, sin_x, cos_x)
+    sine = jnp.where(quadrant == 0, sin_r, jnp.where(quadrant == 1, cos_r, jnp.where(quadrant == 2, -sin_r, -cos_r)))
+    cosine = jnp.where(quadrant == 0, cos_r, jnp.where(quadrant == 1, -sin_r, jnp.where(quadrant == 2, -cos_r, sin_r)))
+    return cosine, sine
+
+
+def shifted(x, axis, shift):
+    count = lax.axis_size(axis)
+    return lax.ppermute(x, axis, [(j, (j + shift) % count) for j in range(count)])
+
+
+def gather_stack(x, axis):
+    count = lax.axis_size(axis)
+    me = lax.axis_index(axis)
+    stack = jnp.stack([x] + [shifted(x, axis, shift) for shift in range(1, count)])
+    return stack[(me - jnp.arange(count)) % count]
 
 
 def scatter_sum(x, axis):
@@ -48,16 +78,14 @@
 
     transform = transform_rows(position * samples, samples, bin_index, NT)
     spectra = jnp.dot(histories, transform, preferred_element_type=jnp.float32)
-    spectra = jnp.sum(lax.all_gather(spectra, "grp"), axis=0)
+    spectra = jnp.sum(gather_stack(spectra, "grp"), axis=0)
     real_t = spectra[:, :bins].T
     imag_t = spectra[:, bins:].T
 
     own_delays = lax.dynamic_slice_in_dim(delays, position * scan_share, scan_share, 1)
     own_weight = 2.0 * lax.dynamic_slice_in_dim(map_adjoint, position * scan_share, scan_share, 0)
     phase_index = (bin_index[:, None, None] * own_delays[None, :, :]) % NT
-    phase_angle = phase_index.astype(jnp.float32) * (two_pi / NT)
-    cosine = jnp.cos(phase_angle)
-    sine_part = jnp.sin(phase_angle)
+    cosine, sine_part = lax.optimization_barrier(circle_point(phase_index, NT))
 
     steer_real = jnp.sum(real_t[:, :, None] * cosine - imag_t[:, :, None] * sine_part, axis=1)
     steer_imag = jnp.sum(real_t[:, :, None] * sine_part + imag_t[:, :, None] * cosine, axis=1)
@@ -75,7 +103,7 @@
     back_real = jnp.sum(bar_real[:, None, :] * cosine + bar_imag[:, None, :] * sine_part, axis=2)
     back_imag = jnp.sum(bar_imag[:, None, :] * cosine - bar_real[:, None, :] * sine_part, axis=2)
     back = jnp.concatenate([back_real.T, back_imag.T], 1) * steer_scale
-    back = jnp.sum(lax.all_gather(back, "grp"), axis=0)
+    back = jnp.sum(gather_stack(back, "grp"), axis=0)
     adjoint = back.astype(jnp.bfloat16)
     local_part = lax.dot_general(
         adjoint, transform, (((1,), (1,)), ((), ())), preferred_element_type=jnp.float32

time: 81.2 us -> 71.7 us (0.88)
  blocking collectives: 31.6 us -> 15.7 us
  starting transfers between devices: 12.6 us -> 22.3 us
  other arithmetic: 20.5 us -> 13.7 us
  waiting for transfers between devices: 11.2 us -> 13.7 us
    all_gather x2 -> x0, blocking collectives: 15.7 us -> none  [the longest x1 8.28 us: on_device(): spectra = jnp.sum(lax.all_gather(spectra, 'grp'), axis=0)]
    ppermute x0 -> x6, starting transfers between devices: none -> 9.76 us  [shifted(): lax.ppermute(x, axis, [(j, (j + shift) % count) for j in range(count)])]
    reduce_sum x1, other arithmetic: 9.3 us -> 2.32 us  [on_device(): jnp.sum(bar_real[:, None, :] * cosine + bar_imag[:, None, :] * sine_part,...]
    select_n x0 -> x2, other arithmetic: none -> 6.29 us  [the longest x1 6.27 us: circle_point(): jnp.where(quadrant == 0, sin_r, jnp.where(quadrant == 1, cos_r, jnp.where...]
    reduce_sum x1, other arithmetic: 9.25 us -> 3.07 us  [on_device(): jnp.sum(real_t[:, :, None] * cosine - imag_t[:, :, None] * sine_part, axi...]
    ppermute x0 -> x6, waiting for transfers between devices: none -> 3.16 us  [shifted(): lax.ppermute(x, axis, [(j, (j + shift) % count) for j in range(count)])]
    gather x0 -> x2, local copies, waits for them, and re-layouts: none -> 1.11 us  [gather_stack(): return stack[(me - jnp.arange(count)) % count]]
  transfers between devices with their start and end apart: 1 -> 7, of which waited for: 1 -> 4; matrix products, arithmetic and copies ran while one was open for 1% -> 10% of each run, Pallas kernels for 0% -> 0%
where the time goes in v5:
time: 71.7 us; the launch traced here: 71.4 us
  starting transfers between devices  22.3 us (31%)
  blocking collectives  15.7 us (22%)
  other arithmetic  13.7 us (19%)
  waiting for transfers between devices  13.7 us (19%)
  local copies, waits for them, and re-layouts  4.01 us (6%)
  matrix products  1.79 us (2%)
    all_to_all x1, blocking collectives, gather_last(): lax.all_to_all(copies, axis, 0, 0, tiled=True).reshape((count,) + x.shape)  15.7 us
    all_to_all x1, starting transfers between devices, scatter_sum(): total = jnp.sum(lax.all_to_all(parts, axis, 0, 0, tiled=True), axis=0)  12.6 us
    all_to_all x1, waiting for transfers between devices, scatter_sum(): total = jnp.sum(lax.all_to_all(parts, axis, 0, 0, tiled=True), axis=0)  10.6 us
    ppermute x6, starting transfers between devices, shifted(): lax.ppermute(x, axis, [(j, (j + shift) % count) for j in range(count)])  9.76 us
    select_n x1, other arithmetic, circle_point(): jnp.where(quadrant == 0, sin_r, jnp.where(quadrant == 1, cos_r, jnp.where...  6.27 us
    ppermute x6, waiting for transfers between devices, shifted(): lax.ppermute(x, axis, [(j, (j + shift) % count) for j in range(count)])  3.16 us
    reduce_sum x1, other arithmetic, on_device(): jnp.sum(real_t[:, :, None] * cosine - imag_t[:, :, None] * sine_part, axi...  3.07 us
    reduce_sum x1, other arithmetic, on_device(): jnp.sum(bar_real[:, None, :] * cosine + bar_imag[:, None, :] * sine_part,...  2.32 us
  transfers between devices with their start and end apart: 7, of which 4 were waited for; matrix products, arithmetic and copies ran while one was open for 10% of the time, Pallas kernels for 0%

profile of v5, /device:TPU:1, one launch (start us, length us, event | category | flops | bytes accessed | tf_op | source)
XLA Modules:
  0.0 71.4 jit_solution(12655530483350000812)
XLA Ops:
  0.0 1.1 %multiply_convert_fusion.1 = (bf16[1024,16]{0,1:T(8,128)(2,1)S(1)}, bf16[1024,16]{0,1:T(8,128)(2,1)S(1)}) fusion(s32[16]{0:T(128)} %param.5, s32[1024]{0:T(1024)S(1)} %iota_add_fusion), kind=kLoop, calls=%fused_computation.49 | loop fusion | flops 311296 | bytes 69696 | tf_op jit(solution)/shard_map/convert
  1.1 1.0 %fusion.11 = f32[32,32]{1,0:T(8,128)S(1)} fusion(bf16[32,1024]{1,0:T(8,128)(2,1)} %param.4, bf16[1024,16]{0,1:T(8,128)(2,1)S(1)} %get-tuple-element.20, bf16[1024,16]{0,1:T(8,128)(2,1)S(1)} %get-tuple-element.19), kind=kOutput, calls=%fused_computation.50 | convolution fusion | flops 2228224 | bytes 135168 | tf_op jit(solution)/shard_map/dot_general | solution.py:80
  2.0 3.0 %collective-permute-start = (f32[32,32]{0,1:T(8,128)S(1)}, f32[32,32]{0,1:T(8,128)S(1)}, u32[]{:S(2)}, u32[]{:S(2)}) collective-permute-start(f32[32,32]{0,1:T(8,128)S(1)} %bitcast.39), channel_id=1, source_target_pairs={{0,1},{1,2},{2,3},{3,0},{4,5},{5,6},{6,7},{7,4},{8,9},{9,10},{10,1... | collective-permute-start | bytes 12296 | tf_op jit(solution)/shard_map/ppermute | solution.py:43
  5.1 1.5 %collective-permute-start.1 = (f32[32,32]{0,1:T(8,128)S(1)}, f32[32,32]{0,1:T(8,128)S(1)}, u32[]{:S(2)}, u32[]{:S(2)}) collective-permute-start(f32[32,32]{0,1:T(8,128)S(1)} %bitcast.40), channel_id=1, source_target_pairs={{0,2},{1,3},{2,0},{3,1},{4,6},{5,7},{6,4},{7,5},{8,10},{9,11},{10,... | collective-permute-start | bytes 12296 | tf_op jit(solution)/shard_map/ppermute | solution.py:43
  6.7 6.3 %select_select_fusion = (f32[16,32,1024]{2,1,0:T(8,128)S(1)}, f32[16,32,1024]{2,1,0:T(8,128)}) fusion(s32[32,1024]{1,0:T(8,128)S(1)} %constant_dynamic-slice_fusion, s32[16]{0:T(128)} %param.5), kind=kLoop, calls=%fused_computation.20 | loop fusion | flops 33030144 | bytes 4325440 | tf_op jit(solution)/shard_map/jit(_where)/select_n | solution.py:36
  13.0 0.6 gather_fusion
  13.6 3.1 %subtract_reduce_fusion.1 = (f32[16,1024]{1,0:T(8,128)S(1)}, f32[16,1024]{1,0:T(8,128)S(1)}) fusion(f32[16,32,1024]{2,1,0:T(8,128)S(1)} %get-tuple-element.8, f32[16,32,1024]{2,1,0:T(8,128)} %get-tuple-element.7, f32[16,32]{1,0:T(8,128)S(1)} %get-tuple-element.18, f32[16,32]{1,0:T(8,128)S(1)} %get-tuple-element.17), kind=kLoop, calls=%fused_computation.19 | loop fusion | flops 4161536 | bytes 4329472 | tf_op jit(solution)/shard_map/reduce_sum | solution.py:90
  16.7 0.2 stack.42
  17.0 0.2 stack.43
  17.5 0.8 %copy.20 = f32[64,1,512]{2,1,0:T(1,128)} copy(f32[64,1,512]{0,2,1:T(8,128)S(1)} %bitcast.34) | data formatting | bytes 262144 | tf_op jit(solution)/shard_map/all_to_all | solution.py:58
  18.3 12.6 %all-to-all-start = ((f32[64,1,512]{2,1,0:T(1,128)}), f32[64,1,512]{2,1,0:T(1,128)S(1)}, u32[]{:S(2)}, u32[]{:S(2)}) async-start(f32[64,1,512]{2,1,0:T(1,128)} %copy.20), calls=%async_computation | async-start | bytes 262144 | tf_op jit(solution)/shard_map/all_to_all | solution.py:58
  30.9 0.7 dynamic-slice_multiply_fusion
  31.7 10.6 %all-to-all-done = f32[64,1,512]{2,1,0:T(1,128)S(1)} async-done(((f32[64,1,512]{2,1,0:T(1,128)}), f32[64,1,512]{2,1,0:T(1,128)S(1)}, u32[]{:S(2)}, u32[]{:S(2)}) %all-to-all-start) | async-done | bytes 131104 | tf_op jit(solution)/shard_map/all_to_all | solution.py:58
  42.5 15.7 %all_to_all.15 = f32[64,1,512]{2,1,0:T(1,128)S(1)} all-to-all(f32[64,1,512]{2,1,0:T(1,128)S(1)} %broadcast_in_dim.2), channel_id=1, replica_groups=mesh['sx'=4,'sz'=4,'sy'=4,'grp'=4] {'sx','sz','sy'}, dimensions={0} | all-to-all | bytes 262144 | tf_op jit(solution)/shard_map/all_to_all | solution.py:65
  58.5 0.3 mul.239
  58.8 0.2 copy.23
  59.0 0.3 mul.242
  59.3 2.3 %add_reduce_fusion = (f32[16,32]{1,0:T(8,128)S(1)}, f32[16,32]{1,0:T(8,128)S(1)}) fusion(f32[16,32,1024]{2,1,0:T(8,128)S(1)} %get-tuple-element.8, f32[16,32,1024]{2,1,0:T(8,128)} %get-tuple-element.7, f32[16,1024]{1,0:T(8,128)S(1)} %mul.242, f32[16,1024]{1,0:T(8,128)S(1)} %mul.239), kind=kLoop, calls=%fused_computation.17 | loop fusion | flops 4193280 | bytes 4329472 | tf_op jit(solution)/shard_map/reduce_sum | solution.py:103
  61.6 4.4 %collective-permute-start.3 = (f32[32,32]{0,1:T(8,128)S(1)}, f32[32,32]{0,1:T(8,128)S(1)}, u32[]{:S(2)}, u32[]{:S(2)}) collective-permute-start(f32[32,32]{0,1:T(8,128)S(1)} %maximum_multiply_fusion.2), channel_id=1, source_target_pairs={{0,1},{1,2},{2,3},{3,0},{4,5},{5,6},{6,7},{7,4},{8,9},{9,10},{10,1... | collective-permute-start | bytes 12296 | tf_op jit(solution)/shard_map/ppermute | solution.py:43
  66.0 0.8 %collective-permute-start.4 = (f32[32,32]{0,1:T(8,128)S(1)}, f32[32,32]{0,1:T(8,128)S(1)}, u32[]{:S(2)}, u32[]{:S(2)}) collective-permute-start(f32[32,32]{0,1:T(8,128)S(1)} %maximum_multiply_fusion.2), channel_id=1, source_target_pairs={{0,2},{1,3},{2,0},{3,1},{4,6},{5,7},{6,4},{7,5},{8,10},{9,11},{10,... | collective-permute-start | bytes 12296 | tf_op jit(solution)/shard_map/ppermute | solution.py:43
  66.9 2.2 %collective-permute-done.4 = f32[32,32]{0,1:T(8,128)S(1)} collective-permute-done((f32[32,32]{0,1:T(8,128)S(1)}, f32[32,32]{0,1:T(8,128)S(1)}, u32[]{:S(2)}, u32[]{:S(2)}) %collective-permute-start.4) | collective-permute-done | bytes 4128 | tf_op jit(solution)/shard_map/ppermute | solution.py:43
  69.0 0.9 %collective-permute-done.5 = f32[32,32]{0,1:T(8,128)S(1)} collective-permute-done((f32[32,32]{0,1:T(8,128)S(1)}, f32[32,32]{0,1:T(8,128)S(1)}, u32[]{:S(2)}, u32[]{:S(2)}) %collective-permute-start.5) | collective-permute-done | bytes 4128 | tf_op jit(solution)/shard_map/ppermute | solution.py:43
  70.0 0.6 gather_fusion.1
  70.5 0.8 %convolution_convert_fusion = bf16[32,1024]{1,0:T(8,128)(2,1)} fusion(bf16[1024,16]{0,1:T(8,128)(2,1)S(1)} %get-tuple-element.20, bf16[1024,16]{0,1:T(8,128)(2,1)S(1)} %get-tuple-element.19, bf16[32,32]{0,1:T(8,128)(2,1)S(1)} %reduce_sum.69), kind=kOutput, calls=%fused_computation.29 | convolution fusion | flops 2260992 | bytes 133120 | tf_op jit(solution)/shard_map/dot_general | solution.py:108
  (31 shorter events, 1.3 us)
Async XLA Ops:
  0.0 6.6 %copy-start = (s32[32,4096]{1,0:T(8,128)S(1)}, s32[32,4096]{1,0:T(8,128)}, u32[]{:S(2)}) copy-start(s32[32,4096]{1,0:T(8,128)} %param.6) | copy-start | bytes 1572868
  2.0 10.9 %collective-permute-start = (f32[32,32]{0,1:T(8,128)S(1)}, f32[32,32]{0,1:T(8,128)S(1)}, u32[]{:S(2)}, u32[]{:S(2)}) collective-permute-start(f32[32,32]{0,1:T(8,128)S(1)} %bitcast.39), channel_id=1, source_target_pairs={{0,1},{1,2},{2,3},{3,0},{4,5},{5,6},{6,7},{7,4},{8,9},{9,10},{10,1... | collective-permute-start | bytes 12296 | tf_op jit(solution)/shard_map/ppermute | solution.py:43
  5.1 7.9 %collective-permute-start.1 = (f32[32,32]{0,1:T(8,128)S(1)}, f32[32,32]{0,1:T(8,128)S(1)}, u32[]{:S(2)}, u32[]{:S(2)}) collective-permute-start(f32[32,32]{0,1:T(8,128)S(1)} %bitcast.40), channel_id=1, source_target_pairs={{0,2},{1,3},{2,0},{3,1},{4,6},{5,7},{6,4},{7,5},{8,10},{9,11},{10,... | collective-permute-start | bytes 12296 | tf_op jit(solution)/shard_map/ppermute | solution.py:43
  6.6 6.4 %collective-permute-start.2 = (f32[32,32]{0,1:T(8,128)S(1)}, f32[32,32]{0,1:T(8,128)S(1)}, u32[]{:S(2)}, u32[]{:S(2)}) collective-permute-start(f32[32,32]{0,1:T(8,128)S(1)} %bitcast.41), channel_id=1, source_target_pairs={{0,3},{1,0},{2,1},{3,2},{4,7},{5,4},{6,5},{7,6},{8,11},{9,8},{10,9... | collective-permute-start | bytes 12296 | tf_op jit(solution)/shard_map/ppermute | solution.py:43
  18.3 24.0 %all-to-all-start = ((f32[64,1,512]{2,1,0:T(1,128)}), f32[64,1,512]{2,1,0:T(1,128)S(1)}, u32[]{:S(2)}, u32[]{:S(2)}) async-start(f32[64,1,512]{2,1,0:T(1,128)} %copy.20), calls=%async_computation | async-start | bytes 262144 | tf_op jit(solution)/shard_map/all_to_all | solution.py:58
  61.6 5.3 %collective-permute-start.3 = (f32[32,32]{0,1:T(8,128)S(1)}, f32[32,32]{0,1:T(8,128)S(1)}, u32[]{:S(2)}, u32[]{:S(2)}) collective-permute-start(f32[32,32]{0,1:T(8,128)S(1)} %maximum_multiply_fusion.2), channel_id=1, source_target_pairs={{0,1},{1,2},{2,3},{3,0},{4,5},{5,6},{6,7},{7,4},{8,9},{9,10},{10,1... | collective-permute-start | bytes 12296 | tf_op jit(solution)/shard_map/ppermute | solution.py:43
  66.0 3.1 %collective-permute-start.4 = (f32[32,32]{0,1:T(8,128)S(1)}, f32[32,32]{0,1:T(8,128)S(1)}, u32[]{:S(2)}, u32[]{:S(2)}) collective-permute-start(f32[32,32]{0,1:T(8,128)S(1)} %maximum_multiply_fusion.2), channel_id=1, source_target_pairs={{0,2},{1,3},{2,0},{3,1},{4,6},{5,7},{6,4},{7,5},{8,10},{9,11},{10,... | collective-permute-start | bytes 12296 | tf_op jit(solution)/shard_map/ppermute | solution.py:43
  66.8 3.2 %collective-permute-start.5 = (f32[32,32]{0,1:T(8,128)S(1)}, f32[32,32]{0,1:T(8,128)S(1)}, u32[]{:S(2)}, u32[]{:S(2)}) collective-permute-start(f32[32,32]{0,1:T(8,128)S(1)} %maximum_multiply_fusion.2), channel_id=1, source_target_pairs={{0,3},{1,0},{2,1},{3,2},{4,7},{5,4},{6,5},{7,6},{8,11},{9,8},{10,9... | collective-permute-start | bytes 12296 | tf_op jit(solution)/shard_map/ppermute | solution.py:43

commit v6 on v5

--- a/solution.py
+++ b/solution.py
@@ -55,14 +55,16 @@
     lead = x.shape[:-1]
     parts = x.reshape(lead + (count, x.shape[-1] // count))
     parts = jnp.moveaxis(parts, -2, 0).reshape(count, -1)
-    total = jnp.sum(lax.all_to_all(parts, axis, 0, 0, tiled=True), axis=0)
+    moved = lax.all_to_all(parts.astype(jnp.bfloat16), axis, 0, 0, tiled=True)
+    total = jnp.sum(moved.astype(jnp.float32), axis=0)
     return total.reshape(lead + (x.shape[-1] // count,))
 
 
 def gather_last(x, axis):
     count = lax.axis_size(axis)
-    copies = jnp.broadcast_to(x.reshape(1, -1), (count, x.size))
-    joined = lax.all_to_all(copies, axis, 0, 0, tiled=True).reshape((count,) + x.shape)
+    copies = jnp.broadcast_to(x.reshape(1, -1).astype(jnp.bfloat16), (count, x.size))
+    joined = lax.all_to_all(copies, axis, 0, 0, tiled=True).astype(jnp.float32)
+    joined = joined.reshape((count,) + x.shape)
     joined = jnp.moveaxis(joined, 0, -2)
     return joined.reshape(x.shape[:-1] + (count * x.shape[-1],))
 

time: 71.7 us -> 73.1 us (1.020)
  other arithmetic: 13.7 us -> 15.4 us
    broadcast_in_dim x0 -> x1, other arithmetic: none -> 0.98 us  [gather_last(): jnp.broadcast_to(x.reshape(1, -1).astype(jnp.bfloat16), (count, x.size))]
    unnamed x2 -> x7, local copies, waits for them, and re-layouts: 0.01 us -> 0.88 us
    all_to_all x2 -> x1, local copies, waits for them, and re-layouts: 0.9 us -> 0.15 us  [gather_last(): joined = lax.all_to_all(copies, axis, 0, 0, tiled=True).astype(jnp.float32)]
where the time goes in v6:
time: 73.1 us; the launch traced here: 72.7 us
  starting transfers between devices  22.3 us (31%)
  other arithmetic  15.4 us (21%)
  blocking collectives  15.1 us (21%)
  waiting for transfers between devices  13.3 us (18%)
  local copies, waits for them, and re-layouts  4.66 us (6%)
  matrix products  1.79 us (2%)
    all_to_all x1, blocking collectives, gather_last(): joined = lax.all_to_all(copies, axis, 0, 0, tiled=True).astype(jnp.float32)  15.1 us
    all_to_all x1, starting transfers between devices, scatter_sum(): moved = lax.all_to_all(parts.astype(jnp.bfloat16), axis, 0, 0, tiled=True)  12.6 us
    all_to_all x1, waiting for transfers between devices, scatter_sum(): moved = lax.all_to_all(parts.astype(jnp.bfloat16), axis, 0, 0, tiled=True)  10.1 us
    ppermute x6, starting transfers between devices, shifted(): lax.ppermute(x, axis, [(j, (j + shift) % count) for j in range(count)])  9.7 us
    select_n x1, other arithmetic, circle_point(): jnp.where(quadrant == 0, sin_r, jnp.where(quadrant == 1, cos_r, jnp.where...  6.27 us
    ppermute x6, waiting for transfers between devices, shifted(): lax.ppermute(x, axis, [(j, (j + shift) % count) for j in range(count)])  3.16 us
    reduce_sum x1, other arithmetic, on_device(): jnp.sum(real_t[:, :, None] * cosine - imag_t[:, :, None] * sine_part, axi...  3.07 us
    reduce_sum x1, other arithmetic, on_device(): jnp.sum(bar_real[:, None, :] * cosine + bar_imag[:, None, :] * sine_part,...  2.32 us
  transfers between devices with their start and end apart: 7, of which 4 were waited for; matrix products, arithmetic and copies ran while one was open for 10% of the time, Pallas kernels for 0%

profile of v6, /device:TPU:1, one launch (start us, length us, event | category | flops | bytes accessed | tf_op | source)
XLA Modules:
  0.0 72.7 jit_solution(684792903608235761)
XLA Ops:
  0.0 1.1 %multiply_convert_fusion.1 = (bf16[1024,16]{0,1:T(8,128)(2,1)S(1)}, bf16[1024,16]{0,1:T(8,128)(2,1)S(1)}) fusion(s32[16]{0:T(128)} %param.5, s32[1024]{0:T(1024)S(1)} %iota_add_fusion), kind=kLoop, calls=%fused_computation.52 | loop fusion | flops 311296 | bytes 69696 | tf_op jit(solution)/shard_map/convert.2
  1.1 1.0 %fusion.12 = f32[32,32]{1,0:T(8,128)S(1)} fusion(bf16[32,1024]{1,0:T(8,128)(2,1)} %param.4, bf16[1024,16]{0,1:T(8,128)(2,1)S(1)} %get-tuple-element.20, bf16[1024,16]{0,1:T(8,128)(2,1)S(1)} %get-tuple-element.19), kind=kOutput, calls=%fused_computation.53 | convolution fusion | flops 2228224 | bytes 135168 | tf_op jit(solution)/shard_map/dot_general | solution.py:82
  2.0 3.0 %collective-permute-start = (f32[32,32]{0,1:T(8,128)S(1)}, f32[32,32]{0,1:T(8,128)S(1)}, u32[]{:S(2)}, u32[]{:S(2)}) collective-permute-start(f32[32,32]{0,1:T(8,128)S(1)} %bitcast.40), channel_id=1, source_target_pairs={{0,1},{1,2},{2,3},{3,0},{4,5},{5,6},{6,7},{7,4},{8,9},{9,10},{10,1... | collective-permute-start | bytes 12296 | tf_op jit(solution)/shard_map/ppermute | solution.py:43
  5.1 1.5 %collective-permute-start.1 = (f32[32,32]{0,1:T(8,128)S(1)}, f32[32,32]{0,1:T(8,128)S(1)}, u32[]{:S(2)}, u32[]{:S(2)}) collective-permute-start(f32[32,32]{0,1:T(8,128)S(1)} %bitcast.41), channel_id=1, source_target_pairs={{0,2},{1,3},{2,0},{3,1},{4,6},{5,7},{6,4},{7,5},{8,10},{9,11},{10,... | collective-permute-start | bytes 12296 | tf_op jit(solution)/shard_map/ppermute | solution.py:43
  6.7 6.3 %select_select_fusion = (f32[16,32,1024]{2,1,0:T(8,128)S(1)}, f32[16,32,1024]{2,1,0:T(8,128)}) fusion(s32[32,1024]{1,0:T(8,128)S(1)} %constant_dynamic-slice_fusion, s32[16]{0:T(128)} %param.5), kind=kLoop, calls=%fused_computation.20 | loop fusion | flops 33030144 | bytes 4325440 | tf_op jit(solution)/shard_map/jit(_where)/select_n | solution.py:36
  13.0 0.6 gather_fusion
  13.6 3.1 %subtract_reduce_fusion.1 = (f32[16,1024]{1,0:T(8,128)S(1)}, f32[16,1024]{1,0:T(8,128)S(1)}) fusion(f32[16,32,1024]{2,1,0:T(8,128)S(1)} %get-tuple-element.8, f32[16,32,1024]{2,1,0:T(8,128)} %get-tuple-element.7, f32[16,32]{1,0:T(8,128)S(1)} %get-tuple-element.18, f32[16,32]{1,0:T(8,128)S(1)} %get-tuple-element.17), kind=kLoop, calls=%fused_computation.19 | loop fusion | flops 4161536 | bytes 4329472 | tf_op jit(solution)/shard_map/reduce_sum | solution.py:92
  17.5 0.5 broadcast.258
  18.0 0.7 reduce.3
  18.8 0.7 reshape.155
  19.4 12.6 %all-to-all-start = ((bf16[64,2,256]{2,1,0:T(2,128)(2,1)}), bf16[64,2,256]{2,1,0:T(2,128)(2,1)S(1)}, u32[]{:S(2)}, u32[]{:S(2)}) async-start(bf16[64,2,256]{2,1,0:T(2,128)(2,1)} %reshape.155), calls=%async_computation | async-start | bytes 131072 | tf_op jit(solution)/shard_map/all_to_all | solution.py:58
  32.0 0.7 dynamic-slice_multiply_fusion
  32.9 10.1 %all-to-all-done = bf16[64,2,256]{2,1,0:T(2,128)(2,1)S(1)} async-done(((bf16[64,2,256]{2,1,0:T(2,128)(2,1)}), bf16[64,2,256]{2,1,0:T(2,128)(2,1)S(1)}, u32[]{:S(2)}, u32[]{:S(2)}) %all-to-all-start) | async-done | bytes 65568 | tf_op jit(solution)/shard_map/all_to_all | solution.py:58
  43.3 1.0 %reduce.4 = bf16[64,512]{1,0:T(8,128)(2,1)S(1)} reduce(bf16[64,1,512]{2,1,0:T(2,128)(2,1)S(1)} %broadcast_in_dim.2, bf16[]{:T(256)} %broadcast.258), dimensions={1}, to_apply=%broadcast_in_dim.2.reduce_sub_computation | reduce | bytes 131074 | tf_op jit(solution)/shard_map/broadcast_in_dim | solution.py:65
  44.3 15.1 %all_to_all.12 = bf16[64,2,256]{2,1,0:T(2,128)(2,1)S(1)} all-to-all(bf16[64,2,256]{2,1,0:T(2,128)(2,1)S(1)} %reshape.157), channel_id=1, replica_groups=mesh['sx'=4,'sz'=4,'sy'=4,'grp'=4] {'sx','sz','sy'}, dimensions={0} | all-to-all | bytes 131072 | tf_op jit(solution)/shard_map/all_to_all | solution.py:66
  59.9 0.3 mul.240
  60.4 0.3 mul.243
  60.7 2.3 %add_reduce_fusion = (f32[16,32]{1,0:T(8,128)S(1)}, f32[16,32]{1,0:T(8,128)S(1)}) fusion(f32[16,32,1024]{2,1,0:T(8,128)S(1)} %get-tuple-element.8, f32[16,32,1024]{2,1,0:T(8,128)} %get-tuple-element.7, f32[16,1024]{1,0:T(8,128)S(1)} %mul.243, f32[16,1024]{1,0:T(8,128)S(1)} %mul.240), kind=kLoop, calls=%fused_computation.17 | loop fusion | flops 4193280 | bytes 4329472 | tf_op jit(solution)/shard_map/reduce_sum | solution.py:105
  63.0 4.4 %collective-permute-start.3 = (f32[32,32]{0,1:T(8,128)S(1)}, f32[32,32]{0,1:T(8,128)S(1)}, u32[]{:S(2)}, u32[]{:S(2)}) collective-permute-start(f32[32,32]{0,1:T(8,128)S(1)} %maximum_multiply_fusion.2), channel_id=1, source_target_pairs={{0,1},{1,2},{2,3},{3,0},{4,5},{5,6},{6,7},{7,4},{8,9},{9,10},{10,1... | collective-permute-start | bytes 12296 | tf_op jit(solution)/shard_map/ppermute | solution.py:43
  67.4 0.7 collective-permute-start.4
  68.3 2.0 %collective-permute-done.4 = f32[32,32]{0,1:T(8,128)S(1)} collective-permute-done((f32[32,32]{0,1:T(8,128)S(1)}, f32[32,32]{0,1:T(8,128)S(1)}, u32[]{:S(2)}, u32[]{:S(2)}) %collective-permute-start.4) | collective-permute-done | bytes 4128 | tf_op jit(solution)/shard_map/ppermute | solution.py:43
  70.4 1.0 %collective-permute-done.5 = f32[32,32]{0,1:T(8,128)S(1)} collective-permute-done((f32[32,32]{0,1:T(8,128)S(1)}, f32[32,32]{0,1:T(8,128)S(1)}, u32[]{:S(2)}, u32[]{:S(2)}) %collective-permute-start.5) | collective-permute-done | bytes 4128 | tf_op jit(solution)/shard_map/ppermute | solution.py:43
  71.3 0.6 gather_fusion.1
  71.9 0.8 %convolution_convert_fusion = bf16[32,1024]{1,0:T(8,128)(2,1)} fusion(bf16[1024,16]{0,1:T(8,128)(2,1)S(1)} %get-tuple-element.20, bf16[1024,16]{0,1:T(8,128)(2,1)S(1)} %get-tuple-element.19, bf16[32,32]{0,1:T(8,128)(2,1)S(1)} %reduce_sum.69), kind=kOutput, calls=%fused_computation.29 | convolution fusion | flops 2260992 | bytes 133120 | tf_op jit(solution)/shard_map/dot_general | solution.py:110
  (39 shorter events, 2.3 us)
Async XLA Ops:
  0.0 6.6 %copy-start = (s32[32,4096]{1,0:T(8,128)S(1)}, s32[32,4096]{1,0:T(8,128)}, u32[]{:S(2)}) copy-start(s32[32,4096]{1,0:T(8,128)} %param.6) | copy-start | bytes 1572868
  2.0 10.9 %collective-permute-start = (f32[32,32]{0,1:T(8,128)S(1)}, f32[32,32]{0,1:T(8,128)S(1)}, u32[]{:S(2)}, u32[]{:S(2)}) collective-permute-start(f32[32,32]{0,1:T(8,128)S(1)} %bitcast.40), channel_id=1, source_target_pairs={{0,1},{1,2},{2,3},{3,0},{4,5},{5,6},{6,7},{7,4},{8,9},{9,10},{10,1... | collective-permute-start | bytes 12296 | tf_op jit(solution)/shard_map/ppermute | solution.py:43
  5.1 7.9 %collective-permute-start.1 = (f32[32,32]{0,1:T(8,128)S(1)}, f32[32,32]{0,1:T(8,128)S(1)}, u32[]{:S(2)}, u32[]{:S(2)}) collective-permute-start(f32[32,32]{0,1:T(8,128)S(1)} %bitcast.41), channel_id=1, source_target_pairs={{0,2},{1,3},{2,0},{3,1},{4,6},{5,7},{6,4},{7,5},{8,10},{9,11},{10,... | collective-permute-start | bytes 12296 | tf_op jit(solution)/shard_map/ppermute | solution.py:43
  6.6 6.4 %collective-permute-start.2 = (f32[32,32]{0,1:T(8,128)S(1)}, f32[32,32]{0,1:T(8,128)S(1)}, u32[]{:S(2)}, u32[]{:S(2)}) collective-permute-start(f32[32,32]{0,1:T(8,128)S(1)} %bitcast.42), channel_id=1, source_target_pairs={{0,3},{1,0},{2,1},{3,2},{4,7},{5,4},{6,5},{7,6},{8,11},{9,8},{10,9... | collective-permute-start | bytes 12296 | tf_op jit(solution)/shard_map/ppermute | solution.py:43
  19.4 23.6 %all-to-all-start = ((bf16[64,2,256]{2,1,0:T(2,128)(2,1)}), bf16[64,2,256]{2,1,0:T(2,128)(2,1)S(1)}, u32[]{:S(2)}, u32[]{:S(2)}) async-start(bf16[64,2,256]{2,1,0:T(2,128)(2,1)} %reshape.155), calls=%async_computation | async-start | bytes 131072 | tf_op jit(solution)/shard_map/all_to_all | solution.py:58
  63.0 5.3 %collective-permute-start.3 = (f32[32,32]{0,1:T(8,128)S(1)}, f32[32,32]{0,1:T(8,128)S(1)}, u32[]{:S(2)}, u32[]{:S(2)}) collective-permute-start(f32[32,32]{0,1:T(8,128)S(1)} %maximum_multiply_fusion.2), channel_id=1, source_target_pairs={{0,1},{1,2},{2,3},{3,0},{4,5},{5,6},{6,7},{7,4},{8,9},{9,10},{10,1... | collective-permute-start | bytes 12296 | tf_op jit(solution)/shard_map/ppermute | solution.py:43
  67.4 2.9 %collective-permute-start.4 = (f32[32,32]{0,1:T(8,128)S(1)}, f32[32,32]{0,1:T(8,128)S(1)}, u32[]{:S(2)}, u32[]{:S(2)}) collective-permute-start(f32[32,32]{0,1:T(8,128)S(1)} %maximum_multiply_fusion.2), channel_id=1, source_target_pairs={{0,2},{1,3},{2,0},{3,1},{4,6},{5,7},{6,4},{7,5},{8,10},{9,11},{10,... | collective-permute-start | bytes 12296 | tf_op jit(solution)/shard_map/ppermute | solution.py:43
  68.2 3.2 %collective-permute-start.5 = (f32[32,32]{0,1:T(8,128)S(1)}, f32[32,32]{0,1:T(8,128)S(1)}, u32[]{:S(2)}, u32[]{:S(2)}) collective-permute-start(f32[32,32]{0,1:T(8,128)S(1)} %maximum_multiply_fusion.2), channel_id=1, source_target_pairs={{0,3},{1,0},{2,1},{3,2},{4,7},{5,4},{6,5},{7,6},{8,11},{9,8},{10,9... | collective-permute-start | bytes 12296 | tf_op jit(solution)/shard_map/ppermute | solution.py:43

commit v7 on v5

--- a/solution.py
+++ b/solution.py
@@ -91,12 +91,14 @@
     steer_imag = jnp.sum(real_t[:, :, None] * sine_part + imag_t[:, :, None] * cosine, axis=1)
     steered = jnp.stack([steer_real, steer_imag]) * steer_scale
     offset = 0
-    for axis in SENS_AXES:
-        offset = offset * lax.axis_size(axis) + lax.axis_index(axis)
-    steered = scatter_sum(steered, SENS_AXES)
+    for axes in REDUCE_GROUPS:
+        steered = scatter_sum(steered, axes)
+        for axis in axes:
+            offset = offset * lax.axis_size(axis) + lax.axis_index(axis)
     width = steered.shape[-1]
     bar = lax.dynamic_slice_in_dim(own_weight, offset * width, width, 0) * steered
-    bar = gather_last(bar, SENS_AXES)
+    for axes in REDUCE_GROUPS[::-1]:
+        bar = gather_last(bar, axes)
     bar_real = bar[0]
     bar_imag = bar[1]
 
@@ -112,6 +114,7 @@
 
 
 SENS_AXES = ("sx", "sz", "sy")
+REDUCE_GROUPS = (("sx", "sy"), ("sz",))
 
 
 def solution(mesh):

time: 71.7 us -> 79.5 us (1.11)
  blocking collectives: 15.7 us -> 31.2 us
  waiting for transfers between devices: 13.7 us -> 8.89 us
  starting transfers between devices: 22.3 us -> 19.8 us
    all_to_all x0 -> x1, blocking collectives: none -> 12.2 us  [scatter_sum(): total = jnp.sum(lax.all_to_all(parts, axis, 0, 0, tiled=True), axis=0)]
    all_to_all x1, starting transfers between devices: 12.6 us -> 7.54 us  [scatter_sum(): total = jnp.sum(lax.all_to_all(parts, axis, 0, 0, tiled=True), axis=0)]
    all_to_all x1, waiting for transfers between devices: 10.6 us -> 5.73 us  [scatter_sum(): total = jnp.sum(lax.all_to_all(parts, axis, 0, 0, tiled=True), axis=0)]
    all_to_all x1 -> x2, blocking collectives: 15.7 us -> 19 us  [gather_last(): lax.all_to_all(copies, axis, 0, 0, tiled=True).reshape((count,) + x.shape)]
    ppermute x6, starting transfers between devices: 9.76 us -> 12.3 us  [shifted(): lax.ppermute(x, axis, [(j, (j + shift) % count) for j in range(count)])]
  transfers between devices with their start and end apart: 7 -> 7, of which waited for: 4 -> 4; matrix products, arithmetic and copies ran while one was open for 10% -> 9% of each run, Pallas kernels for 0% -> 0%
where the time goes in v7:
time: 79.5 us; the launch traced here: 79.1 us
  blocking collectives  31.2 us (39%)
  starting transfers between devices  19.8 us (25%)
  other arithmetic  14 us (18%)
  waiting for transfers between devices  8.89 us (11%)
  local copies, waits for them, and re-layouts  3.25 us (4%)
  matrix products  1.79 us (2%)
    all_to_all x2, blocking collectives, gather_last(): lax.all_to_all(copies, axis, 0, 0, tiled=True).reshape((count,) + x.shape)  19 us
    ppermute x6, starting transfers between devices, shifted(): lax.ppermute(x, axis, [(j, (j + shift) % count) for j in range(count)])  12.3 us
    all_to_all x1, blocking collectives, scatter_sum(): total = jnp.sum(lax.all_to_all(parts, axis, 0, 0, tiled=True), axis=0)  12.2 us
    all_to_all x1, starting transfers between devices, scatter_sum(): total = jnp.sum(lax.all_to_all(parts, axis, 0, 0, tiled=True), axis=0)  7.54 us
    select_n x1, other arithmetic, circle_point(): jnp.where(quadrant == 0, sin_r, jnp.where(quadrant == 1, cos_r, jnp.where...  6.27 us
    all_to_all x1, waiting for transfers between devices, scatter_sum(): total = jnp.sum(lax.all_to_all(parts, axis, 0, 0, tiled=True), axis=0)  5.73 us
    ppermute x6, waiting for transfers between devices, shifted(): lax.ppermute(x, axis, [(j, (j + shift) % count) for j in range(count)])  3.16 us
    reduce_sum x1, other arithmetic, on_device(): jnp.sum(real_t[:, :, None] * cosine - imag_t[:, :, None] * sine_part, axi...  3.07 us
  transfers between devices with their start and end apart: 7, of which 4 were waited for; matrix products, arithmetic and copies ran while one was open for 9% of the time, Pallas kernels for 0%

profile of v7, /device:TPU:1, one launch (start us, length us, event | category | flops | bytes accessed | tf_op | source)
XLA Modules:
  0.0 79.1 jit_solution(7646740305920551032)
XLA Ops:
  0.0 1.1 %multiply_convert_fusion.1 = (bf16[1024,16]{0,1:T(8,128)(2,1)S(1)}, bf16[1024,16]{0,1:T(8,128)(2,1)S(1)}) fusion(s32[16]{0:T(128)} %param.5, s32[1024]{0:T(1024)S(1)} %iota_add_fusion), kind=kLoop, calls=%fused_computation.50 | loop fusion | flops 311296 | bytes 69696 | tf_op jit(solution)/shard_map/convert
  1.1 1.0 %fusion.12 = f32[32,32]{1,0:T(8,128)S(1)} fusion(bf16[32,1024]{1,0:T(8,128)(2,1)} %param.4, bf16[1024,16]{0,1:T(8,128)(2,1)S(1)} %get-tuple-element.20, bf16[1024,16]{0,1:T(8,128)(2,1)S(1)} %get-tuple-element.19), kind=kOutput, calls=%fused_computation.51 | convolution fusion | flops 2228224 | bytes 135168 | tf_op jit(solution)/shard_map/dot_general | solution.py:80
  2.0 3.0 %collective-permute-start = (f32[32,32]{0,1:T(8,128)S(1)}, f32[32,32]{0,1:T(8,128)S(1)}, u32[]{:S(2)}, u32[]{:S(2)}) collective-permute-start(f32[32,32]{0,1:T(8,128)S(1)} %bitcast.43), channel_id=1, source_target_pairs={{0,1},{1,2},{2,3},{3,0},{4,5},{5,6},{6,7},{7,4},{8,9},{9,10},{10,1... | collective-permute-start | bytes 12296 | tf_op jit(solution)/shard_map/ppermute | solution.py:43
  5.1 1.5 %collective-permute-start.1 = (f32[32,32]{0,1:T(8,128)S(1)}, f32[32,32]{0,1:T(8,128)S(1)}, u32[]{:S(2)}, u32[]{:S(2)}) collective-permute-start(f32[32,32]{0,1:T(8,128)S(1)} %bitcast.44), channel_id=1, source_target_pairs={{0,2},{1,3},{2,0},{3,1},{4,6},{5,7},{6,4},{7,5},{8,10},{9,11},{10,... | collective-permute-start | bytes 12296 | tf_op jit(solution)/shard_map/ppermute | solution.py:43
  6.7 6.3 %select_select_fusion = (f32[16,32,1024]{2,1,0:T(8,128)S(1)}, f32[16,32,1024]{2,1,0:T(8,128)}) fusion(s32[32,1024]{1,0:T(8,128)S(1)} %constant_dynamic-slice_fusion, s32[16]{0:T(128)} %param.5), kind=kLoop, calls=%fused_computation.20 | loop fusion | flops 33030144 | bytes 4325440 | tf_op jit(solution)/shard_map/jit(_where)/select_n | solution.py:36
  13.0 0.6 gather_fusion
  13.6 3.1 %subtract_reduce_fusion.1 = (f32[16,1024]{1,0:T(8,128)S(1)}, f32[16,1024]{1,0:T(8,128)S(1)}) fusion(f32[16,32,1024]{2,1,0:T(8,128)S(1)} %get-tuple-element.8, f32[16,32,1024]{2,1,0:T(8,128)} %get-tuple-element.7, f32[16,32]{1,0:T(8,128)S(1)} %get-tuple-element.18, f32[16,32]{1,0:T(8,128)S(1)} %get-tuple-element.17), kind=kLoop, calls=%fused_computation.19 | loop fusion | flops 4161536 | bytes 4329472 | tf_op jit(solution)/shard_map/reduce_sum | solution.py:90
  17.0 0.2 all_to_all.26
  17.1 12.2 %all_to_all.32 = f32[16,1,2048]{2,1,0:T(1,128)S(1)} all-to-all(f32[16,1,2048]{2,1,0:T(1,128)S(1)} %all_to_all.26), channel_id=1, replica_groups=mesh['sx'=4,'sz'=4,'sy'=4,'grp'=4] {'sx','sy'}, dimensions={0} | all-to-all | bytes 262144 | tf_op jit(solution)/shard_map/all_to_all | solution.py:58
  29.5 0.7 all_to_all.27
  30.2 7.5 %all-to-all-start.1 = ((f32[4,1,512]{2,1,0:T(1,128)}), f32[4,1,512]{2,1,0:T(1,128)S(1)}, u32[]{:S(2)}, u32[]{:S(2)}) async-start(f32[4,1,512]{2,1,0:T(1,128)} %all_to_all.27), calls=%async_computation.1 | async-start | bytes 16384 | tf_op jit(solution)/shard_map/all_to_all | solution.py:58
  37.8 0.7 dynamic-slice_multiply_fusion
  38.6 5.7 %all-to-all-done.1 = f32[4,1,512]{2,1,0:T(1,128)S(1)} async-done(((f32[4,1,512]{2,1,0:T(1,128)}), f32[4,1,512]{2,1,0:T(1,128)S(1)}, u32[]{:S(2)}, u32[]{:S(2)}) %all-to-all-start.1) | async-done | bytes 8224 | tf_op jit(solution)/shard_map/all_to_all | solution.py:58
  44.4 8.9 %all_to_all.33 = f32[4,1,512]{2,1,0:T(1,128)S(1)} all-to-all(f32[4,1,512]{2,1,0:T(1,128)S(1)} %broadcast_in_dim.6), channel_id=1, replica_groups=mesh['sx'=4,'sz'=4,'sy'=4,'grp'=4] {'sz'}, dimensions={0} | all-to-all | bytes 16384 | tf_op jit(solution)/shard_map/all_to_all | solution.py:65
  53.7 10.1 %all_to_all.34 = f32[16,1,2048]{2,1,0:T(1,128)S(1)} all-to-all(f32[16,1,2048]{2,1,0:T(1,128)S(1)} %broadcast_in_dim.8), channel_id=1, replica_groups=mesh['sx'=4,'sz'=4,'sy'=4,'grp'=4] {'sx','sy'}, dimensions={0} | all-to-all | bytes 262144 | tf_op jit(solution)/shard_map/all_to_all | solution.py:65
  63.8 0.3 reduce.5
  64.5 2.3 %add_reduce_fusion = (f32[16,32]{1,0:T(8,128)S(1)}, f32[16,32]{1,0:T(8,128)S(1)}) fusion(f32[16,32,1024]{2,1,0:T(8,128)S(1)} %get-tuple-element.8, f32[16,32,1024]{2,1,0:T(8,128)} %get-tuple-element.7, f32[16,1024]{1,0:T(8,128)S(1)} %mul.242, f32[16,1024]{1,0:T(8,128)S(1)} %mul.239), kind=kLoop, calls=%fused_computation.17 | loop fusion | flops 4193280 | bytes 4329472 | tf_op jit(solution)/shard_map/reduce_sum | solution.py:105
  66.9 7.0 %collective-permute-start.3 = (f32[32,32]{0,1:T(8,128)S(1)}, f32[32,32]{0,1:T(8,128)S(1)}, u32[]{:S(2)}, u32[]{:S(2)}) collective-permute-start(f32[32,32]{0,1:T(8,128)S(1)} %maximum_multiply_fusion.2), channel_id=1, source_target_pairs={{0,1},{1,2},{2,3},{3,0},{4,5},{5,6},{6,7},{7,4},{8,9},{9,10},{10,1... | collective-permute-start | bytes 12296 | tf_op jit(solution)/shard_map/ppermute | solution.py:43
  73.8 0.7 collective-permute-start.4
  74.6 0.1 collective-permute-done.3
  74.7 2.1 %collective-permute-done.4 = f32[32,32]{0,1:T(8,128)S(1)} collective-permute-done((f32[32,32]{0,1:T(8,128)S(1)}, f32[32,32]{0,1:T(8,128)S(1)}, u32[]{:S(2)}, u32[]{:S(2)}) %collective-permute-start.4) | collective-permute-done | bytes 4128 | tf_op jit(solution)/shard_map/ppermute | solution.py:43
  76.8 0.9 %collective-permute-done.5 = f32[32,32]{0,1:T(8,128)S(1)} collective-permute-done((f32[32,32]{0,1:T(8,128)S(1)}, f32[32,32]{0,1:T(8,128)S(1)}, u32[]{:S(2)}, u32[]{:S(2)}) %collective-permute-start.5) | collective-permute-done | bytes 4128 | tf_op jit(solution)/shard_map/ppermute | solution.py:43
  77.7 0.6 gather_fusion.1
  78.3 0.8 %convolution_convert_fusion = bf16[32,1024]{1,0:T(8,128)(2,1)} fusion(bf16[1024,16]{0,1:T(8,128)(2,1)S(1)} %get-tuple-element.20, bf16[1024,16]{0,1:T(8,128)(2,1)S(1)} %get-tuple-element.19, bf16[32,32]{0,1:T(8,128)(2,1)S(1)} %reduce_sum.79), kind=kOutput, calls=%fused_computation.29 | convolution fusion | flops 2260992 | bytes 133120 | tf_op jit(solution)/shard_map/dot_general | solution.py:110
  (42 shorter events, 1.5 us)
Async XLA Ops:
  0.0 6.6 %copy-start = (s32[32,4096]{1,0:T(8,128)S(1)}, s32[32,4096]{1,0:T(8,128)}, u32[]{:S(2)}) copy-start(s32[32,4096]{1,0:T(8,128)} %param.6) | copy-start | bytes 1572868
  2.0 10.9 %collective-permute-start = (f32[32,32]{0,1:T(8,128)S(1)}, f32[32,32]{0,1:T(8,128)S(1)}, u32[]{:S(2)}, u32[]{:S(2)}) collective-permute-start(f32[32,32]{0,1:T(8,128)S(1)} %bitcast.43), channel_id=1, source_target_pairs={{0,1},{1,2},{2,3},{3,0},{4,5},{5,6},{6,7},{7,4},{8,9},{9,10},{10,1... | collective-permute-start | bytes 12296 | tf_op jit(solution)/shard_map/ppermute | solution.py:43
  5.1 7.9 %collective-permute-start.1 = (f32[32,32]{0,1:T(8,128)S(1)}, f32[32,32]{0,1:T(8,128)S(1)}, u32[]{:S(2)}, u32[]{:S(2)}) collective-permute-start(f32[32,32]{0,1:T(8,128)S(1)} %bitcast.44), channel_id=1, source_target_pairs={{0,2},{1,3},{2,0},{3,1},{4,6},{5,7},{6,4},{7,5},{8,10},{9,11},{10,... | collective-permute-start | bytes 12296 | tf_op jit(solution)/shard_map/ppermute | solution.py:43
  6.6 6.4 %collective-permute-start.2 = (f32[32,32]{0,1:T(8,128)S(1)}, f32[32,32]{0,1:T(8,128)S(1)}, u32[]{:S(2)}, u32[]{:S(2)}) collective-permute-start(f32[32,32]{0,1:T(8,128)S(1)} %bitcast.45), channel_id=1, source_target_pairs={{0,3},{1,0},{2,1},{3,2},{4,7},{5,4},{6,5},{7,6},{8,11},{9,8},{10,9... | collective-permute-start | bytes 12296 | tf_op jit(solution)/shard_map/ppermute | solution.py:43
  30.2 14.1 %all-to-all-start.1 = ((f32[4,1,512]{2,1,0:T(1,128)}), f32[4,1,512]{2,1,0:T(1,128)S(1)}, u32[]{:S(2)}, u32[]{:S(2)}) async-start(f32[4,1,512]{2,1,0:T(1,128)} %all_to_all.27), calls=%async_computation.1 | async-start | bytes 16384 | tf_op jit(solution)/shard_map/all_to_all | solution.py:58
  66.9 7.8 %collective-permute-start.3 = (f32[32,32]{0,1:T(8,128)S(1)}, f32[32,32]{0,1:T(8,128)S(1)}, u32[]{:S(2)}, u32[]{:S(2)}) collective-permute-start(f32[32,32]{0,1:T(8,128)S(1)} %maximum_multiply_fusion.2), channel_id=1, source_target_pairs={{0,1},{1,2},{2,3},{3,0},{4,5},{5,6},{6,7},{7,4},{8,9},{9,10},{10,1... | collective-permute-start | bytes 12296 | tf_op jit(solution)/shard_map/ppermute | solution.py:43
  73.8 3.0 %collective-permute-start.4 = (f32[32,32]{0,1:T(8,128)S(1)}, f32[32,32]{0,1:T(8,128)S(1)}, u32[]{:S(2)}, u32[]{:S(2)}) collective-permute-start(f32[32,32]{0,1:T(8,128)S(1)} %maximum_multiply_fusion.2), channel_id=1, source_target_pairs={{0,2},{1,3},{2,0},{3,1},{4,6},{5,7},{6,4},{7,5},{8,10},{9,11},{10,... | collective-permute-start | bytes 12296 | tf_op jit(solution)/shard_map/ppermute | solution.py:43
  74.6 3.2 %collective-permute-start.5 = (f32[32,32]{0,1:T(8,128)S(1)}, f32[32,32]{0,1:T(8,128)S(1)}, u32[]{:S(2)}, u32[]{:S(2)}) collective-permute-start(f32[32,32]{0,1:T(8,128)S(1)} %maximum_multiply_fusion.2), channel_id=1, source_target_pairs={{0,3},{1,0},{2,1},{3,2},{4,7},{5,4},{6,5},{7,6},{8,11},{9,8},{10,9... | collective-permute-start | bytes 12296 | tf_op jit(solution)/shard_map/ppermute | solution.py:43

commit v8 on v5

--- a/solution.py
+++ b/solution.py
@@ -21,20 +21,21 @@
 
 
 def circle_point(phase_index, length):
+    eighth_bits = (length // 8).bit_length() - 1
     quarter = length // 4
-    eighth = length // 8
-    quadrant = phase_index // quarter
-    rest = phase_index - quadrant * quarter
-    flip = rest > eighth
-    folded = jnp.where(flip, quarter - rest, rest)
+    quadrant = phase_index >> (eighth_bits + 1)
+    rest = phase_index & (quarter - 1)
+    flip = (rest >> eighth_bits) & (rest != (length // 8)).astype(jnp.int32)
+    folded = jnp.where(flip == 1, quarter - rest, rest)
     x = folded.astype(jnp.float32) * (two_pi / length)
     x2 = x * x
     sin_x = x * (1.0 + x2 * (-1.0 / 6.0 + x2 * (1.0 / 120.0 + x2 * (-1.0 / 5040.0))))
     cos_x = 1.0 + x2 * (-0.5 + x2 * (1.0 / 24.0 + x2 * (-1.0 / 720.0 + x2 * (1.0 / 40320.0))))
-    sin_r = jnp.where(flip, cos_x, sin_x)
-    cos_r = jnp.where(flip, sin_x, cos_x)
-    sine = jnp.where(quadrant == 0, sin_r, jnp.where(quadrant == 1, cos_r, jnp.where(quadrant == 2, -sin_r, -cos_r)))
-    cosine = jnp.where(quadrant == 0, cos_r, jnp.where(quadrant == 1, -sin_r, jnp.where(quadrant == 2, -cos_r, sin_r)))
+    swap = ((quadrant & 1) ^ flip) == 1
+    sine = jnp.where(swap, cos_x, sin_x)
+    cosine = jnp.where(swap, sin_x, cos_x)
+    sine = jnp.where(quadrant >= 2, -sine, sine)
+    cosine = jnp.where(((quadrant ^ (quadrant >> 1)) & 1) == 1, -cosine, cosine)
     return cosine, sine
 
 
@@ -84,7 +85,7 @@
 
     own_delays = lax.dynamic_slice_in_dim(delays, position * scan_share, scan_share, 1)
     own_weight = 2.0 * lax.dynamic_slice_in_dim(map_adjoint, position * scan_share, scan_share, 0)
-    phase_index = (bin_index[:, None, None] * own_delays[None, :, :]) % NT
+    phase_index = (bin_index[:, None, None] * own_delays[None, :, :]) & (NT - 1)
     cosine, sine_part = lax.optimization_barrier(circle_point(phase_index, NT))
 
     steer_real = jnp.sum(real_t[:, :, None] * cosine - imag_t[:, :, None] * sine_part, axis=1)

time: 71.7 us -> 70.2 us (0.979)
  other arithmetic: 13.7 us -> 12.1 us
    select_n x1, other arithmetic: 6.27 us -> 4.77 us  [circle_point(): sine = jnp.where(quadrant >= 2, -sine, sine)]
  transfers between devices with their start and end apart: 7 -> 7, of which waited for: 4 -> 4; matrix products, arithmetic and copies ran while one was open for 10% -> 8% of each run, Pallas kernels for 0% -> 0%
where the time goes in v8:
time: 70.2 us; the launch traced here: 69.9 us
  starting transfers between devices  22.3 us (32%)
  blocking collectives  15.7 us (22%)
  waiting for transfers between devices  13.7 us (20%)
  other arithmetic  12.1 us (17%)
  local copies, waits for them, and re-layouts  4.01 us (6%)
  matrix products  1.79 us (3%)
    all_to_all x1, blocking collectives, gather_last(): lax.all_to_all(copies, axis, 0, 0, tiled=True).reshape((count,) + x.shape)  15.7 us
    all_to_all x1, starting transfers between devices, scatter_sum(): total = jnp.sum(lax.all_to_all(parts, axis, 0, 0, tiled=True), axis=0)  12.6 us
    all_to_all x1, waiting for transfers between devices, scatter_sum(): total = jnp.sum(lax.all_to_all(parts, axis, 0, 0, tiled=True), axis=0)  10.6 us
    ppermute x6, starting transfers between devices, shifted(): lax.ppermute(x, axis, [(j, (j + shift) % count) for j in range(count)])  9.76 us
    select_n x1, other arithmetic, circle_point(): sine = jnp.where(quadrant >= 2, -sine, sine)  4.77 us
    ppermute x6, waiting for transfers between devices, shifted(): lax.ppermute(x, axis, [(j, (j + shift) % count) for j in range(count)])  3.16 us
    reduce_sum x1, other arithmetic, on_device(): jnp.sum(real_t[:, :, None] * cosine - imag_t[:, :, None] * sine_part, axi...  3.07 us
    reduce_sum x1, other arithmetic, on_device(): jnp.sum(bar_real[:, None, :] * cosine + bar_imag[:, None, :] * sine_part,...  2.32 us
  transfers between devices with their start and end apart: 7, of which 4 were waited for; matrix products, arithmetic and copies ran while one was open for 8% of the time, Pallas kernels for 0%

profile of v8, /device:TPU:1, one launch (start us, length us, event | category | flops | bytes accessed | tf_op | source)
XLA Modules:
  0.0 69.9 jit_solution(956843196610221897)
XLA Ops:
  0.0 1.1 %multiply_convert_fusion.1 = (bf16[1024,16]{0,1:T(8,128)(2,1)S(1)}, bf16[1024,16]{0,1:T(8,128)(2,1)S(1)}) fusion(s32[16]{0:T(128)} %param.5, s32[1024]{0:T(1024)S(1)} %iota_add_fusion), kind=kLoop, calls=%fused_computation.40 | loop fusion | flops 311296 | bytes 69696 | tf_op jit(solution)/shard_map/convert
  1.1 1.0 %fusion.13 = f32[32,32]{1,0:T(8,128)S(1)} fusion(bf16[32,1024]{1,0:T(8,128)(2,1)} %param.4, bf16[1024,16]{0,1:T(8,128)(2,1)S(1)} %get-tuple-element.20, bf16[1024,16]{0,1:T(8,128)(2,1)S(1)} %get-tuple-element.19), kind=kOutput, calls=%fused_computation.41 | convolution fusion | flops 2228224 | bytes 135168 | tf_op jit(solution)/shard_map/dot_general | solution.py:81
  2.0 3.0 %collective-permute-start = (f32[32,32]{0,1:T(8,128)S(1)}, f32[32,32]{0,1:T(8,128)S(1)}, u32[]{:S(2)}, u32[]{:S(2)}) collective-permute-start(f32[32,32]{0,1:T(8,128)S(1)} %bitcast.39), channel_id=1, source_target_pairs={{0,1},{1,2},{2,3},{3,0},{4,5},{5,6},{6,7},{7,4},{8,9},{9,10},{10,1... | collective-permute-start | bytes 12296 | tf_op jit(solution)/shard_map/ppermute | solution.py:44
  5.1 1.5 %collective-permute-start.1 = (f32[32,32]{0,1:T(8,128)S(1)}, f32[32,32]{0,1:T(8,128)S(1)}, u32[]{:S(2)}, u32[]{:S(2)}) collective-permute-start(f32[32,32]{0,1:T(8,128)S(1)} %bitcast.40), channel_id=1, source_target_pairs={{0,2},{1,3},{2,0},{3,1},{4,6},{5,7},{6,4},{7,5},{8,10},{9,11},{10,... | collective-permute-start | bytes 12296 | tf_op jit(solution)/shard_map/ppermute | solution.py:44
  6.7 4.8 %negate_select_fusion = (f32[16,32,1024]{2,1,0:T(8,128)S(1)}, f32[16,32,1024]{2,1,0:T(8,128)}) fusion(s32[32,1024]{1,0:T(8,128)S(1)} %constant_dynamic-slice_fusion, s32[16]{0:T(128)} %param.5), kind=kLoop, calls=%fused_computation.2 | loop fusion | flops 22544384 | bytes 4325440 | tf_op jit(solution)/shard_map/jit(_where)/select_n | solution.py:37
  11.5 0.6 gather_fusion
  12.1 3.1 %subtract_reduce_fusion.1 = (f32[16,1024]{1,0:T(8,128)S(1)}, f32[16,1024]{1,0:T(8,128)S(1)}) fusion(f32[16,32,1024]{2,1,0:T(8,128)S(1)} %get-tuple-element.8, f32[16,32,1024]{2,1,0:T(8,128)} %get-tuple-element.7, f32[16,32]{1,0:T(8,128)S(1)} %get-tuple-element.18, f32[16,32]{1,0:T(8,128)S(1)} %get-tuple-element.17), kind=kLoop, calls=%fused_computation.13 | loop fusion | flops 4161536 | bytes 4329472 | tf_op jit(solution)/shard_map/reduce_sum | solution.py:91
  15.2 0.2 stack.42
  15.5 0.2 stack.43
  16.0 0.8 %copy.20 = f32[64,1,512]{2,1,0:T(1,128)} copy(f32[64,1,512]{0,2,1:T(8,128)S(1)} %bitcast.34) | data formatting | bytes 262144 | tf_op jit(solution)/shard_map/all_to_all | solution.py:59
  16.8 12.6 %all-to-all-start = ((f32[64,1,512]{2,1,0:T(1,128)}), f32[64,1,512]{2,1,0:T(1,128)S(1)}, u32[]{:S(2)}, u32[]{:S(2)}) async-start(f32[64,1,512]{2,1,0:T(1,128)} %copy.20), calls=%async_computation | async-start | bytes 262144 | tf_op jit(solution)/shard_map/all_to_all | solution.py:59
  29.4 0.7 dynamic-slice_multiply_fusion
  30.2 10.6 %all-to-all-done = f32[64,1,512]{2,1,0:T(1,128)S(1)} async-done(((f32[64,1,512]{2,1,0:T(1,128)}), f32[64,1,512]{2,1,0:T(1,128)S(1)}, u32[]{:S(2)}, u32[]{:S(2)}) %all-to-all-start) | async-done | bytes 131104 | tf_op jit(solution)/shard_map/all_to_all | solution.py:59
  41.0 15.7 %all_to_all.15 = f32[64,1,512]{2,1,0:T(1,128)S(1)} all-to-all(f32[64,1,512]{2,1,0:T(1,128)S(1)} %broadcast_in_dim.2), channel_id=1, replica_groups=mesh['sx'=4,'sz'=4,'sy'=4,'grp'=4] {'sx','sz','sy'}, dimensions={0} | all-to-all | bytes 262144 | tf_op jit(solution)/shard_map/all_to_all | solution.py:66
  57.0 0.3 mul.235
  57.3 0.2 copy.23
  57.5 0.3 mul.238
  57.8 2.3 %add_reduce_fusion = (f32[16,32]{1,0:T(8,128)S(1)}, f32[16,32]{1,0:T(8,128)S(1)}) fusion(f32[16,32,1024]{2,1,0:T(8,128)S(1)} %get-tuple-element.8, f32[16,32,1024]{2,1,0:T(8,128)} %get-tuple-element.7, f32[16,1024]{1,0:T(8,128)S(1)} %mul.238, f32[16,1024]{1,0:T(8,128)S(1)} %mul.235), kind=kLoop, calls=%fused_computation.11 | loop fusion | flops 4193280 | bytes 4329472 | tf_op jit(solution)/shard_map/reduce_sum | solution.py:104
  60.1 4.4 %collective-permute-start.3 = (f32[32,32]{0,1:T(8,128)S(1)}, f32[32,32]{0,1:T(8,128)S(1)}, u32[]{:S(2)}, u32[]{:S(2)}) collective-permute-start(f32[32,32]{0,1:T(8,128)S(1)} %maximum_multiply_fusion.2), channel_id=1, source_target_pairs={{0,1},{1,2},{2,3},{3,0},{4,5},{5,6},{6,7},{7,4},{8,9},{9,10},{10,1... | collective-permute-start | bytes 12296 | tf_op jit(solution)/shard_map/ppermute | solution.py:44
  64.5 0.8 %collective-permute-start.4 = (f32[32,32]{0,1:T(8,128)S(1)}, f32[32,32]{0,1:T(8,128)S(1)}, u32[]{:S(2)}, u32[]{:S(2)}) collective-permute-start(f32[32,32]{0,1:T(8,128)S(1)} %maximum_multiply_fusion.2), channel_id=1, source_target_pairs={{0,2},{1,3},{2,0},{3,1},{4,6},{5,7},{6,4},{7,5},{8,10},{9,11},{10,... | collective-permute-start | bytes 12296 | tf_op jit(solution)/shard_map/ppermute | solution.py:44
  65.4 2.2 %collective-permute-done.4 = f32[32,32]{0,1:T(8,128)S(1)} collective-permute-done((f32[32,32]{0,1:T(8,128)S(1)}, f32[32,32]{0,1:T(8,128)S(1)}, u32[]{:S(2)}, u32[]{:S(2)}) %collective-permute-start.4) | collective-permute-done | bytes 4128 | tf_op jit(solution)/shard_map/ppermute | solution.py:44
  67.5 0.9 %collective-permute-done.5 = f32[32,32]{0,1:T(8,128)S(1)} collective-permute-done((f32[32,32]{0,1:T(8,128)S(1)}, f32[32,32]{0,1:T(8,128)S(1)}, u32[]{:S(2)}, u32[]{:S(2)}) %collective-permute-start.5) | collective-permute-done | bytes 4128 | tf_op jit(solution)/shard_map/ppermute | solution.py:44
  68.5 0.6 gather_fusion.1
  69.0 0.8 %convolution_convert_fusion = bf16[32,1024]{1,0:T(8,128)(2,1)} fusion(bf16[1024,16]{0,1:T(8,128)(2,1)S(1)} %get-tuple-element.20, bf16[1024,16]{0,1:T(8,128)(2,1)S(1)} %get-tuple-element.19, bf16[32,32]{0,1:T(8,128)(2,1)S(1)} %reduce_sum.69), kind=kOutput, calls=%fused_computation.26 | convolution fusion | flops 2260992 | bytes 133120 | tf_op jit(solution)/shard_map/dot_general | solution.py:109
  (31 shorter events, 1.3 us)
Async XLA Ops:
  0.0 6.6 %copy-start = (s32[32,4096]{1,0:T(8,128)S(1)}, s32[32,4096]{1,0:T(8,128)}, u32[]{:S(2)}) copy-start(s32[32,4096]{1,0:T(8,128)} %param.6) | copy-start | bytes 1572868
  2.0 9.4 %collective-permute-start = (f32[32,32]{0,1:T(8,128)S(1)}, f32[32,32]{0,1:T(8,128)S(1)}, u32[]{:S(2)}, u32[]{:S(2)}) collective-permute-start(f32[32,32]{0,1:T(8,128)S(1)} %bitcast.39), channel_id=1, source_target_pairs={{0,1},{1,2},{2,3},{3,0},{4,5},{5,6},{6,7},{7,4},{8,9},{9,10},{10,1... | collective-permute-start | bytes 12296 | tf_op jit(solution)/shard_map/ppermute | solution.py:44
  5.1 6.4 %collective-permute-start.1 = (f32[32,32]{0,1:T(8,128)S(1)}, f32[32,32]{0,1:T(8,128)S(1)}, u32[]{:S(2)}, u32[]{:S(2)}) collective-permute-start(f32[32,32]{0,1:T(8,128)S(1)} %bitcast.40), channel_id=1, source_target_pairs={{0,2},{1,3},{2,0},{3,1},{4,6},{5,7},{6,4},{7,5},{8,10},{9,11},{10,... | collective-permute-start | bytes 12296 | tf_op jit(solution)/shard_map/ppermute | solution.py:44
  6.6 4.8 %collective-permute-start.2 = (f32[32,32]{0,1:T(8,128)S(1)}, f32[32,32]{0,1:T(8,128)S(1)}, u32[]{:S(2)}, u32[]{:S(2)}) collective-permute-start(f32[32,32]{0,1:T(8,128)S(1)} %bitcast.41), channel_id=1, source_target_pairs={{0,3},{1,0},{2,1},{3,2},{4,7},{5,4},{6,5},{7,6},{8,11},{9,8},{10,9... | collective-permute-start | bytes 12296 | tf_op jit(solution)/shard_map/ppermute | solution.py:44
  16.8 24.0 %all-to-all-start = ((f32[64,1,512]{2,1,0:T(1,128)}), f32[64,1,512]{2,1,0:T(1,128)S(1)}, u32[]{:S(2)}, u32[]{:S(2)}) async-start(f32[64,1,512]{2,1,0:T(1,128)} %copy.20), calls=%async_computation | async-start | bytes 262144 | tf_op jit(solution)/shard_map/all_to_all | solution.py:59
  60.1 5.3 %collective-permute-start.3 = (f32[32,32]{0,1:T(8,128)S(1)}, f32[32,32]{0,1:T(8,128)S(1)}, u32[]{:S(2)}, u32[]{:S(2)}) collective-permute-start(f32[32,32]{0,1:T(8,128)S(1)} %maximum_multiply_fusion.2), channel_id=1, source_target_pairs={{0,1},{1,2},{2,3},{3,0},{4,5},{5,6},{6,7},{7,4},{8,9},{9,10},{10,1... | collective-permute-start | bytes 12296 | tf_op jit(solution)/shard_map/ppermute | solution.py:44
  64.5 3.1 %collective-permute-start.4 = (f32[32,32]{0,1:T(8,128)S(1)}, f32[32,32]{0,1:T(8,128)S(1)}, u32[]{:S(2)}, u32[]{:S(2)}) collective-permute-start(f32[32,32]{0,1:T(8,128)S(1)} %maximum_multiply_fusion.2), channel_id=1, source_target_pairs={{0,2},{1,3},{2,0},{3,1},{4,6},{5,7},{6,4},{7,5},{8,10},{9,11},{10,... | collective-permute-start | bytes 12296 | tf_op jit(solution)/shard_map/ppermute | solution.py:44
  65.3 3.2 %collective-permute-start.5 = (f32[32,32]{0,1:T(8,128)S(1)}, f32[32,32]{0,1:T(8,128)S(1)}, u32[]{:S(2)}, u32[]{:S(2)}) collective-permute-start(f32[32,32]{0,1:T(8,128)S(1)} %maximum_multiply_fusion.2), channel_id=1, source_target_pairs={{0,3},{1,0},{2,1},{3,2},{4,7},{5,4},{6,5},{7,6},{8,11},{9,8},{10,9... | collective-permute-start | bytes 12296 | tf_op jit(solution)/shard_map/ppermute | solution.py:44

commit v9 on v8

--- a/solution.py
+++ b/solution.py
@@ -94,10 +94,13 @@
     offset = 0
     for axis in SENS_AXES:
         offset = offset * lax.axis_size(axis) + lax.axis_index(axis)
-    steered = scatter_sum(steered, SENS_AXES)
-    width = steered.shape[-1]
-    bar = lax.dynamic_slice_in_dim(own_weight, offset * width, width, 0) * steered
-    bar = gather_last(bar, SENS_AXES)
+    count = lax.axis_size(SENS_AXES)
+    parts = steered.reshape(count, steered.size // count)
+    width = parts.shape[1]
+    chunk = jnp.sum(lax.all_to_all(parts, SENS_AXES, 0, 0, tiled=True), axis=0)
+    start = (offset * width) % scan_share
+    chunk = lax.dynamic_slice_in_dim(own_weight, start, width, 0) * chunk
+    bar = lax.all_gather(chunk, SENS_AXES, tiled=True).reshape(steered.shape)
     bar_real = bar[0]
     bar_imag = bar[1]
 

time: 70.2 us -> 238 us (3.39)
  blocking collectives: 15.7 us -> 158 us
  starting transfers between devices: 22.3 us -> 49.2 us
    all_gather x0 -> x1, blocking collectives: none -> 158 us  [on_device(): bar = lax.all_gather(chunk, SENS_AXES, tiled=True).reshape(steered.shape)]
    ppermute x6, starting transfers between devices: 9.76 us -> 36.7 us  [shifted(): lax.ppermute(x, axis, [(j, (j + shift) % count) for j in range(count)])]
    all_to_all x1 -> x0, blocking collectives: 15.7 us -> none  [gather_last(): lax.all_to_all(copies, axis, 0, 0, tiled=True).reshape((count,) + x.shape)]
  transfers between devices with their start and end apart: 7 -> 7, of which waited for: 4 -> 3; matrix products, arithmetic and copies ran while one was open for 8% -> 2% of each run, Pallas kernels for 0% -> 0%
where the time goes in v9:
time: 238 us
  blocking collectives  158 us (66%)
  starting transfers between devices  49.2 us (21%)
  waiting for transfers between devices  13.9 us (6%)
  other arithmetic  12.2 us (5%)
    all_gather x1, blocking collectives, on_device(): bar = lax.all_gather(chunk, SENS_AXES, tiled=True).reshape(steered.shape)  158 us
    ppermute x6, starting transfers between devices, shifted(): lax.ppermute(x, axis, [(j, (j + shift) % count) for j in range(count)])  36.7 us
    all_to_all x1, starting transfers between devices, on_device(): chunk = jnp.sum(lax.all_to_all(parts, SENS_AXES, 0, 0, tiled=True), axis=0)  12.6 us
    all_to_all x1, waiting for transfers between devices, on_device(): chunk = jnp.sum(lax.all_to_all(parts, SENS_AXES, 0, 0, tiled=True), axis=0)  10.7 us
    select_n x1, other arithmetic, circle_point(): sine = jnp.where(quadrant >= 2, -sine, sine)  4.77 us
  transfers between devices with their start and end apart: 7, of which 3 were waited for; matrix products, arithmetic and copies ran while one was open for 2% of the time, Pallas kernels for 0%

profile of v9, /device:TPU:1, one launch (start us, length us, event | category | flops | bytes accessed | tf_op | source)
XLA Modules:
  0.0 237.5 jit_solution(9495438284824854974)
XLA Ops:
  0.0 1.1 multiply_convert_fusion.1
  1.1 1.0 fusion.13
  2.0 3.0 %collective-permute-start = (f32[32,32]{0,1:T(8,128)S(1)}, f32[32,32]{0,1:T(8,128)S(1)}, u32[]{:S(2)}, u32[]{:S(2)}) collective-permute-start(f32[32,32]{0,1:T(8,128)S(1)} %bitcast.32), channel_id=1, source_target_pairs={{0,1},{1,2},{2,3},{3,0},{4,5},{5,6},{6,7},{7,4},{8,9},{9,10},{10,1... | collective-permute-start | bytes 12296 | tf_op jit(solution)/shard_map/ppermute | solution.py:44
  5.1 1.5 collective-permute-start.1
  6.7 4.8 %negate_select_fusion = (f32[16,32,1024]{2,1,0:T(8,128)S(1)}, f32[16,32,1024]{2,1,0:T(8,128)}) fusion(s32[32,1024]{1,0:T(8,128)S(1)} %constant_dynamic-slice_fusion, s32[16]{0:T(128)} %param.5), kind=kLoop, calls=%fused_computation.2 | loop fusion | flops 22544384 | bytes 4325440 | tf_op jit(solution)/shard_map/jit(_where)/select_n | solution.py:37
  11.4 0.0 collective-permute-done.1
  11.5 0.6 gather_fusion
  12.1 3.1 %subtract_reduce_fusion.1 = (f32[16,1024]{1,0:T(8,128)S(1)}, f32[16,1024]{1,0:T(8,128)S(1)}) fusion(f32[16,32,1024]{2,1,0:T(8,128)S(1)} %get-tuple-element.8, f32[16,32,1024]{2,1,0:T(8,128)} %get-tuple-element.7, f32[16,32]{1,0:T(8,128)S(1)} %get-tuple-element.18, f32[16,32]{1,0:T(8,128)S(1)} %get-tuple-element.17), kind=kLoop, calls=%fused_computation.13 | loop fusion | flops 4161536 | bytes 4329472 | tf_op jit(solution)/shard_map/reduce_sum | solution.py:91
  15.2 0.8 mul.239
  16.0 12.6 %all-to-all-start = ((f32[64,1,512]{2,1,0:T(1,128)}), f32[64,1,512]{2,1,0:T(1,128)S(1)}, u32[]{:S(2)}, u32[]{:S(2)}) async-start(f32[64,1,512]{2,1,0:T(1,128)} %mul.239), calls=%async_computation | async-start | bytes 262144 | tf_op jit(solution)/shard_map/all_to_all | solution.py:100
  28.6 0.7 dynamic-slice_multiply_fusion
  29.3 10.7 %all-to-all-done = f32[64,1,512]{2,1,0:T(1,128)S(1)} async-done(((f32[64,1,512]{2,1,0:T(1,128)}), f32[64,1,512]{2,1,0:T(1,128)S(1)}, u32[]{:S(2)}, u32[]{:S(2)}) %all-to-all-start) | async-done | bytes 131104 | tf_op jit(solution)/shard_map/all_to_all | solution.py:100
  40.0 0.1 reduce_sum.66
  40.1 0.1 dynamic-slice_multiply_fusion.1
  40.2 157.9 %all-gather = f32[64,1,512]{2,1,0:T(1,128)S(1)} all-gather(f32[1,1,512]{2,1,0:T(1,128)S(1)} %bitcast.42), channel_id=1, replica_groups=mesh['sx'=4,'sz'=4,'sy'=4,'grp'=4] {'sx','sz','sy'}, dimensions={0}, use_global_device_ids=true | all-gather | bytes 133120 | tf_op jit(solution)/shard_map/all_gather | solution.py:103
  198.1 0.3 slice_reduce_fusion.1
  198.5 2.3 add_reduce_fusion
  200.8 31.0 %collective-permute-start.3 = (f32[32,32]{0,1:T(8,128)S(1)}, f32[32,32]{0,1:T(8,128)S(1)}, u32[]{:S(2)}, u32[]{:S(2)}) collective-permute-start(f32[32,32]{0,1:T(8,128)S(1)} %maximum_multiply_fusion.2), channel_id=1, source_target_pairs={{0,1},{1,2},{2,3},{3,0},{4,5},{5,6},{6,7},{7,4},{8,9},{9,10},{10,1... | collective-permute-start | bytes 12296 | tf_op jit(solution)/shard_map/ppermute | solution.py:44
  231.9 1.1 collective-permute-start.4
  232.9 0.0 collective-permute-start.5
  232.9 1.5 collective-permute-done.4
  234.4 1.6 collective-permute-done.5
  236.1 0.6 gather_fusion.1
  236.7 0.8 convolution_convert_fusion
  (20 shorter events, 0.2 us)
Async XLA Ops:
  0.0 6.6 %copy-start = (s32[32,4096]{1,0:T(8,128)S(1)}, s32[32,4096]{1,0:T(8,128)}, u32[]{:S(2)}) copy-start(s32[32,4096]{1,0:T(8,128)} %param.6) | copy-start | bytes 1572868
  2.0 9.4 %collective-permute-start = (f32[32,32]{0,1:T(8,128)S(1)}, f32[32,32]{0,1:T(8,128)S(1)}, u32[]{:S(2)}, u32[]{:S(2)}) collective-permute-start(f32[32,32]{0,1:T(8,128)S(1)} %bitcast.32), channel_id=1, source_target_pairs={{0,1},{1,2},{2,3},{3,0},{4,5},{5,6},{6,7},{7,4},{8,9},{9,10},{10,1... | collective-permute-start | bytes 12296 | tf_op jit(solution)/shard_map/ppermute | solution.py:44
  5.1 6.4 %collective-permute-start.1 = (f32[32,32]{0,1:T(8,128)S(1)}, f32[32,32]{0,1:T(8,128)S(1)}, u32[]{:S(2)}, u32[]{:S(2)}) collective-permute-start(f32[32,32]{0,1:T(8,128)S(1)} %bitcast.33), channel_id=1, source_target_pairs={{0,2},{1,3},{2,0},{3,1},{4,6},{5,7},{6,4},{7,5},{8,10},{9,11},{10,... | collective-permute-start | bytes 12296 | tf_op jit(solution)/shard_map/ppermute | solution.py:44
  6.6 4.8 %collective-permute-start.2 = (f32[32,32]{0,1:T(8,128)S(1)}, f32[32,32]{0,1:T(8,128)S(1)}, u32[]{:S(2)}, u32[]{:S(2)}) collective-permute-start(f32[32,32]{0,1:T(8,128)S(1)} %bitcast.34), channel_id=1, source_target_pairs={{0,3},{1,0},{2,1},{3,2},{4,7},{5,4},{6,5},{7,6},{8,11},{9,8},{10,9... | collective-permute-start | bytes 12296 | tf_op jit(solution)/shard_map/ppermute | solution.py:44
  16.0 24.0 %all-to-all-start = ((f32[64,1,512]{2,1,0:T(1,128)}), f32[64,1,512]{2,1,0:T(1,128)S(1)}, u32[]{:S(2)}, u32[]{:S(2)}) async-start(f32[64,1,512]{2,1,0:T(1,128)} %mul.239), calls=%async_computation | async-start | bytes 262144 | tf_op jit(solution)/shard_map/all_to_all | solution.py:100
  200.8 32.1 %collective-permute-start.3 = (f32[32,32]{0,1:T(8,128)S(1)}, f32[32,32]{0,1:T(8,128)S(1)}, u32[]{:S(2)}, u32[]{:S(2)}) collective-permute-start(f32[32,32]{0,1:T(8,128)S(1)} %maximum_multiply_fusion.2), channel_id=1, source_target_pairs={{0,1},{1,2},{2,3},{3,0},{4,5},{5,6},{6,7},{7,4},{8,9},{9,10},{10,1... | collective-permute-start | bytes 12296 | tf_op jit(solution)/shard_map/ppermute | solution.py:44
  231.9 2.6 %collective-permute-start.4 = (f32[32,32]{0,1:T(8,128)S(1)}, f32[32,32]{0,1:T(8,128)S(1)}, u32[]{:S(2)}, u32[]{:S(2)}) collective-permute-start(f32[32,32]{0,1:T(8,128)S(1)} %maximum_multiply_fusion.2), channel_id=1, source_target_pairs={{0,2},{1,3},{2,0},{3,1},{4,6},{5,7},{6,4},{7,5},{8,10},{9,11},{10,... | collective-permute-start | bytes 12296 | tf_op jit(solution)/shard_map/ppermute | solution.py:44
  232.9 3.2 %collective-permute-start.5 = (f32[32,32]{0,1:T(8,128)S(1)}, f32[32,32]{0,1:T(8,128)S(1)}, u32[]{:S(2)}, u32[]{:S(2)}) collective-permute-start(f32[32,32]{0,1:T(8,128)S(1)} %maximum_multiply_fusion.2), channel_id=1, source_target_pairs={{0,3},{1,0},{2,1},{3,2},{4,7},{5,4},{6,5},{7,6},{8,11},{9,8},{10,9... | collective-permute-start | bytes 12296 | tf_op jit(solution)/shard_map/ppermute | solution.py:44

commit v10 on v9

--- a/solution.py
+++ b/solution.py
@@ -100,7 +100,8 @@
     chunk = jnp.sum(lax.all_to_all(parts, SENS_AXES, 0, 0, tiled=True), axis=0)
     start = (offset * width) % scan_share
     chunk = lax.dynamic_slice_in_dim(own_weight, start, width, 0) * chunk
-    bar = lax.all_gather(chunk, SENS_AXES, tiled=True).reshape(steered.shape)
+    copies = jnp.broadcast_to(chunk[None], (count, width))
+    bar = lax.all_to_all(copies, SENS_AXES, 0, 0, tiled=True).reshape(steered.shape)
     bar_real = bar[0]
     bar_imag = bar[1]
 

time: 238 us -> 68.8 us (0.29)
  blocking collectives: 158 us -> 15.7 us
  starting transfers between devices: 49.2 us -> 22.3 us
    all_gather x1 -> x0, blocking collectives: 158 us -> none  [on_device(): bar = lax.all_gather(chunk, SENS_AXES, tiled=True).reshape(steered.shape)]
    ppermute x6, starting transfers between devices: 36.7 us -> 9.76 us  [shifted(): lax.ppermute(x, axis, [(j, (j + shift) % count) for j in range(count)])]
    all_to_all x0 -> x1, blocking collectives: none -> 15.7 us  [on_device(): lax.all_to_all(copies, SENS_AXES, 0, 0, tiled=True).reshape(steered.shape)]
  transfers between devices with their start and end apart: 7 -> 7, of which waited for: 3 -> 4; matrix products, arithmetic and copies ran while one was open for 2% -> 8% of each run, Pallas kernels for 0% -> 0%
where the time goes in v10:
time: 68.8 us; the launch traced here: 68.4 us
  starting transfers between devices  22.3 us (32%)
  blocking collectives  15.7 us (23%)
  waiting for transfers between devices  13.9 us (20%)
  other arithmetic  12.2 us (18%)
  local copies, waits for them, and re-layouts  2.38 us (3%)
  matrix products  1.79 us (3%)
    all_to_all x1, blocking collectives, on_device(): lax.all_to_all(copies, SENS_AXES, 0, 0, tiled=True).reshape(steered.shape)  15.7 us
    all_to_all x1, starting transfers between devices, on_device(): chunk = jnp.sum(lax.all_to_all(parts, SENS_AXES, 0, 0, tiled=True), axis=0)  12.6 us
    all_to_all x1, waiting for transfers between devices, on_device(): chunk = jnp.sum(lax.all_to_all(parts, SENS_AXES, 0, 0, tiled=True), axis=0)  10.7 us
    ppermute x6, starting transfers between devices, shifted(): lax.ppermute(x, axis, [(j, (j + shift) % count) for j in range(count)])  9.76 us
    select_n x1, other arithmetic, circle_point(): sine = jnp.where(quadrant >= 2, -sine, sine)  4.77 us
    ppermute x6, waiting for transfers between devices, shifted(): lax.ppermute(x, axis, [(j, (j + shift) % count) for j in range(count)])  3.16 us
    reduce_sum x1, other arithmetic, on_device(): jnp.sum(real_t[:, :, None] * cosine - imag_t[:, :, None] * sine_part, axi...  3.09 us
    reduce_sum x1, other arithmetic, on_device(): jnp.sum(bar_real[:, None, :] * cosine + bar_imag[:, None, :] * sine_part,...  2.32 us
  transfers between devices with their start and end apart: 7, of which 4 were waited for; matrix products, arithmetic and copies ran while one was open for 8% of the time, Pallas kernels for 0%

profile of v10, /device:TPU:1, one launch (start us, length us, event | category | flops | bytes accessed | tf_op | source)
XLA Modules:
  0.0 68.4 jit_solution(2975510089621858343)
XLA Ops:
  0.0 1.1 %multiply_convert_fusion.1 = (bf16[1024,16]{0,1:T(8,128)(2,1)S(1)}, bf16[1024,16]{0,1:T(8,128)(2,1)S(1)}) fusion(s32[16]{0:T(128)} %param.5, s32[1024]{0:T(1024)S(1)} %iota_add_fusion), kind=kLoop, calls=%fused_computation.42 | loop fusion | flops 311296 | bytes 69696 | tf_op jit(solution)/shard_map/convert
  1.1 1.0 %fusion.13 = f32[32,32]{1,0:T(8,128)S(1)} fusion(bf16[32,1024]{1,0:T(8,128)(2,1)} %param.4, bf16[1024,16]{0,1:T(8,128)(2,1)S(1)} %get-tuple-element.20, bf16[1024,16]{0,1:T(8,128)(2,1)S(1)} %get-tuple-element.19), kind=kOutput, calls=%fused_computation.43 | convolution fusion | flops 2228224 | bytes 135168 | tf_op jit(solution)/shard_map/dot_general | solution.py:81
  2.0 3.0 %collective-permute-start = (f32[32,32]{0,1:T(8,128)S(1)}, f32[32,32]{0,1:T(8,128)S(1)}, u32[]{:S(2)}, u32[]{:S(2)}) collective-permute-start(f32[32,32]{0,1:T(8,128)S(1)} %bitcast.31), channel_id=1, source_target_pairs={{0,1},{1,2},{2,3},{3,0},{4,5},{5,6},{6,7},{7,4},{8,9},{9,10},{10,1... | collective-permute-start | bytes 12296 | tf_op jit(solution)/shard_map/ppermute | solution.py:44
  5.1 1.5 %collective-permute-start.1 = (f32[32,32]{0,1:T(8,128)S(1)}, f32[32,32]{0,1:T(8,128)S(1)}, u32[]{:S(2)}, u32[]{:S(2)}) collective-permute-start(f32[32,32]{0,1:T(8,128)S(1)} %bitcast.32), channel_id=1, source_target_pairs={{0,2},{1,3},{2,0},{3,1},{4,6},{5,7},{6,4},{7,5},{8,10},{9,11},{10,... | collective-permute-start | bytes 12296 | tf_op jit(solution)/shard_map/ppermute | solution.py:44
  6.7 4.8 %negate_select_fusion = (f32[16,32,1024]{2,1,0:T(8,128)S(1)}, f32[16,32,1024]{2,1,0:T(8,128)}) fusion(s32[32,1024]{1,0:T(8,128)S(1)} %constant_dynamic-slice_fusion, s32[16]{0:T(128)} %param.5), kind=kLoop, calls=%fused_computation.2 | loop fusion | flops 22544384 | bytes 4325440 | tf_op jit(solution)/shard_map/jit(_where)/select_n | solution.py:37
  11.5 0.6 gather_fusion
  12.1 3.1 %subtract_reduce_fusion.1 = (f32[16,1024]{1,0:T(8,128)S(1)}, f32[16,1024]{1,0:T(8,128)S(1)}) fusion(f32[16,32,1024]{2,1,0:T(8,128)S(1)} %get-tuple-element.8, f32[16,32,1024]{2,1,0:T(8,128)} %get-tuple-element.7, f32[16,32]{1,0:T(8,128)S(1)} %get-tuple-element.18, f32[16,32]{1,0:T(8,128)S(1)} %get-tuple-element.17), kind=kLoop, calls=%fused_computation.13 | loop fusion | flops 4161536 | bytes 4329472 | tf_op jit(solution)/shard_map/reduce_sum | solution.py:91
  15.2 0.8 %mul.245 = f32[64,1,512]{2,1,0:T(1,128)} reshape(f32[2,16,1024]{2,1,0:T(8,128)S(1)} %maximum_multiply_fusion) | data formatting | bytes 262144 | tf_op jit(solution)/shard_map/mul | solution.py:93
  16.0 12.6 %all-to-all-start = ((f32[64,1,512]{2,1,0:T(1,128)}), f32[64,1,512]{2,1,0:T(1,128)S(1)}, u32[]{:S(2)}, u32[]{:S(2)}) async-start(f32[64,1,512]{2,1,0:T(1,128)} %mul.245), calls=%async_computation | async-start | bytes 262144 | tf_op jit(solution)/shard_map/all_to_all | solution.py:100
  28.6 0.7 %dynamic-slice_multiply_fusion = f32[1024]{0:T(1024)S(1)} fusion(f32[4096]{0:T(1024)} %param.7, s32[]{:T(128)S(6)} %select_n.63), kind=kLoop, calls=%fused_computation.51 | loop fusion | flops 1024 | bytes 8196 | tf_op jit(solution)/shard_map/mul | solution.py:87
  29.3 10.7 %all-to-all-done = f32[64,1,512]{2,1,0:T(1,128)S(1)} async-done(((f32[64,1,512]{2,1,0:T(1,128)}), f32[64,1,512]{2,1,0:T(1,128)S(1)}, u32[]{:S(2)}, u32[]{:S(2)}) %all-to-all-start) | async-done | bytes 131104 | tf_op jit(solution)/shard_map/all_to_all | solution.py:100
  40.0 0.1 reduce_sum.66
  40.1 0.1 dynamic-slice_multiply_fusion.1
  40.2 0.1 broadcast_in_dim.2
  40.3 15.7 %all_to_all.12 = f32[64,1,512]{2,1,0:T(1,128)S(1)} all-to-all(f32[64,1,512]{2,1,0:T(1,128)S(1)} %broadcast_in_dim.2), channel_id=1, replica_groups=mesh['sx'=4,'sz'=4,'sy'=4,'grp'=4] {'sx','sz','sy'}, dimensions={0} | all-to-all | bytes 262144 | tf_op jit(solution)/shard_map/all_to_all | solution.py:104
  55.9 0.3 slice_reduce_fusion.1
  56.3 2.3 %add_reduce_fusion = (f32[16,32]{1,0:T(8,128)S(1)}, f32[16,32]{1,0:T(8,128)S(1)}) fusion(f32[16,32,1024]{2,1,0:T(8,128)S(1)} %get-tuple-element.8, f32[16,32,1024]{2,1,0:T(8,128)} %get-tuple-element.7, f32[16,1024]{1,0:T(8,128)S(1)} %mul.236, f32[16,1024]{1,0:T(8,128)S(1)} %mul.233), kind=kLoop, calls=%fused_computation.11 | loop fusion | flops 4193280 | bytes 4329472 | tf_op jit(solution)/shard_map/reduce_sum | solution.py:108
  58.7 4.4 %collective-permute-start.3 = (f32[32,32]{0,1:T(8,128)S(1)}, f32[32,32]{0,1:T(8,128)S(1)}, u32[]{:S(2)}, u32[]{:S(2)}) collective-permute-start(f32[32,32]{0,1:T(8,128)S(1)} %maximum_multiply_fusion.2), channel_id=1, source_target_pairs={{0,1},{1,2},{2,3},{3,0},{4,5},{5,6},{6,7},{7,4},{8,9},{9,10},{10,1... | collective-permute-start | bytes 12296 | tf_op jit(solution)/shard_map/ppermute | solution.py:44
  63.1 0.8 %collective-permute-start.4 = (f32[32,32]{0,1:T(8,128)S(1)}, f32[32,32]{0,1:T(8,128)S(1)}, u32[]{:S(2)}, u32[]{:S(2)}) collective-permute-start(f32[32,32]{0,1:T(8,128)S(1)} %maximum_multiply_fusion.2), channel_id=1, source_target_pairs={{0,2},{1,3},{2,0},{3,1},{4,6},{5,7},{6,4},{7,5},{8,10},{9,11},{10,... | collective-permute-start | bytes 12296 | tf_op jit(solution)/shard_map/ppermute | solution.py:44
  63.9 0.1 collective-permute-done.3
  63.9 2.2 %collective-permute-done.4 = f32[32,32]{0,1:T(8,128)S(1)} collective-permute-done((f32[32,32]{0,1:T(8,128)S(1)}, f32[32,32]{0,1:T(8,128)S(1)}, u32[]{:S(2)}, u32[]{:S(2)}) %collective-permute-start.4) | collective-permute-done | bytes 4128 | tf_op jit(solution)/shard_map/ppermute | solution.py:44
  66.1 0.9 %collective-permute-done.5 = f32[32,32]{0,1:T(8,128)S(1)} collective-permute-done((f32[32,32]{0,1:T(8,128)S(1)}, f32[32,32]{0,1:T(8,128)S(1)}, u32[]{:S(2)}, u32[]{:S(2)}) %collective-permute-start.5) | collective-permute-done | bytes 4128 | tf_op jit(solution)/shard_map/ppermute | solution.py:44
  67.0 0.6 gather_fusion.1
  67.6 0.8 %convolution_convert_fusion = bf16[32,1024]{1,0:T(8,128)(2,1)} fusion(bf16[1024,16]{0,1:T(8,128)(2,1)S(1)} %get-tuple-element.20, bf16[1024,16]{0,1:T(8,128)(2,1)S(1)} %get-tuple-element.19, bf16[32,32]{0,1:T(8,128)(2,1)S(1)} %reduce_sum.69), kind=kOutput, calls=%fused_computation.26 | convolution fusion | flops 2260992 | bytes 133120 | tf_op jit(solution)/shard_map/dot_general | solution.py:113
  (21 shorter events, 0.2 us)
Async XLA Ops:
  0.0 6.6 %copy-start = (s32[32,4096]{1,0:T(8,128)S(1)}, s32[32,4096]{1,0:T(8,128)}, u32[]{:S(2)}) copy-start(s32[32,4096]{1,0:T(8,128)} %param.6) | copy-start | bytes 1572868
  2.0 9.4 %collective-permute-start = (f32[32,32]{0,1:T(8,128)S(1)}, f32[32,32]{0,1:T(8,128)S(1)}, u32[]{:S(2)}, u32[]{:S(2)}) collective-permute-start(f32[32,32]{0,1:T(8,128)S(1)} %bitcast.31), channel_id=1, source_target_pairs={{0,1},{1,2},{2,3},{3,0},{4,5},{5,6},{6,7},{7,4},{8,9},{9,10},{10,1... | collective-permute-start | bytes 12296 | tf_op jit(solution)/shard_map/ppermute | solution.py:44
  5.1 6.4 %collective-permute-start.1 = (f32[32,32]{0,1:T(8,128)S(1)}, f32[32,32]{0,1:T(8,128)S(1)}, u32[]{:S(2)}, u32[]{:S(2)}) collective-permute-start(f32[32,32]{0,1:T(8,128)S(1)} %bitcast.32), channel_id=1, source_target_pairs={{0,2},{1,3},{2,0},{3,1},{4,6},{5,7},{6,4},{7,5},{8,10},{9,11},{10,... | collective-permute-start | bytes 12296 | tf_op jit(solution)/shard_map/ppermute | solution.py:44
  6.6 4.8 %collective-permute-start.2 = (f32[32,32]{0,1:T(8,128)S(1)}, f32[32,32]{0,1:T(8,128)S(1)}, u32[]{:S(2)}, u32[]{:S(2)}) collective-permute-start(f32[32,32]{0,1:T(8,128)S(1)} %bitcast.33), channel_id=1, source_target_pairs={{0,3},{1,0},{2,1},{3,2},{4,7},{5,4},{6,5},{7,6},{8,11},{9,8},{10,9... | collective-permute-start | bytes 12296 | tf_op jit(solution)/shard_map/ppermute | solution.py:44
  16.0 24.0 %all-to-all-start = ((f32[64,1,512]{2,1,0:T(1,128)}), f32[64,1,512]{2,1,0:T(1,128)S(1)}, u32[]{:S(2)}, u32[]{:S(2)}) async-start(f32[64,1,512]{2,1,0:T(1,128)} %mul.245), calls=%async_computation | async-start | bytes 262144 | tf_op jit(solution)/shard_map/all_to_all | solution.py:100
  58.7 5.3 %collective-permute-start.3 = (f32[32,32]{0,1:T(8,128)S(1)}, f32[32,32]{0,1:T(8,128)S(1)}, u32[]{:S(2)}, u32[]{:S(2)}) collective-permute-start(f32[32,32]{0,1:T(8,128)S(1)} %maximum_multiply_fusion.2), channel_id=1, source_target_pairs={{0,1},{1,2},{2,3},{3,0},{4,5},{5,6},{6,7},{7,4},{8,9},{9,10},{10,1... | collective-permute-start | bytes 12296 | tf_op jit(solution)/shard_map/ppermute | solution.py:44
  63.1 3.1 %collective-permute-start.4 = (f32[32,32]{0,1:T(8,128)S(1)}, f32[32,32]{0,1:T(8,128)S(1)}, u32[]{:S(2)}, u32[]{:S(2)}) collective-permute-start(f32[32,32]{0,1:T(8,128)S(1)} %maximum_multiply_fusion.2), channel_id=1, source_target_pairs={{0,2},{1,3},{2,0},{3,1},{4,6},{5,7},{6,4},{7,5},{8,10},{9,11},{10,... | collective-permute-start | bytes 12296 | tf_op jit(solution)/shard_map/ppermute | solution.py:44
  63.9 3.2 %collective-permute-start.5 = (f32[32,32]{0,1:T(8,128)S(1)}, f32[32,32]{0,1:T(8,128)S(1)}, u32[]{:S(2)}, u32[]{:S(2)}) collective-permute-start(f32[32,32]{0,1:T(8,128)S(1)} %maximum_multiply_fusion.2), channel_id=1, source_target_pairs={{0,3},{1,0},{2,1},{3,2},{4,7},{5,4},{6,5},{7,6},{8,11},{9,8},{10,9... | collective-permute-start | bytes 12296 | tf_op jit(solution)/shard_map/ppermute | solution.py:44

commit v11 on v10

--- a/solution.py
+++ b/solution.py
@@ -84,22 +84,24 @@
     imag_t = spectra[:, bins:].T
 
     own_delays = lax.dynamic_slice_in_dim(delays, position * scan_share, scan_share, 1)
-    own_weight = 2.0 * lax.dynamic_slice_in_dim(map_adjoint, position * scan_share, scan_share, 0)
     phase_index = (bin_index[:, None, None] * own_delays[None, :, :]) & (NT - 1)
     cosine, sine_part = lax.optimization_barrier(circle_point(phase_index, NT))
 
     steer_real = jnp.sum(real_t[:, :, None] * cosine - imag_t[:, :, None] * sine_part, axis=1)
     steer_imag = jnp.sum(real_t[:, :, None] * sine_part + imag_t[:, :, None] * cosine, axis=1)
-    steered = jnp.stack([steer_real, steer_imag]) * steer_scale
+    steered = jnp.stack([steer_real, steer_imag])
     offset = 0
     for axis in SENS_AXES:
         offset = offset * lax.axis_size(axis) + lax.axis_index(axis)
     count = lax.axis_size(SENS_AXES)
     parts = steered.reshape(count, steered.size // count)
     width = parts.shape[1]
-    chunk = jnp.sum(lax.all_to_all(parts, SENS_AXES, 0, 0, tiled=True), axis=0)
-    start = (offset * width) % scan_share
-    chunk = lax.dynamic_slice_in_dim(own_weight, start, width, 0) * chunk
+    moved, held_weight = lax.optimization_barrier(
+        (lax.all_to_all(parts, SENS_AXES, 0, 0, tiled=True), map_adjoint)
+    )
+    start = position * scan_share + (offset * width) % scan_share
+    chunk_weight = (2.0 * steer_scale) * lax.dynamic_slice_in_dim(held_weight, start, width, 0)
+    chunk = chunk_weight * jnp.sum(moved, axis=0)
     copies = jnp.broadcast_to(chunk[None], (count, width))
     bar = lax.all_to_all(copies, SENS_AXES, 0, 0, tiled=True).reshape(steered.shape)
     bar_real = bar[0]

time: 68.8 us -> 67.7 us (0.984)
  waiting for transfers between devices: 13.9 us -> 12.3 us
  starting transfers between devices: 22.3 us -> 23 us
    ppermute x6, waiting for transfers between devices: 3.16 us -> 0.87 us  [shifted(): lax.ppermute(x, axis, [(j, (j + shift) % count) for j in range(count)])]
    all_to_all x0 -> x1, local copies, waits for them, and re-layouts: none -> 0.8 us  [on_device(): lax.all_to_all(parts, SENS_AXES, 0, 0, tiled=True)]
    mul x1 -> x0, local copies, waits for them, and re-layouts: 0.8 us -> none  [on_device(): steered = jnp.stack([steer_real, steer_imag]) * steer_scale]
    all_to_all x1, waiting for transfers between devices: 10.7 us -> 11.4 us  [on_device(): lax.all_to_all(parts, SENS_AXES, 0, 0, tiled=True)]
  transfers between devices with their start and end apart: 7 -> 7, of which waited for: 4 -> 3; matrix products, arithmetic and copies ran while one was open for 8% -> 7% of each run, Pallas kernels for 0% -> 0%
where the time goes in v11:
time: 67.7 us; the launch traced here: 67.4 us
  starting transfers between devices  23 us (34%)
  blocking collectives  15.6 us (23%)
  waiting for transfers between devices  12.3 us (18%)
  other arithmetic  12.1 us (18%)
  local copies, waits for them, and re-layouts  2.39 us (4%)
  matrix products  1.79 us (3%)
    all_to_all x1, blocking collectives, on_device(): lax.all_to_all(copies, SENS_AXES, 0, 0, tiled=True).reshape(steered.shape)  15.6 us
    all_to_all x1, starting transfers between devices, on_device(): lax.all_to_all(parts, SENS_AXES, 0, 0, tiled=True)  12.6 us
    all_to_all x1, waiting for transfers between devices, on_device(): lax.all_to_all(parts, SENS_AXES, 0, 0, tiled=True)  11.4 us
    ppermute x6, starting transfers between devices, shifted(): lax.ppermute(x, axis, [(j, (j + shift) % count) for j in range(count)])  10.4 us
    select_n x1, other arithmetic, circle_point(): sine = jnp.where(quadrant >= 2, -sine, sine)  4.77 us
    reduce_sum x1, other arithmetic, on_device(): jnp.sum(real_t[:, :, None] * cosine - imag_t[:, :, None] * sine_part, axi...  3.09 us
    reduce_sum x1, other arithmetic, on_device(): jnp.sum(bar_real[:, None, :] * cosine + bar_imag[:, None, :] * sine_part,...  2.32 us
  transfers between devices with their start and end apart: 7, of which 3 were waited for; matrix products, arithmetic and copies ran while one was open for 7% of the time, Pallas kernels for 0%

profile of v11, /device:TPU:1, one launch (start us, length us, event | category | flops | bytes accessed | tf_op | source)
XLA Modules:
  0.0 67.4 jit_solution(15992822605690329384)
XLA Ops:
  0.0 1.1 %multiply_convert_fusion.1 = (bf16[1024,16]{0,1:T(8,128)(2,1)S(1)}, bf16[1024,16]{0,1:T(8,128)(2,1)S(1)}) fusion(s32[16]{0:T(128)} %param.5, s32[1024]{0:T(1024)S(1)} %iota_add_fusion), kind=kLoop, calls=%fused_computation.43 | loop fusion | flops 311296 | bytes 69696 | tf_op jit(solution)/shard_map/convert
  1.1 1.0 %fusion.13 = f32[32,32]{1,0:T(8,128)S(1)} fusion(bf16[32,1024]{1,0:T(8,128)(2,1)} %param.4, bf16[1024,16]{0,1:T(8,128)(2,1)S(1)} %get-tuple-element.24, bf16[1024,16]{0,1:T(8,128)(2,1)S(1)} %get-tuple-element.23), kind=kOutput, calls=%fused_computation.44 | convolution fusion | flops 2228224 | bytes 135168 | tf_op jit(solution)/shard_map/dot_general | solution.py:81
  2.0 2.5 %collective-permute-start.1 = (f32[32,32]{0,1:T(8,128)S(1)}, f32[32,32]{0,1:T(8,128)S(1)}, u32[]{:S(2)}, u32[]{:S(2)}) collective-permute-start(f32[32,32]{0,1:T(8,128)S(1)} %bitcast.35), channel_id=1, source_target_pairs={{0,2},{1,3},{2,0},{3,1},{4,6},{5,7},{6,4},{7,5},{8,10},{9,11},{10,... | collective-permute-start | bytes 12296 | tf_op jit(solution)/shard_map/ppermute | solution.py:44
  4.5 2.4 %collective-permute-start = (f32[32,32]{0,1:T(8,128)S(1)}, f32[32,32]{0,1:T(8,128)S(1)}, u32[]{:S(2)}, u32[]{:S(2)}) collective-permute-start(f32[32,32]{0,1:T(8,128)S(1)} %bitcast.36), channel_id=1, source_target_pairs={{0,1},{1,2},{2,3},{3,0},{4,5},{5,6},{6,7},{7,4},{8,9},{9,10},{10,1... | collective-permute-start | bytes 12296 | tf_op jit(solution)/shard_map/ppermute | solution.py:44
  6.9 4.8 %negate_select_fusion = (f32[16,32,1024]{2,1,0:T(8,128)S(1)}, f32[16,32,1024]{2,1,0:T(8,128)}) fusion(s32[32,1024]{1,0:T(8,128)S(1)} %constant_dynamic-slice_fusion, s32[16]{0:T(128)} %param.5), kind=kLoop, calls=%fused_computation.2 | loop fusion | flops 22544384 | bytes 4325440 | tf_op jit(solution)/shard_map/jit(_where)/select_n | solution.py:37
  11.7 0.0 collective-permute-done
  11.8 0.6 gather_fusion
  12.4 3.1 %subtract_reduce_fusion.1 = (f32[16,1024]{1,0:T(8,128)S(1)}, f32[16,1024]{1,0:T(8,128)S(1)}) fusion(f32[16,32,1024]{2,1,0:T(8,128)S(1)} %get-tuple-element.10, f32[16,32,1024]{2,1,0:T(8,128)} %get-tuple-element.9, f32[16,32]{1,0:T(8,128)S(1)} %get-tuple-element.22, f32[16,32]{1,0:T(8,128)S(1)} %get-tuple-element.21), kind=kLoop, calls=%fused_computation.13 | loop fusion | flops 4161536 | bytes 4329472 | tf_op jit(solution)/shard_map/reduce_sum | solution.py:90
  15.5 0.8 %all_to_all.16 = f32[64,1,512]{2,1,0:T(1,128)} reshape(f32[2,16,1024]{2,1,0:T(8,128)S(1)} %pad_maximum_fusion) | data formatting | bytes 262144 | tf_op jit(solution)/shard_map/all_to_all | solution.py:100
  16.3 12.6 %all-to-all-start = ((f32[64,1,512]{2,1,0:T(1,128)}), f32[64,1,512]{2,1,0:T(1,128)S(1)}, u32[]{:S(2)}, u32[]{:S(2)}) async-start(f32[64,1,512]{2,1,0:T(1,128)} %all_to_all.16), calls=%async_computation | async-start | bytes 262144 | tf_op jit(solution)/shard_map/all_to_all | solution.py:100
  28.9 11.4 %all-to-all-done = f32[64,1,512]{2,1,0:T(1,128)S(1)} async-done(((f32[64,1,512]{2,1,0:T(1,128)}), f32[64,1,512]{2,1,0:T(1,128)S(1)}, u32[]{:S(2)}, u32[]{:S(2)}) %all-to-all-start) | async-done | bytes 131104 | tf_op jit(solution)/shard_map/all_to_all | solution.py:100
  40.3 0.8 %multiply_multiply_fusion.1 = f32[512]{0:T(512)S(1)} fusion(f32[512]{0:T(512)S(1)} %reduce_sum.66, f32[4096]{0:T(1024)} %param.7, s32[]{:T(128)S(6)} %select_n.72), kind=kLoop, calls=%fused_computation.55 | loop fusion | flops 1024 | bytes 6148 | tf_op jit(solution)/shard_map/mul | solution.py:104
  41.1 0.1 broadcast_in_dim.2
  41.2 15.6 %all_to_all.19 = f32[64,1,512]{2,1,0:T(1,128)S(1)} all-to-all(f32[64,1,512]{2,1,0:T(1,128)S(1)} %broadcast_in_dim.2), channel_id=1, replica_groups=mesh['sx'=4,'sz'=4,'sy'=4,'grp'=4] {'sx','sz','sy'}, dimensions={0} | all-to-all | bytes 262144 | tf_op jit(solution)/shard_map/all_to_all | solution.py:106
  56.8 0.3 slice_reduce_fusion.1
  57.2 2.3 %add_reduce_fusion = (f32[16,32]{1,0:T(8,128)S(1)}, f32[16,32]{1,0:T(8,128)S(1)}) fusion(f32[16,32,1024]{2,1,0:T(8,128)S(1)} %get-tuple-element.10, f32[16,32,1024]{2,1,0:T(8,128)} %get-tuple-element.9, f32[16,1024]{1,0:T(8,128)S(1)} %mul.216, f32[16,1024]{1,0:T(8,128)S(1)} %mul.213), kind=kLoop, calls=%fused_computation.11 | loop fusion | flops 4193280 | bytes 4329472 | tf_op jit(solution)/shard_map/reduce_sum | solution.py:110
  59.6 3.8 %collective-permute-start.5 = (f32[32,32]{0,1:T(8,128)S(1)}, f32[32,32]{0,1:T(8,128)S(1)}, u32[]{:S(2)}, u32[]{:S(2)}) collective-permute-start(f32[32,32]{0,1:T(8,128)S(1)} %maximum_multiply_fusion.1), channel_id=1, source_target_pairs={{0,3},{1,0},{2,1},{3,2},{4,7},{5,4},{6,5},{7,6},{8,11},{9,8},{10,9... | collective-permute-start | bytes 12296 | tf_op jit(solution)/shard_map/ppermute | solution.py:44
  63.4 0.7 collective-permute-start.4
  64.1 1.1 %collective-permute-start.3 = (f32[32,32]{0,1:T(8,128)S(1)}, f32[32,32]{0,1:T(8,128)S(1)}, u32[]{:S(2)}, u32[]{:S(2)}) collective-permute-start(f32[32,32]{0,1:T(8,128)S(1)} %maximum_multiply_fusion.1), channel_id=1, source_target_pairs={{0,1},{1,2},{2,3},{3,0},{4,5},{5,6},{6,7},{7,4},{8,9},{9,10},{10,1... | collective-permute-start | bytes 12296 | tf_op jit(solution)/shard_map/ppermute | solution.py:44
  65.1 0.2 collective-permute-done.5
  65.4 0.6 collective-permute-done.4
  66.0 0.0 collective-permute-done.3
  66.0 0.6 gather_fusion.1
  66.6 0.8 %convolution_convert_fusion = bf16[32,1024]{1,0:T(8,128)(2,1)} fusion(bf16[1024,16]{0,1:T(8,128)(2,1)S(1)} %get-tuple-element.24, bf16[1024,16]{0,1:T(8,128)(2,1)S(1)} %get-tuple-element.23, bf16[32,32]{0,1:T(8,128)(2,1)S(1)} %reduce_sum.69), kind=kOutput, calls=%fused_computation.26 | convolution fusion | flops 2260992 | bytes 133120 | tf_op jit(solution)/shard_map/dot_general | solution.py:115
  (21 shorter events, 0.2 us)
Async XLA Ops:
  0.0 6.9 %copy-start = (s32[32,4096]{1,0:T(8,128)S(1)}, s32[32,4096]{1,0:T(8,128)}, u32[]{:S(2)}) copy-start(s32[32,4096]{1,0:T(8,128)} %param.6) | copy-start | bytes 1572868
  2.0 9.7 %collective-permute-start.1 = (f32[32,32]{0,1:T(8,128)S(1)}, f32[32,32]{0,1:T(8,128)S(1)}, u32[]{:S(2)}, u32[]{:S(2)}) collective-permute-start(f32[32,32]{0,1:T(8,128)S(1)} %bitcast.35), channel_id=1, source_target_pairs={{0,2},{1,3},{2,0},{3,1},{4,6},{5,7},{6,4},{7,5},{8,10},{9,11},{10,... | collective-permute-start | bytes 12296 | tf_op jit(solution)/shard_map/ppermute | solution.py:44
  4.5 7.2 %collective-permute-start = (f32[32,32]{0,1:T(8,128)S(1)}, f32[32,32]{0,1:T(8,128)S(1)}, u32[]{:S(2)}, u32[]{:S(2)}) collective-permute-start(f32[32,32]{0,1:T(8,128)S(1)} %bitcast.36), channel_id=1, source_target_pairs={{0,1},{1,2},{2,3},{3,0},{4,5},{5,6},{6,7},{7,4},{8,9},{9,10},{10,1... | collective-permute-start | bytes 12296 | tf_op jit(solution)/shard_map/ppermute | solution.py:44
  6.9 4.8 %collective-permute-start.2 = (f32[32,32]{0,1:T(8,128)S(1)}, f32[32,32]{0,1:T(8,128)S(1)}, u32[]{:S(2)}, u32[]{:S(2)}) collective-permute-start(f32[32,32]{0,1:T(8,128)S(1)} %bitcast.37), channel_id=1, source_target_pairs={{0,3},{1,0},{2,1},{3,2},{4,7},{5,4},{6,5},{7,6},{8,11},{9,8},{10,9... | collective-permute-start | bytes 12296 | tf_op jit(solution)/shard_map/ppermute | solution.py:44
  16.3 24.0 %all-to-all-start = ((f32[64,1,512]{2,1,0:T(1,128)}), f32[64,1,512]{2,1,0:T(1,128)S(1)}, u32[]{:S(2)}, u32[]{:S(2)}) async-start(f32[64,1,512]{2,1,0:T(1,128)} %all_to_all.16), calls=%async_computation | async-start | bytes 262144 | tf_op jit(solution)/shard_map/all_to_all | solution.py:100
  59.6 5.8 %collective-permute-start.5 = (f32[32,32]{0,1:T(8,128)S(1)}, f32[32,32]{0,1:T(8,128)S(1)}, u32[]{:S(2)}, u32[]{:S(2)}) collective-permute-start(f32[32,32]{0,1:T(8,128)S(1)} %maximum_multiply_fusion.1), channel_id=1, source_target_pairs={{0,3},{1,0},{2,1},{3,2},{4,7},{5,4},{6,5},{7,6},{8,11},{9,8},{10,9... | collective-permute-start | bytes 12296 | tf_op jit(solution)/shard_map/ppermute | solution.py:44
  63.4 2.6 %collective-permute-start.4 = (f32[32,32]{0,1:T(8,128)S(1)}, f32[32,32]{0,1:T(8,128)S(1)}, u32[]{:S(2)}, u32[]{:S(2)}) collective-permute-start(f32[32,32]{0,1:T(8,128)S(1)} %maximum_multiply_fusion.1), channel_id=1, source_target_pairs={{0,2},{1,3},{2,0},{3,1},{4,6},{5,7},{6,4},{7,5},{8,10},{9,11},{10,... | collective-permute-start | bytes 12296 | tf_op jit(solution)/shard_map/ppermute | solution.py:44
  64.1 1.9 %collective-permute-start.3 = (f32[32,32]{0,1:T(8,128)S(1)}, f32[32,32]{0,1:T(8,128)S(1)}, u32[]{:S(2)}, u32[]{:S(2)}) collective-permute-start(f32[32,32]{0,1:T(8,128)S(1)} %maximum_multiply_fusion.1), channel_id=1, source_target_pairs={{0,1},{1,2},{2,3},{3,0},{4,5},{5,6},{6,7},{7,4},{8,9},{9,10},{10,1... | collective-permute-start | bytes 12296 | tf_op jit(solution)/shard_map/ppermute | solution.py:44

commit v12 on v11

--- a/solution.py
+++ b/solution.py
@@ -44,6 +44,13 @@
     return lax.ppermute(x, axis, [(j, (j + shift) % count) for j in range(count)])
 
 
+def ring_sum(x, axis):
+    total = x
+    for shift in range(1, lax.axis_size(axis)):
+        total = total + shifted(x, axis, shift)
+    return total
+
+
 def gather_stack(x, axis):
     count = lax.axis_size(axis)
     me = lax.axis_index(axis)
@@ -79,7 +86,7 @@
 
     transform = transform_rows(position * samples, samples, bin_index, NT)
     spectra = jnp.dot(histories, transform, preferred_element_type=jnp.float32)
-    spectra = jnp.sum(gather_stack(spectra, "grp"), axis=0)
+    spectra = ring_sum(spectra, "grp")
     real_t = spectra[:, :bins].T
     imag_t = spectra[:, bins:].T
 
@@ -96,11 +103,10 @@
     count = lax.axis_size(SENS_AXES)
     parts = steered.reshape(count, steered.size // count)
     width = parts.shape[1]
-    moved, held_weight = lax.optimization_barrier(
-        (lax.all_to_all(parts, SENS_AXES, 0, 0, tiled=True), map_adjoint)
-    )
     start = position * scan_share + (offset * width) % scan_share
-    chunk_weight = (2.0 * steer_scale) * lax.dynamic_slice_in_dim(held_weight, start, width, 0)
+    chunk_weight = (2.0 * steer_scale) * lax.dynamic_slice_in_dim(map_adjoint, start, width, 0)
+    parts, chunk_weight = lax.optimization_barrier((parts, chunk_weight))
+    moved = lax.all_to_all(parts, SENS_AXES, 0, 0, tiled=True)
     chunk = chunk_weight * jnp.sum(moved, axis=0)
     copies = jnp.broadcast_to(chunk[None], (count, width))
     bar = lax.all_to_all(copies, SENS_AXES, 0, 0, tiled=True).reshape(steered.shape)
@@ -110,7 +116,7 @@
     back_real = jnp.sum(bar_real[:, None, :] * cosine + bar_imag[:, None, :] * sine_part, axis=2)
     back_imag = jnp.sum(bar_imag[:, None, :] * cosine - bar_real[:, None, :] * sine_part, axis=2)
     back = jnp.concatenate([back_real.T, back_imag.T], 1) * steer_scale
-    back = jnp.sum(gather_stack(back, "grp"), axis=0)
+    back = ring_sum(back, "grp")
     adjoint = back.astype(jnp.bfloat16)
     local_part = lax.dot_general(
         adjoint, transform, (((1,), (1,)), ((), ())), preferred_element_type=jnp.float32

time: 67.7 us -> 67 us (0.990)
  blocking collectives: 15.6 us -> 40.8 us
  starting transfers between devices: 23 us -> 9.35 us
  waiting for transfers between devices: 12.3 us -> 1.92 us
  local copies, waits for them, and re-layouts: 2.39 us -> 0.58 us
    all_to_all x0 -> x1, blocking collectives: none -> 25.3 us  [on_device(): moved = lax.all_to_all(parts, SENS_AXES, 0, 0, tiled=True)]
    all_to_all x1 -> x0, starting transfers between devices: 12.6 us -> none  [on_device(): lax.all_to_all(parts, SENS_AXES, 0, 0, tiled=True)]
    all_to_all x1 -> x0, waiting for transfers between devices: 11.4 us -> none  [on_device(): lax.all_to_all(parts, SENS_AXES, 0, 0, tiled=True)]
    gather x2 -> x0, local copies, waits for them, and re-layouts: 1.1 us -> none  [gather_stack(): return stack[(me - jnp.arange(count)) % count]]
    ppermute x6, starting transfers between devices: 10.4 us -> 9.35 us  [shifted(): lax.ppermute(x, axis, [(j, (j + shift) % count) for j in range(count)])]
    ppermute x6, waiting for transfers between devices: 0.87 us -> 1.92 us  [shifted(): lax.ppermute(x, axis, [(j, (j + shift) % count) for j in range(count)])]
    mul x1, other arithmetic: 0.78 us -> 0.01 us  [on_device(): chunk = chunk_weight * jnp.sum(moved, axis=0)]
    mul x0 -> x1, other arithmetic: none -> 0.77 us  [on_device(): 2.0 * steer_scale * lax.dynamic_slice_in_dim(map_adjoint, start, width, 0)]
  transfers between devices with their start and end apart: 7 -> 6, of which waited for: 3 -> 1; matrix products, arithmetic and copies ran while one was open for 7% -> 8% of each run, Pallas kernels for 0% -> 0%
where the time goes in v12:
time: 67 us; the launch traced here: 66.7 us
  blocking collectives  40.8 us (61%)
  other arithmetic  12.2 us (18%)
  starting transfers between devices  9.35 us (14%)
  waiting for transfers between devices  1.92 us (3%)
  matrix products  1.8 us (3%)
    all_to_all x1, blocking collectives, on_device(): moved = lax.all_to_all(parts, SENS_AXES, 0, 0, tiled=True)  25.3 us
    all_to_all x1, blocking collectives, on_device(): lax.all_to_all(copies, SENS_AXES, 0, 0, tiled=True).reshape(steered.shape)  15.5 us
    ppermute x6, starting transfers between devices, shifted(): lax.ppermute(x, axis, [(j, (j + shift) % count) for j in range(count)])  9.35 us
    select_n x1, other arithmetic, circle_point(): sine = jnp.where(quadrant >= 2, -sine, sine)  4.77 us
    reduce_sum x1, other arithmetic, on_device(): jnp.sum(real_t[:, :, None] * cosine - imag_t[:, :, None] * sine_part, axi...  3.09 us
    reduce_sum x1, other arithmetic, on_device(): jnp.sum(bar_real[:, None, :] * cosine + bar_imag[:, None, :] * sine_part,...  2.32 us
    ppermute x6, waiting for transfers between devices, shifted(): lax.ppermute(x, axis, [(j, (j + shift) % count) for j in range(count)])  1.92 us
  transfers between devices with their start and end apart: 6, of which 1 were waited for; matrix products, arithmetic and copies ran while one was open for 8% of the time, Pallas kernels for 0%

profile of v12, /device:TPU:1, one launch (start us, length us, event | category | flops | bytes accessed | tf_op | source)
XLA Modules:
  0.0 66.7 jit_solution(784140855245304328)
XLA Ops:
  0.0 1.1 %multiply_convert_fusion.1 = (bf16[1024,16]{0,1:T(8,128)(2,1)S(1)}, bf16[1024,16]{0,1:T(8,128)(2,1)S(1)}) fusion(s32[16]{0:T(128)} %param.5, s32[1024]{0:T(1024)S(1)} %iota_add_fusion), kind=kLoop, calls=%fused_computation.39 | loop fusion | flops 311296 | bytes 69696 | tf_op jit(solution)/shard_map/convert
  1.1 1.0 %convolution_bitcast_fusion = f32[32,32]{0,1:T(8,128)S(1)} fusion(bf16[32,1024]{1,0:T(8,128)(2,1)} %param.4, bf16[1024,16]{0,1:T(8,128)(2,1)S(1)} %get-tuple-element.24, bf16[1024,16]{0,1:T(8,128)(2,1)S(1)} %get-tuple-element.23), kind=kOutput, calls=%fused_computation.25 | convolution fusion | flops 2228224 | bytes 135168 | tf_op jit(solution)/shard_map/dot_general | solution.py:88
  2.0 3.2 %collective-permute-start.2 = (f32[32,32]{0,1:T(8,128)S(1)}, f32[32,32]{0,1:T(8,128)S(1)}, u32[]{:S(2)}, u32[]{:S(2)}) collective-permute-start(f32[32,32]{0,1:T(8,128)S(1)} %convolution_bitcast_fusion), channel_id=1, source_target_pairs={{0,3},{1,0},{2,1},{3,2},{4,7},{5,4},{6,5},{7,6},{8,11},{9,8},{10,9... | collective-permute-start | bytes 12296 | tf_op jit(solution)/shard_map/ppermute | solution.py:44
  5.3 0.0 collective-permute-start.1
  5.3 1.7 %collective-permute-start = (f32[32,32]{0,1:T(8,128)S(1)}, f32[32,32]{0,1:T(8,128)S(1)}, u32[]{:S(2)}, u32[]{:S(2)}) collective-permute-start(f32[32,32]{0,1:T(8,128)S(1)} %convolution_bitcast_fusion), channel_id=1, source_target_pairs={{0,1},{1,2},{2,3},{3,0},{4,5},{5,6},{6,7},{7,4},{8,9},{9,10},{10,1... | collective-permute-start | bytes 12296 | tf_op jit(solution)/shard_map/ppermute | solution.py:44
  7.0 4.8 %negate_select_fusion = (f32[16,32,1024]{2,1,0:T(8,128)S(1)}, f32[16,32,1024]{2,1,0:T(8,128)}) fusion(s32[32,1024]{1,0:T(8,128)S(1)} %constant_dynamic-slice_fusion, s32[16]{0:T(128)} %param.5), kind=kLoop, calls=%fused_computation | loop fusion | flops 22544384 | bytes 4325440 | tf_op jit(solution)/shard_map/jit(_where)/select_n | solution.py:37
  11.8 0.8 %dynamic-slice_multiply_fusion = f32[512]{0:T(512)S(1)} fusion(f32[4096]{0:T(1024)} %param.7, s32[]{:T(128)S(6)} %select_n.44), kind=kLoop, calls=%fused_computation.46 | loop fusion | flops 512 | bytes 4100 | tf_op jit(solution)/shard_map/mul | solution.py:107
  12.5 0.0 collective-permute-done.2
  12.5 0.0 collective-permute-done.1
  12.5 0.0 collective-permute-done
  12.6 3.1 %subtract_reduce_fusion.1 = (f32[16,1024]{1,0:T(8,128)S(1)}, f32[16,1024]{1,0:T(8,128)S(1)}) fusion(f32[16,32,1024]{2,1,0:T(8,128)S(1)} %get-tuple-element.10, f32[16,32,1024]{2,1,0:T(8,128)} %get-tuple-element.9, f32[16,32]{1,0:T(8,128)S(1)} %get-tuple-element.22, f32[16,32]{1,0:T(8,128)S(1)} %get-tuple-element.21), kind=kLoop, calls=%fused_computation.11 | loop fusion | flops 4161536 | bytes 4329472 | tf_op jit(solution)/shard_map/reduce_sum | solution.py:97
  15.7 0.1 all_to_all.10
  15.8 25.3 %all_to_all.15 = f32[64,1,512]{2,1,0:T(1,128)S(1)} all-to-all(f32[64,1,512]{2,1,0:T(1,128)S(1)} %all_to_all.10), channel_id=1, replica_groups=mesh['sx'=4,'sz'=4,'sy'=4,'grp'=4] {'sx','sz','sy'}, dimensions={0} | all-to-all | bytes 262144 | tf_op jit(solution)/shard_map/all_to_all | solution.py:109
  41.1 0.1 reduce_sum.47
  41.3 0.1 broadcast_in_dim.2
  41.3 15.5 %all_to_all.16 = f32[64,1,512]{2,1,0:T(1,128)S(1)} all-to-all(f32[64,1,512]{2,1,0:T(1,128)S(1)} %broadcast_in_dim.2), channel_id=1, replica_groups=mesh['sx'=4,'sz'=4,'sy'=4,'grp'=4] {'sx','sz','sy'}, dimensions={0} | all-to-all | bytes 262144 | tf_op jit(solution)/shard_map/all_to_all | solution.py:112
  56.8 0.3 slice_reduce_fusion.1
  57.2 2.3 %add_reduce_fusion = (f32[16,32]{1,0:T(8,128)S(1)}, f32[16,32]{1,0:T(8,128)S(1)}) fusion(f32[16,32,1024]{2,1,0:T(8,128)S(1)} %get-tuple-element.10, f32[16,32,1024]{2,1,0:T(8,128)} %get-tuple-element.9, f32[16,1024]{1,0:T(8,128)S(1)} %mul.205, f32[16,1024]{1,0:T(8,128)S(1)} %mul.202), kind=kLoop, calls=%fused_computation.9 | loop fusion | flops 4193280 | bytes 4329472 | tf_op jit(solution)/shard_map/reduce_sum | solution.py:116
  59.5 0.9 %collective-permute-start.4 = (f32[32,32]{0,1:T(8,128)S(1)}, f32[32,32]{0,1:T(8,128)S(1)}, u32[]{:S(2)}, u32[]{:S(2)}) collective-permute-start(f32[32,32]{0,1:T(8,128)S(1)} %maximum_multiply_fusion), channel_id=1, source_target_pairs={{0,2},{1,3},{2,0},{3,1},{4,6},{5,7},{6,4},{7,5},{8,10},{9,11},{10,... | collective-permute-start | bytes 12296 | tf_op jit(solution)/shard_map/ppermute | solution.py:44
  60.4 2.5 %collective-permute-start.5 = (f32[32,32]{0,1:T(8,128)S(1)}, f32[32,32]{0,1:T(8,128)S(1)}, u32[]{:S(2)}, u32[]{:S(2)}) collective-permute-start(f32[32,32]{0,1:T(8,128)S(1)} %maximum_multiply_fusion), channel_id=1, source_target_pairs={{0,3},{1,0},{2,1},{3,2},{4,7},{5,4},{6,5},{7,6},{8,11},{9,8},{10,9... | collective-permute-start | bytes 12296 | tf_op jit(solution)/shard_map/ppermute | solution.py:44
  62.9 1.0 %collective-permute-start.3 = (f32[32,32]{0,1:T(8,128)S(1)}, f32[32,32]{0,1:T(8,128)S(1)}, u32[]{:S(2)}, u32[]{:S(2)}) collective-permute-start(f32[32,32]{0,1:T(8,128)S(1)} %maximum_multiply_fusion), channel_id=1, source_target_pairs={{0,1},{1,2},{2,3},{3,0},{4,5},{5,6},{6,7},{7,4},{8,9},{9,10},{10,1... | collective-permute-start | bytes 12296 | tf_op jit(solution)/shard_map/ppermute | solution.py:44
  63.9 0.0 collective-permute-done.4
  63.9 1.9 %collective-permute-done.5 = f32[32,32]{0,1:T(8,128)S(1)} collective-permute-done((f32[32,32]{0,1:T(8,128)S(1)}, f32[32,32]{0,1:T(8,128)S(1)}, u32[]{:S(2)}, u32[]{:S(2)}) %collective-permute-start.5) | collective-permute-done | bytes 4128 | tf_op jit(solution)/shard_map/ppermute | solution.py:44
  65.9 0.8 %convolution_convert_fusion = bf16[32,1024]{1,0:T(8,128)(2,1)} fusion(bf16[1024,16]{0,1:T(8,128)(2,1)S(1)} %get-tuple-element.24, bf16[1024,16]{0,1:T(8,128)(2,1)S(1)} %get-tuple-element.23, f32[32,32]{0,1:T(8,128)S(1)} %collective-permute-done.5, f32[32,32]{0,1:T(8,128)S(1)} %collective-permute-done.4, f32[32,32]{0,1:T(8,128)S(1)} %collective-permute-done.3, ...), kind=kOutput, calls=%fused_computation.24 | convolution fusion | flops 2267136 | bytes 147456 | tf_op jit(solution)/shard_map/dot_general | solution.py:121
  (13 shorter events, 0.1 us)
Async XLA Ops:
  0.0 7.0 %copy-start = (s32[32,4096]{1,0:T(8,128)S(1)}, s32[32,4096]{1,0:T(8,128)}, u32[]{:S(2)}) copy-start(s32[32,4096]{1,0:T(8,128)} %param.6) | copy-start | bytes 1572868
  2.0 10.5 %collective-permute-start.2 = (f32[32,32]{0,1:T(8,128)S(1)}, f32[32,32]{0,1:T(8,128)S(1)}, u32[]{:S(2)}, u32[]{:S(2)}) collective-permute-start(f32[32,32]{0,1:T(8,128)S(1)} %convolution_bitcast_fusion), channel_id=1, source_target_pairs={{0,3},{1,0},{2,1},{3,2},{4,7},{5,4},{6,5},{7,6},{8,11},{9,8},{10,9... | collective-permute-start | bytes 12296 | tf_op jit(solution)/shard_map/ppermute | solution.py:44
  5.3 7.3 %collective-permute-start.1 = (f32[32,32]{0,1:T(8,128)S(1)}, f32[32,32]{0,1:T(8,128)S(1)}, u32[]{:S(2)}, u32[]{:S(2)}) collective-permute-start(f32[32,32]{0,1:T(8,128)S(1)} %convolution_bitcast_fusion), channel_id=1, source_target_pairs={{0,2},{1,3},{2,0},{3,1},{4,6},{5,7},{6,4},{7,5},{8,10},{9,11},{10,... | collective-permute-start | bytes 12296 | tf_op jit(solution)/shard_map/ppermute | solution.py:44
  5.3 7.3 %collective-permute-start = (f32[32,32]{0,1:T(8,128)S(1)}, f32[32,32]{0,1:T(8,128)S(1)}, u32[]{:S(2)}, u32[]{:S(2)}) collective-permute-start(f32[32,32]{0,1:T(8,128)S(1)} %convolution_bitcast_fusion), channel_id=1, source_target_pairs={{0,1},{1,2},{2,3},{3,0},{4,5},{5,6},{6,7},{7,4},{8,9},{9,10},{10,1... | collective-permute-start | bytes 12296 | tf_op jit(solution)/shard_map/ppermute | solution.py:44
  59.5 4.4 %collective-permute-start.4 = (f32[32,32]{0,1:T(8,128)S(1)}, f32[32,32]{0,1:T(8,128)S(1)}, u32[]{:S(2)}, u32[]{:S(2)}) collective-permute-start(f32[32,32]{0,1:T(8,128)S(1)} %maximum_multiply_fusion), channel_id=1, source_target_pairs={{0,2},{1,3},{2,0},{3,1},{4,6},{5,7},{6,4},{7,5},{8,10},{9,11},{10,... | collective-permute-start | bytes 12296 | tf_op jit(solution)/shard_map/ppermute | solution.py:44
  60.4 5.5 %collective-permute-start.5 = (f32[32,32]{0,1:T(8,128)S(1)}, f32[32,32]{0,1:T(8,128)S(1)}, u32[]{:S(2)}, u32[]{:S(2)}) collective-permute-start(f32[32,32]{0,1:T(8,128)S(1)} %maximum_multiply_fusion), channel_id=1, source_target_pairs={{0,3},{1,0},{2,1},{3,2},{4,7},{5,4},{6,5},{7,6},{8,11},{9,8},{10,9... | collective-permute-start | bytes 12296 | tf_op jit(solution)/shard_map/ppermute | solution.py:44
  62.9 2.9 %collective-permute-start.3 = (f32[32,32]{0,1:T(8,128)S(1)}, f32[32,32]{0,1:T(8,128)S(1)}, u32[]{:S(2)}, u32[]{:S(2)}) collective-permute-start(f32[32,32]{0,1:T(8,128)S(1)} %maximum_multiply_fusion), channel_id=1, source_target_pairs={{0,1},{1,2},{2,3},{3,0},{4,5},{5,6},{6,7},{7,4},{8,9},{9,10},{10,1... | collective-permute-start | bytes 12296 | tf_op jit(solution)/shard_map/ppermute | solution.py:44

commit v13 on v12

--- a/solution.py
+++ b/solution.py
@@ -4,6 +4,9 @@
 import jax.numpy as jnp
 from jax import lax
 from jax.sharding import PartitionSpec as P
+from jax.experimental import pallas as pl
+from jax.experimental.pallas import tpu as pltpu
+import functools
 
 NT = 4096
 
@@ -37,6 +40,59 @@
     sine = jnp.where(quadrant >= 2, -sine, sine)
     cosine = jnp.where(((quadrant ^ (quadrant >> 1)) & 1) == 1, -cosine, cosine)
     return cosine, sine
+
+
+LANE_TILE = 128
+
+def forward_kernel(length, bins_ref, delays_ref, xr_ref, xi_ref, cos_ref, sin_ref, steer_ref):
+    group = cos_ref.shape[0]
+    width = delays_ref.shape[1]
+    first = pl.program_id(0) * group
+    for i in range(group):
+        b = bins_ref[first + i]
+        xr = xr_ref[i]
+        xi = xi_ref[i]
+        for j in range(width // LANE_TILE):
+            cols = pl.ds(j * LANE_TILE, LANE_TILE)
+            k = (delays_ref[:, cols] * b) & (length - 1)
+            c, s = circle_point(k, length)
+            cos_ref[i, :, cols] = c
+            sin_ref[i, :, cols] = s
+            steer_ref[i, 0:1, cols] = jnp.sum(xr * c - xi * s, axis=0, keepdims=True)
+            steer_ref[i, 1:2, cols] = jnp.sum(xr * s + xi * c, axis=0, keepdims=True)
+
+
+BIN_GROUP = 4
+
+
+def trig_forward(bin_index, delays, real_t, imag_t, length):
+    bins = bin_index.shape[0]
+    rows, width = delays.shape
+    group = math.gcd(bins, BIN_GROUP)
+    elems = bins * rows * width
+    return pl.pallas_call(
+        functools.partial(forward_kernel, length),
+        grid=(bins // group,),
+        out_shape=(
+            jax.ShapeDtypeStruct((bins, rows, width), jnp.float32),
+            jax.ShapeDtypeStruct((bins, rows, width), jnp.float32),
+            jax.ShapeDtypeStruct((bins, 2, width), jnp.float32),
+        ),
+        in_specs=[
+            pl.BlockSpec(memory_space=pltpu.SMEM),
+            pl.BlockSpec((rows, width), lambda g: (0, 0)),
+            pl.BlockSpec((group, rows, 1), lambda g: (g, 0, 0)),
+            pl.BlockSpec((group, rows, 1), lambda g: (g, 0, 0)),
+        ],
+        out_specs=(
+            pl.BlockSpec((group, rows, width), lambda g: (g, 0, 0)),
+            pl.BlockSpec((group, rows, width), lambda g: (g, 0, 0)),
+            pl.BlockSpec((group, 2, width), lambda g: (g, 0, 0)),
+        ),
+        cost_estimate=pl.CostEstimate(
+            flops=60 * elems, transcendentals=0, bytes_accessed=8 * elems + 4 * rows * width
+        ),
+    )(bin_index, delays, real_t[:, :, None], imag_t[:, :, None])
 
 
 def shifted(x, axis, shift):
@@ -91,12 +147,7 @@
     imag_t = spectra[:, bins:].T
 
     own_delays = lax.dynamic_slice_in_dim(delays, position * scan_share, scan_share, 1)
-    phase_index = (bin_index[:, None, None] * own_delays[None, :, :]) & (NT - 1)
-    cosine, sine_part = lax.optimization_barrier(circle_point(phase_index, NT))
-
-    steer_real = jnp.sum(real_t[:, :, None] * cosine - imag_t[:, :, None] * sine_part, axis=1)
-    steer_imag = jnp.sum(real_t[:, :, None] * sine_part + imag_t[:, :, None] * cosine, axis=1)
-    steered = jnp.stack([steer_real, steer_imag])
+    cosine, sine_part, steered = trig_forward(bin_index, own_delays, real_t, imag_t, NT)
     offset = 0
     for axis in SENS_AXES:
         offset = offset * lax.axis_size(axis) + lax.axis_index(axis)
@@ -110,8 +161,8 @@
     chunk = chunk_weight * jnp.sum(moved, axis=0)
     copies = jnp.broadcast_to(chunk[None], (count, width))
     bar = lax.all_to_all(copies, SENS_AXES, 0, 0, tiled=True).reshape(steered.shape)
-    bar_real = bar[0]
-    bar_imag = bar[1]
+    bar_real = bar[:, 0]
+    bar_imag = bar[:, 1]
 
     back_real = jnp.sum(bar_real[:, None, :] * cosine + bar_imag[:, None, :] * sine_part, axis=2)
     back_imag = jnp.sum(bar_imag[:, None, :] * cosine - bar_real[:, None, :] * sine_part, axis=2)

time: 67 us -> 70.7 us (1.055)
  other arithmetic: 12.2 us -> 4.66 us
  Pallas kernels: 0 us -> 5.78 us
  local copies, waits for them, and re-layouts: 0.58 us -> 3.97 us
  waiting for transfers between devices: 1.92 us -> 4.88 us
    pallas_call x0 -> x1, Pallas kernels: none -> 5.78 us  [trig_forward(): pl.pallas_call(functools.partial(forward_kernel, length), grid=(bins // g...]
    select_n x1 -> x0, other arithmetic: 4.77 us -> none  [circle_point(): sine = jnp.where(quadrant >= 2, -sine, sine)]
    reduce_sum x1 -> x0, other arithmetic: 3.09 us -> none  [on_device(): jnp.sum(real_t[:, :, None] * cosine - imag_t[:, :, None] * sine_part, axi...]
    ppermute x6, waiting for transfers between devices: 1.92 us -> 4.88 us  [shifted(): lax.ppermute(x, axis, [(j, (j + shift) % count) for j in range(count)])]
    broadcast_in_dim x0 -> x3, local copies, waits for them, and re-layouts: none -> 1.76 us  [the longest x2 0.89 us: trig_forward(): imag_t[:, :, None]]
    reshape x1, local copies, waits for them, and re-layouts: 0.02 us -> 1.16 us  [on_device(): parts = steered.reshape(count, steered.size // count)]
  transfers between devices with their start and end apart: 6 -> 6, of which waited for: 1 -> 3; matrix products, arithmetic and copies ran while one was open for 8% -> 2% of each run, Pallas kernels for 0% -> 0%
where the time goes in v13:
time: 70.7 us; the launch traced here: 70.3 us
  blocking collectives  40.4 us (57%)
  starting transfers between devices  8.69 us (12%)
  Pallas kernels  5.78 us (8%)
  waiting for transfers between devices  4.88 us (7%)
  other arithmetic  4.66 us (7%)
  local copies, waits for them, and re-layouts  3.97 us (6%)
  matrix products  1.8 us (3%)
    all_to_all x1, blocking collectives, on_device(): moved = lax.all_to_all(parts, SENS_AXES, 0, 0, tiled=True)  24.9 us
    all_to_all x1, blocking collectives, on_device(): lax.all_to_all(copies, SENS_AXES, 0, 0, tiled=True).reshape(steered.shape)  15.5 us
    ppermute x6, starting transfers between devices, shifted(): lax.ppermute(x, axis, [(j, (j + shift) % count) for j in range(count)])  8.69 us
    pallas_call x1, Pallas kernels, trig_forward(): pl.pallas_call(functools.partial(forward_kernel, length), grid=(bins // g...  5.78 us
    ppermute x6, waiting for transfers between devices, shifted(): lax.ppermute(x, axis, [(j, (j + shift) % count) for j in range(count)])  4.88 us
    reduce_sum x1, other arithmetic, on_device(): jnp.sum(bar_real[:, None, :] * cosine + bar_imag[:, None, :] * sine_part,...  2.38 us
  transfers between devices with their start and end apart: 6, of which 3 were waited for; matrix products, arithmetic and copies ran while one was open for 2% of the time, Pallas kernels for 0%

profile of v13, /device:TPU:1, one launch (start us, length us, event | category | flops | bytes accessed | tf_op | source)
XLA Modules:
  0.0 70.3 jit_solution(783509235333717768)
XLA Ops:
  0.0 1.1 %multiply_convert_fusion.1 = (bf16[1024,16]{0,1:T(8,128)(2,1)S(1)}, bf16[1024,16]{0,1:T(8,128)(2,1)S(1)}) fusion(s32[16]{0:T(128)} %bins_ref.1, s32[1024]{0:T(1024)S(1)} %iota_add_fusion), kind=kLoop, calls=%fused_computation.16 | loop fusion | flops 311296 | bytes 69696 | tf_op jit(solution)/shard_map/convert
  1.1 1.0 %convolution_bitcast_fusion = f32[32,32]{0,1:T(8,128)S(1)} fusion(bf16[32,1024]{1,0:T(8,128)(2,1)} %param.4, bf16[1024,16]{0,1:T(8,128)(2,1)S(1)} %get-tuple-element.22, bf16[1024,16]{0,1:T(8,128)(2,1)S(1)} %get-tuple-element.21), kind=kOutput, calls=%fused_computation.3 | convolution fusion | flops 2228224 | bytes 135168 | tf_op jit(solution)/shard_map/dot_general | solution.py:144
  2.0 3.0 %collective-permute-start = (f32[32,32]{0,1:T(8,128)S(1)}, f32[32,32]{0,1:T(8,128)S(1)}, u32[]{:S(2)}, u32[]{:S(2)}) collective-permute-start(f32[32,32]{0,1:T(8,128)S(1)} %convolution_bitcast_fusion), channel_id=1, source_target_pairs={{0,1},{1,2},{2,3},{3,0},{4,5},{5,6},{6,7},{7,4},{8,9},{9,10},{10,1... | collective-permute-start | bytes 12296 | tf_op jit(solution)/shard_map/ppermute | solution.py:100
  5.1 1.5 %collective-permute-start.1 = (f32[32,32]{0,1:T(8,128)S(1)}, f32[32,32]{0,1:T(8,128)S(1)}, u32[]{:S(2)}, u32[]{:S(2)}) collective-permute-start(f32[32,32]{0,1:T(8,128)S(1)} %convolution_bitcast_fusion), channel_id=1, source_target_pairs={{0,2},{1,3},{2,0},{3,1},{4,6},{5,7},{6,4},{7,5},{8,10},{9,11},{10,... | collective-permute-start | bytes 12296 | tf_op jit(solution)/shard_map/ppermute | solution.py:100
  6.6 0.7 constant_dynamic-slice_fusion.delays_ref
  7.3 0.8 %dynamic-slice_multiply_fusion = f32[512]{0:T(512)S(1)} fusion(f32[4096]{0:T(1024)} %param.7, s32[]{:T(128)S(6)} %select_n.22), kind=kLoop, calls=%fused_computation.23 | loop fusion | flops 512 | bytes 4100 | tf_op jit(solution)/shard_map/mul | solution.py:158
  8.1 1.7 %collective-permute-done.2 = f32[32,32]{0,1:T(8,128)S(1)} collective-permute-done((f32[32,32]{0,1:T(8,128)S(1)}, f32[32,32]{0,1:T(8,128)S(1)}, u32[]{:S(2)}, u32[]{:S(2)}) %collective-permute-start.2) | collective-permute-done | bytes 4128 | tf_op jit(solution)/shard_map/ppermute | solution.py:100
  9.8 0.9 %copy.10.xi_ref = f32[16,32,1]{2,1,0:T(8,128)} copy(f32[16,32,1]{1,0,2:T(8,128)S(1)} %get-tuple-element.19) | data formatting | bytes 4096 | tf_op jit(solution)/shard_map/broadcast_in_dim | solution.py:95
  10.7 0.9 %copy.9.xr_ref = f32[16,32,1]{2,1,0:T(8,128)} copy(f32[16,32,1]{1,0,2:T(8,128)S(1)} %get-tuple-element.20) | data formatting | bytes 4096 | tf_op jit(solution)/shard_map/broadcast_in_dim | solution.py:95
  11.5 5.8 %shard_map.46 = (f32[16,32,1024]{2,1,0:T(8,128)}, f32[16,32,1024]{2,1,0:T(8,128)}, f32[16,2,1024]{2,1,0:T(2,128)}) custom-call(s32[16]{0:T(128)} %bins_ref.1, s32[32,1024]{1,0:T(8,128)} %constant_dynamic-slice_fusion.delays_ref, f32[16,32,1]{2,1,0:T(8,128)} %copy.9.xr_ref, f32[16,32,1]{2,1,0:T(8,128)} %copy.10.xi_ref), custom_call_target="tpu_custom_call" | custom-call | flops 31457280 | bytes 4325376 | tf_op jit(solution)/shard_map/pallas_call | solution.py:73
  17.3 1.2 %reshape.20 = f32[64,512]{1,0:T(8,128)S(1)} reshape(f32[16,2,1024]{2,1,0:T(2,128)} %get-tuple-element.10) | data formatting | bytes 262144 | tf_op jit(solution)/shard_map/reshape | solution.py:155
  18.5 0.1 all_to_all.10
  18.6 24.9 %all_to_all.15 = f32[64,1,512]{2,1,0:T(1,128)S(1)} all-to-all(f32[64,1,512]{2,1,0:T(1,128)S(1)} %all_to_all.10), channel_id=1, replica_groups=mesh['sx'=4,'sz'=4,'sy'=4,'grp'=4] {'sx','sz','sy'}, dimensions={0} | all-to-all | bytes 262144 | tf_op jit(solution)/shard_map/all_to_all | solution.py:160
  43.5 0.1 reduce_sum.27
  43.7 15.5 %all_to_all.16 = f32[64,1,512]{2,1,0:T(1,128)S(1)} all-to-all(f32[64,1,512]{2,1,0:T(1,128)S(1)} %broadcast_in_dim.16), channel_id=1, replica_groups=mesh['sx'=4,'sz'=4,'sy'=4,'grp'=4] {'sx','sz','sy'}, dimensions={0} | all-to-all | bytes 262144 | tf_op jit(solution)/shard_map/all_to_all | solution.py:163
  59.2 0.3 reduce.1
  59.5 0.1 reshape.21
  59.6 0.1 fusion.5
  59.8 2.4 %add_reduce_fusion = (f32[16,32]{1,0:T(8,128)S(1)}, f32[16,32]{1,0:T(8,128)S(1)}) fusion(f32[16,32,1024]{2,1,0:T(8,128)} %get-tuple-element.14, f32[16,32,1024]{2,1,0:T(8,128)S(1)} %copy-done.1, f32[16,1024]{1,0:T(8,128)S(1)} %get-tuple-element.23, f32[16,1024]{1,0:T(8,128)S(1)} %get-tuple-element.24), kind=kLoop, calls=%fused_computation.1 | loop fusion | flops 4193280 | bytes 4329472 | tf_op jit(solution)/shard_map/reduce_sum | solution.py:167
  62.2 3.0 %collective-permute-start.3 = (f32[32,32]{0,1:T(8,128)S(1)}, f32[32,32]{0,1:T(8,128)S(1)}, u32[]{:S(2)}, u32[]{:S(2)}) collective-permute-start(f32[32,32]{0,1:T(8,128)S(1)} %maximum_multiply_fusion), channel_id=1, source_target_pairs={{0,1},{1,2},{2,3},{3,0},{4,5},{5,6},{6,7},{7,4},{8,9},{9,10},{10,1... | collective-permute-start | bytes 12296 | tf_op jit(solution)/shard_map/ppermute | solution.py:100
  65.2 1.1 %collective-permute-start.4 = (f32[32,32]{0,1:T(8,128)S(1)}, f32[32,32]{0,1:T(8,128)S(1)}, u32[]{:S(2)}, u32[]{:S(2)}) collective-permute-start(f32[32,32]{0,1:T(8,128)S(1)} %maximum_multiply_fusion), channel_id=1, source_target_pairs={{0,2},{1,3},{2,0},{3,1},{4,6},{5,7},{6,4},{7,5},{8,10},{9,11},{10,... | collective-permute-start | bytes 12296 | tf_op jit(solution)/shard_map/ppermute | solution.py:100
  66.3 1.5 %collective-permute-done.4 = f32[32,32]{0,1:T(8,128)S(1)} collective-permute-done((f32[32,32]{0,1:T(8,128)S(1)}, f32[32,32]{0,1:T(8,128)S(1)}, u32[]{:S(2)}, u32[]{:S(2)}) %collective-permute-start.4) | collective-permute-done | bytes 4128 | tf_op jit(solution)/shard_map/ppermute | solution.py:100
  67.7 1.7 %collective-permute-done.5 = f32[32,32]{0,1:T(8,128)S(1)} collective-permute-done((f32[32,32]{0,1:T(8,128)S(1)}, f32[32,32]{0,1:T(8,128)S(1)}, u32[]{:S(2)}, u32[]{:S(2)}) %collective-permute-start.5) | collective-permute-done | bytes 4128 | tf_op jit(solution)/shard_map/ppermute | solution.py:100
  69.4 0.8 %convolution_convert_fusion = bf16[32,1024]{1,0:T(8,128)(2,1)} fusion(bf16[1024,16]{0,1:T(8,128)(2,1)S(1)} %get-tuple-element.22, bf16[1024,16]{0,1:T(8,128)(2,1)S(1)} %get-tuple-element.21, f32[32,32]{0,1:T(8,128)S(1)} %collective-permute-done.5, f32[32,32]{0,1:T(8,128)S(1)} %collective-permute-done.4, f32[32,32]{0,1:T(8,128)S(1)} %collective-permute-done.3, ...), kind=kOutput, calls=%fused_computation.2 | convolution fusion | flops 2267136 | bytes 147456 | tf_op jit(solution)/shard_map/dot_general | solution.py:172
  (16 shorter events, 0.1 us)
Async XLA Ops:
  0.0 6.6 %copy-start = (s32[32,4096]{1,0:T(8,128)S(1)}, s32[32,4096]{1,0:T(8,128)}, u32[]{:S(2)}) copy-start(s32[32,4096]{1,0:T(8,128)} %param.6) | copy-start | bytes 1572868
  2.0 6.0 %collective-permute-start = (f32[32,32]{0,1:T(8,128)S(1)}, f32[32,32]{0,1:T(8,128)S(1)}, u32[]{:S(2)}, u32[]{:S(2)}) collective-permute-start(f32[32,32]{0,1:T(8,128)S(1)} %convolution_bitcast_fusion), channel_id=1, source_target_pairs={{0,1},{1,2},{2,3},{3,0},{4,5},{5,6},{6,7},{7,4},{8,9},{9,10},{10,1... | collective-permute-start | bytes 12296 | tf_op jit(solution)/shard_map/ppermute | solution.py:100
  5.1 3.0 %collective-permute-start.1 = (f32[32,32]{0,1:T(8,128)S(1)}, f32[32,32]{0,1:T(8,128)S(1)}, u32[]{:S(2)}, u32[]{:S(2)}) collective-permute-start(f32[32,32]{0,1:T(8,128)S(1)} %convolution_bitcast_fusion), channel_id=1, source_target_pairs={{0,2},{1,3},{2,0},{3,1},{4,6},{5,7},{6,4},{7,5},{8,10},{9,11},{10,... | collective-permute-start | bytes 12296 | tf_op jit(solution)/shard_map/ppermute | solution.py:100
  6.6 3.2 %collective-permute-start.2 = (f32[32,32]{0,1:T(8,128)S(1)}, f32[32,32]{0,1:T(8,128)S(1)}, u32[]{:S(2)}, u32[]{:S(2)}) collective-permute-start(f32[32,32]{0,1:T(8,128)S(1)} %convolution_bitcast_fusion), channel_id=1, source_target_pairs={{0,3},{1,0},{2,1},{3,2},{4,7},{5,4},{6,5},{7,6},{8,11},{9,8},{10,9... | collective-permute-start | bytes 12296 | tf_op jit(solution)/shard_map/ppermute | solution.py:100
  17.3 42.4 %copy-start.1 = (f32[16,32,1024]{2,1,0:T(8,128)S(1)}, f32[16,32,1024]{2,1,0:T(8,128)}, u32[]{:S(2)}) copy-start(f32[16,32,1024]{2,1,0:T(8,128)} %get-tuple-element.13) | copy-start | bytes 6291460
  62.2 4.1 %collective-permute-start.3 = (f32[32,32]{0,1:T(8,128)S(1)}, f32[32,32]{0,1:T(8,128)S(1)}, u32[]{:S(2)}, u32[]{:S(2)}) collective-permute-start(f32[32,32]{0,1:T(8,128)S(1)} %maximum_multiply_fusion), channel_id=1, source_target_pairs={{0,1},{1,2},{2,3},{3,0},{4,5},{5,6},{6,7},{7,4},{8,9},{9,10},{10,1... | collective-permute-start | bytes 12296 | tf_op jit(solution)/shard_map/ppermute | solution.py:100
  65.2 2.6 %collective-permute-start.4 = (f32[32,32]{0,1:T(8,128)S(1)}, f32[32,32]{0,1:T(8,128)S(1)}, u32[]{:S(2)}, u32[]{:S(2)}) collective-permute-start(f32[32,32]{0,1:T(8,128)S(1)} %maximum_multiply_fusion), channel_id=1, source_target_pairs={{0,2},{1,3},{2,0},{3,1},{4,6},{5,7},{6,4},{7,5},{8,10},{9,11},{10,... | collective-permute-start | bytes 12296 | tf_op jit(solution)/shard_map/ppermute | solution.py:100
  66.3 3.2 %collective-permute-start.5 = (f32[32,32]{0,1:T(8,128)S(1)}, f32[32,32]{0,1:T(8,128)S(1)}, u32[]{:S(2)}, u32[]{:S(2)}) collective-permute-start(f32[32,32]{0,1:T(8,128)S(1)} %maximum_multiply_fusion), channel_id=1, source_target_pairs={{0,3},{1,0},{2,1},{3,2},{4,7},{5,4},{6,5},{7,6},{8,11},{9,8},{10,9... | collective-permute-start | bytes 12296 | tf_op jit(solution)/shard_map/ppermute | solution.py:100

commit v14 on v12

--- a/solution.py
+++ b/solution.py
@@ -12,30 +12,27 @@
 
 def transform_rows(first, count, bin_index, length):
     sample_times = first + lax.iota(jnp.int32, count)
-    phase_index = sample_times[:, None] * bin_index[None, :] % length
-    phase_angle = phase_index.astype(jnp.float32) * (two_pi / length)
+    phase_index = (sample_times[:, None] * bin_index[None, :]) & (length - 1)
     factor = 1.0 / math.sqrt(length)
-    cosine = jnp.cos(phase_angle) * factor
-    sine_part = -jnp.sin(phase_angle) * factor
+    cosine, sine = circle_point(phase_index, length)
+    cosine = cosine * factor
+    sine_part = -sine * factor
     return jnp.concatenate([cosine, sine_part], 1).astype(jnp.bfloat16)
 
 
 def circle_point(phase_index, length):
-    eighth_bits = (length // 8).bit_length() - 1
-    quarter = length // 4
-    quadrant = phase_index >> (eighth_bits + 1)
-    rest = phase_index & (quarter - 1)
-    flip = (rest >> eighth_bits) & (rest != (length // 8)).astype(jnp.int32)
-    folded = jnp.where(flip == 1, quarter - rest, rest)
-    x = folded.astype(jnp.float32) * (two_pi / length)
+    quarter_bits = (length // 4).bit_length() - 1
+    nearest = (phase_index + length // 8) >> quarter_bits
+    rest = phase_index - (nearest << quarter_bits)
+    x = rest.astype(jnp.float32) * (two_pi / length)
     x2 = x * x
     sin_x = x * (1.0 + x2 * (-1.0 / 6.0 + x2 * (1.0 / 120.0 + x2 * (-1.0 / 5040.0))))
     cos_x = 1.0 + x2 * (-0.5 + x2 * (1.0 / 24.0 + x2 * (-1.0 / 720.0 + x2 * (1.0 / 40320.0))))
-    swap = ((quadrant & 1) ^ flip) == 1
+    swap = (nearest & 1) == 1
     sine = jnp.where(swap, cos_x, sin_x)
     cosine = jnp.where(swap, sin_x, cos_x)
-    sine = jnp.where(quadrant >= 2, -sine, sine)
-    cosine = jnp.where(((quadrant ^ (quadrant >> 1)) & 1) == 1, -cosine, cosine)
+    sine = jnp.where((nearest & 2) != 0, -sine, sine)
+    cosine = jnp.where(((nearest + 1) & 2) != 0, -cosine, cosine)
     return cosine, sine
 
 

time: 67 us -> 66.4 us (level)
  no operation moved by 1% of the time
where the time goes in v14:
time: 66.4 us; the launch traced here: 66.1 us
  blocking collectives  40.8 us (61%)
  other arithmetic  11.6 us (17%)
  starting transfers between devices  9.35 us (14%)
  waiting for transfers between devices  1.92 us (3%)
  matrix products  1.8 us (3%)
    all_to_all x1, blocking collectives, on_device(): moved = lax.all_to_all(parts, SENS_AXES, 0, 0, tiled=True)  25.3 us
    all_to_all x1, blocking collectives, on_device(): lax.all_to_all(copies, SENS_AXES, 0, 0, tiled=True).reshape(steered.shape)  15.5 us
    ppermute x6, starting transfers between devices, shifted(): lax.ppermute(x, axis, [(j, (j + shift) % count) for j in range(count)])  9.35 us
    select_n x1, other arithmetic, circle_point(): sine = jnp.where(nearest & 2 != 0, -sine, sine)  4.39 us
    reduce_sum x1, other arithmetic, on_device(): jnp.sum(real_t[:, :, None] * cosine - imag_t[:, :, None] * sine_part, axi...  3.09 us
    reduce_sum x1, other arithmetic, on_device(): jnp.sum(bar_real[:, None, :] * cosine + bar_imag[:, None, :] * sine_part,...  2.32 us
    ppermute x6, waiting for transfers between devices, shifted(): lax.ppermute(x, axis, [(j, (j + shift) % count) for j in range(count)])  1.92 us
  transfers between devices with their start and end apart: 6, of which 1 were waited for; matrix products, arithmetic and copies ran while one was open for 8% of the time, Pallas kernels for 0%

profile of v14, /device:TPU:1, one launch (start us, length us, event | category | flops | bytes accessed | tf_op | source)
XLA Modules:
  0.0 66.1 jit_solution(6454876272114626486)
XLA Ops:
  0.0 0.9 %fusion.2 = (bf16[1024,16]{0,1:T(8,128)(2,1)S(1)}, bf16[1024,16]{0,1:T(8,128)(2,1)S(1)}) fusion(s32[16]{0:T(128)} %param.5, s32[1024]{0:T(1024)S(1)} %iota_add_fusion), kind=kLoop, calls=%fused_computation.22 | loop fusion | flops 688128 | bytes 69696 | tf_op jit(solution)/shard_map/convert
  0.9 1.0 %convolution_bitcast_fusion = f32[32,32]{0,1:T(8,128)S(1)} fusion(bf16[32,1024]{1,0:T(8,128)(2,1)} %param.4, bf16[1024,16]{0,1:T(8,128)(2,1)S(1)} %get-tuple-element.24, bf16[1024,16]{0,1:T(8,128)(2,1)S(1)} %get-tuple-element.23), kind=kOutput, calls=%fused_computation.17 | convolution fusion | flops 2228224 | bytes 135168 | tf_op jit(solution)/shard_map/dot_general | solution.py:85
  1.9 3.2 %collective-permute-start.2 = (f32[32,32]{0,1:T(8,128)S(1)}, f32[32,32]{0,1:T(8,128)S(1)}, u32[]{:S(2)}, u32[]{:S(2)}) collective-permute-start(f32[32,32]{0,1:T(8,128)S(1)} %convolution_bitcast_fusion), channel_id=1, source_target_pairs={{0,3},{1,0},{2,1},{3,2},{4,7},{5,4},{6,5},{7,6},{8,11},{9,8},{10,9... | collective-permute-start | bytes 12296 | tf_op jit(solution)/shard_map/ppermute | solution.py:41
  5.1 0.0 collective-permute-start.1
  5.1 1.7 %collective-permute-start = (f32[32,32]{0,1:T(8,128)S(1)}, f32[32,32]{0,1:T(8,128)S(1)}, u32[]{:S(2)}, u32[]{:S(2)}) collective-permute-start(f32[32,32]{0,1:T(8,128)S(1)} %convolution_bitcast_fusion), channel_id=1, source_target_pairs={{0,1},{1,2},{2,3},{3,0},{4,5},{5,6},{6,7},{7,4},{8,9},{9,10},{10,1... | collective-permute-start | bytes 12296 | tf_op jit(solution)/shard_map/ppermute | solution.py:41
  6.8 4.4 %negate_select_fusion = (f32[16,32,1024]{2,1,0:T(8,128)S(1)}, f32[16,32,1024]{2,1,0:T(8,128)}) fusion(s32[32,1024]{1,0:T(8,128)S(1)} %constant_dynamic-slice_fusion, s32[16]{0:T(128)} %param.5), kind=kLoop, calls=%fused_computation | loop fusion | flops 19398656 | bytes 4325440 | tf_op jit(solution)/shard_map/jit(_where)/select_n | solution.py:34
  11.2 0.8 %dynamic-slice_multiply_fusion = f32[512]{0:T(512)S(1)} fusion(f32[4096]{0:T(1024)} %param.7, s32[]{:T(128)S(6)} %select_n.49), kind=kLoop, calls=%fused_computation.45 | loop fusion | flops 512 | bytes 4100 | tf_op jit(solution)/shard_map/mul | solution.py:104
  12.0 0.0 collective-permute-done.2
  12.0 0.0 collective-permute-done.1
  12.0 0.0 collective-permute-done
  12.0 3.1 %subtract_reduce_fusion.1 = (f32[16,1024]{1,0:T(8,128)S(1)}, f32[16,1024]{1,0:T(8,128)S(1)}) fusion(f32[16,32,1024]{2,1,0:T(8,128)S(1)} %get-tuple-element.10, f32[16,32,1024]{2,1,0:T(8,128)} %get-tuple-element.9, f32[16,32]{1,0:T(8,128)S(1)} %get-tuple-element.22, f32[16,32]{1,0:T(8,128)S(1)} %get-tuple-element.21), kind=kLoop, calls=%fused_computation.5 | loop fusion | flops 4161536 | bytes 4329472 | tf_op jit(solution)/shard_map/reduce_sum | solution.py:94
  15.1 0.1 all_to_all.10
  15.2 25.3 %all_to_all.15 = f32[64,1,512]{2,1,0:T(1,128)S(1)} all-to-all(f32[64,1,512]{2,1,0:T(1,128)S(1)} %all_to_all.10), channel_id=1, replica_groups=mesh['sx'=4,'sz'=4,'sy'=4,'grp'=4] {'sx','sz','sy'}, dimensions={0} | all-to-all | bytes 262144 | tf_op jit(solution)/shard_map/all_to_all | solution.py:106
  40.6 0.1 reduce_sum.47
  40.7 0.1 broadcast_in_dim.2
  40.8 15.5 %all_to_all.16 = f32[64,1,512]{2,1,0:T(1,128)S(1)} all-to-all(f32[64,1,512]{2,1,0:T(1,128)S(1)} %broadcast_in_dim.2), channel_id=1, replica_groups=mesh['sx'=4,'sz'=4,'sy'=4,'grp'=4] {'sx','sz','sy'}, dimensions={0} | all-to-all | bytes 262144 | tf_op jit(solution)/shard_map/all_to_all | solution.py:109
  56.2 0.3 slice_reduce_fusion.1
  56.6 2.3 %add_reduce_fusion = (f32[16,32]{1,0:T(8,128)S(1)}, f32[16,32]{1,0:T(8,128)S(1)}) fusion(f32[16,32,1024]{2,1,0:T(8,128)S(1)} %get-tuple-element.10, f32[16,32,1024]{2,1,0:T(8,128)} %get-tuple-element.9, f32[16,1024]{1,0:T(8,128)S(1)} %mul.249, f32[16,1024]{1,0:T(8,128)S(1)} %mul.246), kind=kLoop, calls=%fused_computation.3 | loop fusion | flops 4193280 | bytes 4329472 | tf_op jit(solution)/shard_map/reduce_sum | solution.py:113
  58.9 0.9 %collective-permute-start.4 = (f32[32,32]{0,1:T(8,128)S(1)}, f32[32,32]{0,1:T(8,128)S(1)}, u32[]{:S(2)}, u32[]{:S(2)}) collective-permute-start(f32[32,32]{0,1:T(8,128)S(1)} %maximum_multiply_fusion), channel_id=1, source_target_pairs={{0,2},{1,3},{2,0},{3,1},{4,6},{5,7},{6,4},{7,5},{8,10},{9,11},{10,... | collective-permute-start | bytes 12296 | tf_op jit(solution)/shard_map/ppermute | solution.py:41
  59.8 2.5 %collective-permute-start.5 = (f32[32,32]{0,1:T(8,128)S(1)}, f32[32,32]{0,1:T(8,128)S(1)}, u32[]{:S(2)}, u32[]{:S(2)}) collective-permute-start(f32[32,32]{0,1:T(8,128)S(1)} %maximum_multiply_fusion), channel_id=1, source_target_pairs={{0,3},{1,0},{2,1},{3,2},{4,7},{5,4},{6,5},{7,6},{8,11},{9,8},{10,9... | collective-permute-start | bytes 12296 | tf_op jit(solution)/shard_map/ppermute | solution.py:41
  62.3 1.0 %collective-permute-start.3 = (f32[32,32]{0,1:T(8,128)S(1)}, f32[32,32]{0,1:T(8,128)S(1)}, u32[]{:S(2)}, u32[]{:S(2)}) collective-permute-start(f32[32,32]{0,1:T(8,128)S(1)} %maximum_multiply_fusion), channel_id=1, source_target_pairs={{0,1},{1,2},{2,3},{3,0},{4,5},{5,6},{6,7},{7,4},{8,9},{9,10},{10,1... | collective-permute-start | bytes 12296 | tf_op jit(solution)/shard_map/ppermute | solution.py:41
  63.4 0.0 collective-permute-done.4
  63.4 1.9 %collective-permute-done.5 = f32[32,32]{0,1:T(8,128)S(1)} collective-permute-done((f32[32,32]{0,1:T(8,128)S(1)}, f32[32,32]{0,1:T(8,128)S(1)}, u32[]{:S(2)}, u32[]{:S(2)}) %collective-permute-start.5) | collective-permute-done | bytes 4128 | tf_op jit(solution)/shard_map/ppermute | solution.py:41
  65.3 0.8 %convolution_convert_fusion = bf16[32,1024]{1,0:T(8,128)(2,1)} fusion(bf16[1024,16]{0,1:T(8,128)(2,1)S(1)} %get-tuple-element.24, bf16[1024,16]{0,1:T(8,128)(2,1)S(1)} %get-tuple-element.23, f32[32,32]{0,1:T(8,128)S(1)} %collective-permute-done.5, f32[32,32]{0,1:T(8,128)S(1)} %collective-permute-done.4, f32[32,32]{0,1:T(8,128)S(1)} %collective-permute-done.3, ...), kind=kOutput, calls=%fused_computation.16 | convolution fusion | flops 2267136 | bytes 147456 | tf_op jit(solution)/shard_map/dot_general | solution.py:118
  (13 shorter events, 0.1 us)
Async XLA Ops:
  0.0 6.8 %copy-start = (s32[32,4096]{1,0:T(8,128)S(1)}, s32[32,4096]{1,0:T(8,128)}, u32[]{:S(2)}) copy-start(s32[32,4096]{1,0:T(8,128)} %param.6) | copy-start | bytes 1572868
  1.9 10.1 %collective-permute-start.2 = (f32[32,32]{0,1:T(8,128)S(1)}, f32[32,32]{0,1:T(8,128)S(1)}, u32[]{:S(2)}, u32[]{:S(2)}) collective-permute-start(f32[32,32]{0,1:T(8,128)S(1)} %convolution_bitcast_fusion), channel_id=1, source_target_pairs={{0,3},{1,0},{2,1},{3,2},{4,7},{5,4},{6,5},{7,6},{8,11},{9,8},{10,9... | collective-permute-start | bytes 12296 | tf_op jit(solution)/shard_map/ppermute | solution.py:41
  5.1 6.9 %collective-permute-start.1 = (f32[32,32]{0,1:T(8,128)S(1)}, f32[32,32]{0,1:T(8,128)S(1)}, u32[]{:S(2)}, u32[]{:S(2)}) collective-permute-start(f32[32,32]{0,1:T(8,128)S(1)} %convolution_bitcast_fusion), channel_id=1, source_target_pairs={{0,2},{1,3},{2,0},{3,1},{4,6},{5,7},{6,4},{7,5},{8,10},{9,11},{10,... | collective-permute-start | bytes 12296 | tf_op jit(solution)/shard_map/ppermute | solution.py:41
  5.1 6.9 %collective-permute-start = (f32[32,32]{0,1:T(8,128)S(1)}, f32[32,32]{0,1:T(8,128)S(1)}, u32[]{:S(2)}, u32[]{:S(2)}) collective-permute-start(f32[32,32]{0,1:T(8,128)S(1)} %convolution_bitcast_fusion), channel_id=1, source_target_pairs={{0,1},{1,2},{2,3},{3,0},{4,5},{5,6},{6,7},{7,4},{8,9},{9,10},{10,1... | collective-permute-start | bytes 12296 | tf_op jit(solution)/shard_map/ppermute | solution.py:41
  58.9 4.4 %collective-permute-start.4 = (f32[32,32]{0,1:T(8,128)S(1)}, f32[32,32]{0,1:T(8,128)S(1)}, u32[]{:S(2)}, u32[]{:S(2)}) collective-permute-start(f32[32,32]{0,1:T(8,128)S(1)} %maximum_multiply_fusion), channel_id=1, source_target_pairs={{0,2},{1,3},{2,0},{3,1},{4,6},{5,7},{6,4},{7,5},{8,10},{9,11},{10,... | collective-permute-start | bytes 12296 | tf_op jit(solution)/shard_map/ppermute | solution.py:41
  59.8 5.5 %collective-permute-start.5 = (f32[32,32]{0,1:T(8,128)S(1)}, f32[32,32]{0,1:T(8,128)S(1)}, u32[]{:S(2)}, u32[]{:S(2)}) collective-permute-start(f32[32,32]{0,1:T(8,128)S(1)} %maximum_multiply_fusion), channel_id=1, source_target_pairs={{0,3},{1,0},{2,1},{3,2},{4,7},{5,4},{6,5},{7,6},{8,11},{9,8},{10,9... | collective-permute-start | bytes 12296 | tf_op jit(solution)/shard_map/ppermute | solution.py:41
  62.3 2.9 %collective-permute-start.3 = (f32[32,32]{0,1:T(8,128)S(1)}, f32[32,32]{0,1:T(8,128)S(1)}, u32[]{:S(2)}, u32[]{:S(2)}) collective-permute-start(f32[32,32]{0,1:T(8,128)S(1)} %maximum_multiply_fusion), channel_id=1, source_target_pairs={{0,1},{1,2},{2,3},{3,0},{4,5},{5,6},{6,7},{7,4},{8,9},{9,10},{10,1... | collective-permute-start | bytes 12296 | tf_op jit(solution)/shard_map/ppermute | solution.py:41

commit v15 on v14

--- a/solution.py
+++ b/solution.py
@@ -100,13 +100,15 @@
     count = lax.axis_size(SENS_AXES)
     parts = steered.reshape(count, steered.size // count)
     width = parts.shape[1]
-    start = position * scan_share + (offset * width) % scan_share
-    chunk_weight = (2.0 * steer_scale) * lax.dynamic_slice_in_dim(map_adjoint, start, width, 0)
-    parts, chunk_weight = lax.optimization_barrier((parts, chunk_weight))
+    own_weight = (2.0 * steer_scale) * lax.dynamic_slice_in_dim(
+        map_adjoint, position * scan_share, scan_share, 0
+    )
+    parts, own_weight = lax.optimization_barrier((parts, own_weight))
     moved = lax.all_to_all(parts, SENS_AXES, 0, 0, tiled=True)
-    chunk = chunk_weight * jnp.sum(moved, axis=0)
+    chunk = jnp.sum(moved, axis=0)
     copies = jnp.broadcast_to(chunk[None], (count, width))
-    bar = lax.all_to_all(copies, SENS_AXES, 0, 0, tiled=True).reshape(steered.shape)
+    gathered = lax.all_to_all(copies, SENS_AXES, 0, 0, tiled=True).reshape(steered.shape)
+    bar = own_weight * gathered
     bar_real = bar[0]
     bar_imag = bar[1]
 

time: 66.4 us -> 63.7 us (0.959)
  other arithmetic: 11.6 us -> 9.12 us
    reduce_sum x1, other arithmetic: 3.09 us -> 1.42 us  [on_device(): jnp.sum(real_t[:, :, None] * cosine - imag_t[:, :, None] * sine_part, axi...]
    select_n x1, other arithmetic: 4.39 us -> 3.23 us  [circle_point(): sine = jnp.where(nearest & 2 != 0, -sine, sine)]
  transfers between devices with their start and end apart: 6 -> 6, of which waited for: 1 -> 1; matrix products, arithmetic and copies ran while one was open for 8% -> 6% of each run, Pallas kernels for 0% -> 0%
where the time goes in v15:
time: 63.7 us; the launch traced here: 63.4 us
  blocking collectives  40.8 us (64%)
  starting transfers between devices  9.35 us (15%)
  other arithmetic  9.12 us (14%)
  waiting for transfers between devices  1.97 us (3%)
  matrix products  1.8 us (3%)
    all_to_all x1, blocking collectives, on_device(): moved = lax.all_to_all(parts, SENS_AXES, 0, 0, tiled=True)  25.3 us
    all_to_all x1, blocking collectives, on_device(): lax.all_to_all(copies, SENS_AXES, 0, 0, tiled=True).reshape(steered.shape)  15.4 us
    ppermute x6, starting transfers between devices, shifted(): lax.ppermute(x, axis, [(j, (j + shift) % count) for j in range(count)])  9.35 us
    select_n x1, other arithmetic, circle_point(): sine = jnp.where(nearest & 2 != 0, -sine, sine)  3.23 us
    reduce_sum x1, other arithmetic, on_device(): jnp.sum(bar_real[:, None, :] * cosine + bar_imag[:, None, :] * sine_part,...  2.38 us
    ppermute x6, waiting for transfers between devices, shifted(): lax.ppermute(x, axis, [(j, (j + shift) % count) for j in range(count)])  1.97 us
    reduce_sum x1, other arithmetic, on_device(): jnp.sum(real_t[:, :, None] * cosine - imag_t[:, :, None] * sine_part, axi...  1.42 us
  transfers between devices with their start and end apart: 6, of which 1 were waited for; matrix products, arithmetic and copies ran while one was open for 6% of the time, Pallas kernels for 0%

profile of v15, /device:TPU:1, one launch (start us, length us, event | category | flops | bytes accessed | tf_op | source)
XLA Modules:
  0.0 63.4 jit_solution(1885233605974862646)
XLA Ops:
  0.0 0.9 %fusion.2 = (bf16[1024,16]{0,1:T(8,128)(2,1)S(1)}, bf16[1024,16]{0,1:T(8,128)(2,1)S(1)}) fusion(s32[16]{0:T(128)} %param.5, s32[1024]{0:T(1024)S(1)} %iota_add_fusion), kind=kLoop, calls=%fused_computation.22 | loop fusion | flops 688128 | bytes 69696 | tf_op jit(solution)/shard_map/convert
  0.9 1.0 %convolution_bitcast_fusion = f32[32,32]{0,1:T(8,128)S(1)} fusion(bf16[32,1024]{1,0:T(8,128)(2,1)} %param.4, bf16[1024,16]{0,1:T(8,128)(2,1)S(1)} %get-tuple-element.24, bf16[1024,16]{0,1:T(8,128)(2,1)S(1)} %get-tuple-element.23), kind=kOutput, calls=%fused_computation.17 | convolution fusion | flops 2228224 | bytes 135168 | tf_op jit(solution)/shard_map/dot_general | solution.py:85
  1.9 3.2 %collective-permute-start.2 = (f32[32,32]{0,1:T(8,128)S(1)}, f32[32,32]{0,1:T(8,128)S(1)}, u32[]{:S(2)}, u32[]{:S(2)}) collective-permute-start(f32[32,32]{0,1:T(8,128)S(1)} %convolution_bitcast_fusion), channel_id=1, source_target_pairs={{0,3},{1,0},{2,1},{3,2},{4,7},{5,4},{6,5},{7,6},{8,11},{9,8},{10,9... | collective-permute-start | bytes 12296 | tf_op jit(solution)/shard_map/ppermute | solution.py:41
  5.1 0.0 collective-permute-start.1
  5.1 1.7 %collective-permute-start = (f32[32,32]{0,1:T(8,128)S(1)}, f32[32,32]{0,1:T(8,128)S(1)}, u32[]{:S(2)}, u32[]{:S(2)}) collective-permute-start(f32[32,32]{0,1:T(8,128)S(1)} %convolution_bitcast_fusion), channel_id=1, source_target_pairs={{0,1},{1,2},{2,3},{3,0},{4,5},{5,6},{6,7},{7,4},{8,9},{9,10},{10,1... | collective-permute-start | bytes 12296 | tf_op jit(solution)/shard_map/ppermute | solution.py:41
  6.8 3.2 %negate_select_fusion = (f32[16,32,1024]{2,1,0:T(8,128)S(1)}, f32[16,32,1024]{2,1,0:T(8,128)S(1)}) fusion(s32[32,1024]{1,0:T(8,128)S(1)} %constant_dynamic-slice_fusion, s32[16]{0:T(128)} %param.5), kind=kLoop, calls=%fused_computation | loop fusion | flops 19398656 | bytes 4325440 | tf_op jit(solution)/shard_map/jit(_where)/select_n | solution.py:34
  10.0 0.7 %dynamic-slice_multiply_fusion = f32[1024]{0:T(1024)S(1)} fusion(f32[4096]{0:T(1024)} %param.7, s32[]{:T(128)S(6)} %select_n.34), kind=kLoop, calls=%fused_computation.45 | loop fusion | flops 1024 | bytes 8196 | tf_op jit(solution)/shard_map/mul | solution.py:103
  10.8 0.0 collective-permute-done.2
  10.8 0.0 collective-permute-done.1
  10.8 0.0 collective-permute-done
  10.8 1.4 %subtract_reduce_fusion.1 = (f32[16,1024]{1,0:T(8,128)S(1)}, f32[16,1024]{1,0:T(8,128)S(1)}) fusion(f32[16,32,1024]{2,1,0:T(8,128)S(1)} %get-tuple-element.10, f32[16,32,1024]{2,1,0:T(8,128)S(1)} %get-tuple-element.9, f32[16,32]{1,0:T(8,128)S(1)} %get-tuple-element.22, f32[16,32]{1,0:T(8,128)S(1)} %get-tuple-element.21), kind=kLoop, calls=%fused_computation.5 | loop fusion | flops 4161536 | bytes 4329472 | tf_op jit(solution)/shard_map/reduce_sum | solution.py:94
  12.3 0.1 all_to_all.10
  12.4 25.3 %all_to_all.15 = f32[64,1,512]{2,1,0:T(1,128)S(1)} all-to-all(f32[64,1,512]{2,1,0:T(1,128)S(1)} %all_to_all.10), channel_id=1, replica_groups=mesh['sx'=4,'sz'=4,'sy'=4,'grp'=4] {'sx','sz','sy'}, dimensions={0} | all-to-all | bytes 262144 | tf_op jit(solution)/shard_map/all_to_all | solution.py:107
  37.8 0.1 reduce_sum.47
  37.9 0.1 broadcast_in_dim.2
  37.9 15.4 %all_to_all.16 = f32[64,1,512]{2,1,0:T(1,128)S(1)} all-to-all(f32[64,1,512]{2,1,0:T(1,128)S(1)} %broadcast_in_dim.2), channel_id=1, replica_groups=mesh['sx'=4,'sz'=4,'sy'=4,'grp'=4] {'sx','sz','sy'}, dimensions={0} | all-to-all | bytes 262144 | tf_op jit(solution)/shard_map/all_to_all | solution.py:110
  53.4 0.3 reduce.1
  53.8 2.4 %add_reduce_fusion = (f32[16,32]{1,0:T(8,128)S(1)}, f32[16,32]{1,0:T(8,128)S(1)}) fusion(f32[16,32,1024]{2,1,0:T(8,128)S(1)} %get-tuple-element.10, f32[16,32,1024]{2,1,0:T(8,128)} %copy-done.1, f32[16,1024]{1,0:T(8,128)S(1)} %get-tuple-element.20, f32[16,1024]{1,0:T(8,128)S(1)} %get-tuple-element.19), kind=kLoop, calls=%fused_computation.3 | loop fusion | flops 4193280 | bytes 4329472 | tf_op jit(solution)/shard_map/reduce_sum | solution.py:115
  56.2 0.9 %collective-permute-start.4 = (f32[32,32]{0,1:T(8,128)S(1)}, f32[32,32]{0,1:T(8,128)S(1)}, u32[]{:S(2)}, u32[]{:S(2)}) collective-permute-start(f32[32,32]{0,1:T(8,128)S(1)} %maximum_multiply_fusion), channel_id=1, source_target_pairs={{0,2},{1,3},{2,0},{3,1},{4,6},{5,7},{6,4},{7,5},{8,10},{9,11},{10,... | collective-permute-start | bytes 12296 | tf_op jit(solution)/shard_map/ppermute | solution.py:41
  57.1 2.6 %collective-permute-start.5 = (f32[32,32]{0,1:T(8,128)S(1)}, f32[32,32]{0,1:T(8,128)S(1)}, u32[]{:S(2)}, u32[]{:S(2)}) collective-permute-start(f32[32,32]{0,1:T(8,128)S(1)} %maximum_multiply_fusion), channel_id=1, source_target_pairs={{0,3},{1,0},{2,1},{3,2},{4,7},{5,4},{6,5},{7,6},{8,11},{9,8},{10,9... | collective-permute-start | bytes 12296 | tf_op jit(solution)/shard_map/ppermute | solution.py:41
  59.6 1.0 %collective-permute-start.3 = (f32[32,32]{0,1:T(8,128)S(1)}, f32[32,32]{0,1:T(8,128)S(1)}, u32[]{:S(2)}, u32[]{:S(2)}) collective-permute-start(f32[32,32]{0,1:T(8,128)S(1)} %maximum_multiply_fusion), channel_id=1, source_target_pairs={{0,1},{1,2},{2,3},{3,0},{4,5},{5,6},{6,7},{7,4},{8,9},{9,10},{10,1... | collective-permute-start | bytes 12296 | tf_op jit(solution)/shard_map/ppermute | solution.py:41
  60.6 0.0 collective-permute-done.4
  60.6 2.0 %collective-permute-done.5 = f32[32,32]{0,1:T(8,128)S(1)} collective-permute-done((f32[32,32]{0,1:T(8,128)S(1)}, f32[32,32]{0,1:T(8,128)S(1)}, u32[]{:S(2)}, u32[]{:S(2)}) %collective-permute-start.5) | collective-permute-done | bytes 4128 | tf_op jit(solution)/shard_map/ppermute | solution.py:41
  62.6 0.8 %convolution_convert_fusion = bf16[32,1024]{1,0:T(8,128)(2,1)} fusion(bf16[1024,16]{0,1:T(8,128)(2,1)S(1)} %get-tuple-element.24, bf16[1024,16]{0,1:T(8,128)(2,1)S(1)} %get-tuple-element.23, f32[32,32]{0,1:T(8,128)S(1)} %collective-permute-done.5, f32[32,32]{0,1:T(8,128)S(1)} %collective-permute-done.4, f32[32,32]{0,1:T(8,128)S(1)} %collective-permute-done.3, ...), kind=kOutput, calls=%fused_computation.16 | convolution fusion | flops 2267136 | bytes 147456 | tf_op jit(solution)/shard_map/dot_general | solution.py:120
  (15 shorter events, 0.1 us)
Async XLA Ops:
  0.0 6.8 %copy-start = (s32[32,4096]{1,0:T(8,128)S(1)}, s32[32,4096]{1,0:T(8,128)}, u32[]{:S(2)}) copy-start(s32[32,4096]{1,0:T(8,128)} %param.6) | copy-start | bytes 1572868
  1.9 8.9 %collective-permute-start.2 = (f32[32,32]{0,1:T(8,128)S(1)}, f32[32,32]{0,1:T(8,128)S(1)}, u32[]{:S(2)}, u32[]{:S(2)}) collective-permute-start(f32[32,32]{0,1:T(8,128)S(1)} %convolution_bitcast_fusion), channel_id=1, source_target_pairs={{0,3},{1,0},{2,1},{3,2},{4,7},{5,4},{6,5},{7,6},{8,11},{9,8},{10,9... | collective-permute-start | bytes 12296 | tf_op jit(solution)/shard_map/ppermute | solution.py:41
  5.1 5.7 %collective-permute-start.1 = (f32[32,32]{0,1:T(8,128)S(1)}, f32[32,32]{0,1:T(8,128)S(1)}, u32[]{:S(2)}, u32[]{:S(2)}) collective-permute-start(f32[32,32]{0,1:T(8,128)S(1)} %convolution_bitcast_fusion), channel_id=1, source_target_pairs={{0,2},{1,3},{2,0},{3,1},{4,6},{5,7},{6,4},{7,5},{8,10},{9,11},{10,... | collective-permute-start | bytes 12296 | tf_op jit(solution)/shard_map/ppermute | solution.py:41
  5.1 5.7 %collective-permute-start = (f32[32,32]{0,1:T(8,128)S(1)}, f32[32,32]{0,1:T(8,128)S(1)}, u32[]{:S(2)}, u32[]{:S(2)}) collective-permute-start(f32[32,32]{0,1:T(8,128)S(1)} %convolution_bitcast_fusion), channel_id=1, source_target_pairs={{0,1},{1,2},{2,3},{3,0},{4,5},{5,6},{6,7},{7,4},{8,9},{9,10},{10,1... | collective-permute-start | bytes 12296 | tf_op jit(solution)/shard_map/ppermute | solution.py:41
  10.0 2.2 %copy-start.1 = (f32[16,32,1024]{2,1,0:T(8,128)}, f32[16,32,1024]{2,1,0:T(8,128)S(1)}, u32[]{:S(2)}) copy-start(f32[16,32,1024]{2,1,0:T(8,128)S(1)} %get-tuple-element.9) | copy-start | bytes 6291460
  56.2 4.4 %collective-permute-start.4 = (f32[32,32]{0,1:T(8,128)S(1)}, f32[32,32]{0,1:T(8,128)S(1)}, u32[]{:S(2)}, u32[]{:S(2)}) collective-permute-start(f32[32,32]{0,1:T(8,128)S(1)} %maximum_multiply_fusion), channel_id=1, source_target_pairs={{0,2},{1,3},{2,0},{3,1},{4,6},{5,7},{6,4},{7,5},{8,10},{9,11},{10,... | collective-permute-start | bytes 12296 | tf_op jit(solution)/shard_map/ppermute | solution.py:41
  57.1 5.5 %collective-permute-start.5 = (f32[32,32]{0,1:T(8,128)S(1)}, f32[32,32]{0,1:T(8,128)S(1)}, u32[]{:S(2)}, u32[]{:S(2)}) collective-permute-start(f32[32,32]{0,1:T(8,128)S(1)} %maximum_multiply_fusion), channel_id=1, source_target_pairs={{0,3},{1,0},{2,1},{3,2},{4,7},{5,4},{6,5},{7,6},{8,11},{9,8},{10,9... | collective-permute-start | bytes 12296 | tf_op jit(solution)/shard_map/ppermute | solution.py:41
  59.6 2.9 %collective-permute-start.3 = (f32[32,32]{0,1:T(8,128)S(1)}, f32[32,32]{0,1:T(8,128)S(1)}, u32[]{:S(2)}, u32[]{:S(2)}) collective-permute-start(f32[32,32]{0,1:T(8,128)S(1)} %maximum_multiply_fusion), channel_id=1, source_target_pairs={{0,1},{1,2},{2,3},{3,0},{4,5},{5,6},{6,7},{7,4},{8,9},{9,10},{10,1... | collective-permute-start | bytes 12296 | tf_op jit(solution)/shard_map/ppermute | solution.py:41

commit v16 on v15

--- a/solution.py
+++ b/solution.py
@@ -73,13 +73,11 @@
 
 
 def on_device(histories, bin_index, delays, map_adjoint):
-    groups = lax.axis_size("grp")
     position = lax.axis_index("grp")
     bins = bin_index.shape[0]
     sensors = delays.shape[0] * lax.axis_size(SENS_AXES)
     steer_scale = 1.0 / math.sqrt(sensors)
     samples = histories.shape[1]
-    scan_share = delays.shape[1] // groups
 
     transform = transform_rows(position * samples, samples, bin_index, NT)
     spectra = jnp.dot(histories, transform, preferred_element_type=jnp.float32)
@@ -87,7 +85,7 @@
     real_t = spectra[:, :bins].T
     imag_t = spectra[:, bins:].T
 
-    own_delays = lax.dynamic_slice_in_dim(delays, position * scan_share, scan_share, 1)
+    own_delays = delays
     phase_index = (bin_index[:, None, None] * own_delays[None, :, :]) & (NT - 1)
     cosine, sine_part = lax.optimization_barrier(circle_point(phase_index, NT))
 
@@ -100,9 +98,7 @@
     count = lax.axis_size(SENS_AXES)
     parts = steered.reshape(count, steered.size // count)
     width = parts.shape[1]
-    own_weight = (2.0 * steer_scale) * lax.dynamic_slice_in_dim(
-        map_adjoint, position * scan_share, scan_share, 0
-    )
+    own_weight = (2.0 * steer_scale) * map_adjoint
     parts, own_weight = lax.optimization_barrier((parts, own_weight))
     moved = lax.all_to_all(parts, SENS_AXES, 0, 0, tiled=True)
     chunk = jnp.sum(moved, axis=0)
@@ -133,7 +129,7 @@
     fine = jax.sharding.Mesh(
         mesh.devices.reshape(side, side, side, mesh.shape["grp"]), SENS_AXES + ("grp",)
     )
-    placed = (P(SENS_AXES, "grp"), P(), P(SENS_AXES, None), P())
+    placed = (P(SENS_AXES, "grp"), P(), P(SENS_AXES, "grp"), P("grp"))
     return jax.shard_map(
         on_device, mesh=fine, in_specs=placed, out_specs=P(SENS_AXES, "grp"), check_vma=False
     )

time: 63.7 us -> 67.6 us (1.061)
  local copies, waits for them, and re-layouts: 0.26 us -> 3.44 us
    another operation x0 -> x3, local copies, waits for them, and re-layouts: none -> 3.19 us
  transfers between devices with their start and end apart: 6 -> 6, of which waited for: 1 -> 1; matrix products, arithmetic and copies ran while one was open for 6% -> 11% of each run, Pallas kernels for 0% -> 0%
where the time goes in v16:
time: 67.6 us; the launch traced here: 67.2 us
  blocking collectives  40.8 us (60%)
  starting transfers between devices  9.35 us (14%)
  other arithmetic  9.12 us (13%)
  local copies, waits for them, and re-layouts  3.44 us (5%)
  waiting for transfers between devices  1.97 us (3%)
  matrix products  1.8 us (3%)
  between operations  0.79 us (1%)
    all_to_all x1, blocking collectives, on_device(): moved = lax.all_to_all(parts, SENS_AXES, 0, 0, tiled=True)  25.3 us
    all_to_all x1, blocking collectives, on_device(): lax.all_to_all(copies, SENS_AXES, 0, 0, tiled=True).reshape(steered.shape)  15.4 us
    ppermute x6, starting transfers between devices, shifted(): lax.ppermute(x, axis, [(j, (j + shift) % count) for j in range(count)])  9.35 us
    select_n x1, other arithmetic, circle_point(): sine = jnp.where(nearest & 2 != 0, -sine, sine)  3.23 us
    another operation x3, local copies, waits for them, and re-layouts  3.19 us
    reduce_sum x1, other arithmetic, on_device(): jnp.sum(bar_real[:, None, :] * cosine + bar_imag[:, None, :] * sine_part,...  2.38 us
    ppermute x6, waiting for transfers between devices, shifted(): lax.ppermute(x, axis, [(j, (j + shift) % count) for j in range(count)])  1.97 us
    reduce_sum x1, other arithmetic, on_device(): jnp.sum(real_t[:, :, None] * cosine - imag_t[:, :, None] * sine_part, axi...  1.42 us
  transfers between devices with their start and end apart: 6, of which 1 were waited for; matrix products, arithmetic and copies ran while one was open for 11% of the time, Pallas kernels for 0%

profile of v16, /device:TPU:1, one launch (start us, length us, event | category | flops | bytes accessed | tf_op | source)
XLA Modules:
  0.0 67.2 jit_solution(1400764781274389825)
XLA Ops:
  0.0 0.9 %fusion.2 = (bf16[1024,16]{0,1:T(8,128)(2,1)S(1)}, bf16[1024,16]{0,1:T(8,128)(2,1)S(1)}) fusion(s32[16]{0:T(128)} %param.5, s32[1024]{0:T(1024)S(1)} %iota_add_fusion), kind=kLoop, calls=%fused_computation.22 | loop fusion | flops 688128 | bytes 69696 | tf_op jit(solution)/shard_map/convert
  0.9 1.0 %convolution_bitcast_fusion = f32[32,32]{0,1:T(8,128)S(1)} fusion(bf16[32,1024]{1,0:T(8,128)(2,1)} %param.4, bf16[1024,16]{0,1:T(8,128)(2,1)S(1)} %get-tuple-element.24, bf16[1024,16]{0,1:T(8,128)(2,1)S(1)} %get-tuple-element.23), kind=kOutput, calls=%fused_computation.17 | convolution fusion | flops 2228224 | bytes 135168 | tf_op jit(solution)/shard_map/dot_general | solution.py:83
  1.9 3.2 %collective-permute-start.2 = (f32[32,32]{0,1:T(8,128)S(1)}, f32[32,32]{0,1:T(8,128)S(1)}, u32[]{:S(2)}, u32[]{:S(2)}) collective-permute-start(f32[32,32]{0,1:T(8,128)S(1)} %convolution_bitcast_fusion), channel_id=1, source_target_pairs={{0,3},{1,0},{2,1},{3,2},{4,7},{5,4},{6,5},{7,6},{8,11},{9,8},{10,9... | collective-permute-start | bytes 12296 | tf_op jit(solution)/shard_map/ppermute | solution.py:41
  5.1 0.0 collective-permute-start.1
  5.1 1.7 %collective-permute-start = (f32[32,32]{0,1:T(8,128)S(1)}, f32[32,32]{0,1:T(8,128)S(1)}, u32[]{:S(2)}, u32[]{:S(2)}) collective-permute-start(f32[32,32]{0,1:T(8,128)S(1)} %convolution_bitcast_fusion), channel_id=1, source_target_pairs={{0,1},{1,2},{2,3},{3,0},{4,5},{5,6},{6,7},{7,4},{8,9},{9,10},{10,1... | collective-permute-start | bytes 12296 | tf_op jit(solution)/shard_map/ppermute | solution.py:41
  6.8 1.3 %dynamic-slice.5 = u32[1]{0:T(128)} dynamic-slice(u32[256]{0:T(256)} %constant.15, u32[]{:T(128)S(6)} %axis_index.10), dynamic_slice_sizes={1} | dynamic-slice | bytes 12 | tf_op jit(solution)/call_exported
  8.7 1.3 %dynamic-slice.2 = s32[1]{0:T(128)} dynamic-slice(s32[256]{0:T(256)} %constant.11, u32[]{:T(128)S(6)} %axis_index.10), dynamic_slice_sizes={1} | dynamic-slice | bytes 12 | tf_op jit(solution)/call_exported
  10.0 0.7 constant_dynamic-slice_fusion
  10.6 3.2 %negate_select_fusion = (f32[16,32,1024]{2,1,0:T(8,128)S(1)}, f32[16,32,1024]{2,1,0:T(8,128)S(1)}) fusion(s32[32,1024]{1,0:T(8,128)S(1)} %constant_dynamic-slice_fusion, s32[16]{0:T(128)} %param.5), kind=kLoop, calls=%fused_computation | loop fusion | flops 19398656 | bytes 4325440 | tf_op jit(solution)/shard_map/jit(_where)/select_n | solution.py:34
  13.9 0.7 %dynamic-slice_multiply_fusion = f32[1024]{0:T(1024)S(1)} fusion(f32[4096]{0:T(1024)} %param.7, s32[]{:T(128)} %bitcast.6), kind=kLoop, calls=%fused_computation.46 | loop fusion | flops 1024 | bytes 8196 | tf_op jit(solution)/shard_map/mul | solution.py:101
  14.6 0.0 collective-permute-done
  14.7 1.4 %subtract_reduce_fusion.1 = (f32[16,1024]{1,0:T(8,128)S(1)}, f32[16,1024]{1,0:T(8,128)S(1)}) fusion(f32[16,32,1024]{2,1,0:T(8,128)S(1)} %get-tuple-element.10, f32[16,32,1024]{2,1,0:T(8,128)S(1)} %get-tuple-element.9, f32[16,32]{1,0:T(8,128)S(1)} %get-tuple-element.22, f32[16,32]{1,0:T(8,128)S(1)} %get-tuple-element.21), kind=kLoop, calls=%fused_computation.5 | loop fusion | flops 4161536 | bytes 4329472 | tf_op jit(solution)/shard_map/reduce_sum | solution.py:92
  16.2 0.1 all_to_all.10
  16.3 25.3 %all_to_all.15 = f32[64,1,512]{2,1,0:T(1,128)S(1)} all-to-all(f32[64,1,512]{2,1,0:T(1,128)S(1)} %all_to_all.10), channel_id=1, replica_groups=mesh['sx'=4,'sz'=4,'sy'=4,'grp'=4] {'sx','sz','sy'}, dimensions={0} | all-to-all | bytes 262144 | tf_op jit(solution)/shard_map/all_to_all | solution.py:103
  41.6 0.1 reduce_sum.47
  41.7 0.1 broadcast_in_dim.2
  41.8 15.4 %all_to_all.16 = f32[64,1,512]{2,1,0:T(1,128)S(1)} all-to-all(f32[64,1,512]{2,1,0:T(1,128)S(1)} %broadcast_in_dim.2), channel_id=1, replica_groups=mesh['sx'=4,'sz'=4,'sy'=4,'grp'=4] {'sx','sz','sy'}, dimensions={0} | all-to-all | bytes 262144 | tf_op jit(solution)/shard_map/all_to_all | solution.py:106
  57.2 0.3 reduce.1
  57.6 2.4 %add_reduce_fusion = (f32[16,32]{1,0:T(8,128)S(1)}, f32[16,32]{1,0:T(8,128)S(1)}) fusion(f32[16,32,1024]{2,1,0:T(8,128)S(1)} %get-tuple-element.10, f32[16,32,1024]{2,1,0:T(8,128)} %copy-done.1, f32[16,1024]{1,0:T(8,128)S(1)} %get-tuple-element.20, f32[16,1024]{1,0:T(8,128)S(1)} %get-tuple-element.19), kind=kLoop, calls=%fused_computation.3 | loop fusion | flops 4193280 | bytes 4329472 | tf_op jit(solution)/shard_map/reduce_sum | solution.py:111
  60.0 0.9 %collective-permute-start.4 = (f32[32,32]{0,1:T(8,128)S(1)}, f32[32,32]{0,1:T(8,128)S(1)}, u32[]{:S(2)}, u32[]{:S(2)}) collective-permute-start(f32[32,32]{0,1:T(8,128)S(1)} %maximum_multiply_fusion), channel_id=1, source_target_pairs={{0,2},{1,3},{2,0},{3,1},{4,6},{5,7},{6,4},{7,5},{8,10},{9,11},{10,... | collective-permute-start | bytes 12296 | tf_op jit(solution)/shard_map/ppermute | solution.py:41
  60.9 2.6 %collective-permute-start.5 = (f32[32,32]{0,1:T(8,128)S(1)}, f32[32,32]{0,1:T(8,128)S(1)}, u32[]{:S(2)}, u32[]{:S(2)}) collective-permute-start(f32[32,32]{0,1:T(8,128)S(1)} %maximum_multiply_fusion), channel_id=1, source_target_pairs={{0,3},{1,0},{2,1},{3,2},{4,7},{5,4},{6,5},{7,6},{8,11},{9,8},{10,9... | collective-permute-start | bytes 12296 | tf_op jit(solution)/shard_map/ppermute | solution.py:41
  63.5 1.0 %collective-permute-start.3 = (f32[32,32]{0,1:T(8,128)S(1)}, f32[32,32]{0,1:T(8,128)S(1)}, u32[]{:S(2)}, u32[]{:S(2)}) collective-permute-start(f32[32,32]{0,1:T(8,128)S(1)} %maximum_multiply_fusion), channel_id=1, source_target_pairs={{0,1},{1,2},{2,3},{3,0},{4,5},{5,6},{6,7},{7,4},{8,9},{9,10},{10,1... | collective-permute-start | bytes 12296 | tf_op jit(solution)/shard_map/ppermute | solution.py:41
  64.5 2.0 %collective-permute-done.5 = f32[32,32]{0,1:T(8,128)S(1)} collective-permute-done((f32[32,32]{0,1:T(8,128)S(1)}, f32[32,32]{0,1:T(8,128)S(1)}, u32[]{:S(2)}, u32[]{:S(2)}) %collective-permute-start.5) | collective-permute-done | bytes 4128 | tf_op jit(solution)/shard_map/ppermute | solution.py:41
  66.4 0.8 %convolution_convert_fusion = bf16[32,1024]{1,0:T(8,128)(2,1)} fusion(bf16[1024,16]{0,1:T(8,128)(2,1)S(1)} %get-tuple-element.24, bf16[1024,16]{0,1:T(8,128)(2,1)S(1)} %get-tuple-element.23, f32[32,32]{0,1:T(8,128)S(1)} %collective-permute-done.5, f32[32,32]{0,1:T(8,128)S(1)} %collective-permute-done.4, f32[32,32]{0,1:T(8,128)S(1)} %collective-permute-done.3, ...), kind=kOutput, calls=%fused_computation.16 | convolution fusion | flops 2267136 | bytes 147456 | tf_op jit(solution)/shard_map/dot_general | solution.py:116
  (17 shorter events, 0.1 us)
Async XLA Ops:
  0.0 10.0 %copy-start = (s32[32,4096]{1,0:T(8,128)S(1)}, s32[32,4096]{1,0:T(8,128)}, u32[]{:S(2)}) copy-start(s32[32,4096]{1,0:T(8,128)} %param.6) | copy-start | bytes 1572868
  1.9 12.8 %collective-permute-start.2 = (f32[32,32]{0,1:T(8,128)S(1)}, f32[32,32]{0,1:T(8,128)S(1)}, u32[]{:S(2)}, u32[]{:S(2)}) collective-permute-start(f32[32,32]{0,1:T(8,128)S(1)} %convolution_bitcast_fusion), channel_id=1, source_target_pairs={{0,3},{1,0},{2,1},{3,2},{4,7},{5,4},{6,5},{7,6},{8,11},{9,8},{10,9... | collective-permute-start | bytes 12296 | tf_op jit(solution)/shard_map/ppermute | solution.py:41
  5.1 9.6 %collective-permute-start.1 = (f32[32,32]{0,1:T(8,128)S(1)}, f32[32,32]{0,1:T(8,128)S(1)}, u32[]{:S(2)}, u32[]{:S(2)}) collective-permute-start(f32[32,32]{0,1:T(8,128)S(1)} %convolution_bitcast_fusion), channel_id=1, source_target_pairs={{0,2},{1,3},{2,0},{3,1},{4,6},{5,7},{6,4},{7,5},{8,10},{9,11},{10,... | collective-permute-start | bytes 12296 | tf_op jit(solution)/shard_map/ppermute | solution.py:41
  5.1 9.6 %collective-permute-start = (f32[32,32]{0,1:T(8,128)S(1)}, f32[32,32]{0,1:T(8,128)S(1)}, u32[]{:S(2)}, u32[]{:S(2)}) collective-permute-start(f32[32,32]{0,1:T(8,128)S(1)} %convolution_bitcast_fusion), channel_id=1, source_target_pairs={{0,1},{1,2},{2,3},{3,0},{4,5},{5,6},{6,7},{7,4},{8,9},{9,10},{10,1... | collective-permute-start | bytes 12296 | tf_op jit(solution)/shard_map/ppermute | solution.py:41
  13.9 2.2 %copy-start.1 = (f32[16,32,1024]{2,1,0:T(8,128)}, f32[16,32,1024]{2,1,0:T(8,128)S(1)}, u32[]{:S(2)}) copy-start(f32[16,32,1024]{2,1,0:T(8,128)S(1)} %get-tuple-element.9) | copy-start | bytes 6291460
  60.0 4.4 %collective-permute-start.4 = (f32[32,32]{0,1:T(8,128)S(1)}, f32[32,32]{0,1:T(8,128)S(1)}, u32[]{:S(2)}, u32[]{:S(2)}) collective-permute-start(f32[32,32]{0,1:T(8,128)S(1)} %maximum_multiply_fusion), channel_id=1, source_target_pairs={{0,2},{1,3},{2,0},{3,1},{4,6},{5,7},{6,4},{7,5},{8,10},{9,11},{10,... | collective-permute-start | bytes 12296 | tf_op jit(solution)/shard_map/ppermute | solution.py:41
  60.9 5.5 %collective-permute-start.5 = (f32[32,32]{0,1:T(8,128)S(1)}, f32[32,32]{0,1:T(8,128)S(1)}, u32[]{:S(2)}, u32[]{:S(2)}) collective-permute-start(f32[32,32]{0,1:T(8,128)S(1)} %maximum_multiply_fusion), channel_id=1, source_target_pairs={{0,3},{1,0},{2,1},{3,2},{4,7},{5,4},{6,5},{7,6},{8,11},{9,8},{10,9... | collective-permute-start | bytes 12296 | tf_op jit(solution)/shard_map/ppermute | solution.py:41
  63.5 2.9 %collective-permute-start.3 = (f32[32,32]{0,1:T(8,128)S(1)}, f32[32,32]{0,1:T(8,128)S(1)}, u32[]{:S(2)}, u32[]{:S(2)}) collective-permute-start(f32[32,32]{0,1:T(8,128)S(1)} %maximum_multiply_fusion), channel_id=1, source_target_pairs={{0,1},{1,2},{2,3},{3,0},{4,5},{5,6},{6,7},{7,4},{8,9},{9,10},{10,1... | collective-permute-start | bytes 12296 | tf_op jit(solution)/shard_map/ppermute | solution.py:41

commit v17 on v15

--- a/solution.py
+++ b/solution.py
@@ -104,10 +104,10 @@
         map_adjoint, position * scan_share, scan_share, 0
     )
     parts, own_weight = lax.optimization_barrier((parts, own_weight))
-    moved = lax.all_to_all(parts, SENS_AXES, 0, 0, tiled=True)
+    moved = lax.all_to_all(parts, EXCHANGE_ORDER, 0, 0, tiled=True)
     chunk = jnp.sum(moved, axis=0)
     copies = jnp.broadcast_to(chunk[None], (count, width))
-    gathered = lax.all_to_all(copies, SENS_AXES, 0, 0, tiled=True).reshape(steered.shape)
+    gathered = lax.all_to_all(copies, EXCHANGE_ORDER, 0, 0, tiled=True).reshape(steered.shape)
     bar = own_weight * gathered
     bar_real = bar[0]
     bar_imag = bar[1]
@@ -124,6 +124,7 @@
 
 
 SENS_AXES = ("sx", "sz", "sy")
+EXCHANGE_ORDER = ("sy", "sz", "sx")
 
 
 def solution(mesh):

time: 63.7 us -> 63.7 us (level)
  no operation moved by 1% of the time
where the time goes in v17:
time: 63.7 us; the launch traced here: 63.4 us
  blocking collectives  40.8 us (64%)
  starting transfers between devices  9.35 us (15%)
  other arithmetic  9.12 us (14%)
  waiting for transfers between devices  1.97 us (3%)
  matrix products  1.8 us (3%)
    all_to_all x1, blocking collectives, on_device(): moved = lax.all_to_all(parts, EXCHANGE_ORDER, 0, 0, tiled=True)  25.3 us
    all_to_all x1, blocking collectives, on_device(): lax.all_to_all(copies, EXCHANGE_ORDER, 0, 0, tiled=True)  15.4 us
    ppermute x6, starting transfers between devices, shifted(): lax.ppermute(x, axis, [(j, (j + shift) % count) for j in range(count)])  9.35 us
    select_n x1, other arithmetic, circle_point(): sine = jnp.where(nearest & 2 != 0, -sine, sine)  3.23 us
    reduce_sum x1, other arithmetic, on_device(): jnp.sum(bar_real[:, None, :] * cosine + bar_imag[:, None, :] * sine_part,...  2.38 us
    ppermute x6, waiting for transfers between devices, shifted(): lax.ppermute(x, axis, [(j, (j + shift) % count) for j in range(count)])  1.97 us
    reduce_sum x1, other arithmetic, on_device(): jnp.sum(real_t[:, :, None] * cosine - imag_t[:, :, None] * sine_part, axi...  1.42 us
  transfers between devices with their start and end apart: 6, of which 1 were waited for; matrix products, arithmetic and copies ran while one was open for 6% of the time, Pallas kernels for 0%

profile of v17, /device:TPU:1, one launch (start us, length us, event | category | flops | bytes accessed | tf_op | source)
XLA Modules:
  0.0 63.4 jit_solution(7175007036973334509)
XLA Ops:
  0.0 0.9 %fusion.2 = (bf16[1024,16]{0,1:T(8,128)(2,1)S(1)}, bf16[1024,16]{0,1:T(8,128)(2,1)S(1)}) fusion(s32[16]{0:T(128)} %param.5, s32[1024]{0:T(1024)S(1)} %iota_add_fusion), kind=kLoop, calls=%fused_computation.22 | loop fusion | flops 688128 | bytes 69696 | tf_op jit(solution)/shard_map/convert
  0.9 1.0 %convolution_bitcast_fusion = f32[32,32]{0,1:T(8,128)S(1)} fusion(bf16[32,1024]{1,0:T(8,128)(2,1)} %param.4, bf16[1024,16]{0,1:T(8,128)(2,1)S(1)} %get-tuple-element.24, bf16[1024,16]{0,1:T(8,128)(2,1)S(1)} %get-tuple-element.23), kind=kOutput, calls=%fused_computation.17 | convolution fusion | flops 2228224 | bytes 135168 | tf_op jit(solution)/shard_map/dot_general | solution.py:85
  1.9 3.2 %collective-permute-start.2 = (f32[32,32]{0,1:T(8,128)S(1)}, f32[32,32]{0,1:T(8,128)S(1)}, u32[]{:S(2)}, u32[]{:S(2)}) collective-permute-start(f32[32,32]{0,1:T(8,128)S(1)} %convolution_bitcast_fusion), channel_id=1, source_target_pairs={{0,3},{1,0},{2,1},{3,2},{4,7},{5,4},{6,5},{7,6},{8,11},{9,8},{10,9... | collective-permute-start | bytes 12296 | tf_op jit(solution)/shard_map/ppermute | solution.py:41
  5.1 0.0 collective-permute-start.1
  5.1 1.7 %collective-permute-start = (f32[32,32]{0,1:T(8,128)S(1)}, f32[32,32]{0,1:T(8,128)S(1)}, u32[]{:S(2)}, u32[]{:S(2)}) collective-permute-start(f32[32,32]{0,1:T(8,128)S(1)} %convolution_bitcast_fusion), channel_id=1, source_target_pairs={{0,1},{1,2},{2,3},{3,0},{4,5},{5,6},{6,7},{7,4},{8,9},{9,10},{10,1... | collective-permute-start | bytes 12296 | tf_op jit(solution)/shard_map/ppermute | solution.py:41
  6.8 3.2 %negate_select_fusion = (f32[16,32,1024]{2,1,0:T(8,128)S(1)}, f32[16,32,1024]{2,1,0:T(8,128)S(1)}) fusion(s32[32,1024]{1,0:T(8,128)S(1)} %constant_dynamic-slice_fusion, s32[16]{0:T(128)} %param.5), kind=kLoop, calls=%fused_computation | loop fusion | flops 19398656 | bytes 4325440 | tf_op jit(solution)/shard_map/jit(_where)/select_n | solution.py:34
  10.0 0.7 %dynamic-slice_multiply_fusion = f32[1024]{0:T(1024)S(1)} fusion(f32[4096]{0:T(1024)} %param.7, s32[]{:T(128)S(6)} %select_n.34), kind=kLoop, calls=%fused_computation.45 | loop fusion | flops 1024 | bytes 8196 | tf_op jit(solution)/shard_map/mul | solution.py:103
  10.8 0.0 collective-permute-done.2
  10.8 0.0 collective-permute-done.1
  10.8 0.0 collective-permute-done
  10.8 1.4 %subtract_reduce_fusion.1 = (f32[16,1024]{1,0:T(8,128)S(1)}, f32[16,1024]{1,0:T(8,128)S(1)}) fusion(f32[16,32,1024]{2,1,0:T(8,128)S(1)} %get-tuple-element.10, f32[16,32,1024]{2,1,0:T(8,128)S(1)} %get-tuple-element.9, f32[16,32]{1,0:T(8,128)S(1)} %get-tuple-element.22, f32[16,32]{1,0:T(8,128)S(1)} %get-tuple-element.21), kind=kLoop, calls=%fused_computation.5 | loop fusion | flops 4161536 | bytes 4329472 | tf_op jit(solution)/shard_map/reduce_sum | solution.py:94
  12.3 0.1 all_to_all.10
  12.4 25.3 %all_to_all.15 = f32[64,1,512]{2,1,0:T(1,128)S(1)} all-to-all(f32[64,1,512]{2,1,0:T(1,128)S(1)} %all_to_all.10), channel_id=1, replica_groups=mesh['sx'=4,'sz'=4,'sy'=4,'grp'=4] {'sy','sz','sx'}, dimensions={0} | all-to-all | bytes 262144 | tf_op jit(solution)/shard_map/all_to_all | solution.py:107
  37.8 0.1 reduce_sum.47
  37.9 0.1 broadcast_in_dim.2
  37.9 15.4 %all_to_all.16 = f32[64,1,512]{2,1,0:T(1,128)S(1)} all-to-all(f32[64,1,512]{2,1,0:T(1,128)S(1)} %broadcast_in_dim.2), channel_id=1, replica_groups=mesh['sx'=4,'sz'=4,'sy'=4,'grp'=4] {'sy','sz','sx'}, dimensions={0} | all-to-all | bytes 262144 | tf_op jit(solution)/shard_map/all_to_all | solution.py:110
  53.4 0.3 reduce.1
  53.8 2.4 %add_reduce_fusion = (f32[16,32]{1,0:T(8,128)S(1)}, f32[16,32]{1,0:T(8,128)S(1)}) fusion(f32[16,32,1024]{2,1,0:T(8,128)S(1)} %get-tuple-element.10, f32[16,32,1024]{2,1,0:T(8,128)} %copy-done.1, f32[16,1024]{1,0:T(8,128)S(1)} %get-tuple-element.20, f32[16,1024]{1,0:T(8,128)S(1)} %get-tuple-element.19), kind=kLoop, calls=%fused_computation.3 | loop fusion | flops 4193280 | bytes 4329472 | tf_op jit(solution)/shard_map/reduce_sum | solution.py:115
  56.2 0.9 %collective-permute-start.4 = (f32[32,32]{0,1:T(8,128)S(1)}, f32[32,32]{0,1:T(8,128)S(1)}, u32[]{:S(2)}, u32[]{:S(2)}) collective-permute-start(f32[32,32]{0,1:T(8,128)S(1)} %maximum_multiply_fusion), channel_id=1, source_target_pairs={{0,2},{1,3},{2,0},{3,1},{4,6},{5,7},{6,4},{7,5},{8,10},{9,11},{10,... | collective-permute-start | bytes 12296 | tf_op jit(solution)/shard_map/ppermute | solution.py:41
  57.1 2.6 %collective-permute-start.5 = (f32[32,32]{0,1:T(8,128)S(1)}, f32[32,32]{0,1:T(8,128)S(1)}, u32[]{:S(2)}, u32[]{:S(2)}) collective-permute-start(f32[32,32]{0,1:T(8,128)S(1)} %maximum_multiply_fusion), channel_id=1, source_target_pairs={{0,3},{1,0},{2,1},{3,2},{4,7},{5,4},{6,5},{7,6},{8,11},{9,8},{10,9... | collective-permute-start | bytes 12296 | tf_op jit(solution)/shard_map/ppermute | solution.py:41
  59.6 1.0 %collective-permute-start.3 = (f32[32,32]{0,1:T(8,128)S(1)}, f32[32,32]{0,1:T(8,128)S(1)}, u32[]{:S(2)}, u32[]{:S(2)}) collective-permute-start(f32[32,32]{0,1:T(8,128)S(1)} %maximum_multiply_fusion), channel_id=1, source_target_pairs={{0,1},{1,2},{2,3},{3,0},{4,5},{5,6},{6,7},{7,4},{8,9},{9,10},{10,1... | collective-permute-start | bytes 12296 | tf_op jit(solution)/shard_map/ppermute | solution.py:41
  60.6 0.0 collective-permute-done.4
  60.6 2.0 %collective-permute-done.5 = f32[32,32]{0,1:T(8,128)S(1)} collective-permute-done((f32[32,32]{0,1:T(8,128)S(1)}, f32[32,32]{0,1:T(8,128)S(1)}, u32[]{:S(2)}, u32[]{:S(2)}) %collective-permute-start.5) | collective-permute-done | bytes 4128 | tf_op jit(solution)/shard_map/ppermute | solution.py:41
  62.6 0.8 %convolution_convert_fusion = bf16[32,1024]{1,0:T(8,128)(2,1)} fusion(bf16[1024,16]{0,1:T(8,128)(2,1)S(1)} %get-tuple-element.24, bf16[1024,16]{0,1:T(8,128)(2,1)S(1)} %get-tuple-element.23, f32[32,32]{0,1:T(8,128)S(1)} %collective-permute-done.5, f32[32,32]{0,1:T(8,128)S(1)} %collective-permute-done.4, f32[32,32]{0,1:T(8,128)S(1)} %collective-permute-done.3, ...), kind=kOutput, calls=%fused_computation.16 | convolution fusion | flops 2267136 | bytes 147456 | tf_op jit(solution)/shard_map/dot_general | solution.py:120
  (15 shorter events, 0.1 us)
Async XLA Ops:
  0.0 6.8 %copy-start = (s32[32,4096]{1,0:T(8,128)S(1)}, s32[32,4096]{1,0:T(8,128)}, u32[]{:S(2)}) copy-start(s32[32,4096]{1,0:T(8,128)} %param.6) | copy-start | bytes 1572868
  1.9 8.9 %collective-permute-start.2 = (f32[32,32]{0,1:T(8,128)S(1)}, f32[32,32]{0,1:T(8,128)S(1)}, u32[]{:S(2)}, u32[]{:S(2)}) collective-permute-start(f32[32,32]{0,1:T(8,128)S(1)} %convolution_bitcast_fusion), channel_id=1, source_target_pairs={{0,3},{1,0},{2,1},{3,2},{4,7},{5,4},{6,5},{7,6},{8,11},{9,8},{10,9... | collective-permute-start | bytes 12296 | tf_op jit(solution)/shard_map/ppermute | solution.py:41
  5.1 5.7 %collective-permute-start.1 = (f32[32,32]{0,1:T(8,128)S(1)}, f32[32,32]{0,1:T(8,128)S(1)}, u32[]{:S(2)}, u32[]{:S(2)}) collective-permute-start(f32[32,32]{0,1:T(8,128)S(1)} %convolution_bitcast_fusion), channel_id=1, source_target_pairs={{0,2},{1,3},{2,0},{3,1},{4,6},{5,7},{6,4},{7,5},{8,10},{9,11},{10,... | collective-permute-start | bytes 12296 | tf_op jit(solution)/shard_map/ppermute | solution.py:41
  5.1 5.7 %collective-permute-start = (f32[32,32]{0,1:T(8,128)S(1)}, f32[32,32]{0,1:T(8,128)S(1)}, u32[]{:S(2)}, u32[]{:S(2)}) collective-permute-start(f32[32,32]{0,1:T(8,128)S(1)} %convolution_bitcast_fusion), channel_id=1, source_target_pairs={{0,1},{1,2},{2,3},{3,0},{4,5},{5,6},{6,7},{7,4},{8,9},{9,10},{10,1... | collective-permute-start | bytes 12296 | tf_op jit(solution)/shard_map/ppermute | solution.py:41
  10.0 2.2 %copy-start.1 = (f32[16,32,1024]{2,1,0:T(8,128)}, f32[16,32,1024]{2,1,0:T(8,128)S(1)}, u32[]{:S(2)}) copy-start(f32[16,32,1024]{2,1,0:T(8,128)S(1)} %get-tuple-element.9) | copy-start | bytes 6291460
  56.2 4.4 %collective-permute-start.4 = (f32[32,32]{0,1:T(8,128)S(1)}, f32[32,32]{0,1:T(8,128)S(1)}, u32[]{:S(2)}, u32[]{:S(2)}) collective-permute-start(f32[32,32]{0,1:T(8,128)S(1)} %maximum_multiply_fusion), channel_id=1, source_target_pairs={{0,2},{1,3},{2,0},{3,1},{4,6},{5,7},{6,4},{7,5},{8,10},{9,11},{10,... | collective-permute-start | bytes 12296 | tf_op jit(solution)/shard_map/ppermute | solution.py:41
  57.1 5.5 %collective-permute-start.5 = (f32[32,32]{0,1:T(8,128)S(1)}, f32[32,32]{0,1:T(8,128)S(1)}, u32[]{:S(2)}, u32[]{:S(2)}) collective-permute-start(f32[32,32]{0,1:T(8,128)S(1)} %maximum_multiply_fusion), channel_id=1, source_target_pairs={{0,3},{1,0},{2,1},{3,2},{4,7},{5,4},{6,5},{7,6},{8,11},{9,8},{10,9... | collective-permute-start | bytes 12296 | tf_op jit(solution)/shard_map/ppermute | solution.py:41
  59.6 2.9 %collective-permute-start.3 = (f32[32,32]{0,1:T(8,128)S(1)}, f32[32,32]{0,1:T(8,128)S(1)}, u32[]{:S(2)}, u32[]{:S(2)}) collective-permute-start(f32[32,32]{0,1:T(8,128)S(1)} %maximum_multiply_fusion), channel_id=1, source_target_pairs={{0,1},{1,2},{2,3},{3,0},{4,5},{5,6},{6,7},{7,4},{8,9},{9,10},{10,1... | collective-permute-start | bytes 12296 | tf_op jit(solution)/shard_map/ppermute | solution.py:41

commit v18 on v15

--- a/solution.py
+++ b/solution.py
@@ -46,6 +46,15 @@
     for shift in range(1, lax.axis_size(axis)):
         total = total + shifted(x, axis, shift)
     return total
+
+
+def butterfly_sum(x, axis):
+    count = lax.axis_size(axis)
+    step = 1
+    while step < count:
+        x = x + lax.ppermute(x, axis, [(j, j ^ step) for j in range(count)])
+        step *= 2
+    return x
 
 
 def gather_stack(x, axis):
@@ -115,7 +124,7 @@
     back_real = jnp.sum(bar_real[:, None, :] * cosine + bar_imag[:, None, :] * sine_part, axis=2)
     back_imag = jnp.sum(bar_imag[:, None, :] * cosine - bar_real[:, None, :] * sine_part, axis=2)
     back = jnp.concatenate([back_real.T, back_imag.T], 1) * steer_scale
-    back = ring_sum(back, "grp")
+    back = butterfly_sum(back, "grp")
     adjoint = back.astype(jnp.bfloat16)
     local_part = lax.dot_general(
         adjoint, transform, (((1,), (1,)), ((), ())), preferred_element_type=jnp.float32

time: 63.7 us -> 63.5 us (level)
  starting transfers between devices: 9.35 us -> 8.08 us
  waiting for transfers between devices: 1.97 us -> 3.07 us
    ppermute x6 -> x3, starting transfers between devices: 9.35 us -> 4.93 us  [shifted(): lax.ppermute(x, axis, [(j, (j + shift) % count) for j in range(count)])]
    ppermute x0 -> x2, starting transfers between devices: none -> 3.15 us  [butterfly_sum(): x = x + lax.ppermute(x, axis, [(j, j ^ step) for j in range(count)])]
    ppermute x0 -> x2, waiting for transfers between devices: none -> 3.06 us  [butterfly_sum(): x = x + lax.ppermute(x, axis, [(j, j ^ step) for j in range(count)])]
    ppermute x6 -> x3, waiting for transfers between devices: 1.97 us -> 0.01 us  [shifted(): lax.ppermute(x, axis, [(j, (j + shift) % count) for j in range(count)])]
  transfers between devices with their start and end apart: 6 -> 5, of which waited for: 1 -> 2; matrix products, arithmetic and copies ran while one was open for 6% -> 6% of each run, Pallas kernels for 0% -> 0%
where the time goes in v18:
time: 63.5 us; the launch traced here: 63.2 us
  blocking collectives  40.8 us (64%)
  other arithmetic  9.13 us (14%)
  starting transfers between devices  8.08 us (13%)
  waiting for transfers between devices  3.07 us (5%)
  matrix products  1.79 us (3%)
    all_to_all x1, blocking collectives, on_device(): moved = lax.all_to_all(parts, SENS_AXES, 0, 0, tiled=True)  25.3 us
    all_to_all x1, blocking collectives, on_device(): lax.all_to_all(copies, SENS_AXES, 0, 0, tiled=True).reshape(steered.shape)  15.4 us
    ppermute x3, starting transfers between devices, shifted(): lax.ppermute(x, axis, [(j, (j + shift) % count) for j in range(count)])  4.93 us
    select_n x1, other arithmetic, circle_point(): sine = jnp.where(nearest & 2 != 0, -sine, sine)  3.23 us
    ppermute x2, starting transfers between devices, butterfly_sum(): x = x + lax.ppermute(x, axis, [(j, j ^ step) for j in range(count)])  3.15 us
    ppermute x2, waiting for transfers between devices, butterfly_sum(): x = x + lax.ppermute(x, axis, [(j, j ^ step) for j in range(count)])  3.06 us
    reduce_sum x1, other arithmetic, on_device(): jnp.sum(bar_real[:, None, :] * cosine + bar_imag[:, None, :] * sine_part,...  2.38 us
    reduce_sum x1, other arithmetic, on_device(): jnp.sum(real_t[:, :, None] * cosine - imag_t[:, :, None] * sine_part, axi...  1.42 us
  transfers between devices with their start and end apart: 5, of which 2 were waited for; matrix products, arithmetic and copies ran while one was open for 6% of the time, Pallas kernels for 0%

profile of v18, /device:TPU:1, one launch (start us, length us, event | category | flops | bytes accessed | tf_op | source)
XLA Modules:
  0.0 63.2 jit_solution(4869112755197078033)
XLA Ops:
  0.0 0.0 copy-start
  0.0 0.9 %fusion.2 = (bf16[1024,16]{0,1:T(8,128)(2,1)S(1)}, bf16[1024,16]{0,1:T(8,128)(2,1)S(1)}) fusion(s32[16]{0:T(128)} %param.5, s32[1024]{0:T(1024)S(1)} %iota_add_fusion), kind=kLoop, calls=%fused_computation.22 | loop fusion | flops 688128 | bytes 69696 | tf_op jit(solution)/shard_map/convert
  0.9 1.0 %convolution_bitcast_fusion = f32[32,32]{0,1:T(8,128)S(1)} fusion(bf16[32,1024]{1,0:T(8,128)(2,1)} %param.4, bf16[1024,16]{0,1:T(8,128)(2,1)S(1)} %get-tuple-element.24, bf16[1024,16]{0,1:T(8,128)(2,1)S(1)} %get-tuple-element.23), kind=kOutput, calls=%fused_computation.17 | convolution fusion | flops 2228224 | bytes 135168 | tf_op jit(solution)/shard_map/dot_general | solution.py:94
  1.9 3.2 %collective-permute-start.2 = (f32[32,32]{0,1:T(8,128)S(1)}, f32[32,32]{0,1:T(8,128)S(1)}, u32[]{:S(2)}, u32[]{:S(2)}) collective-permute-start(f32[32,32]{0,1:T(8,128)S(1)} %convolution_bitcast_fusion), channel_id=1, source_target_pairs={{0,3},{1,0},{2,1},{3,2},{4,7},{5,4},{6,5},{7,6},{8,11},{9,8},{10,9... | collective-permute-start | bytes 12296 | tf_op jit(solution)/shard_map/ppermute | solution.py:41
  5.1 0.0 collective-permute-start.1
  5.1 1.7 %collective-permute-start = (f32[32,32]{0,1:T(8,128)S(1)}, f32[32,32]{0,1:T(8,128)S(1)}, u32[]{:S(2)}, u32[]{:S(2)}) collective-permute-start(f32[32,32]{0,1:T(8,128)S(1)} %convolution_bitcast_fusion), channel_id=1, source_target_pairs={{0,1},{1,2},{2,3},{3,0},{4,5},{5,6},{6,7},{7,4},{8,9},{9,10},{10,1... | collective-permute-start | bytes 12296 | tf_op jit(solution)/shard_map/ppermute | solution.py:41
  6.8 3.2 %negate_select_fusion = (f32[16,32,1024]{2,1,0:T(8,128)S(1)}, f32[16,32,1024]{2,1,0:T(8,128)S(1)}) fusion(s32[32,1024]{1,0:T(8,128)S(1)} %constant_dynamic-slice_fusion, s32[16]{0:T(128)} %param.5), kind=kLoop, calls=%fused_computation | loop fusion | flops 19398656 | bytes 4325440 | tf_op jit(solution)/shard_map/jit(_where)/select_n | solution.py:34
  10.0 0.7 %dynamic-slice_multiply_fusion = f32[1024]{0:T(1024)S(1)} fusion(f32[4096]{0:T(1024)} %param.7, s32[]{:T(128)S(6)} %select_n.34), kind=kLoop, calls=%fused_computation.45 | loop fusion | flops 1024 | bytes 8196 | tf_op jit(solution)/shard_map/mul | solution.py:112
  10.8 0.0 collective-permute-done.2
  10.8 0.0 collective-permute-done.1
  10.8 0.0 collective-permute-done
  10.8 1.4 %subtract_reduce_fusion.1 = (f32[16,1024]{1,0:T(8,128)S(1)}, f32[16,1024]{1,0:T(8,128)S(1)}) fusion(f32[16,32,1024]{2,1,0:T(8,128)S(1)} %get-tuple-element.10, f32[16,32,1024]{2,1,0:T(8,128)S(1)} %get-tuple-element.9, f32[16,32]{1,0:T(8,128)S(1)} %get-tuple-element.22, f32[16,32]{1,0:T(8,128)S(1)} %get-tuple-element.21), kind=kLoop, calls=%fused_computation.5 | loop fusion | flops 4161536 | bytes 4329472 | tf_op jit(solution)/shard_map/reduce_sum | solution.py:103
  12.3 0.1 all_to_all.10
  12.4 25.3 %all_to_all.15 = f32[64,1,512]{2,1,0:T(1,128)S(1)} all-to-all(f32[64,1,512]{2,1,0:T(1,128)S(1)} %all_to_all.10), channel_id=1, replica_groups=mesh['sx'=4,'sz'=4,'sy'=4,'grp'=4] {'sx','sz','sy'}, dimensions={0} | all-to-all | bytes 262144 | tf_op jit(solution)/shard_map/all_to_all | solution.py:116
  37.8 0.1 reduce_sum.47
  37.9 0.1 broadcast_in_dim.2
  37.9 15.4 %all_to_all.16 = f32[64,1,512]{2,1,0:T(1,128)S(1)} all-to-all(f32[64,1,512]{2,1,0:T(1,128)S(1)} %broadcast_in_dim.2), channel_id=1, replica_groups=mesh['sx'=4,'sz'=4,'sy'=4,'grp'=4] {'sx','sz','sy'}, dimensions={0} | all-to-all | bytes 262144 | tf_op jit(solution)/shard_map/all_to_all | solution.py:119
  53.4 0.3 reduce.1
  53.8 2.4 %add_reduce_fusion = (f32[16,32]{1,0:T(8,128)S(1)}, f32[16,32]{1,0:T(8,128)S(1)}) fusion(f32[16,32,1024]{2,1,0:T(8,128)S(1)} %get-tuple-element.10, f32[16,32,1024]{2,1,0:T(8,128)} %copy-done.1, f32[16,1024]{1,0:T(8,128)S(1)} %get-tuple-element.20, f32[16,1024]{1,0:T(8,128)S(1)} %get-tuple-element.19), kind=kLoop, calls=%fused_computation.3 | loop fusion | flops 4193280 | bytes 4329472 | tf_op jit(solution)/shard_map/reduce_sum | solution.py:124
  56.2 2.8 %collective-permute-start.3 = (f32[32,32]{0,1:T(8,128)S(1)}, f32[32,32]{0,1:T(8,128)S(1)}, u32[]{:S(2)}, u32[]{:S(2)}) collective-permute-start(f32[32,32]{0,1:T(8,128)S(1)} %maximum_multiply_fusion), channel_id=1, source_target_pairs={{0,1},{1,0},{2,3},{3,2},{4,5},{5,4},{6,7},{7,6},{8,9},{9,8},{10,11... | collective-permute-start | bytes 12296 | tf_op jit(solution)/shard_map/ppermute | solution.py:55
  59.0 0.8 %collective-permute-done.3 = f32[32,32]{0,1:T(8,128)S(1)} collective-permute-done((f32[32,32]{0,1:T(8,128)S(1)}, f32[32,32]{0,1:T(8,128)S(1)}, u32[]{:S(2)}, u32[]{:S(2)}) %collective-permute-start.3) | collective-permute-done | bytes 4128 | tf_op jit(solution)/shard_map/ppermute | solution.py:55
  59.8 0.4 collective-permute-start.4
  60.2 2.2 %collective-permute-done.4 = f32[32,32]{0,1:T(8,128)S(1)} collective-permute-done((f32[32,32]{0,1:T(8,128)S(1)}, f32[32,32]{0,1:T(8,128)S(1)}, u32[]{:S(2)}, u32[]{:S(2)}) %collective-permute-start.4) | collective-permute-done | bytes 4128 | tf_op jit(solution)/shard_map/ppermute | solution.py:55
  62.4 0.8 %convolution_convert_fusion = bf16[32,1024]{1,0:T(8,128)(2,1)} fusion(bf16[1024,16]{0,1:T(8,128)(2,1)S(1)} %get-tuple-element.24, bf16[1024,16]{0,1:T(8,128)(2,1)S(1)} %get-tuple-element.23, f32[32,32]{0,1:T(8,128)S(1)} %fusion.9, f32[32,32]{0,1:T(8,128)S(1)} %collective-permute-done.4), kind=kOutput, calls=%fused_computation.16 | convolution fusion | flops 2263040 | bytes 139264 | tf_op jit(solution)/shard_map/dot_general | solution.py:129
  (14 shorter events, 0.1 us)
Async XLA Ops:
  0.0 6.8 %copy-start = (s32[32,4096]{1,0:T(8,128)S(1)}, s32[32,4096]{1,0:T(8,128)}, u32[]{:S(2)}) copy-start(s32[32,4096]{1,0:T(8,128)} %param.6) | copy-start | bytes 1572868
  1.9 8.9 %collective-permute-start.2 = (f32[32,32]{0,1:T(8,128)S(1)}, f32[32,32]{0,1:T(8,128)S(1)}, u32[]{:S(2)}, u32[]{:S(2)}) collective-permute-start(f32[32,32]{0,1:T(8,128)S(1)} %convolution_bitcast_fusion), channel_id=1, source_target_pairs={{0,3},{1,0},{2,1},{3,2},{4,7},{5,4},{6,5},{7,6},{8,11},{9,8},{10,9... | collective-permute-start | bytes 12296 | tf_op jit(solution)/shard_map/ppermute | solution.py:41
  5.1 5.7 %collective-permute-start.1 = (f32[32,32]{0,1:T(8,128)S(1)}, f32[32,32]{0,1:T(8,128)S(1)}, u32[]{:S(2)}, u32[]{:S(2)}) collective-permute-start(f32[32,32]{0,1:T(8,128)S(1)} %convolution_bitcast_fusion), channel_id=1, source_target_pairs={{0,2},{1,3},{2,0},{3,1},{4,6},{5,7},{6,4},{7,5},{8,10},{9,11},{10,... | collective-permute-start | bytes 12296 | tf_op jit(solution)/shard_map/ppermute | solution.py:41
  5.1 5.7 %collective-permute-start = (f32[32,32]{0,1:T(8,128)S(1)}, f32[32,32]{0,1:T(8,128)S(1)}, u32[]{:S(2)}, u32[]{:S(2)}) collective-permute-start(f32[32,32]{0,1:T(8,128)S(1)} %convolution_bitcast_fusion), channel_id=1, source_target_pairs={{0,1},{1,2},{2,3},{3,0},{4,5},{5,6},{6,7},{7,4},{8,9},{9,10},{10,1... | collective-permute-start | bytes 12296 | tf_op jit(solution)/shard_map/ppermute | solution.py:41
  10.0 2.2 %copy-start.1 = (f32[16,32,1024]{2,1,0:T(8,128)}, f32[16,32,1024]{2,1,0:T(8,128)S(1)}, u32[]{:S(2)}) copy-start(f32[16,32,1024]{2,1,0:T(8,128)S(1)} %get-tuple-element.9) | copy-start | bytes 6291460
  56.2 3.6 %collective-permute-start.3 = (f32[32,32]{0,1:T(8,128)S(1)}, f32[32,32]{0,1:T(8,128)S(1)}, u32[]{:S(2)}, u32[]{:S(2)}) collective-permute-start(f32[32,32]{0,1:T(8,128)S(1)} %maximum_multiply_fusion), channel_id=1, source_target_pairs={{0,1},{1,0},{2,3},{3,2},{4,5},{5,4},{6,7},{7,6},{8,9},{9,8},{10,11... | collective-permute-start | bytes 12296 | tf_op jit(solution)/shard_map/ppermute | solution.py:55
  59.8 2.6 %collective-permute-start.4 = (f32[32,32]{0,1:T(8,128)S(1)}, f32[32,32]{0,1:T(8,128)S(1)}, u32[]{:S(2)}, u32[]{:S(2)}) collective-permute-start(f32[32,32]{0,1:T(8,128)S(1)} %fusion.9), channel_id=1, source_target_pairs={{0,2},{1,3},{2,0},{3,1},{4,6},{5,7},{6,4},{7,5},{8,10},{9,11},{10,... | collective-permute-start | bytes 12296 | tf_op jit(solution)/shard_map/ppermute | solution.py:55

commit v19 on v15

--- a/solution.py
+++ b/solution.py
@@ -12,7 +12,7 @@
 
 def transform_rows(first, count, bin_index, length):
     sample_times = first + lax.iota(jnp.int32, count)
-    phase_index = (sample_times[:, None] * bin_index[None, :]) & (length - 1)
+    phase_index = sample_times[:, None] * bin_index[None, :]
     factor = 1.0 / math.sqrt(length)
     cosine, sine = circle_point(phase_index, length)
     cosine = cosine * factor
@@ -22,8 +22,9 @@
 
 def circle_point(phase_index, length):
     quarter_bits = (length // 4).bit_length() - 1
-    nearest = (phase_index + length // 8) >> quarter_bits
-    rest = phase_index - (nearest << quarter_bits)
+    shifted_index = phase_index + length // 8
+    nearest = shifted_index >> quarter_bits
+    rest = (shifted_index & (length // 4 - 1)) - length // 8
     x = rest.astype(jnp.float32) * (two_pi / length)
     x2 = x * x
     sin_x = x * (1.0 + x2 * (-1.0 / 6.0 + x2 * (1.0 / 120.0 + x2 * (-1.0 / 5040.0))))
@@ -88,7 +89,7 @@
     imag_t = spectra[:, bins:].T
 
     own_delays = lax.dynamic_slice_in_dim(delays, position * scan_share, scan_share, 1)
-    phase_index = (bin_index[:, None, None] * own_delays[None, :, :]) & (NT - 1)
+    phase_index = bin_index[:, None, None] * own_delays[None, :, :]
     cosine, sine_part = lax.optimization_barrier(circle_point(phase_index, NT))
 
     steer_real = jnp.sum(real_t[:, :, None] * cosine - imag_t[:, :, None] * sine_part, axis=1)

time: 63.7 us -> 63.6 us (level)
  no operation moved by 1% of the time
where the time goes in v19:
time: 63.6 us; the launch traced here: 63.3 us
  blocking collectives  40.8 us (64%)
  starting transfers between devices  9.35 us (15%)
  other arithmetic  9.04 us (14%)
  waiting for transfers between devices  1.97 us (3%)
  matrix products  1.79 us (3%)
    all_to_all x1, blocking collectives, on_device(): moved = lax.all_to_all(parts, SENS_AXES, 0, 0, tiled=True)  25.3 us
    all_to_all x1, blocking collectives, on_device(): lax.all_to_all(copies, SENS_AXES, 0, 0, tiled=True).reshape(steered.shape)  15.4 us
    ppermute x6, starting transfers between devices, shifted(): lax.ppermute(x, axis, [(j, (j + shift) % count) for j in range(count)])  9.35 us
    select_n x1, other arithmetic, circle_point(): sine = jnp.where(nearest & 2 != 0, -sine, sine)  3.16 us
    reduce_sum x1, other arithmetic, on_device(): jnp.sum(bar_real[:, None, :] * cosine + bar_imag[:, None, :] * sine_part,...  2.38 us
    ppermute x6, waiting for transfers between devices, shifted(): lax.ppermute(x, axis, [(j, (j + shift) % count) for j in range(count)])  1.97 us
    reduce_sum x1, other arithmetic, on_device(): jnp.sum(real_t[:, :, None] * cosine - imag_t[:, :, None] * sine_part, axi...  1.42 us
  transfers between devices with their start and end apart: 6, of which 1 were waited for; matrix products, arithmetic and copies ran while one was open for 6% of the time, Pallas kernels for 0%

profile of v19, /device:TPU:1, one launch (start us, length us, event | category | flops | bytes accessed | tf_op | source)
XLA Modules:
  0.0 63.3 jit_solution(18002099071442329838)
XLA Ops:
  0.0 0.9 %fusion.3 = (bf16[1024,16]{0,1:T(8,128)(2,1)S(1)}, bf16[1024,16]{0,1:T(8,128)(2,1)S(1)}) fusion(s32[16]{0:T(128)} %param.5, s32[1024]{0:T(1024)S(1)} %iota_add_fusion), kind=kLoop, calls=%fused_computation.22 | loop fusion | flops 671744 | bytes 69696 | tf_op jit(solution)/shard_map/convert
  0.9 1.0 %convolution_bitcast_fusion = f32[32,32]{0,1:T(8,128)S(1)} fusion(bf16[32,1024]{1,0:T(8,128)(2,1)} %param.4, bf16[1024,16]{0,1:T(8,128)(2,1)S(1)} %get-tuple-element.24, bf16[1024,16]{0,1:T(8,128)(2,1)S(1)} %get-tuple-element.23), kind=kOutput, calls=%fused_computation.17 | convolution fusion | flops 2228224 | bytes 135168 | tf_op jit(solution)/shard_map/dot_general | solution.py:86
  1.9 3.2 %collective-permute-start.2 = (f32[32,32]{0,1:T(8,128)S(1)}, f32[32,32]{0,1:T(8,128)S(1)}, u32[]{:S(2)}, u32[]{:S(2)}) collective-permute-start(f32[32,32]{0,1:T(8,128)S(1)} %convolution_bitcast_fusion), channel_id=1, source_target_pairs={{0,3},{1,0},{2,1},{3,2},{4,7},{5,4},{6,5},{7,6},{8,11},{9,8},{10,9... | collective-permute-start | bytes 12296 | tf_op jit(solution)/shard_map/ppermute | solution.py:42
  5.1 0.0 collective-permute-start.1
  5.1 1.7 %collective-permute-start = (f32[32,32]{0,1:T(8,128)S(1)}, f32[32,32]{0,1:T(8,128)S(1)}, u32[]{:S(2)}, u32[]{:S(2)}) collective-permute-start(f32[32,32]{0,1:T(8,128)S(1)} %convolution_bitcast_fusion), channel_id=1, source_target_pairs={{0,1},{1,2},{2,3},{3,0},{4,5},{5,6},{6,7},{7,4},{8,9},{9,10},{10,1... | collective-permute-start | bytes 12296 | tf_op jit(solution)/shard_map/ppermute | solution.py:42
  6.8 3.2 %negate_select_fusion = (f32[16,32,1024]{2,1,0:T(8,128)S(1)}, f32[16,32,1024]{2,1,0:T(8,128)S(1)}) fusion(s32[32,1024]{1,0:T(8,128)S(1)} %constant_dynamic-slice_fusion, s32[16]{0:T(128)} %param.5), kind=kLoop, calls=%fused_computation | loop fusion | flops 18874368 | bytes 4325440 | tf_op jit(solution)/shard_map/jit(_where)/select_n | solution.py:35
  10.0 0.7 %dynamic-slice_multiply_fusion = f32[1024]{0:T(1024)S(1)} fusion(f32[4096]{0:T(1024)} %param.7, s32[]{:T(128)S(6)} %select_n.34), kind=kLoop, calls=%fused_computation.45 | loop fusion | flops 1024 | bytes 8196 | tf_op jit(solution)/shard_map/mul | solution.py:104
  10.7 0.0 collective-permute-done.2
  10.7 0.0 collective-permute-done.1
  10.7 0.0 collective-permute-done
  10.8 1.4 %subtract_reduce_fusion.1 = (f32[16,1024]{1,0:T(8,128)S(1)}, f32[16,1024]{1,0:T(8,128)S(1)}) fusion(f32[16,32,1024]{2,1,0:T(8,128)S(1)} %get-tuple-element.10, f32[16,32,1024]{2,1,0:T(8,128)S(1)} %get-tuple-element.9, f32[16,32]{1,0:T(8,128)S(1)} %get-tuple-element.22, f32[16,32]{1,0:T(8,128)S(1)} %get-tuple-element.21), kind=kLoop, calls=%fused_computation.5 | loop fusion | flops 4161536 | bytes 4329472 | tf_op jit(solution)/shard_map/reduce_sum | solution.py:95
  12.2 0.1 all_to_all.10
  12.3 25.3 %all_to_all.15 = f32[64,1,512]{2,1,0:T(1,128)S(1)} all-to-all(f32[64,1,512]{2,1,0:T(1,128)S(1)} %all_to_all.10), channel_id=1, replica_groups=mesh['sx'=4,'sz'=4,'sy'=4,'grp'=4] {'sx','sz','sy'}, dimensions={0} | all-to-all | bytes 262144 | tf_op jit(solution)/shard_map/all_to_all | solution.py:108
  37.7 0.1 reduce_sum.47
  37.8 0.1 broadcast_in_dim.2
  37.9 15.4 %all_to_all.16 = f32[64,1,512]{2,1,0:T(1,128)S(1)} all-to-all(f32[64,1,512]{2,1,0:T(1,128)S(1)} %broadcast_in_dim.2), channel_id=1, replica_groups=mesh['sx'=4,'sz'=4,'sy'=4,'grp'=4] {'sx','sz','sy'}, dimensions={0} | all-to-all | bytes 262144 | tf_op jit(solution)/shard_map/all_to_all | solution.py:111
  53.3 0.3 reduce.1
  53.7 2.4 %add_reduce_fusion = (f32[16,32]{1,0:T(8,128)S(1)}, f32[16,32]{1,0:T(8,128)S(1)}) fusion(f32[16,32,1024]{2,1,0:T(8,128)S(1)} %get-tuple-element.10, f32[16,32,1024]{2,1,0:T(8,128)} %copy-done.1, f32[16,1024]{1,0:T(8,128)S(1)} %get-tuple-element.20, f32[16,1024]{1,0:T(8,128)S(1)} %get-tuple-element.19), kind=kLoop, calls=%fused_computation.3 | loop fusion | flops 4193280 | bytes 4329472 | tf_op jit(solution)/shard_map/reduce_sum | solution.py:116
  56.1 0.9 %collective-permute-start.4 = (f32[32,32]{0,1:T(8,128)S(1)}, f32[32,32]{0,1:T(8,128)S(1)}, u32[]{:S(2)}, u32[]{:S(2)}) collective-permute-start(f32[32,32]{0,1:T(8,128)S(1)} %maximum_multiply_fusion), channel_id=1, source_target_pairs={{0,2},{1,3},{2,0},{3,1},{4,6},{5,7},{6,4},{7,5},{8,10},{9,11},{10,... | collective-permute-start | bytes 12296 | tf_op jit(solution)/shard_map/ppermute | solution.py:42
  57.0 2.6 %collective-permute-start.5 = (f32[32,32]{0,1:T(8,128)S(1)}, f32[32,32]{0,1:T(8,128)S(1)}, u32[]{:S(2)}, u32[]{:S(2)}) collective-permute-start(f32[32,32]{0,1:T(8,128)S(1)} %maximum_multiply_fusion), channel_id=1, source_target_pairs={{0,3},{1,0},{2,1},{3,2},{4,7},{5,4},{6,5},{7,6},{8,11},{9,8},{10,9... | collective-permute-start | bytes 12296 | tf_op jit(solution)/shard_map/ppermute | solution.py:42
  59.5 1.0 %collective-permute-start.3 = (f32[32,32]{0,1:T(8,128)S(1)}, f32[32,32]{0,1:T(8,128)S(1)}, u32[]{:S(2)}, u32[]{:S(2)}) collective-permute-start(f32[32,32]{0,1:T(8,128)S(1)} %maximum_multiply_fusion), channel_id=1, source_target_pairs={{0,1},{1,2},{2,3},{3,0},{4,5},{5,6},{6,7},{7,4},{8,9},{9,10},{10,1... | collective-permute-start | bytes 12296 | tf_op jit(solution)/shard_map/ppermute | solution.py:42
  60.5 0.0 collective-permute-done.4
  60.5 2.0 %collective-permute-done.5 = f32[32,32]{0,1:T(8,128)S(1)} collective-permute-done((f32[32,32]{0,1:T(8,128)S(1)}, f32[32,32]{0,1:T(8,128)S(1)}, u32[]{:S(2)}, u32[]{:S(2)}) %collective-permute-start.5) | collective-permute-done | bytes 4128 | tf_op jit(solution)/shard_map/ppermute | solution.py:42
  62.5 0.8 %convolution_convert_fusion = bf16[32,1024]{1,0:T(8,128)(2,1)} fusion(bf16[1024,16]{0,1:T(8,128)(2,1)S(1)} %get-tuple-element.24, bf16[1024,16]{0,1:T(8,128)(2,1)S(1)} %get-tuple-element.23, f32[32,32]{0,1:T(8,128)S(1)} %collective-permute-done.5, f32[32,32]{0,1:T(8,128)S(1)} %collective-permute-done.4, f32[32,32]{0,1:T(8,128)S(1)} %collective-permute-done.3, ...), kind=kOutput, calls=%fused_computation.16 | convolution fusion | flops 2267136 | bytes 147456 | tf_op jit(solution)/shard_map/dot_general | solution.py:121
  (15 shorter events, 0.1 us)
Async XLA Ops:
  0.0 6.8 %copy-start = (s32[32,4096]{1,0:T(8,128)S(1)}, s32[32,4096]{1,0:T(8,128)}, u32[]{:S(2)}) copy-start(s32[32,4096]{1,0:T(8,128)} %param.6) | copy-start | bytes 1572868
  1.9 8.9 %collective-permute-start.2 = (f32[32,32]{0,1:T(8,128)S(1)}, f32[32,32]{0,1:T(8,128)S(1)}, u32[]{:S(2)}, u32[]{:S(2)}) collective-permute-start(f32[32,32]{0,1:T(8,128)S(1)} %convolution_bitcast_fusion), channel_id=1, source_target_pairs={{0,3},{1,0},{2,1},{3,2},{4,7},{5,4},{6,5},{7,6},{8,11},{9,8},{10,9... | collective-permute-start | bytes 12296 | tf_op jit(solution)/shard_map/ppermute | solution.py:42
  5.1 5.6 %collective-permute-start.1 = (f32[32,32]{0,1:T(8,128)S(1)}, f32[32,32]{0,1:T(8,128)S(1)}, u32[]{:S(2)}, u32[]{:S(2)}) collective-permute-start(f32[32,32]{0,1:T(8,128)S(1)} %convolution_bitcast_fusion), channel_id=1, source_target_pairs={{0,2},{1,3},{2,0},{3,1},{4,6},{5,7},{6,4},{7,5},{8,10},{9,11},{10,... | collective-permute-start | bytes 12296 | tf_op jit(solution)/shard_map/ppermute | solution.py:42
  5.1 5.6 %collective-permute-start = (f32[32,32]{0,1:T(8,128)S(1)}, f32[32,32]{0,1:T(8,128)S(1)}, u32[]{:S(2)}, u32[]{:S(2)}) collective-permute-start(f32[32,32]{0,1:T(8,128)S(1)} %convolution_bitcast_fusion), channel_id=1, source_target_pairs={{0,1},{1,2},{2,3},{3,0},{4,5},{5,6},{6,7},{7,4},{8,9},{9,10},{10,1... | collective-permute-start | bytes 12296 | tf_op jit(solution)/shard_map/ppermute | solution.py:42
  10.0 2.2 %copy-start.1 = (f32[16,32,1024]{2,1,0:T(8,128)}, f32[16,32,1024]{2,1,0:T(8,128)S(1)}, u32[]{:S(2)}) copy-start(f32[16,32,1024]{2,1,0:T(8,128)S(1)} %get-tuple-element.9) | copy-start | bytes 6291460
  56.1 4.4 %collective-permute-start.4 = (f32[32,32]{0,1:T(8,128)S(1)}, f32[32,32]{0,1:T(8,128)S(1)}, u32[]{:S(2)}, u32[]{:S(2)}) collective-permute-start(f32[32,32]{0,1:T(8,128)S(1)} %maximum_multiply_fusion), channel_id=1, source_target_pairs={{0,2},{1,3},{2,0},{3,1},{4,6},{5,7},{6,4},{7,5},{8,10},{9,11},{10,... | collective-permute-start | bytes 12296 | tf_op jit(solution)/shard_map/ppermute | solution.py:42
  57.0 5.5 %collective-permute-start.5 = (f32[32,32]{0,1:T(8,128)S(1)}, f32[32,32]{0,1:T(8,128)S(1)}, u32[]{:S(2)}, u32[]{:S(2)}) collective-permute-start(f32[32,32]{0,1:T(8,128)S(1)} %maximum_multiply_fusion), channel_id=1, source_target_pairs={{0,3},{1,0},{2,1},{3,2},{4,7},{5,4},{6,5},{7,6},{8,11},{9,8},{10,9... | collective-permute-start | bytes 12296 | tf_op jit(solution)/shard_map/ppermute | solution.py:42
  59.5 2.9 %collective-permute-start.3 = (f32[32,32]{0,1:T(8,128)S(1)}, f32[32,32]{0,1:T(8,128)S(1)}, u32[]{:S(2)}, u32[]{:S(2)}) collective-permute-start(f32[32,32]{0,1:T(8,128)S(1)} %maximum_multiply_fusion), channel_id=1, source_target_pairs={{0,1},{1,2},{2,3},{3,0},{4,5},{5,6},{6,7},{7,4},{8,9},{9,10},{10,1... | collective-permute-start | bytes 12296 | tf_op jit(solution)/shard_map/ppermute | solution.py:42

commit v20 on v19

--- a/solution.py
+++ b/solution.py
@@ -92,24 +92,23 @@
     phase_index = bin_index[:, None, None] * own_delays[None, :, :]
     cosine, sine_part = lax.optimization_barrier(circle_point(phase_index, NT))
 
+    own_weight = (2.0 * steer_scale) * lax.dynamic_slice_in_dim(
+        map_adjoint, position * scan_share, scan_share, 0
+    )
     steer_real = jnp.sum(real_t[:, :, None] * cosine - imag_t[:, :, None] * sine_part, axis=1)
     steer_imag = jnp.sum(real_t[:, :, None] * sine_part + imag_t[:, :, None] * cosine, axis=1)
-    steered = jnp.stack([steer_real, steer_imag])
+    steered = jnp.stack([steer_real, steer_imag]) * own_weight
     offset = 0
     for axis in SENS_AXES:
         offset = offset * lax.axis_size(axis) + lax.axis_index(axis)
     count = lax.axis_size(SENS_AXES)
     parts = steered.reshape(count, steered.size // count)
     width = parts.shape[1]
-    own_weight = (2.0 * steer_scale) * lax.dynamic_slice_in_dim(
-        map_adjoint, position * scan_share, scan_share, 0
-    )
-    parts, own_weight = lax.optimization_barrier((parts, own_weight))
     moved = lax.all_to_all(parts, SENS_AXES, 0, 0, tiled=True)
     chunk = jnp.sum(moved, axis=0)
     copies = jnp.broadcast_to(chunk[None], (count, width))
     gathered = lax.all_to_all(copies, SENS_AXES, 0, 0, tiled=True).reshape(steered.shape)
-    bar = own_weight * gathered
+    bar = gathered
     bar_real = bar[0]
     bar_imag = bar[1]
 

time: 63.6 us -> 63.6 us (level)
  no operation moved by 1% of the time
where the time goes in v20:
time: 63.6 us; the launch traced here: 63.3 us
  blocking collectives  40.8 us (64%)
  starting transfers between devices  9.35 us (15%)
  other arithmetic  8.66 us (14%)
  waiting for transfers between devices  1.97 us (3%)
  matrix products  1.8 us (3%)
    all_to_all x1, blocking collectives, on_device(): moved = lax.all_to_all(parts, SENS_AXES, 0, 0, tiled=True)  25.3 us
    all_to_all x1, blocking collectives, on_device(): lax.all_to_all(copies, SENS_AXES, 0, 0, tiled=True).reshape(steered.shape)  15.4 us
    ppermute x6, starting transfers between devices, shifted(): lax.ppermute(x, axis, [(j, (j + shift) % count) for j in range(count)])  9.35 us
    select_n x1, other arithmetic, circle_point(): sine = jnp.where(nearest & 2 != 0, -sine, sine)  3.16 us
    reduce_sum x1, other arithmetic, on_device(): jnp.sum(bar_real[:, None, :] * cosine + bar_imag[:, None, :] * sine_part,...  2.32 us
    ppermute x6, waiting for transfers between devices, shifted(): lax.ppermute(x, axis, [(j, (j + shift) % count) for j in range(count)])  1.97 us
    reduce_sum x1, other arithmetic, on_device(): jnp.sum(real_t[:, :, None] * cosine - imag_t[:, :, None] * sine_part, axi...  1.42 us
  transfers between devices with their start and end apart: 6, of which 1 were waited for; matrix products, arithmetic and copies ran while one was open for 6% of the time, Pallas kernels for 0%

profile of v20, /device:TPU:1, one launch (start us, length us, event | category | flops | bytes accessed | tf_op | source)
XLA Modules:
  0.0 63.3 jit_solution(12578750598021525363)
XLA Ops:
  0.0 0.9 %fusion.3 = (bf16[1024,16]{0,1:T(8,128)(2,1)S(1)}, bf16[1024,16]{0,1:T(8,128)(2,1)S(1)}) fusion(s32[16]{0:T(128)} %param.5, s32[1024]{0:T(1024)S(1)} %iota_add_fusion), kind=kLoop, calls=%fused_computation.22 | loop fusion | flops 671744 | bytes 69696 | tf_op jit(solution)/shard_map/convert
  0.9 1.0 %convolution_bitcast_fusion = f32[32,32]{0,1:T(8,128)S(1)} fusion(bf16[32,1024]{1,0:T(8,128)(2,1)} %param.4, bf16[1024,16]{0,1:T(8,128)(2,1)S(1)} %get-tuple-element.20, bf16[1024,16]{0,1:T(8,128)(2,1)S(1)} %get-tuple-element.19), kind=kOutput, calls=%fused_computation.17 | convolution fusion | flops 2228224 | bytes 135168 | tf_op jit(solution)/shard_map/dot_general | solution.py:86
  1.9 3.2 %collective-permute-start.2 = (f32[32,32]{0,1:T(8,128)S(1)}, f32[32,32]{0,1:T(8,128)S(1)}, u32[]{:S(2)}, u32[]{:S(2)}) collective-permute-start(f32[32,32]{0,1:T(8,128)S(1)} %convolution_bitcast_fusion), channel_id=1, source_target_pairs={{0,3},{1,0},{2,1},{3,2},{4,7},{5,4},{6,5},{7,6},{8,11},{9,8},{10,9... | collective-permute-start | bytes 12296 | tf_op jit(solution)/shard_map/ppermute | solution.py:42
  5.1 1.7 %collective-permute-start = (f32[32,32]{0,1:T(8,128)S(1)}, f32[32,32]{0,1:T(8,128)S(1)}, u32[]{:S(2)}, u32[]{:S(2)}) collective-permute-start(f32[32,32]{0,1:T(8,128)S(1)} %convolution_bitcast_fusion), channel_id=1, source_target_pairs={{0,1},{1,2},{2,3},{3,0},{4,5},{5,6},{6,7},{7,4},{8,9},{9,10},{10,1... | collective-permute-start | bytes 12296 | tf_op jit(solution)/shard_map/ppermute | solution.py:42
  6.8 3.2 %negate_select_fusion = (f32[16,32,1024]{2,1,0:T(8,128)S(1)}, f32[16,32,1024]{2,1,0:T(8,128)S(1)}) fusion(s32[32,1024]{1,0:T(8,128)S(1)} %constant_dynamic-slice_fusion, s32[16]{0:T(128)} %param.5), kind=kLoop, calls=%fused_computation | loop fusion | flops 18874368 | bytes 4325440 | tf_op jit(solution)/shard_map/jit(_where)/select_n | solution.py:35
  10.0 0.7 %dynamic-slice_multiply_fusion = f32[1024]{0:T(1024)S(1)} fusion(f32[4096]{0:T(1024)} %param.7, s32[]{:T(128)S(6)} %select_n.34), kind=kLoop, calls=%fused_computation.44 | loop fusion | flops 1024 | bytes 8196 | tf_op jit(solution)/shard_map/mul | solution.py:95
  10.7 0.0 collective-permute-done.2
  10.7 0.0 collective-permute-done.1
  10.7 0.0 collective-permute-done
  10.8 1.4 %subtract_reduce_fusion.1 = (f32[16,1024]{1,0:T(8,128)S(1)}, f32[16,1024]{1,0:T(8,128)S(1)}) fusion(f32[16,32,1024]{2,1,0:T(8,128)S(1)} %get-tuple-element.8, f32[16,32,1024]{2,1,0:T(8,128)S(1)} %get-tuple-element.7, f32[16,32]{1,0:T(8,128)S(1)} %get-tuple-element.18, f32[16,32]{1,0:T(8,128)S(1)} %get-tuple-element.17), kind=kLoop, calls=%fused_computation.5 | loop fusion | flops 4161536 | bytes 4329472 | tf_op jit(solution)/shard_map/reduce_sum | solution.py:98
  12.2 0.2 mul.262
  12.4 25.3 %all_to_all.12 = f32[64,1,512]{2,1,0:T(1,128)S(1)} all-to-all(f32[64,1,512]{2,1,0:T(1,128)S(1)} %mul.262), channel_id=1, replica_groups=mesh['sx'=4,'sz'=4,'sy'=4,'grp'=4] {'sx','sz','sy'}, dimensions={0} | all-to-all | bytes 262144 | tf_op jit(solution)/shard_map/all_to_all | solution.py:107
  37.7 0.1 reduce_sum.47
  37.8 0.1 broadcast_in_dim.2
  37.9 15.4 %all_to_all.13 = f32[64,1,512]{2,1,0:T(1,128)S(1)} all-to-all(f32[64,1,512]{2,1,0:T(1,128)S(1)} %broadcast_in_dim.2), channel_id=1, replica_groups=mesh['sx'=4,'sz'=4,'sy'=4,'grp'=4] {'sx','sz','sy'}, dimensions={0} | all-to-all | bytes 262144 | tf_op jit(solution)/shard_map/all_to_all | solution.py:110
  53.3 0.3 slice_reduce_fusion.1
  53.7 2.3 %add_reduce_fusion = (f32[16,32]{1,0:T(8,128)S(1)}, f32[16,32]{1,0:T(8,128)S(1)}) fusion(f32[16,32,1024]{2,1,0:T(8,128)S(1)} %get-tuple-element.8, f32[16,32,1024]{2,1,0:T(8,128)} %copy-done.1, f32[16,1024]{1,0:T(8,128)S(1)} %mul.255, f32[16,1024]{1,0:T(8,128)S(1)} %mul.252), kind=kLoop, calls=%fused_computation.3 | loop fusion | flops 4193280 | bytes 4329472 | tf_op jit(solution)/shard_map/reduce_sum | solution.py:115
  56.1 0.9 %collective-permute-start.4 = (f32[32,32]{0,1:T(8,128)S(1)}, f32[32,32]{0,1:T(8,128)S(1)}, u32[]{:S(2)}, u32[]{:S(2)}) collective-permute-start(f32[32,32]{0,1:T(8,128)S(1)} %maximum_multiply_fusion.1), channel_id=1, source_target_pairs={{0,2},{1,3},{2,0},{3,1},{4,6},{5,7},{6,4},{7,5},{8,10},{9,11},{10,... | collective-permute-start | bytes 12296 | tf_op jit(solution)/shard_map/ppermute | solution.py:42
  56.9 2.6 %collective-permute-start.5 = (f32[32,32]{0,1:T(8,128)S(1)}, f32[32,32]{0,1:T(8,128)S(1)}, u32[]{:S(2)}, u32[]{:S(2)}) collective-permute-start(f32[32,32]{0,1:T(8,128)S(1)} %maximum_multiply_fusion.1), channel_id=1, source_target_pairs={{0,3},{1,0},{2,1},{3,2},{4,7},{5,4},{6,5},{7,6},{8,11},{9,8},{10,9... | collective-permute-start | bytes 12296 | tf_op jit(solution)/shard_map/ppermute | solution.py:42
  59.5 1.0 %collective-permute-start.3 = (f32[32,32]{0,1:T(8,128)S(1)}, f32[32,32]{0,1:T(8,128)S(1)}, u32[]{:S(2)}, u32[]{:S(2)}) collective-permute-start(f32[32,32]{0,1:T(8,128)S(1)} %maximum_multiply_fusion.1), channel_id=1, source_target_pairs={{0,1},{1,2},{2,3},{3,0},{4,5},{5,6},{6,7},{7,4},{8,9},{9,10},{10,1... | collective-permute-start | bytes 12296 | tf_op jit(solution)/shard_map/ppermute | solution.py:42
  60.5 0.0 collective-permute-done.4
  60.5 2.0 %collective-permute-done.5 = f32[32,32]{0,1:T(8,128)S(1)} collective-permute-done((f32[32,32]{0,1:T(8,128)S(1)}, f32[32,32]{0,1:T(8,128)S(1)}, u32[]{:S(2)}, u32[]{:S(2)}) %collective-permute-start.5) | collective-permute-done | bytes 4128 | tf_op jit(solution)/shard_map/ppermute | solution.py:42
  62.4 0.0 collective-permute-done.3
  62.4 0.8 %convolution_convert_fusion = bf16[32,1024]{1,0:T(8,128)(2,1)} fusion(bf16[1024,16]{0,1:T(8,128)(2,1)S(1)} %get-tuple-element.20, bf16[1024,16]{0,1:T(8,128)(2,1)S(1)} %get-tuple-element.19, f32[32,32]{0,1:T(8,128)S(1)} %collective-permute-done.5, f32[32,32]{0,1:T(8,128)S(1)} %collective-permute-done.4, f32[32,32]{0,1:T(8,128)S(1)} %collective-permute-done.3, ...), kind=kOutput, calls=%fused_computation.16 | convolution fusion | flops 2267136 | bytes 147456 | tf_op jit(solution)/shard_map/dot_general | solution.py:120
  (13 shorter events, 0.1 us)
Async XLA Ops:
  0.0 6.8 %copy-start = (s32[32,4096]{1,0:T(8,128)S(1)}, s32[32,4096]{1,0:T(8,128)}, u32[]{:S(2)}) copy-start(s32[32,4096]{1,0:T(8,128)} %param.6) | copy-start | bytes 1572868
  1.9 8.9 %collective-permute-start.2 = (f32[32,32]{0,1:T(8,128)S(1)}, f32[32,32]{0,1:T(8,128)S(1)}, u32[]{:S(2)}, u32[]{:S(2)}) collective-permute-start(f32[32,32]{0,1:T(8,128)S(1)} %convolution_bitcast_fusion), channel_id=1, source_target_pairs={{0,3},{1,0},{2,1},{3,2},{4,7},{5,4},{6,5},{7,6},{8,11},{9,8},{10,9... | collective-permute-start | bytes 12296 | tf_op jit(solution)/shard_map/ppermute | solution.py:42
  5.1 5.6 %collective-permute-start.1 = (f32[32,32]{0,1:T(8,128)S(1)}, f32[32,32]{0,1:T(8,128)S(1)}, u32[]{:S(2)}, u32[]{:S(2)}) collective-permute-start(f32[32,32]{0,1:T(8,128)S(1)} %convolution_bitcast_fusion), channel_id=1, source_target_pairs={{0,2},{1,3},{2,0},{3,1},{4,6},{5,7},{6,4},{7,5},{8,10},{9,11},{10,... | collective-permute-start | bytes 12296 | tf_op jit(solution)/shard_map/ppermute | solution.py:42
  5.1 5.6 %collective-permute-start = (f32[32,32]{0,1:T(8,128)S(1)}, f32[32,32]{0,1:T(8,128)S(1)}, u32[]{:S(2)}, u32[]{:S(2)}) collective-permute-start(f32[32,32]{0,1:T(8,128)S(1)} %convolution_bitcast_fusion), channel_id=1, source_target_pairs={{0,1},{1,2},{2,3},{3,0},{4,5},{5,6},{6,7},{7,4},{8,9},{9,10},{10,1... | collective-permute-start | bytes 12296 | tf_op jit(solution)/shard_map/ppermute | solution.py:42
  10.0 2.2 %copy-start.1 = (f32[16,32,1024]{2,1,0:T(8,128)}, f32[16,32,1024]{2,1,0:T(8,128)S(1)}, u32[]{:S(2)}) copy-start(f32[16,32,1024]{2,1,0:T(8,128)S(1)} %get-tuple-element.7) | copy-start | bytes 6291460
  56.1 4.4 %collective-permute-start.4 = (f32[32,32]{0,1:T(8,128)S(1)}, f32[32,32]{0,1:T(8,128)S(1)}, u32[]{:S(2)}, u32[]{:S(2)}) collective-permute-start(f32[32,32]{0,1:T(8,128)S(1)} %maximum_multiply_fusion.1), channel_id=1, source_target_pairs={{0,2},{1,3},{2,0},{3,1},{4,6},{5,7},{6,4},{7,5},{8,10},{9,11},{10,... | collective-permute-start | bytes 12296 | tf_op jit(solution)/shard_map/ppermute | solution.py:42
  56.9 5.5 %collective-permute-start.5 = (f32[32,32]{0,1:T(8,128)S(1)}, f32[32,32]{0,1:T(8,128)S(1)}, u32[]{:S(2)}, u32[]{:S(2)}) collective-permute-start(f32[32,32]{0,1:T(8,128)S(1)} %maximum_multiply_fusion.1), channel_id=1, source_target_pairs={{0,3},{1,0},{2,1},{3,2},{4,7},{5,4},{6,5},{7,6},{8,11},{9,8},{10,9... | collective-permute-start | bytes 12296 | tf_op jit(solution)/shard_map/ppermute | solution.py:42
  59.5 2.9 %collective-permute-start.3 = (f32[32,32]{0,1:T(8,128)S(1)}, f32[32,32]{0,1:T(8,128)S(1)}, u32[]{:S(2)}, u32[]{:S(2)}) collective-permute-start(f32[32,32]{0,1:T(8,128)S(1)} %maximum_multiply_fusion.1), channel_id=1, source_target_pairs={{0,1},{1,2},{2,3},{3,0},{4,5},{5,6},{6,7},{7,4},{8,9},{9,10},{10,1... | collective-permute-start | bytes 12296 | tf_op jit(solution)/shard_map/ppermute | solution.py:42

commit v21 on v19

--- a/solution.py
+++ b/solution.py
@@ -25,10 +25,12 @@
     shifted_index = phase_index + length // 8
     nearest = shifted_index >> quarter_bits
     rest = (shifted_index & (length // 4 - 1)) - length // 8
-    x = rest.astype(jnp.float32) * (two_pi / length)
-    x2 = x * x
-    sin_x = x * (1.0 + x2 * (-1.0 / 6.0 + x2 * (1.0 / 120.0 + x2 * (-1.0 / 5040.0))))
-    cos_x = 1.0 + x2 * (-0.5 + x2 * (1.0 / 24.0 + x2 * (-1.0 / 720.0 + x2 * (1.0 / 40320.0))))
+    step = two_pi / length
+    r = rest.astype(jnp.float32)
+    r2 = r * r
+    s2 = step * step
+    sin_x = r * (step + r2 * (-step * s2 / 6.0 + r2 * (step * s2 * s2 / 120.0 + r2 * (-step * s2 ** 3 / 5040.0))))
+    cos_x = 1.0 + r2 * (-s2 / 2.0 + r2 * (s2 ** 2 / 24.0 + r2 * (-s2 ** 3 / 720.0 + r2 * (s2 ** 4 / 40320.0))))
     swap = (nearest & 1) == 1
     sine = jnp.where(swap, cos_x, sin_x)
     cosine = jnp.where(swap, sin_x, cos_x)

time: 63.6 us -> 63.6 us (level)
  no operation moved by 1% of the time
where the time goes in v21:
time: 63.6 us; the launch traced here: 63.3 us
  blocking collectives  40.8 us (64%)
  starting transfers between devices  9.35 us (15%)
  other arithmetic  8.99 us (14%)
  waiting for transfers between devices  1.97 us (3%)
  matrix products  1.8 us (3%)
    all_to_all x1, blocking collectives, on_device(): moved = lax.all_to_all(parts, SENS_AXES, 0, 0, tiled=True)  25.3 us
    all_to_all x1, blocking collectives, on_device(): lax.all_to_all(copies, SENS_AXES, 0, 0, tiled=True).reshape(steered.shape)  15.4 us
    ppermute x6, starting transfers between devices, shifted(): lax.ppermute(x, axis, [(j, (j + shift) % count) for j in range(count)])  9.35 us
    select_n x1, other arithmetic, circle_point(): sine = jnp.where(nearest & 2 != 0, -sine, sine)  3.11 us
    reduce_sum x1, other arithmetic, on_device(): jnp.sum(bar_real[:, None, :] * cosine + bar_imag[:, None, :] * sine_part,...  2.38 us
    ppermute x6, waiting for transfers between devices, shifted(): lax.ppermute(x, axis, [(j, (j + shift) % count) for j in range(count)])  1.97 us
    reduce_sum x1, other arithmetic, on_device(): jnp.sum(real_t[:, :, None] * cosine - imag_t[:, :, None] * sine_part, axi...  1.42 us
  transfers between devices with their start and end apart: 6, of which 1 were waited for; matrix products, arithmetic and copies ran while one was open for 6% of the time, Pallas kernels for 0%

profile of v21, /device:TPU:1, one launch (start us, length us, event | category | flops | bytes accessed | tf_op | source)
XLA Modules:
  0.0 63.3 jit_solution(12467504203459764669)
XLA Ops:
  0.0 0.9 %fusion.3 = (bf16[1024,16]{0,1:T(8,128)(2,1)S(1)}, bf16[1024,16]{0,1:T(8,128)(2,1)S(1)}) fusion(s32[16]{0:T(128)} %param.5, s32[1024]{0:T(1024)S(1)} %iota_add_fusion), kind=kLoop, calls=%fused_computation.22 | loop fusion | flops 655360 | bytes 69696 | tf_op jit(solution)/shard_map/convert
  0.9 1.0 %convolution_bitcast_fusion = f32[32,32]{0,1:T(8,128)S(1)} fusion(bf16[32,1024]{1,0:T(8,128)(2,1)} %param.4, bf16[1024,16]{0,1:T(8,128)(2,1)S(1)} %get-tuple-element.24, bf16[1024,16]{0,1:T(8,128)(2,1)S(1)} %get-tuple-element.23), kind=kOutput, calls=%fused_computation.17 | convolution fusion | flops 2228224 | bytes 135168 | tf_op jit(solution)/shard_map/dot_general | solution.py:88
  1.8 3.2 %collective-permute-start.2 = (f32[32,32]{0,1:T(8,128)S(1)}, f32[32,32]{0,1:T(8,128)S(1)}, u32[]{:S(2)}, u32[]{:S(2)}) collective-permute-start(f32[32,32]{0,1:T(8,128)S(1)} %convolution_bitcast_fusion), channel_id=1, source_target_pairs={{0,3},{1,0},{2,1},{3,2},{4,7},{5,4},{6,5},{7,6},{8,11},{9,8},{10,9... | collective-permute-start | bytes 12296 | tf_op jit(solution)/shard_map/ppermute | solution.py:44
  5.1 0.0 collective-permute-start.1
  5.1 1.7 %collective-permute-start = (f32[32,32]{0,1:T(8,128)S(1)}, f32[32,32]{0,1:T(8,128)S(1)}, u32[]{:S(2)}, u32[]{:S(2)}) collective-permute-start(f32[32,32]{0,1:T(8,128)S(1)} %convolution_bitcast_fusion), channel_id=1, source_target_pairs={{0,1},{1,2},{2,3},{3,0},{4,5},{5,6},{6,7},{7,4},{8,9},{9,10},{10,1... | collective-permute-start | bytes 12296 | tf_op jit(solution)/shard_map/ppermute | solution.py:44
  6.8 3.1 %negate_select_fusion = (f32[16,32,1024]{2,1,0:T(8,128)S(1)}, f32[16,32,1024]{2,1,0:T(8,128)S(1)}) fusion(s32[32,1024]{1,0:T(8,128)S(1)} %constant_dynamic-slice_fusion, s32[16]{0:T(128)} %param.5), kind=kLoop, calls=%fused_computation | loop fusion | flops 18350080 | bytes 4325440 | tf_op jit(solution)/shard_map/jit(_where)/select_n | solution.py:37
  9.9 0.7 %dynamic-slice_multiply_fusion = f32[1024]{0:T(1024)S(1)} fusion(f32[4096]{0:T(1024)} %param.7, s32[]{:T(128)S(6)} %select_n.34), kind=kLoop, calls=%fused_computation.45 | loop fusion | flops 1024 | bytes 8196 | tf_op jit(solution)/shard_map/mul | solution.py:106
  10.7 0.0 collective-permute-done.2
  10.7 0.0 collective-permute-done.1
  10.7 0.0 collective-permute-done
  10.7 1.4 %subtract_reduce_fusion.1 = (f32[16,1024]{1,0:T(8,128)S(1)}, f32[16,1024]{1,0:T(8,128)S(1)}) fusion(f32[16,32,1024]{2,1,0:T(8,128)S(1)} %get-tuple-element.10, f32[16,32,1024]{2,1,0:T(8,128)S(1)} %get-tuple-element.9, f32[16,32]{1,0:T(8,128)S(1)} %get-tuple-element.22, f32[16,32]{1,0:T(8,128)S(1)} %get-tuple-element.21), kind=kLoop, calls=%fused_computation.5 | loop fusion | flops 4161536 | bytes 4329472 | tf_op jit(solution)/shard_map/reduce_sum | solution.py:97
  12.2 0.1 all_to_all.10
  12.3 25.3 %all_to_all.15 = f32[64,1,512]{2,1,0:T(1,128)S(1)} all-to-all(f32[64,1,512]{2,1,0:T(1,128)S(1)} %all_to_all.10), channel_id=1, replica_groups=mesh['sx'=4,'sz'=4,'sy'=4,'grp'=4] {'sx','sz','sy'}, dimensions={0} | all-to-all | bytes 262144 | tf_op jit(solution)/shard_map/all_to_all | solution.py:110
  37.6 0.1 reduce_sum.47
  37.7 0.1 broadcast_in_dim.2
  37.8 15.4 %all_to_all.16 = f32[64,1,512]{2,1,0:T(1,128)S(1)} all-to-all(f32[64,1,512]{2,1,0:T(1,128)S(1)} %broadcast_in_dim.2), channel_id=1, replica_groups=mesh['sx'=4,'sz'=4,'sy'=4,'grp'=4] {'sx','sz','sy'}, dimensions={0} | all-to-all | bytes 262144 | tf_op jit(solution)/shard_map/all_to_all | solution.py:113
  53.3 0.3 reduce.1
  53.7 2.4 %add_reduce_fusion = (f32[16,32]{1,0:T(8,128)S(1)}, f32[16,32]{1,0:T(8,128)S(1)}) fusion(f32[16,32,1024]{2,1,0:T(8,128)S(1)} %get-tuple-element.10, f32[16,32,1024]{2,1,0:T(8,128)} %copy-done.1, f32[16,1024]{1,0:T(8,128)S(1)} %get-tuple-element.20, f32[16,1024]{1,0:T(8,128)S(1)} %get-tuple-element.19), kind=kLoop, calls=%fused_computation.3 | loop fusion | flops 4193280 | bytes 4329472 | tf_op jit(solution)/shard_map/reduce_sum | solution.py:118
  56.1 0.9 %collective-permute-start.4 = (f32[32,32]{0,1:T(8,128)S(1)}, f32[32,32]{0,1:T(8,128)S(1)}, u32[]{:S(2)}, u32[]{:S(2)}) collective-permute-start(f32[32,32]{0,1:T(8,128)S(1)} %maximum_multiply_fusion), channel_id=1, source_target_pairs={{0,2},{1,3},{2,0},{3,1},{4,6},{5,7},{6,4},{7,5},{8,10},{9,11},{10,... | collective-permute-start | bytes 12296 | tf_op jit(solution)/shard_map/ppermute | solution.py:44
  56.9 2.6 %collective-permute-start.5 = (f32[32,32]{0,1:T(8,128)S(1)}, f32[32,32]{0,1:T(8,128)S(1)}, u32[]{:S(2)}, u32[]{:S(2)}) collective-permute-start(f32[32,32]{0,1:T(8,128)S(1)} %maximum_multiply_fusion), channel_id=1, source_target_pairs={{0,3},{1,0},{2,1},{3,2},{4,7},{5,4},{6,5},{7,6},{8,11},{9,8},{10,9... | collective-permute-start | bytes 12296 | tf_op jit(solution)/shard_map/ppermute | solution.py:44
  59.5 1.0 %collective-permute-start.3 = (f32[32,32]{0,1:T(8,128)S(1)}, f32[32,32]{0,1:T(8,128)S(1)}, u32[]{:S(2)}, u32[]{:S(2)}) collective-permute-start(f32[32,32]{0,1:T(8,128)S(1)} %maximum_multiply_fusion), channel_id=1, source_target_pairs={{0,1},{1,2},{2,3},{3,0},{4,5},{5,6},{6,7},{7,4},{8,9},{9,10},{10,1... | collective-permute-start | bytes 12296 | tf_op jit(solution)/shard_map/ppermute | solution.py:44
  60.5 0.0 collective-permute-done.4
  60.5 2.0 %collective-permute-done.5 = f32[32,32]{0,1:T(8,128)S(1)} collective-permute-done((f32[32,32]{0,1:T(8,128)S(1)}, f32[32,32]{0,1:T(8,128)S(1)}, u32[]{:S(2)}, u32[]{:S(2)}) %collective-permute-start.5) | collective-permute-done | bytes 4128 | tf_op jit(solution)/shard_map/ppermute | solution.py:44
  62.4 0.8 %convolution_convert_fusion = bf16[32,1024]{1,0:T(8,128)(2,1)} fusion(bf16[1024,16]{0,1:T(8,128)(2,1)S(1)} %get-tuple-element.24, bf16[1024,16]{0,1:T(8,128)(2,1)S(1)} %get-tuple-element.23, f32[32,32]{0,1:T(8,128)S(1)} %collective-permute-done.5, f32[32,32]{0,1:T(8,128)S(1)} %collective-permute-done.4, f32[32,32]{0,1:T(8,128)S(1)} %collective-permute-done.3, ...), kind=kOutput, calls=%fused_computation.16 | convolution fusion | flops 2267136 | bytes 147456 | tf_op jit(solution)/shard_map/dot_general | solution.py:123
  (15 shorter events, 0.1 us)
Async XLA Ops:
  0.0 6.8 %copy-start = (s32[32,4096]{1,0:T(8,128)S(1)}, s32[32,4096]{1,0:T(8,128)}, u32[]{:S(2)}) copy-start(s32[32,4096]{1,0:T(8,128)} %param.6) | copy-start | bytes 1572868
  1.8 8.8 %collective-permute-start.2 = (f32[32,32]{0,1:T(8,128)S(1)}, f32[32,32]{0,1:T(8,128)S(1)}, u32[]{:S(2)}, u32[]{:S(2)}) collective-permute-start(f32[32,32]{0,1:T(8,128)S(1)} %convolution_bitcast_fusion), channel_id=1, source_target_pairs={{0,3},{1,0},{2,1},{3,2},{4,7},{5,4},{6,5},{7,6},{8,11},{9,8},{10,9... | collective-permute-start | bytes 12296 | tf_op jit(solution)/shard_map/ppermute | solution.py:44
  5.1 5.6 %collective-permute-start.1 = (f32[32,32]{0,1:T(8,128)S(1)}, f32[32,32]{0,1:T(8,128)S(1)}, u32[]{:S(2)}, u32[]{:S(2)}) collective-permute-start(f32[32,32]{0,1:T(8,128)S(1)} %convolution_bitcast_fusion), channel_id=1, source_target_pairs={{0,2},{1,3},{2,0},{3,1},{4,6},{5,7},{6,4},{7,5},{8,10},{9,11},{10,... | collective-permute-start | bytes 12296 | tf_op jit(solution)/shard_map/ppermute | solution.py:44
  5.1 5.6 %collective-permute-start = (f32[32,32]{0,1:T(8,128)S(1)}, f32[32,32]{0,1:T(8,128)S(1)}, u32[]{:S(2)}, u32[]{:S(2)}) collective-permute-start(f32[32,32]{0,1:T(8,128)S(1)} %convolution_bitcast_fusion), channel_id=1, source_target_pairs={{0,1},{1,2},{2,3},{3,0},{4,5},{5,6},{6,7},{7,4},{8,9},{9,10},{10,1... | collective-permute-start | bytes 12296 | tf_op jit(solution)/shard_map/ppermute | solution.py:44
  9.9 2.2 %copy-start.1 = (f32[16,32,1024]{2,1,0:T(8,128)}, f32[16,32,1024]{2,1,0:T(8,128)S(1)}, u32[]{:S(2)}) copy-start(f32[16,32,1024]{2,1,0:T(8,128)S(1)} %get-tuple-element.9) | copy-start | bytes 6291460
  56.1 4.4 %collective-permute-start.4 = (f32[32,32]{0,1:T(8,128)S(1)}, f32[32,32]{0,1:T(8,128)S(1)}, u32[]{:S(2)}, u32[]{:S(2)}) collective-permute-start(f32[32,32]{0,1:T(8,128)S(1)} %maximum_multiply_fusion), channel_id=1, source_target_pairs={{0,2},{1,3},{2,0},{3,1},{4,6},{5,7},{6,4},{7,5},{8,10},{9,11},{10,... | collective-permute-start | bytes 12296 | tf_op jit(solution)/shard_map/ppermute | solution.py:44
  56.9 5.5 %collective-permute-start.5 = (f32[32,32]{0,1:T(8,128)S(1)}, f32[32,32]{0,1:T(8,128)S(1)}, u32[]{:S(2)}, u32[]{:S(2)}) collective-permute-start(f32[32,32]{0,1:T(8,128)S(1)} %maximum_multiply_fusion), channel_id=1, source_target_pairs={{0,3},{1,0},{2,1},{3,2},{4,7},{5,4},{6,5},{7,6},{8,11},{9,8},{10,9... | collective-permute-start | bytes 12296 | tf_op jit(solution)/shard_map/ppermute | solution.py:44
  59.5 2.9 %collective-permute-start.3 = (f32[32,32]{0,1:T(8,128)S(1)}, f32[32,32]{0,1:T(8,128)S(1)}, u32[]{:S(2)}, u32[]{:S(2)}) collective-permute-start(f32[32,32]{0,1:T(8,128)S(1)} %maximum_multiply_fusion), channel_id=1, source_target_pairs={{0,1},{1,2},{2,3},{3,0},{4,5},{5,6},{6,7},{7,4},{8,9},{9,10},{10,1... | collective-permute-start | bytes 12296 | tf_op jit(solution)/shard_map/ppermute | solution.py:44

commit v22 on v19

--- a/solution.py
+++ b/solution.py
@@ -43,8 +43,10 @@
 
 
 def ring_sum(x, axis):
+    count = lax.axis_size(axis)
+    order = sorted(range(1, count), key=lambda shift: (shift != count // 2, shift))
     total = x
-    for shift in range(1, lax.axis_size(axis)):
+    for shift in order:
         total = total + shifted(x, axis, shift)
     return total
 

time: 63.6 us -> 63.2 us (level)
  starting transfers between devices: 9.35 us -> 8.28 us
    ppermute x6, starting transfers between devices: 9.35 us -> 8.28 us  [shifted(): lax.ppermute(x, axis, [(j, (j + shift) % count) for j in range(count)])]
    all_to_all x1, blocking collectives: 15.4 us -> 16.2 us  [on_device(): lax.all_to_all(copies, SENS_AXES, 0, 0, tiled=True).reshape(steered.shape)]
  transfers between devices with their start and end apart: 6 -> 6, of which waited for: 1 -> 2; matrix products, arithmetic and copies ran while one was open for 6% -> 6% of each run, Pallas kernels for 0% -> 0%
where the time goes in v22:
time: 63.2 us; the launch traced here: 62.9 us
  blocking collectives  40.9 us (65%)
  other arithmetic  9.04 us (14%)
  starting transfers between devices  8.28 us (13%)
  waiting for transfers between devices  2.54 us (4%)
  matrix products  1.8 us (3%)
    all_to_all x1, blocking collectives, on_device(): moved = lax.all_to_all(parts, SENS_AXES, 0, 0, tiled=True)  24.7 us
    all_to_all x1, blocking collectives, on_device(): lax.all_to_all(copies, SENS_AXES, 0, 0, tiled=True).reshape(steered.shape)  16.2 us
    ppermute x6, starting transfers between devices, shifted(): lax.ppermute(x, axis, [(j, (j + shift) % count) for j in range(count)])  8.28 us
    select_n x1, other arithmetic, circle_point(): sine = jnp.where(nearest & 2 != 0, -sine, sine)  3.16 us
    ppermute x6, waiting for transfers between devices, shifted(): lax.ppermute(x, axis, [(j, (j + shift) % count) for j in range(count)])  2.54 us
    reduce_sum x1, other arithmetic, on_device(): jnp.sum(bar_real[:, None, :] * cosine + bar_imag[:, None, :] * sine_part,...  2.38 us
    reduce_sum x1, other arithmetic, on_device(): jnp.sum(real_t[:, :, None] * cosine - imag_t[:, :, None] * sine_part, axi...  1.42 us
  transfers between devices with their start and end apart: 6, of which 2 were waited for; matrix products, arithmetic and copies ran while one was open for 6% of the time, Pallas kernels for 0%

profile of v22, /device:TPU:1, one launch (start us, length us, event | category | flops | bytes accessed | tf_op | source)
XLA Modules:
  0.0 62.9 jit_solution(17026080554965964775)
XLA Ops:
  0.0 0.9 %fusion.3 = (bf16[1024,16]{0,1:T(8,128)(2,1)S(1)}, bf16[1024,16]{0,1:T(8,128)(2,1)S(1)}) fusion(s32[16]{0:T(128)} %param.5, s32[1024]{0:T(1024)S(1)} %iota_add_fusion), kind=kLoop, calls=%fused_computation.22 | loop fusion | flops 671744 | bytes 69696 | tf_op jit(solution)/shard_map/convert
  0.9 1.0 %convolution_bitcast_fusion = f32[32,32]{0,1:T(8,128)S(1)} fusion(bf16[32,1024]{1,0:T(8,128)(2,1)} %param.4, bf16[1024,16]{0,1:T(8,128)(2,1)S(1)} %get-tuple-element.24, bf16[1024,16]{0,1:T(8,128)(2,1)S(1)} %get-tuple-element.23), kind=kOutput, calls=%fused_computation.17 | convolution fusion | flops 2228224 | bytes 135168 | tf_op jit(solution)/shard_map/dot_general | solution.py:88
  1.9 3.2 %collective-permute-start.2 = (f32[32,32]{0,1:T(8,128)S(1)}, f32[32,32]{0,1:T(8,128)S(1)}, u32[]{:S(2)}, u32[]{:S(2)}) collective-permute-start(f32[32,32]{0,1:T(8,128)S(1)} %convolution_bitcast_fusion), channel_id=1, source_target_pairs={{0,3},{1,0},{2,1},{3,2},{4,7},{5,4},{6,5},{7,6},{8,11},{9,8},{10,9... | collective-permute-start | bytes 12296 | tf_op jit(solution)/shard_map/ppermute | solution.py:42
  5.1 1.4 %collective-permute-start = (f32[32,32]{0,1:T(8,128)S(1)}, f32[32,32]{0,1:T(8,128)S(1)}, u32[]{:S(2)}, u32[]{:S(2)}) collective-permute-start(f32[32,32]{0,1:T(8,128)S(1)} %convolution_bitcast_fusion), channel_id=1, source_target_pairs={{0,2},{1,3},{2,0},{3,1},{4,6},{5,7},{6,4},{7,5},{8,10},{9,11},{10,... | collective-permute-start | bytes 12296 | tf_op jit(solution)/shard_map/ppermute | solution.py:42
  6.5 3.2 %negate_select_fusion = (f32[16,32,1024]{2,1,0:T(8,128)S(1)}, f32[16,32,1024]{2,1,0:T(8,128)S(1)}) fusion(s32[32,1024]{1,0:T(8,128)S(1)} %constant_dynamic-slice_fusion, s32[16]{0:T(128)} %param.5), kind=kLoop, calls=%fused_computation | loop fusion | flops 18874368 | bytes 4325440 | tf_op jit(solution)/shard_map/jit(_where)/select_n | solution.py:35
  9.7 0.7 %dynamic-slice_multiply_fusion = f32[1024]{0:T(1024)S(1)} fusion(f32[4096]{0:T(1024)} %param.7, s32[]{:T(128)S(6)} %select_n.34), kind=kLoop, calls=%fused_computation.45 | loop fusion | flops 1024 | bytes 8196 | tf_op jit(solution)/shard_map/mul | solution.py:106
  10.4 0.0 collective-permute-done.2
  10.4 0.0 collective-permute-done.1
  10.4 0.0 collective-permute-done
  10.5 1.4 %subtract_reduce_fusion.1 = (f32[16,1024]{1,0:T(8,128)S(1)}, f32[16,1024]{1,0:T(8,128)S(1)}) fusion(f32[16,32,1024]{2,1,0:T(8,128)S(1)} %get-tuple-element.10, f32[16,32,1024]{2,1,0:T(8,128)S(1)} %get-tuple-element.9, f32[16,32]{1,0:T(8,128)S(1)} %get-tuple-element.22, f32[16,32]{1,0:T(8,128)S(1)} %get-tuple-element.21), kind=kLoop, calls=%fused_computation.5 | loop fusion | flops 4161536 | bytes 4329472 | tf_op jit(solution)/shard_map/reduce_sum | solution.py:97
  12.0 0.1 all_to_all.10
  12.1 24.7 %all_to_all.15 = f32[64,1,512]{2,1,0:T(1,128)S(1)} all-to-all(f32[64,1,512]{2,1,0:T(1,128)S(1)} %all_to_all.10), channel_id=1, replica_groups=mesh['sx'=4,'sz'=4,'sy'=4,'grp'=4] {'sx','sz','sy'}, dimensions={0} | all-to-all | bytes 262144 | tf_op jit(solution)/shard_map/all_to_all | solution.py:110
  36.8 0.1 reduce_sum.47
  36.9 0.1 broadcast_in_dim.2
  37.0 16.2 %all_to_all.16 = f32[64,1,512]{2,1,0:T(1,128)S(1)} all-to-all(f32[64,1,512]{2,1,0:T(1,128)S(1)} %broadcast_in_dim.2), channel_id=1, replica_groups=mesh['sx'=4,'sz'=4,'sy'=4,'grp'=4] {'sx','sz','sy'}, dimensions={0} | all-to-all | bytes 262144 | tf_op jit(solution)/shard_map/all_to_all | solution.py:113
  53.1 0.3 reduce.1
  53.5 2.4 %add_reduce_fusion = (f32[16,32]{1,0:T(8,128)S(1)}, f32[16,32]{1,0:T(8,128)S(1)}) fusion(f32[16,32,1024]{2,1,0:T(8,128)S(1)} %get-tuple-element.10, f32[16,32,1024]{2,1,0:T(8,128)} %copy-done.1, f32[16,1024]{1,0:T(8,128)S(1)} %get-tuple-element.20, f32[16,1024]{1,0:T(8,128)S(1)} %get-tuple-element.19), kind=kLoop, calls=%fused_computation.3 | loop fusion | flops 4193280 | bytes 4329472 | tf_op jit(solution)/shard_map/reduce_sum | solution.py:118
  55.9 3.0 %collective-permute-start.4 = (f32[32,32]{0,1:T(8,128)S(1)}, f32[32,32]{0,1:T(8,128)S(1)}, u32[]{:S(2)}, u32[]{:S(2)}) collective-permute-start(f32[32,32]{0,1:T(8,128)S(1)} %maximum_multiply_fusion), channel_id=1, source_target_pairs={{0,1},{1,2},{2,3},{3,0},{4,5},{5,6},{6,7},{7,4},{8,9},{9,10},{10,1... | collective-permute-start | bytes 12296 | tf_op jit(solution)/shard_map/ppermute | solution.py:42
  58.9 0.0 collective-permute-start.5
  58.9 0.6 collective-permute-start.3
  59.6 0.2 collective-permute-done.4
  59.8 2.3 %collective-permute-done.5 = f32[32,32]{0,1:T(8,128)S(1)} collective-permute-done((f32[32,32]{0,1:T(8,128)S(1)}, f32[32,32]{0,1:T(8,128)S(1)}, u32[]{:S(2)}, u32[]{:S(2)}) %collective-permute-start.5) | collective-permute-done | bytes 4128 | tf_op jit(solution)/shard_map/ppermute | solution.py:42
  62.1 0.0 collective-permute-done.3
  62.1 0.8 %convolution_convert_fusion = bf16[32,1024]{1,0:T(8,128)(2,1)} fusion(bf16[1024,16]{0,1:T(8,128)(2,1)S(1)} %get-tuple-element.24, bf16[1024,16]{0,1:T(8,128)(2,1)S(1)} %get-tuple-element.23, f32[32,32]{0,1:T(8,128)S(1)} %collective-permute-done.5, f32[32,32]{0,1:T(8,128)S(1)} %collective-permute-done.4, f32[32,32]{0,1:T(8,128)S(1)} %collective-permute-done.3, ...), kind=kOutput, calls=%fused_computation.16 | convolution fusion | flops 2267136 | bytes 147456 | tf_op jit(solution)/shard_map/dot_general | solution.py:123
  (15 shorter events, 0.1 us)
Async XLA Ops:
  0.0 6.5 %copy-start = (s32[32,4096]{1,0:T(8,128)S(1)}, s32[32,4096]{1,0:T(8,128)}, u32[]{:S(2)}) copy-start(s32[32,4096]{1,0:T(8,128)} %param.6) | copy-start | bytes 1572868
  1.9 8.6 %collective-permute-start.2 = (f32[32,32]{0,1:T(8,128)S(1)}, f32[32,32]{0,1:T(8,128)S(1)}, u32[]{:S(2)}, u32[]{:S(2)}) collective-permute-start(f32[32,32]{0,1:T(8,128)S(1)} %convolution_bitcast_fusion), channel_id=1, source_target_pairs={{0,3},{1,0},{2,1},{3,2},{4,7},{5,4},{6,5},{7,6},{8,11},{9,8},{10,9... | collective-permute-start | bytes 12296 | tf_op jit(solution)/shard_map/ppermute | solution.py:42
  5.1 5.4 %collective-permute-start.1 = (f32[32,32]{0,1:T(8,128)S(1)}, f32[32,32]{0,1:T(8,128)S(1)}, u32[]{:S(2)}, u32[]{:S(2)}) collective-permute-start(f32[32,32]{0,1:T(8,128)S(1)} %convolution_bitcast_fusion), channel_id=1, source_target_pairs={{0,1},{1,2},{2,3},{3,0},{4,5},{5,6},{6,7},{7,4},{8,9},{9,10},{10,1... | collective-permute-start | bytes 12296 | tf_op jit(solution)/shard_map/ppermute | solution.py:42
  5.1 5.4 %collective-permute-start = (f32[32,32]{0,1:T(8,128)S(1)}, f32[32,32]{0,1:T(8,128)S(1)}, u32[]{:S(2)}, u32[]{:S(2)}) collective-permute-start(f32[32,32]{0,1:T(8,128)S(1)} %convolution_bitcast_fusion), channel_id=1, source_target_pairs={{0,2},{1,3},{2,0},{3,1},{4,6},{5,7},{6,4},{7,5},{8,10},{9,11},{10,... | collective-permute-start | bytes 12296 | tf_op jit(solution)/shard_map/ppermute | solution.py:42
  9.7 2.2 %copy-start.1 = (f32[16,32,1024]{2,1,0:T(8,128)}, f32[16,32,1024]{2,1,0:T(8,128)S(1)}, u32[]{:S(2)}) copy-start(f32[16,32,1024]{2,1,0:T(8,128)S(1)} %get-tuple-element.9) | copy-start | bytes 6291460
  55.9 3.9 %collective-permute-start.4 = (f32[32,32]{0,1:T(8,128)S(1)}, f32[32,32]{0,1:T(8,128)S(1)}, u32[]{:S(2)}, u32[]{:S(2)}) collective-permute-start(f32[32,32]{0,1:T(8,128)S(1)} %maximum_multiply_fusion), channel_id=1, source_target_pairs={{0,1},{1,2},{2,3},{3,0},{4,5},{5,6},{6,7},{7,4},{8,9},{9,10},{10,1... | collective-permute-start | bytes 12296 | tf_op jit(solution)/shard_map/ppermute | solution.py:42
  58.9 3.2 %collective-permute-start.5 = (f32[32,32]{0,1:T(8,128)S(1)}, f32[32,32]{0,1:T(8,128)S(1)}, u32[]{:S(2)}, u32[]{:S(2)}) collective-permute-start(f32[32,32]{0,1:T(8,128)S(1)} %maximum_multiply_fusion), channel_id=1, source_target_pairs={{0,3},{1,0},{2,1},{3,2},{4,7},{5,4},{6,5},{7,6},{8,11},{9,8},{10,9... | collective-permute-start | bytes 12296 | tf_op jit(solution)/shard_map/ppermute | solution.py:42
  58.9 3.2 %collective-permute-start.3 = (f32[32,32]{0,1:T(8,128)S(1)}, f32[32,32]{0,1:T(8,128)S(1)}, u32[]{:S(2)}, u32[]{:S(2)}) collective-permute-start(f32[32,32]{0,1:T(8,128)S(1)} %maximum_multiply_fusion), channel_id=1, source_target_pairs={{0,2},{1,3},{2,0},{3,1},{4,6},{5,7},{6,4},{7,5},{8,10},{9,11},{10,... | collective-permute-start | bytes 12296 | tf_op jit(solution)/shard_map/ppermute | solution.py:42

commit v23 on v19

--- a/solution.py
+++ b/solution.py
@@ -113,8 +113,17 @@
     bar_real = bar[0]
     bar_imag = bar[1]
 
-    back_real = jnp.sum(bar_real[:, None, :] * cosine + bar_imag[:, None, :] * sine_part, axis=2)
-    back_imag = jnp.sum(bar_imag[:, None, :] * cosine - bar_real[:, None, :] * sine_part, axis=2)
+    lanes = 128
+    grouped = cosine.shape[:2] + (cosine.shape[2] // lanes, lanes)
+    first_real = jnp.sum(
+        (bar_real[:, None, :] * cosine + bar_imag[:, None, :] * sine_part).reshape(grouped), axis=2
+    )
+    first_imag = jnp.sum(
+        (bar_imag[:, None, :] * cosine - bar_real[:, None, :] * sine_part).reshape(grouped), axis=2
+    )
+    first_real, first_imag = lax.optimization_barrier((first_real, first_imag))
+    back_real = jnp.sum(first_real, axis=2)
+    back_imag = jnp.sum(first_imag, axis=2)
     back = jnp.concatenate([back_real.T, back_imag.T], 1) * steer_scale
     back = ring_sum(back, "grp")
     adjoint = back.astype(jnp.bfloat16)

time: 63.6 us -> 65.7 us (1.033)
  other arithmetic: 9.04 us -> 10.2 us
  local copies, waits for them, and re-layouts: 0.26 us -> 1.2 us
    sub x0 -> x1, other arithmetic: none -> 2.22 us  [on_device(): bar_imag[:, None, :] * cosine - bar_real[:, None, :] * sine_part]
    reduce_sum x1 -> x3, other arithmetic: 2.38 us -> 1.32 us  [the longest x1 1.05 us: on_device(): jnp.sum((bar_imag[:, None, :] * cosine - bar_real[:, None, :] * sine_part...]
    unnamed x4 -> x6, local copies, waits for them, and re-layouts: 0.01 us -> 0.95 us
where the time goes in v23:
time: 65.7 us; the launch traced here: 65.5 us
  blocking collectives  40.8 us (62%)
  other arithmetic  10.2 us (16%)
  starting transfers between devices  9.35 us (14%)
  waiting for transfers between devices  1.97 us (3%)
  matrix products  1.8 us (3%)
  local copies, waits for them, and re-layouts  1.2 us (2%)
    all_to_all x1, blocking collectives, on_device(): moved = lax.all_to_all(parts, SENS_AXES, 0, 0, tiled=True)  25.3 us
    all_to_all x1, blocking collectives, on_device(): lax.all_to_all(copies, SENS_AXES, 0, 0, tiled=True).reshape(steered.shape)  15.4 us
    ppermute x6, starting transfers between devices, shifted(): lax.ppermute(x, axis, [(j, (j + shift) % count) for j in range(count)])  9.35 us
    select_n x1, other arithmetic, circle_point(): sine = jnp.where(nearest & 2 != 0, -sine, sine)  3.16 us
    sub x1, other arithmetic, on_device(): bar_imag[:, None, :] * cosine - bar_real[:, None, :] * sine_part  2.22 us
    ppermute x6, waiting for transfers between devices, shifted(): lax.ppermute(x, axis, [(j, (j + shift) % count) for j in range(count)])  1.97 us
    reduce_sum x1, other arithmetic, on_device(): jnp.sum(real_t[:, :, None] * cosine - imag_t[:, :, None] * sine_part, axi...  1.42 us
  transfers between devices with their start and end apart: 6, of which 1 were waited for; matrix products, arithmetic and copies ran while one was open for 6% of the time, Pallas kernels for 0%

profile of v23, /device:TPU:1, one launch (start us, length us, event | category | flops | bytes accessed | tf_op | source)
XLA Modules:
  0.0 65.5 jit_solution(8441430426679131001)
XLA Ops:
  0.0 0.9 %fusion.3 = (bf16[1024,16]{0,1:T(8,128)(2,1)S(1)}, bf16[1024,16]{0,1:T(8,128)(2,1)S(1)}) fusion(s32[16]{0:T(128)} %param.5, s32[1024]{0:T(1024)S(1)} %iota_add_fusion), kind=kLoop, calls=%fused_computation.24 | loop fusion | flops 671744 | bytes 69696 | tf_op jit(solution)/shard_map/convert
  0.9 1.0 %convolution_bitcast_fusion = f32[32,32]{0,1:T(8,128)S(1)} fusion(bf16[32,1024]{1,0:T(8,128)(2,1)} %param.4, bf16[1024,16]{0,1:T(8,128)(2,1)S(1)} %get-tuple-element.28, bf16[1024,16]{0,1:T(8,128)(2,1)S(1)} %get-tuple-element.27), kind=kOutput, calls=%fused_computation.19 | convolution fusion | flops 2228224 | bytes 135168 | tf_op jit(solution)/shard_map/dot_general | solution.py:86
  1.9 3.2 %collective-permute-start.2 = (f32[32,32]{0,1:T(8,128)S(1)}, f32[32,32]{0,1:T(8,128)S(1)}, u32[]{:S(2)}, u32[]{:S(2)}) collective-permute-start(f32[32,32]{0,1:T(8,128)S(1)} %convolution_bitcast_fusion), channel_id=1, source_target_pairs={{0,3},{1,0},{2,1},{3,2},{4,7},{5,4},{6,5},{7,6},{8,11},{9,8},{10,9... | collective-permute-start | bytes 12296 | tf_op jit(solution)/shard_map/ppermute | solution.py:42
  5.1 1.7 %collective-permute-start = (f32[32,32]{0,1:T(8,128)S(1)}, f32[32,32]{0,1:T(8,128)S(1)}, u32[]{:S(2)}, u32[]{:S(2)}) collective-permute-start(f32[32,32]{0,1:T(8,128)S(1)} %convolution_bitcast_fusion), channel_id=1, source_target_pairs={{0,1},{1,2},{2,3},{3,0},{4,5},{5,6},{6,7},{7,4},{8,9},{9,10},{10,1... | collective-permute-start | bytes 12296 | tf_op jit(solution)/shard_map/ppermute | solution.py:42
  6.8 3.2 %negate_select_fusion = (f32[16,32,1024]{2,1,0:T(8,128)S(1)}, f32[16,32,1024]{2,1,0:T(8,128)S(1)}) fusion(s32[32,1024]{1,0:T(8,128)S(1)} %constant_dynamic-slice_fusion, s32[16]{0:T(128)} %param.5), kind=kLoop, calls=%fused_computation | loop fusion | flops 18874368 | bytes 4325440 | tf_op jit(solution)/shard_map/jit(_where)/select_n | solution.py:35
  10.0 0.7 %dynamic-slice_multiply_fusion = f32[1024]{0:T(1024)S(1)} fusion(f32[4096]{0:T(1024)} %param.7, s32[]{:T(128)S(6)} %select_n.34), kind=kLoop, calls=%fused_computation.47 | loop fusion | flops 1024 | bytes 8196 | tf_op jit(solution)/shard_map/mul | solution.py:104
  10.8 1.4 %subtract_reduce_fusion = (f32[16,1024]{1,0:T(8,128)S(1)}, f32[16,1024]{1,0:T(8,128)S(1)}) fusion(f32[16,32,1024]{2,1,0:T(8,128)S(1)} %get-tuple-element.12, f32[16,32,1024]{2,1,0:T(8,128)S(1)} %get-tuple-element.11, f32[16,32]{1,0:T(8,128)S(1)} %get-tuple-element.26, f32[16,32]{1,0:T(8,128)S(1)} %get-tuple-element.25), kind=kLoop, calls=%fused_computation.7 | loop fusion | flops 4161536 | bytes 4329472 | tf_op jit(solution)/shard_map/reduce_sum | solution.py:95
  12.2 0.1 all_to_all.10
  12.3 25.3 %all_to_all.15 = f32[64,1,512]{2,1,0:T(1,128)S(1)} all-to-all(f32[64,1,512]{2,1,0:T(1,128)S(1)} %all_to_all.10), channel_id=1, replica_groups=mesh['sx'=4,'sz'=4,'sy'=4,'grp'=4] {'sx','sz','sy'}, dimensions={0} | all-to-all | bytes 262144 | tf_op jit(solution)/shard_map/all_to_all | solution.py:108
  37.7 0.1 reduce_sum.65
  37.8 0.1 broadcast_in_dim.2
  37.9 15.4 %all_to_all.16 = f32[64,1,512]{2,1,0:T(1,128)S(1)} all-to-all(f32[64,1,512]{2,1,0:T(1,128)S(1)} %broadcast_in_dim.2), channel_id=1, replica_groups=mesh['sx'=4,'sz'=4,'sy'=4,'grp'=4] {'sx','sz','sy'}, dimensions={0} | all-to-all | bytes 262144 | tf_op jit(solution)/shard_map/all_to_all | solution.py:111
  53.3 0.3 reduce.1
  53.7 2.2 %multiply_subtract_fusion = (f32[16,32,1024]{2,1,0:T(8,128)S(1)}, f32[16,32,1024]{2,1,0:T(8,128)S(1)}) fusion(f32[16,32,1024]{2,1,0:T(8,128)S(1)} %get-tuple-element.12, f32[16,32,1024]{2,1,0:T(8,128)} %copy-done.1, f32[16,1024]{1,0:T(8,128)S(1)} %get-tuple-element.24, f32[16,1024]{1,0:T(8,128)S(1)} %get-tuple-element.23), kind=kLoop, calls=%fused_computation.4 | loop fusion | flops 3145728 | bytes 8519680 | tf_op jit(solution)/shard_map/sub | solution.py:122
  55.9 0.5 copy.6
  56.4 0.5 copy.5
  56.9 1.0 %bitcast_reduce_fusion = (f32[16,32,128]{2,1,0:T(8,128)S(1)}, f32[16,32,128]{2,1,0:T(8,128)S(1)}) fusion(f32[16,32,8,128]{3,2,1,0:T(8,128)S(1)} %bitcast.26, f32[16,32,8,128]{3,2,1,0:T(8,128)S(1)} %bitcast.27), kind=kLoop, calls=%fused_computation.2 | loop fusion | flops 917504 | bytes 4718592 | tf_op jit(solution)/shard_map/reduce_sum | solution.py:121
  58.0 0.1 reduce_sum.68
  58.1 0.1 reduce_sum.69
  58.3 0.9 %collective-permute-start.4 = (f32[32,32]{0,1:T(8,128)S(1)}, f32[32,32]{0,1:T(8,128)S(1)}, u32[]{:S(2)}, u32[]{:S(2)}) collective-permute-start(f32[32,32]{0,1:T(8,128)S(1)} %maximum_multiply_fusion), channel_id=1, source_target_pairs={{0,2},{1,3},{2,0},{3,1},{4,6},{5,7},{6,4},{7,5},{8,10},{9,11},{10,... | collective-permute-start | bytes 12296 | tf_op jit(solution)/shard_map/ppermute | solution.py:42
  59.1 2.6 %collective-permute-start.5 = (f32[32,32]{0,1:T(8,128)S(1)}, f32[32,32]{0,1:T(8,128)S(1)}, u32[]{:S(2)}, u32[]{:S(2)}) collective-permute-start(f32[32,32]{0,1:T(8,128)S(1)} %maximum_multiply_fusion), channel_id=1, source_target_pairs={{0,3},{1,0},{2,1},{3,2},{4,7},{5,4},{6,5},{7,6},{8,11},{9,8},{10,9... | collective-permute-start | bytes 12296 | tf_op jit(solution)/shard_map/ppermute | solution.py:42
  61.7 1.0 %collective-permute-start.3 = (f32[32,32]{0,1:T(8,128)S(1)}, f32[32,32]{0,1:T(8,128)S(1)}, u32[]{:S(2)}, u32[]{:S(2)}) collective-permute-start(f32[32,32]{0,1:T(8,128)S(1)} %maximum_multiply_fusion), channel_id=1, source_target_pairs={{0,1},{1,2},{2,3},{3,0},{4,5},{5,6},{6,7},{7,4},{8,9},{9,10},{10,1... | collective-permute-start | bytes 12296 | tf_op jit(solution)/shard_map/ppermute | solution.py:42
  62.7 2.0 %collective-permute-done.5 = f32[32,32]{0,1:T(8,128)S(1)} collective-permute-done((f32[32,32]{0,1:T(8,128)S(1)}, f32[32,32]{0,1:T(8,128)S(1)}, u32[]{:S(2)}, u32[]{:S(2)}) %collective-permute-start.5) | collective-permute-done | bytes 4128 | tf_op jit(solution)/shard_map/ppermute | solution.py:42
  64.6 0.8 %convolution_convert_fusion = bf16[32,1024]{1,0:T(8,128)(2,1)} fusion(bf16[1024,16]{0,1:T(8,128)(2,1)S(1)} %get-tuple-element.28, bf16[1024,16]{0,1:T(8,128)(2,1)S(1)} %get-tuple-element.27, f32[32,32]{0,1:T(8,128)S(1)} %collective-permute-done.5, f32[32,32]{0,1:T(8,128)S(1)} %collective-permute-done.4, f32[32,32]{0,1:T(8,128)S(1)} %collective-permute-done.3, ...), kind=kOutput, calls=%fused_computation.18 | convolution fusion | flops 2267136 | bytes 147456 | tf_op jit(solution)/shard_map/dot_general | solution.py:130
  (20 shorter events, 0.2 us)
Async XLA Ops:
  0.0 6.8 %copy-start = (s32[32,4096]{1,0:T(8,128)S(1)}, s32[32,4096]{1,0:T(8,128)}, u32[]{:S(2)}) copy-start(s32[32,4096]{1,0:T(8,128)} %param.6) | copy-start | bytes 1572868
  1.9 8.9 %collective-permute-start.2 = (f32[32,32]{0,1:T(8,128)S(1)}, f32[32,32]{0,1:T(8,128)S(1)}, u32[]{:S(2)}, u32[]{:S(2)}) collective-permute-start(f32[32,32]{0,1:T(8,128)S(1)} %convolution_bitcast_fusion), channel_id=1, source_target_pairs={{0,3},{1,0},{2,1},{3,2},{4,7},{5,4},{6,5},{7,6},{8,11},{9,8},{10,9... | collective-permute-start | bytes 12296 | tf_op jit(solution)/shard_map/ppermute | solution.py:42
  5.1 5.6 %collective-permute-start.1 = (f32[32,32]{0,1:T(8,128)S(1)}, f32[32,32]{0,1:T(8,128)S(1)}, u32[]{:S(2)}, u32[]{:S(2)}) collective-permute-start(f32[32,32]{0,1:T(8,128)S(1)} %convolution_bitcast_fusion), channel_id=1, source_target_pairs={{0,2},{1,3},{2,0},{3,1},{4,6},{5,7},{6,4},{7,5},{8,10},{9,11},{10,... | collective-permute-start | bytes 12296 | tf_op jit(solution)/shard_map/ppermute | solution.py:42
  5.1 5.6 %collective-permute-start = (f32[32,32]{0,1:T(8,128)S(1)}, f32[32,32]{0,1:T(8,128)S(1)}, u32[]{:S(2)}, u32[]{:S(2)}) collective-permute-start(f32[32,32]{0,1:T(8,128)S(1)} %convolution_bitcast_fusion), channel_id=1, source_target_pairs={{0,1},{1,2},{2,3},{3,0},{4,5},{5,6},{6,7},{7,4},{8,9},{9,10},{10,1... | collective-permute-start | bytes 12296 | tf_op jit(solution)/shard_map/ppermute | solution.py:42
  10.0 2.2 %copy-start.1 = (f32[16,32,1024]{2,1,0:T(8,128)}, f32[16,32,1024]{2,1,0:T(8,128)S(1)}, u32[]{:S(2)}) copy-start(f32[16,32,1024]{2,1,0:T(8,128)S(1)} %get-tuple-element.11) | copy-start | bytes 6291460
  58.3 4.4 %collective-permute-start.4 = (f32[32,32]{0,1:T(8,128)S(1)}, f32[32,32]{0,1:T(8,128)S(1)}, u32[]{:S(2)}, u32[]{:S(2)}) collective-permute-start(f32[32,32]{0,1:T(8,128)S(1)} %maximum_multiply_fusion), channel_id=1, source_target_pairs={{0,2},{1,3},{2,0},{3,1},{4,6},{5,7},{6,4},{7,5},{8,10},{9,11},{10,... | collective-permute-start | bytes 12296 | tf_op jit(solution)/shard_map/ppermute | solution.py:42
  59.1 5.5 %collective-permute-start.5 = (f32[32,32]{0,1:T(8,128)S(1)}, f32[32,32]{0,1:T(8,128)S(1)}, u32[]{:S(2)}, u32[]{:S(2)}) collective-permute-start(f32[32,32]{0,1:T(8,128)S(1)} %maximum_multiply_fusion), channel_id=1, source_target_pairs={{0,3},{1,0},{2,1},{3,2},{4,7},{5,4},{6,5},{7,6},{8,11},{9,8},{10,9... | collective-permute-start | bytes 12296 | tf_op jit(solution)/shard_map/ppermute | solution.py:42
  61.7 2.9 %collective-permute-start.3 = (f32[32,32]{0,1:T(8,128)S(1)}, f32[32,32]{0,1:T(8,128)S(1)}, u32[]{:S(2)}, u32[]{:S(2)}) collective-permute-start(f32[32,32]{0,1:T(8,128)S(1)} %maximum_multiply_fusion), channel_id=1, source_target_pairs={{0,1},{1,2},{2,3},{3,0},{4,5},{5,6},{6,7},{7,4},{8,9},{9,10},{10,1... | collective-permute-start | bytes 12296 | tf_op jit(solution)/shard_map/ppermute | solution.py:42

commit v24 on v19

--- a/solution.py
+++ b/solution.py
@@ -101,7 +101,7 @@
     count = lax.axis_size(SENS_AXES)
     parts = steered.reshape(count, steered.size // count)
     width = parts.shape[1]
-    own_weight = (2.0 * steer_scale) * lax.dynamic_slice_in_dim(
+    own_weight = (2.0 * steer_scale * steer_scale) * lax.dynamic_slice_in_dim(
         map_adjoint, position * scan_share, scan_share, 0
     )
     parts, own_weight = lax.optimization_barrier((parts, own_weight))
@@ -115,7 +115,7 @@
 
     back_real = jnp.sum(bar_real[:, None, :] * cosine + bar_imag[:, None, :] * sine_part, axis=2)
     back_imag = jnp.sum(bar_imag[:, None, :] * cosine - bar_real[:, None, :] * sine_part, axis=2)
-    back = jnp.concatenate([back_real.T, back_imag.T], 1) * steer_scale
+    back = jnp.concatenate([back_real.T, back_imag.T], 1)
     back = ring_sum(back, "grp")
     adjoint = back.astype(jnp.bfloat16)
     local_part = lax.dot_general(

time: 63.6 us -> 63.6 us (level)
  no operation moved by 1% of the time
where the time goes in v24:
time: 63.6 us; the launch traced here: 63.3 us
  blocking collectives  40.8 us (64%)
  starting transfers between devices  9.35 us (15%)
  other arithmetic  9.04 us (14%)
  waiting for transfers between devices  1.97 us (3%)
  matrix products  1.79 us (3%)
    all_to_all x1, blocking collectives, on_device(): moved = lax.all_to_all(parts, SENS_AXES, 0, 0, tiled=True)  25.3 us
    all_to_all x1, blocking collectives, on_device(): lax.all_to_all(copies, SENS_AXES, 0, 0, tiled=True).reshape(steered.shape)  15.4 us
    ppermute x6, starting transfers between devices, shifted(): lax.ppermute(x, axis, [(j, (j + shift) % count) for j in range(count)])  9.35 us
    select_n x1, other arithmetic, circle_point(): sine = jnp.where(nearest & 2 != 0, -sine, sine)  3.16 us
    reduce_sum x1, other arithmetic, on_device(): jnp.sum(bar_real[:, None, :] * cosine + bar_imag[:, None, :] * sine_part,...  2.38 us
    ppermute x6, waiting for transfers between devices, shifted(): lax.ppermute(x, axis, [(j, (j + shift) % count) for j in range(count)])  1.97 us
    reduce_sum x1, other arithmetic, on_device(): jnp.sum(real_t[:, :, None] * cosine - imag_t[:, :, None] * sine_part, axi...  1.42 us
  transfers between devices with their start and end apart: 6, of which 1 were waited for; matrix products, arithmetic and copies ran while one was open for 6% of the time, Pallas kernels for 0%

profile of v24, /device:TPU:1, one launch (start us, length us, event | category | flops | bytes accessed | tf_op | source)
XLA Modules:
  0.0 63.3 jit_solution(14458188546084386374)
XLA Ops:
  0.0 0.9 %fusion.3 = (bf16[1024,16]{0,1:T(8,128)(2,1)S(1)}, bf16[1024,16]{0,1:T(8,128)(2,1)S(1)}) fusion(s32[16]{0:T(128)} %param.5, s32[1024]{0:T(1024)S(1)} %iota_add_fusion), kind=kLoop, calls=%fused_computation.22 | loop fusion | flops 671744 | bytes 69696 | tf_op jit(solution)/shard_map/convert
  0.9 1.0 %convolution_bitcast_fusion = f32[32,32]{0,1:T(8,128)S(1)} fusion(bf16[32,1024]{1,0:T(8,128)(2,1)} %param.4, bf16[1024,16]{0,1:T(8,128)(2,1)S(1)} %get-tuple-element.24, bf16[1024,16]{0,1:T(8,128)(2,1)S(1)} %get-tuple-element.23), kind=kOutput, calls=%fused_computation.17 | convolution fusion | flops 2228224 | bytes 135168 | tf_op jit(solution)/shard_map/dot_general | solution.py:86
  1.9 3.2 %collective-permute-start.2 = (f32[32,32]{0,1:T(8,128)S(1)}, f32[32,32]{0,1:T(8,128)S(1)}, u32[]{:S(2)}, u32[]{:S(2)}) collective-permute-start(f32[32,32]{0,1:T(8,128)S(1)} %convolution_bitcast_fusion), channel_id=1, source_target_pairs={{0,3},{1,0},{2,1},{3,2},{4,7},{5,4},{6,5},{7,6},{8,11},{9,8},{10,9... | collective-permute-start | bytes 12296 | tf_op jit(solution)/shard_map/ppermute | solution.py:42
  5.1 1.7 %collective-permute-start = (f32[32,32]{0,1:T(8,128)S(1)}, f32[32,32]{0,1:T(8,128)S(1)}, u32[]{:S(2)}, u32[]{:S(2)}) collective-permute-start(f32[32,32]{0,1:T(8,128)S(1)} %convolution_bitcast_fusion), channel_id=1, source_target_pairs={{0,1},{1,2},{2,3},{3,0},{4,5},{5,6},{6,7},{7,4},{8,9},{9,10},{10,1... | collective-permute-start | bytes 12296 | tf_op jit(solution)/shard_map/ppermute | solution.py:42
  6.8 3.2 %negate_select_fusion = (f32[16,32,1024]{2,1,0:T(8,128)S(1)}, f32[16,32,1024]{2,1,0:T(8,128)S(1)}) fusion(s32[32,1024]{1,0:T(8,128)S(1)} %constant_dynamic-slice_fusion, s32[16]{0:T(128)} %param.5), kind=kLoop, calls=%fused_computation | loop fusion | flops 18874368 | bytes 4325440 | tf_op jit(solution)/shard_map/jit(_where)/select_n | solution.py:35
  10.0 0.7 %dynamic-slice_multiply_fusion = f32[1024]{0:T(1024)S(1)} fusion(f32[4096]{0:T(1024)} %param.7, s32[]{:T(128)S(6)} %select_n.34), kind=kLoop, calls=%fused_computation.45 | loop fusion | flops 1024 | bytes 8196 | tf_op jit(solution)/shard_map/mul | solution.py:104
  10.7 0.0 collective-permute-done.2
  10.7 0.0 collective-permute-done.1
  10.7 0.0 collective-permute-done
  10.8 1.4 %subtract_reduce_fusion.1 = (f32[16,1024]{1,0:T(8,128)S(1)}, f32[16,1024]{1,0:T(8,128)S(1)}) fusion(f32[16,32,1024]{2,1,0:T(8,128)S(1)} %get-tuple-element.10, f32[16,32,1024]{2,1,0:T(8,128)S(1)} %get-tuple-element.9, f32[16,32]{1,0:T(8,128)S(1)} %get-tuple-element.22, f32[16,32]{1,0:T(8,128)S(1)} %get-tuple-element.21), kind=kLoop, calls=%fused_computation.5 | loop fusion | flops 4161536 | bytes 4329472 | tf_op jit(solution)/shard_map/reduce_sum | solution.py:95
  12.2 0.1 all_to_all.10
  12.3 25.3 %all_to_all.15 = f32[64,1,512]{2,1,0:T(1,128)S(1)} all-to-all(f32[64,1,512]{2,1,0:T(1,128)S(1)} %all_to_all.10), channel_id=1, replica_groups=mesh['sx'=4,'sz'=4,'sy'=4,'grp'=4] {'sx','sz','sy'}, dimensions={0} | all-to-all | bytes 262144 | tf_op jit(solution)/shard_map/all_to_all | solution.py:108
  37.7 0.1 reduce_sum.47
  37.8 0.1 broadcast_in_dim.2
  37.9 15.4 %all_to_all.16 = f32[64,1,512]{2,1,0:T(1,128)S(1)} all-to-all(f32[64,1,512]{2,1,0:T(1,128)S(1)} %broadcast_in_dim.2), channel_id=1, replica_groups=mesh['sx'=4,'sz'=4,'sy'=4,'grp'=4] {'sx','sz','sy'}, dimensions={0} | all-to-all | bytes 262144 | tf_op jit(solution)/shard_map/all_to_all | solution.py:111
  53.3 0.3 reduce.1
  53.7 2.4 %add_reduce_fusion = (f32[16,32]{1,0:T(8,128)S(1)}, f32[16,32]{1,0:T(8,128)S(1)}) fusion(f32[16,32,1024]{2,1,0:T(8,128)S(1)} %get-tuple-element.10, f32[16,32,1024]{2,1,0:T(8,128)} %copy-done.1, f32[16,1024]{1,0:T(8,128)S(1)} %get-tuple-element.20, f32[16,1024]{1,0:T(8,128)S(1)} %get-tuple-element.19), kind=kLoop, calls=%fused_computation.3 | loop fusion | flops 4193280 | bytes 4329472 | tf_op jit(solution)/shard_map/reduce_sum | solution.py:116
  56.1 0.9 %collective-permute-start.4 = (f32[32,32]{0,1:T(8,128)S(1)}, f32[32,32]{0,1:T(8,128)S(1)}, u32[]{:S(2)}, u32[]{:S(2)}) collective-permute-start(f32[32,32]{0,1:T(8,128)S(1)} %pad_maximum_fusion.4), channel_id=1, source_target_pairs={{0,2},{1,3},{2,0},{3,1},{4,6},{5,7},{6,4},{7,5},{8,10},{9,11},{10,... | collective-permute-start | bytes 12296 | tf_op jit(solution)/shard_map/ppermute | solution.py:42
  57.0 2.6 %collective-permute-start.5 = (f32[32,32]{0,1:T(8,128)S(1)}, f32[32,32]{0,1:T(8,128)S(1)}, u32[]{:S(2)}, u32[]{:S(2)}) collective-permute-start(f32[32,32]{0,1:T(8,128)S(1)} %pad_maximum_fusion.4), channel_id=1, source_target_pairs={{0,3},{1,0},{2,1},{3,2},{4,7},{5,4},{6,5},{7,6},{8,11},{9,8},{10,9... | collective-permute-start | bytes 12296 | tf_op jit(solution)/shard_map/ppermute | solution.py:42
  59.5 1.0 %collective-permute-start.3 = (f32[32,32]{0,1:T(8,128)S(1)}, f32[32,32]{0,1:T(8,128)S(1)}, u32[]{:S(2)}, u32[]{:S(2)}) collective-permute-start(f32[32,32]{0,1:T(8,128)S(1)} %pad_maximum_fusion.4), channel_id=1, source_target_pairs={{0,1},{1,2},{2,3},{3,0},{4,5},{5,6},{6,7},{7,4},{8,9},{9,10},{10,1... | collective-permute-start | bytes 12296 | tf_op jit(solution)/shard_map/ppermute | solution.py:42
  60.5 0.0 collective-permute-done.4
  60.5 2.0 %collective-permute-done.5 = f32[32,32]{0,1:T(8,128)S(1)} collective-permute-done((f32[32,32]{0,1:T(8,128)S(1)}, f32[32,32]{0,1:T(8,128)S(1)}, u32[]{:S(2)}, u32[]{:S(2)}) %collective-permute-start.5) | collective-permute-done | bytes 4128 | tf_op jit(solution)/shard_map/ppermute | solution.py:42
  62.5 0.0 collective-permute-done.3
  62.5 0.8 %convolution_convert_fusion = bf16[32,1024]{1,0:T(8,128)(2,1)} fusion(bf16[1024,16]{0,1:T(8,128)(2,1)S(1)} %get-tuple-element.24, bf16[1024,16]{0,1:T(8,128)(2,1)S(1)} %get-tuple-element.23, f32[32,32]{0,1:T(8,128)S(1)} %collective-permute-done.5, f32[32,32]{0,1:T(8,128)S(1)} %collective-permute-done.4, f32[32,32]{0,1:T(8,128)S(1)} %collective-permute-done.3, ...), kind=kOutput, calls=%fused_computation.16 | convolution fusion | flops 2266112 | bytes 147456 | tf_op jit(solution)/shard_map/dot_general | solution.py:121
  (15 shorter events, 0.1 us)
Async XLA Ops:
  0.0 6.8 %copy-start = (s32[32,4096]{1,0:T(8,128)S(1)}, s32[32,4096]{1,0:T(8,128)}, u32[]{:S(2)}) copy-start(s32[32,4096]{1,0:T(8,128)} %param.6) | copy-start | bytes 1572868
  1.9 8.9 %collective-permute-start.2 = (f32[32,32]{0,1:T(8,128)S(1)}, f32[32,32]{0,1:T(8,128)S(1)}, u32[]{:S(2)}, u32[]{:S(2)}) collective-permute-start(f32[32,32]{0,1:T(8,128)S(1)} %convolution_bitcast_fusion), channel_id=1, source_target_pairs={{0,3},{1,0},{2,1},{3,2},{4,7},{5,4},{6,5},{7,6},{8,11},{9,8},{10,9... | collective-permute-start | bytes 12296 | tf_op jit(solution)/shard_map/ppermute | solution.py:42
  5.1 5.6 %collective-permute-start.1 = (f32[32,32]{0,1:T(8,128)S(1)}, f32[32,32]{0,1:T(8,128)S(1)}, u32[]{:S(2)}, u32[]{:S(2)}) collective-permute-start(f32[32,32]{0,1:T(8,128)S(1)} %convolution_bitcast_fusion), channel_id=1, source_target_pairs={{0,2},{1,3},{2,0},{3,1},{4,6},{5,7},{6,4},{7,5},{8,10},{9,11},{10,... | collective-permute-start | bytes 12296 | tf_op jit(solution)/shard_map/ppermute | solution.py:42
  5.1 5.6 %collective-permute-start = (f32[32,32]{0,1:T(8,128)S(1)}, f32[32,32]{0,1:T(8,128)S(1)}, u32[]{:S(2)}, u32[]{:S(2)}) collective-permute-start(f32[32,32]{0,1:T(8,128)S(1)} %convolution_bitcast_fusion), channel_id=1, source_target_pairs={{0,1},{1,2},{2,3},{3,0},{4,5},{5,6},{6,7},{7,4},{8,9},{9,10},{10,1... | collective-permute-start | bytes 12296 | tf_op jit(solution)/shard_map/ppermute | solution.py:42
  10.0 2.2 %copy-start.1 = (f32[16,32,1024]{2,1,0:T(8,128)}, f32[16,32,1024]{2,1,0:T(8,128)S(1)}, u32[]{:S(2)}) copy-start(f32[16,32,1024]{2,1,0:T(8,128)S(1)} %get-tuple-element.9) | copy-start | bytes 6291460
  56.1 4.4 %collective-permute-start.4 = (f32[32,32]{0,1:T(8,128)S(1)}, f32[32,32]{0,1:T(8,128)S(1)}, u32[]{:S(2)}, u32[]{:S(2)}) collective-permute-start(f32[32,32]{0,1:T(8,128)S(1)} %pad_maximum_fusion.4), channel_id=1, source_target_pairs={{0,2},{1,3},{2,0},{3,1},{4,6},{5,7},{6,4},{7,5},{8,10},{9,11},{10,... | collective-permute-start | bytes 12296 | tf_op jit(solution)/shard_map/ppermute | solution.py:42
  57.0 5.5 %collective-permute-start.5 = (f32[32,32]{0,1:T(8,128)S(1)}, f32[32,32]{0,1:T(8,128)S(1)}, u32[]{:S(2)}, u32[]{:S(2)}) collective-permute-start(f32[32,32]{0,1:T(8,128)S(1)} %pad_maximum_fusion.4), channel_id=1, source_target_pairs={{0,3},{1,0},{2,1},{3,2},{4,7},{5,4},{6,5},{7,6},{8,11},{9,8},{10,9... | collective-permute-start | bytes 12296 | tf_op jit(solution)/shard_map/ppermute | solution.py:42
  59.5 2.9 %collective-permute-start.3 = (f32[32,32]{0,1:T(8,128)S(1)}, f32[32,32]{0,1:T(8,128)S(1)}, u32[]{:S(2)}, u32[]{:S(2)}) collective-permute-start(f32[32,32]{0,1:T(8,128)S(1)} %pad_maximum_fusion.4), channel_id=1, source_target_pairs={{0,1},{1,2},{2,3},{3,0},{4,5},{5,6},{6,7},{7,4},{8,9},{9,10},{10,1... | collective-permute-start | bytes 12296 | tf_op jit(solution)/shard_map/ppermute | solution.py:42
